TPU v7x, 32 devices: a whole 2x2x4 slice. The times are simulated.
32 devices in a mesh: member: 2 (over y), lon: 4 (over z), lev: 4 (over x, core).
Axes of the slice: x: 2, y: 2, z: 4, core: 2. Of those that a mesh axis runs over, the one named last changes fastest.
Arguments:
- latent: bfloat16 [512, 8, 512], P('lev', 'member', 'lon'), parts along dimension 1, may hold values from -9 to 9
- att_gain: float32 [512], replicated, may hold values from 0.1 to 1.9
- qkv_weight: bfloat16 [3, 512, 512], P(None, 'lev'), may hold values from -0.25 to 0.25
- out_weight: bfloat16 [512, 512], P('lev'), may hold values from -0.25 to 0.25
- stencil_weight: float32 [2, 9, 512], P(None, None, 'lev'), may hold values from -2.5 to 2.5
- block_gain: float32 [2, 512], replicated, may hold values from 0.1 to 1.9
- up_weight: bfloat16 [2, 2048, 512], P(None, 'lev'), may hold values from -0.25 to 0.25
- down_weight: bfloat16 [2, 2048, 512], P(None, 'lev'), may hold values from -0.125 to 0.125
Outputs:
- decoded: bfloat16 [512, 8, 512], P('lev', 'member', 'lon'), parts along dimension 1
There are 2 independent parts, one for each index of `member`. A program takes and returns all parts, laid end to end along the dimension named above; an argument that names none is the same for every part. Nothing has to cross between parts.
All inputs are finite; a program needn't handle non-finite values.
Results may differ from a plain program's by a relative error of at most 0.017.
Values may be sent and summed in bfloat16 or wider, within the bound.
No kernel may reach another device: no remote copies, remote signals or barrier semaphores. Data moves between devices by JAX's collectives and lax.ppermute only.
A program may use at most 64 MiB of HBM per device.

v0:
```python
import math

import jax
import jax.numpy as jnp
from jax import lax
from jax.sharding import PartitionSpec as P

C = 512
H = 8
BLOCKS = 2


attention_scale = 24.0
band_start = 30.0
grid_step = 0.25
epsilon = 1e-06


def with_halo(array, sides, width):
    for axis, dim in sides:
        devices, length = (lax.axis_size(axis), array.shape[dim])
        up = [(i, (i + 1) % devices) for i in range(devices)]
        down = [(j, i) for i, j in up]
        last = lax.slice_in_dim(array, length - width, length, axis=dim)
        leading = lax.slice_in_dim(array, 0, width, axis=dim)
        before = lax.ppermute(last, axis, up)
        after = lax.ppermute(leading, axis, down)
        array = jnp.concatenate([before, array, after], axis=dim)
    return array


def secant_rows(count):
    rows = jnp.arange(count).astype(jnp.float32)
    return 1.0 / jnp.cos((band_start + grid_step * rows) * (math.pi / 180.0))


def norm_channels(values, gain):
    scale = lax.rsqrt(jnp.mean(values * values, axis=0, keepdims=True) + epsilon)
    return values * scale * gain[:, None, None]


def unit_heads(values):
    return values * lax.rsqrt(jnp.sum(values * values, axis=1, keepdims=True) + epsilon)


def gather_channels(values):
    return lax.all_gather(values, "lev", axis=0, tiled=True)


def spread_sum(weight, activation):
    return lax.psum_scatter(
        lax.dot_general(
            weight, activation, (((0,), (0,)), ((), ())), preferred_element_type=jnp.float32
        ).astype(jnp.bfloat16),
        "lev",
        scatter_dimension=0,
        tiled=True,
    ).astype(jnp.float32)


def make_fold(queries, pieces):
    key_part, value_part = pieces
    scores = (
        jnp.einsum("hdri,hdrj->hrij", queries, key_part, preferred_element_type=jnp.float32)
        * attention_scale
    )
    weights = jnp.exp(scores)
    numerator = jnp.einsum(
        "hrij,hdrj->hdri",
        weights.astype(jnp.bfloat16),
        value_part,
        preferred_element_type=jnp.float32,
    )
    return (numerator, jnp.sum(weights, axis=3))


def block_apply(extended, block_index, stencil_weight, block_gain, up_weight, down_weight):
    lat_rows = extended.shape[1]
    out_cols = extended.shape[2] - 2
    secants = secant_rows(lat_rows)[None, :, None]
    padded = jnp.pad(extended.astype(jnp.float32), ((0, 0), (1, 1), (0, 0)))
    tap_weights = stencil_weight[block_index]
    stencil_sum = jnp.zeros((extended.shape[0], lat_rows, out_cols), jnp.float32)
    for row_step in (-1, 0, 1):
        for col_step in (-1, 0, 1):
            shifted = padded[
                :, 1 + row_step : 1 + row_step + lat_rows, 1 + col_step : 1 + col_step + out_cols
            ]
            tap_row = tap_weights[3 * (row_step + 1) + col_step + 1][:, None, None]
            if col_step != 0:
                stencil_sum = stencil_sum + tap_row * secants * shifted
            else:
                stencil_sum = stencil_sum + tap_row * shifted
    smoothed = stencil_sum.astype(jnp.bfloat16)
    full_channels = gather_channels(smoothed)
    block_normed = norm_channels(full_channels.astype(jnp.float32), block_gain[block_index]).astype(
        jnp.bfloat16
    )
    block_normed = block_normed.reshape(full_channels.shape[0], -1)
    hidden = jax.nn.gelu(
        jnp.dot(up_weight[block_index], block_normed, preferred_element_type=jnp.float32)
    ).astype(jnp.bfloat16)
    update = spread_sum(down_weight[block_index], hidden)
    center = extended[:, :, 1:-1]
    return (center.astype(jnp.float32) + update.reshape(center.shape)).astype(jnp.bfloat16)


def per_device(
    latent, att_gain, qkv_weight, out_weight, stencil_weight, block_gain, up_weight, down_weight
):
    ch_local, lat_rows, columns = latent.shape
    head_size = C // H
    heads_local = qkv_weight.shape[1] // head_size
    gathered = gather_channels(latent)
    normed = norm_channels(gathered.astype(jnp.float32), att_gain).astype(jnp.bfloat16)
    projected = jnp.einsum("koc,crw->korw", qkv_weight, normed, preferred_element_type=jnp.float32)
    projected = projected.reshape(3, heads_local, head_size, lat_rows, columns)
    queries = unit_heads(projected[0]).astype(jnp.bfloat16)
    key_rows = unit_heads(projected[1]).astype(jnp.bfloat16)
    value_rows = projected[2].astype(jnp.bfloat16)
    numerator, denominator = make_fold(
        queries,
        (
            lax.all_gather(key_rows, "lon", axis=3, tiled=True),
            lax.all_gather(value_rows, "lon", axis=3, tiled=True),
        ),
    )
    attended = (numerator / denominator[:, None]).astype(jnp.bfloat16)
    update = spread_sum(out_weight, attended.reshape(ch_local, -1))
    latent_state = (latent.astype(jnp.float32) + update.reshape(latent.shape)).astype(jnp.bfloat16)
    current = latent_state
    for block_index in range(BLOCKS):
        extended = with_halo(current, (("lon", 2),), 1)
        current = block_apply(
            extended, block_index, stencil_weight, block_gain, up_weight, down_weight
        )
    return current


def solution(mesh):
    placed = (
        P("lev", "member", "lon"),
        P(),
        P(None, "lev", None),
        P("lev", None),
        P(None, None, "lev"),
        P(),
        P(None, "lev", None),
        P(None, "lev", None),
    )
    return jax.shard_map(
        per_device, mesh=mesh, in_specs=placed, out_specs=P("lev", "member", "lon"), check_vma=False
    )
```

profile of v0, /device:TPU:0, one launch (start us, length us, event | category | flops | bytes accessed | tf_op | source)
XLA Modules:
  0.0 174.2 jit_solution(6126228288966084654)
XLA Ops:
  6.5 0.0 copy-start
  6.5 0.0 reduce-scatter.10.cloned.1.call-start
  6.5 8.9 %all_gather.15 = bf16[512,4,128]{2,1,0:T(4,128)(2,1)S(1)} all-gather(bf16[128,4,128]{2,1,0:T(4,128)(2,1)} %param.8), channel_id=1, replica_groups=mesh['member'=2,'lon'=4,'lev'=4] {'lev'}, dimensions={0}, use_global_device_ids=true | all-gather | bytes 655360 | tf_op jit(solution)/shard_map/all_gather | solution.py:47
  15.5 0.5 fusion.7
  16.0 1.9 %fusion.34 = bf16[512,4,128,1]{2,1,0,3:T(4,128)(2,1)S(1)} fusion(bf16[512,4,128]{2,1,0:T(4,128)(2,1)S(1)} %all_gather.15, f32[512]{0:T(512)} %param.9, f32[4,128]{1,0:T(4,128)S(1)} %add_rsqrt_fusion.4), kind=kLoop, calls=%fused_computation.61 | loop fusion | flops 1048576 | bytes 1052672 | tf_op jit(solution)/shard_map/convert_element_type | solution.py:115
  18.0 0.0 copy-done
  18.0 0.4 convolution_bitcast_fusion.2
  18.5 15.7 %all_gather.16 = bf16[2,64,4,512]{3,1,2,0:T(8,128)(2,1)S(1)} all-gather(bf16[2,64,4,128]{3,1,2,0:T(8,128)(2,1)S(1)} %copy.25), channel_id=1, replica_groups=mesh['member'=2,'lon'=4,'lev'=4] {'lon'}, dimensions={3}, use_global_device_ids=true | all-gather | bytes 655360 | tf_op jit(solution)/shard_map/all_gather | solution.py:125
  34.2 15.2 %all_gather.17 = bf16[2,64,4,512]{3,1,2,0:T(8,128)(2,1)S(1)} all-gather(bf16[2,64,4,128]{3,1,2,0:T(8,128)(2,1)S(1)} %fusion.93), channel_id=1, replica_groups=mesh['member'=2,'lon'=4,'lev'=4] {'lon'}, dimensions={3}, use_global_device_ids=true | all-gather | bytes 655360 | tf_op jit(solution)/shard_map/all_gather | solution.py:124
  49.5 0.6 fusion
  50.1 0.0 copy-start.3
  50.1 0.5 fusion.6
  50.6 0.0 copy-start.1
  50.6 0.1 copy.29
  50.7 0.3 copy-done.2
  51.0 0.3 fusion.2
  51.3 0.0 copy-start.4
  51.3 1.0 copy.38
  52.3 0.0 reduce-scatter.10.cloned.1.call-update
  52.4 0.0 reduce-scatter.12.cloned.1.call-start
  52.5 0.0 copy-done.3
  52.5 0.3 broadcast_multiply_fusion.5
  52.8 19.7 %reduce-scatter.10.cloned.1.call-done = bf16[128,512]{1,0:T(8,128)(2,1)} async-done(((bf16[512,512]{1,0:T(8,128)(2,1)}), bf16[128,512]{1,0:T(8,128)(2,1)}) %reduce-scatter.10.cloned.1.call-update) | async-done | bytes 131088
  72.5 1.0 copy.39
  73.5 0.1 copy.30
  73.6 0.0 copy-done.1
  73.6 0.1 add_convert_fusion.2
  73.7 0.1 fusion.111
  73.9 3.4 %collective-permute-start.1 = (bf16[128,4,1]{2,1,0:T(4,128)(2,1)S(1)}, bf16[128,4,1]{2,1,0:T(4,128)(2,1)S(1)}, u32[]{:S(2)}, u32[]{:S(2)}) collective-permute-start(bf16[128,4,1]{2,1,0:T(4,128)(2,1)S(1)} %get-tuple-element.10), channel_id=1, source_target_pairs={{4,0},{8,4},{12,8},{0,12},{5,1},{9,5},{13,9},{1,13},{6,2},{10,6},{... | collective-permute-start | bytes 3080 | tf_op jit(solution)/shard_map/ppermute | solution.py:27
  77.3 0.0 collective-permute-start
  77.3 0.0 copy-done.4
  77.3 3.9 %collective-permute-done.1 = bf16[128,4,1]{2,1,0:T(4,128)(2,1)S(1)} collective-permute-done((bf16[128,4,1]{2,1,0:T(4,128)(2,1)S(1)}, bf16[128,4,1]{2,1,0:T(4,128)(2,1)S(1)}, u32[]{:S(2)}, u32[]{:S(2)}) %collective-permute-start.1) | collective-permute-done | bytes 1056 | tf_op jit(solution)/shard_map/ppermute | solution.py:27
  81.2 2.9 %collective-permute-done = bf16[128,4,1]{2,1,0:T(4,128)(2,1)S(1)} collective-permute-done((bf16[128,4,1]{2,1,0:T(4,128)(2,1)S(1)}, bf16[128,4,1]{2,1,0:T(4,128)(2,1)S(1)}, u32[]{:S(2)}, u32[]{:S(2)}) %collective-permute-start) | collective-permute-done | bytes 1056 | tf_op jit(solution)/shard_map/ppermute | solution.py:26
  84.0 0.4 maximum_convert_fusion
  84.4 0.0 copy-start.5
  84.4 2.4 %fusion.95 = bf16[128,4,128]{2,1,0:T(4,128)(2,1)S(1)} fusion(f32[128,4,130]{2,1,0:T(4,128)S(1)} %maximum_convert_fusion, f32[128,4]{1,0:T(8,128)S(1)} %get-tuple-element.36, f32[128]{0:T(128)S(1)} %get-tuple-element.19, f32[128,4]{1,0:T(8,128)S(1)} %get-tuple-element.35, f32[128,4]{1,0:T(8,128)S(1)} %get-tuple-element.34, f32[128]{0:T(128)S(1)} %get-tuple-element.22, ...), kind=kLoop, calls=%fused_computation.130 | loop fusion | flops 1179648 | bytes 1836544 | tf_op jit(solution)/shard_map/convert_element_type | solution.py:94
  86.8 6.5 %all_gather.18 = bf16[512,4,128]{2,1,0:T(4,128)(2,1)S(1)} all-gather(bf16[128,4,128]{2,1,0:T(4,128)(2,1)S(1)} %fusion.95), channel_id=1, replica_groups=mesh['member'=2,'lon'=4,'lev'=4] {'lev'}, dimensions={0}, use_global_device_ids=true | all-gather | bytes 655360 | tf_op jit(solution)/shard_map/all_gather | solution.py:47
  93.3 0.5 fusion.10
  93.8 1.5 fusion.12
  95.4 2.0 %fusion.3 = bf16[512,512]{0,1:T(8,128)(2,1)S(1)} fusion(bf16[64,8,4,128]{3,2,1,0:T(4,128)(2,1)S(1)} %bitcast.120, bf16[2,512,512]{2,1,0:T(8,128)(2,1)S(1)} %copy-done.5, bf16[2,512,512]{2,1,0:T(8,128)(2,1)} %param.14), kind=kOutput, calls=%fused_computation.30 | convolution fusion | flops 539492352 | bytes 2097152 | tf_op jit(solution)/shard_map/dot_general | solution.py:52
  97.3 1.0 copy.40
  98.3 0.0 reduce-scatter.12.cloned.1.call-update
  98.4 0.0 reduce-scatter.14.cloned.1.call-start
  98.4 20.6 %reduce-scatter.12.cloned.1.call-done = bf16[128,512]{1,0:T(8,128)(2,1)} async-done(((bf16[512,512]{1,0:T(8,128)(2,1)}), bf16[128,512]{1,0:T(8,128)(2,1)}) %reduce-scatter.12.cloned.1.call-update) | async-done | bytes 131088
  119.1 1.0 copy.41
  120.1 0.1 copy.36
  120.2 0.1 add_convert_fusion.1
  120.3 0.1 fusion.110
  120.5 3.4 %collective-permute-start.3 = (bf16[128,4,1]{2,1,0:T(4,128)(2,1)S(1)}, bf16[128,4,1]{2,1,0:T(4,128)(2,1)S(1)}, u32[]{:S(2)}, u32[]{:S(2)}) collective-permute-start(bf16[128,4,1]{2,1,0:T(4,128)(2,1)S(1)} %get-tuple-element.8), channel_id=1, source_target_pairs={{4,0},{8,4},{12,8},{0,12},{5,1},{9,5},{13,9},{1,13},{6,2},{10,6},{... | collective-permute-start | bytes 3080 | tf_op jit(solution)/shard_map/ppermute | solution.py:27
  123.9 0.0 collective-permute-start.2
  123.9 3.9 %collective-permute-done.3 = bf16[128,4,1]{2,1,0:T(4,128)(2,1)S(1)} collective-permute-done((bf16[128,4,1]{2,1,0:T(4,128)(2,1)S(1)}, bf16[128,4,1]{2,1,0:T(4,128)(2,1)S(1)}, u32[]{:S(2)}, u32[]{:S(2)}) %collective-permute-start.3) | collective-permute-done | bytes 1056 | tf_op jit(solution)/shard_map/ppermute | solution.py:27
  127.8 2.9 %collective-permute-done.2 = bf16[128,4,1]{2,1,0:T(4,128)(2,1)S(1)} collective-permute-done((bf16[128,4,1]{2,1,0:T(4,128)(2,1)S(1)}, bf16[128,4,1]{2,1,0:T(4,128)(2,1)S(1)}, u32[]{:S(2)}, u32[]{:S(2)}) %collective-permute-start.2) | collective-permute-done | bytes 1056 | tf_op jit(solution)/shard_map/ppermute | solution.py:26
  130.6 0.3 maximum_convert_fusion.1
  131.0 2.3 %fusion.94 = bf16[128,4,128]{2,1,0:T(4,128)(2,1)S(1)} fusion(f32[128,4,130]{2,1,0:T(4,128)S(1)} %maximum_convert_fusion.1, f32[128,4]{1,0:T(8,128)S(1)} %get-tuple-element.41, f32[128]{0:T(128)S(1)} %get-tuple-element.28, f32[128,4]{1,0:T(8,128)S(1)} %get-tuple-element.40, f32[128,4]{1,0:T(8,128)S(1)} %get-tuple-element.39, f32[128]{0:T(128)S(1)} %get-tuple-element.14, ...), kind=kLoop, calls=%fused_computation.129 | loop fusion | flops 1179648 | bytes 1836544 | tf_op jit(solution)/shard_map/convert_element_type | solution.py:94
  133.3 6.7 %all_gather.19 = bf16[512,4,128]{2,1,0:T(4,128)(2,1)S(1)} all-gather(bf16[128,4,128]{2,1,0:T(4,128)(2,1)S(1)} %fusion.94), channel_id=1, replica_groups=mesh['member'=2,'lon'=4,'lev'=4] {'lev'}, dimensions={0}, use_global_device_ids=true | all-gather | bytes 655360 | tf_op jit(solution)/shard_map/all_gather | solution.py:47
  140.0 0.5 fusion.13
  140.6 1.5 fusion.15
  142.1 2.0 %fusion.4 = bf16[512,512]{0,1:T(8,128)(2,1)S(1)} fusion(bf16[64,8,4,128]{3,2,1,0:T(4,128)(2,1)S(1)} %bitcast.121, bf16[2,512,512]{2,1,0:T(8,128)(2,1)S(1)} %copy-done.5, bf16[2,512,512]{2,1,0:T(8,128)(2,1)} %param.14), kind=kOutput, calls=%fused_computation.31 | convolution fusion | flops 539492352 | bytes 2097152 | tf_op jit(solution)/shard_map/dot_general | solution.py:52
  144.1 1.0 copy.42
  145.1 0.0 reduce-scatter.14.cloned.1.call-update
  145.1 20.7 %reduce-scatter.14.cloned.1.call-done = bf16[128,512]{1,0:T(8,128)(2,1)} async-done(((bf16[512,512]{1,0:T(8,128)(2,1)}), bf16[128,512]{1,0:T(8,128)(2,1)}) %reduce-scatter.14.cloned.1.call-update) | async-done | bytes 131088
  165.8 1.0 copy.43
  166.8 0.1 copy.37
  167.0 0.7 add_convert_fusion
  (17 shorter events, 0.3 us)
Async XLA Ops:
  6.5 11.5 %copy-start = (bf16[3,128,512]{2,1,0:T(8,128)(2,1)S(1)}, bf16[3,128,512]{2,1,0:T(8,128)(2,1)}, u32[]{:S(2)}) copy-start(bf16[3,128,512]{2,1,0:T(8,128)(2,1)} %param.10) | copy-start | bytes 1179652
  6.5 65.9 %reduce-scatter.10.cloned.1.call-start = ((), (), s32[]{:S(2)}) async-start(), calls=%async_computation.3 | async-start | bytes 655360
  50.1 0.9 copy-start.2
  50.1 2.4 %copy-start.3 = (f32[2,9,128]{2,0,1:T(2,128)S(1)}, f32[2,9,128]{2,0,1:T(2,128)}, u32[]{:S(2)}) copy-start(f32[2,9,128]{2,0,1:T(2,128)} %param.12) | copy-start | bytes 27652
  50.6 23.0 %copy-start.1 = (bf16[128,4,128]{2,1,0:T(4,128)(2,1)S(1)}, bf16[128,4,128]{2,1,0:T(4,128)(2,1)}, u32[]{:S(2)}) copy-start(bf16[128,4,128]{2,1,0:T(4,128)(2,1)} %param.8) | copy-start | bytes 393220
  51.3 25.9 %copy-start.4 = (f32[2,512]{1,0:T(2,128)S(1)}, f32[2,512]{1,0:T(2,128)}, u32[]{:S(2)}) copy-start(f32[2,512]{1,0:T(2,128)} %param.13) | copy-start | bytes 12292
  52.4 66.7 %reduce-scatter.12.cloned.1.call-start = ((), (), s32[]{:S(2)}) async-start(), calls=%async_computation.4 | async-start | bytes 655360
  73.9 7.3 %collective-permute-start.1 = (bf16[128,4,1]{2,1,0:T(4,128)(2,1)S(1)}, bf16[128,4,1]{2,1,0:T(4,128)(2,1)S(1)}, u32[]{:S(2)}, u32[]{:S(2)}) collective-permute-start(bf16[128,4,1]{2,1,0:T(4,128)(2,1)S(1)} %get-tuple-element.10), channel_id=1, source_target_pairs={{4,0},{8,4},{12,8},{0,12},{5,1},{9,5},{13,9},{1,13},{6,2},{10,6},{... | collective-permute-start | bytes 3080 | tf_op jit(solution)/shard_map/ppermute | solution.py:27
  77.3 6.8 %collective-permute-start = (bf16[128,4,1]{2,1,0:T(4,128)(2,1)S(1)}, bf16[128,4,1]{2,1,0:T(4,128)(2,1)S(1)}, u32[]{:S(2)}, u32[]{:S(2)}) collective-permute-start(bf16[128,4,1]{2,1,0:T(4,128)(2,1)S(1)} %get-tuple-element.9), channel_id=1, source_target_pairs={{0,4},{4,8},{8,12},{12,0},{1,5},{5,9},{9,13},{13,1},{2,6},{6,10},{... | collective-permute-start | bytes 3080 | tf_op jit(solution)/shard_map/ppermute | solution.py:26
  84.4 11.0 %copy-start.5 = (bf16[2,512,512]{2,1,0:T(8,128)(2,1)S(1)}, bf16[2,512,512]{2,1,0:T(8,128)(2,1)}, u32[]{:S(2)}) copy-start(bf16[2,512,512]{2,1,0:T(8,128)(2,1)} %param.15) | copy-start | bytes 3145732
  98.4 67.4 %reduce-scatter.14.cloned.1.call-start = ((), (), s32[]{:S(2)}) async-start(), calls=%async_computation.5 | async-start | bytes 655360
  120.5 7.3 %collective-permute-start.3 = (bf16[128,4,1]{2,1,0:T(4,128)(2,1)S(1)}, bf16[128,4,1]{2,1,0:T(4,128)(2,1)S(1)}, u32[]{:S(2)}, u32[]{:S(2)}) collective-permute-start(bf16[128,4,1]{2,1,0:T(4,128)(2,1)S(1)} %get-tuple-element.8), channel_id=1, source_target_pairs={{4,0},{8,4},{12,8},{0,12},{5,1},{9,5},{13,9},{1,13},{6,2},{10,6},{... | collective-permute-start | bytes 3080 | tf_op jit(solution)/shard_map/ppermute | solution.py:27
  123.9 6.8 %collective-permute-start.2 = (bf16[128,4,1]{2,1,0:T(4,128)(2,1)S(1)}, bf16[128,4,1]{2,1,0:T(4,128)(2,1)S(1)}, u32[]{:S(2)}, u32[]{:S(2)}) collective-permute-start(bf16[128,4,1]{2,1,0:T(4,128)(2,1)S(1)} %get-tuple-element.7), channel_id=1, source_target_pairs={{0,4},{4,8},{8,12},{12,0},{1,5},{5,9},{9,13},{13,1},{2,6},{6,10},{... | collective-permute-start | bytes 3080 | tf_op jit(solution)/shard_map/ppermute | solution.py:26
Sparse Core Ops, SparseCore 0:
  52.5 19.9 reduce-scatter.9
  98.5 20.5 reduce-scatter.11
  145.2 20.5 reduce-scatter.13
where the time goes:
time: 175 us; the launch traced here: 174 us
  waiting for transfers between devices  74.6 us (43%)
  blocking collectives  53 us (30%)
  between operations  13.4 us (8%)
  other arithmetic  13.3 us (8%)
  local copies, waits for them, and re-layouts  7.24 us (4%)
  starting transfers between devices  6.89 us (4%)
  matrix products  5.79 us (3%)
    unnamed x6, waiting for transfers between devices  61 us
    all_gather x3, blocking collectives, gather_channels(): return lax.all_gather(values, 'lev', axis=0, tiled=True)  22.1 us
    all_gather x1, blocking collectives, per_device(): lax.all_gather(value_rows, 'lon', axis=3, tiled=True)  15.7 us
    all_gather x1, blocking collectives, per_device(): lax.all_gather(key_rows, 'lon', axis=3, tiled=True)  15.2 us
    ppermute x2, waiting for transfers between devices, with_halo(): after = lax.ppermute(leading, axis, down)  7.8 us
    ppermute x2, starting transfers between devices, with_halo(): after = lax.ppermute(leading, axis, down)  6.79 us
    unnamed x18, local copies, waits for them, and re-layouts  6.36 us
    ppermute x2, waiting for transfers between devices, with_halo(): before = lax.ppermute(last, axis, up)  5.72 us
  transfers between devices with their start and end apart: 7, of which 7 were waited for; matrix products, arithmetic and copies ran while one was open for 0% of the time, Pallas kernels for 0%

commit v1 on v0

--- a/solution.py
+++ b/solution.py
@@ -47,15 +47,32 @@
     return lax.all_gather(values, "lev", axis=0, tiled=True)
 
 
+def scatter_sum(partial, axis):
+    devices = lax.axis_size(axis)
+    me = lax.axis_index(axis)
+    blocks = partial.reshape(devices, -1, *partial.shape[1:])
+    total = jnp.take(blocks, me, axis=0).astype(jnp.float32)
+    for shift in range(1, devices):
+        pairs = [(i, (i + shift) % devices) for i in range(devices)]
+        chunk = jnp.take(blocks, (me + shift) % devices, axis=0)
+        total = total + lax.ppermute(chunk, axis, pairs).astype(jnp.float32)
+    return total
+
+
 def spread_sum(weight, activation):
-    return lax.psum_scatter(
-        lax.dot_general(
-            weight, activation, (((0,), (0,)), ((), ())), preferred_element_type=jnp.float32
-        ).astype(jnp.bfloat16),
-        "lev",
-        scatter_dimension=0,
-        tiled=True,
-    ).astype(jnp.float32)
+    partial = lax.dot_general(
+        weight, activation, (((0,), (0,)), ((), ())), preferred_element_type=jnp.float32
+    ).astype(jnp.bfloat16)
+    return scatter_sum(partial, "lev")
+
+
+def gather_strips(values, axis):
+    devices = lax.axis_size(axis)
+    pieces = [values]
+    for shift in range(1, devices):
+        pairs = [(i, (i + shift) % devices) for i in range(devices)]
+        pieces.append(lax.ppermute(values, axis, pairs))
+    return jnp.concatenate(pieces, axis=-1)
 
 
 def make_fold(queries, pieces):
@@ -118,13 +135,8 @@
     queries = unit_heads(projected[0]).astype(jnp.bfloat16)
     key_rows = unit_heads(projected[1]).astype(jnp.bfloat16)
     value_rows = projected[2].astype(jnp.bfloat16)
-    numerator, denominator = make_fold(
-        queries,
-        (
-            lax.all_gather(key_rows, "lon", axis=3, tiled=True),
-            lax.all_gather(value_rows, "lon", axis=3, tiled=True),
-        ),
-    )
+    key_value = gather_strips(jnp.stack([key_rows, value_rows]), "lon")
+    numerator, denominator = make_fold(queries, (key_value[0], key_value[1]))
     attended = (numerator / denominator[:, None]).astype(jnp.bfloat16)
     update = spread_sum(out_weight, attended.reshape(ch_local, -1))
     latent_state = (latent.astype(jnp.float32) + update.reshape(latent.shape)).astype(jnp.bfloat16)

time: 175 us -> 113 us (0.65)
  waiting for transfers between devices: 74.6 us -> 43.8 us
  blocking collectives: 53 us -> 22.8 us
  starting transfers between devices: 6.89 us -> 24 us
  between operations: 13.4 us -> 0.42 us
  local copies, waits for them, and re-layouts: 7.24 us -> 1.01 us
    unnamed x6 -> x0, waiting for transfers between devices: 61 us -> none
    ppermute x0 -> x12, waiting for transfers between devices: none -> 32 us  [the longest x3 16.1 us: gather_strips(): pieces.append(lax.ppermute(values, axis, pairs))]
    all_gather x2 -> x0, blocking collectives: 30.9 us -> none  [the longest x1 15.7 us: per_device(): lax.all_gather(value_rows, 'lon', axis=3, tiled=True)]
    ppermute x0 -> x12, starting transfers between devices: none -> 12.9 us  [the longest x9 7.31 us: scatter_sum(): total = total + lax.ppermute(chunk, axis, pairs).astype(jnp.float32)]
    ppermute x2, starting transfers between devices: 0.01 us -> 6.62 us  [with_halo(): before = lax.ppermute(last, axis, up)]
    unnamed x18 -> x12, local copies, waits for them, and re-layouts: 6.36 us -> 0.31 us
    ppermute x2, waiting for transfers between devices: 7.8 us -> 3.45 us  [with_halo(): after = lax.ppermute(leading, axis, down)]
    ppermute x2, waiting for transfers between devices: 5.72 us -> 8.36 us  [with_halo(): before = lax.ppermute(last, axis, up)]
  transfers between devices with their start and end apart: 7 -> 16, of which waited for: 7 -> 15; matrix products, arithmetic and copies ran while one was open for 0% -> 0% of each run, Pallas kernels for 0% -> 0%
where the time goes in v1:
time: 113 us; the launch traced here: 112 us
  waiting for transfers between devices  43.8 us (39%)
  starting transfers between devices  24 us (21%)
  blocking collectives  22.8 us (20%)
  other arithmetic  13.9 us (12%)
  matrix products  5.92 us (5%)
    all_gather x3, blocking collectives, gather_channels(): return lax.all_gather(values, 'lev', axis=0, tiled=True)  22.8 us
    ppermute x3, waiting for transfers between devices, gather_strips(): pieces.append(lax.ppermute(values, axis, pairs))  16.1 us
    ppermute x9, waiting for transfers between devices, scatter_sum(): total = total + lax.ppermute(chunk, axis, pairs).astype(jnp.float32)  15.9 us
    ppermute x2, waiting for transfers between devices, with_halo(): before = lax.ppermute(last, axis, up)  8.36 us
    ppermute x9, starting transfers between devices, scatter_sum(): total = total + lax.ppermute(chunk, axis, pairs).astype(jnp.float32)  7.31 us
    ppermute x2, starting transfers between devices, with_halo(): before = lax.ppermute(last, axis, up)  6.62 us
    ppermute x3, starting transfers between devices, gather_strips(): pieces.append(lax.ppermute(values, axis, pairs))  5.57 us
    convert_element_type x2, other arithmetic, block_apply(): smoothed = stencil_sum.astype(jnp.bfloat16)  4.7 us
  transfers between devices with their start and end apart: 16, of which 15 were waited for; matrix products, arithmetic and copies ran while one was open for 0% of the time, Pallas kernels for 0%

profile of v1, /device:TPU:0, one launch (start us, length us, event | category | flops | bytes accessed | tf_op | source)
XLA Modules:
  0.0 111.8 jit_solution(14311635145778814326)
XLA Ops:
  0.0 8.9 %all_gather.9 = bf16[512,4,128]{2,1,0:T(4,128)(2,1)S(1)} all-gather(bf16[128,4,128]{2,1,0:T(4,128)(2,1)} %param.10), channel_id=1, replica_groups=mesh['member'=2,'lon'=4,'lev'=4] {'lev'}, dimensions={0}, use_global_device_ids=true | all-gather | bytes 655360 | tf_op jit(solution)/shard_map/all_gather | solution.py:47
  9.0 0.5 fusion.4
  9.5 1.9 %fusion.31 = bf16[512,4,128,1]{2,1,0,3:T(4,128)(2,1)S(1)} fusion(bf16[512,4,128]{2,1,0:T(4,128)(2,1)S(1)} %all_gather.9, f32[512]{0:T(512)} %param.11, f32[4,128]{1,0:T(4,128)S(1)} %add_rsqrt_fusion.4), kind=kLoop, calls=%fused_computation.59 | loop fusion | flops 1048576 | bytes 1052672 | tf_op jit(solution)/shard_map/convert_element_type | solution.py:132
  11.5 0.4 convolution_bitcast_fusion.2
  12.1 1.6 %collective-permute-start = (bf16[2,2,64,4,128]{4,2,3,1,0:T(8,128)(2,1)S(1)}, bf16[2,2,64,4,128]{4,2,3,1,0:T(8,128)(2,1)S(1)}, u32[]{:S(2)}, u32[]{:S(2)}) collective-permute-start(bf16[2,2,64,4,128]{4,2,3,1,0:T(8,128)(2,1)S(1)} %pad_maximum_fusion.1), channel_id=1, source_target_pairs={{0,4},{4,8},{8,12},{12,0},{1,5},{5,9},{9,13},{13,1},{2,6},{6,10},{... | collective-permute-start | bytes 786440 | tf_op jit(solution)/shard_map/ppermute | solution.py:74
  13.7 2.6 %collective-permute-start.1 = (bf16[2,2,64,4,128]{4,2,3,1,0:T(8,128)(2,1)S(1)}, bf16[2,2,64,4,128]{4,2,3,1,0:T(8,128)(2,1)S(1)}, u32[]{:S(2)}, u32[]{:S(2)}) collective-permute-start(bf16[2,2,64,4,128]{4,2,3,1,0:T(8,128)(2,1)S(1)} %pad_maximum_fusion.1), channel_id=1, source_target_pairs={{0,8},{4,12},{8,0},{12,4},{1,9},{5,13},{9,1},{13,5},{2,10},{6,14},... | collective-permute-start | bytes 786440 | tf_op jit(solution)/shard_map/ppermute | solution.py:74
  16.3 1.3 %collective-permute-start.2 = (bf16[2,2,64,4,128]{4,2,3,1,0:T(8,128)(2,1)S(1)}, bf16[2,2,64,4,128]{4,2,3,1,0:T(8,128)(2,1)S(1)}, u32[]{:S(2)}, u32[]{:S(2)}) collective-permute-start(bf16[2,2,64,4,128]{4,2,3,1,0:T(8,128)(2,1)S(1)} %pad_maximum_fusion.1), channel_id=1, source_target_pairs={{0,12},{4,0},{8,4},{12,8},{1,13},{5,1},{9,5},{13,9},{2,14},{6,2},{... | collective-permute-start | bytes 786440 | tf_op jit(solution)/shard_map/ppermute | solution.py:74
  17.8 5.3 %collective-permute-done = bf16[2,2,64,4,128]{4,2,3,1,0:T(8,128)(2,1)S(1)} collective-permute-done((bf16[2,2,64,4,128]{4,2,3,1,0:T(8,128)(2,1)S(1)}, bf16[2,2,64,4,128]{4,2,3,1,0:T(8,128)(2,1)S(1)}, u32[]{:S(2)}, u32[]{:S(2)}) %collective-permute-start) | collective-permute-done | bytes 262176 | tf_op jit(solution)/shard_map/ppermute | solution.py:74
  23.2 10.7 %collective-permute-done.1 = bf16[2,2,64,4,128]{4,2,3,1,0:T(8,128)(2,1)S(1)} collective-permute-done((bf16[2,2,64,4,128]{4,2,3,1,0:T(8,128)(2,1)S(1)}, bf16[2,2,64,4,128]{4,2,3,1,0:T(8,128)(2,1)S(1)}, u32[]{:S(2)}, u32[]{:S(2)}) %collective-permute-start.1) | collective-permute-done | bytes 262176 | tf_op jit(solution)/shard_map/ppermute | solution.py:74
  33.9 0.1 pad_maximum_fusion
  34.1 0.6 fusion
  34.7 0.5 fusion.3
  35.2 0.1 copy.23
  35.3 0.3 copy-done.2
  35.6 0.3 convolution_convert_fusion.2
  36.0 0.1 collective-permute-start.3
  36.1 1.2 %collective-permute-start.4 = (bf16[128,512]{1,0:T(8,128)(2,1)S(1)}, bf16[128,512]{1,0:T(8,128)(2,1)S(1)}, u32[]{:S(2)}, u32[]{:S(2)}) collective-permute-start(bf16[128,512]{1,0:T(8,128)(2,1)S(1)} %get-tuple-element.28), channel_id=1, source_target_pairs={{0,2},{1,3},{2,0},{3,1},{4,6},{5,7},{6,4},{7,5},{8,10},{9,11},{10,... | collective-permute-start | bytes 393224 | tf_op jit(solution)/shard_map/ppermute | solution.py:58
  37.2 1.4 %collective-permute-start.5 = (bf16[128,512]{1,0:T(8,128)(2,1)S(1)}, bf16[128,512]{1,0:T(8,128)(2,1)S(1)}, u32[]{:S(2)}, u32[]{:S(2)}) collective-permute-start(bf16[128,512]{1,0:T(8,128)(2,1)S(1)} %get-tuple-element.27), channel_id=1, source_target_pairs={{0,3},{1,0},{2,1},{3,2},{4,7},{5,4},{6,5},{7,6},{8,11},{9,8},{10,9... | collective-permute-start | bytes 393224 | tf_op jit(solution)/shard_map/ppermute | solution.py:58
  38.6 0.3 broadcast_multiply_fusion.5
  38.9 2.3 %collective-permute-done.3 = bf16[128,512]{1,0:T(8,128)(2,1)S(1)} collective-permute-done((bf16[128,512]{1,0:T(8,128)(2,1)S(1)}, bf16[128,512]{1,0:T(8,128)(2,1)S(1)}, u32[]{:S(2)}, u32[]{:S(2)}) %collective-permute-start.3) | collective-permute-done | bytes 131104 | tf_op jit(solution)/shard_map/ppermute | solution.py:58
  41.2 1.2 %collective-permute-done.4 = bf16[128,512]{1,0:T(8,128)(2,1)S(1)} collective-permute-done((bf16[128,512]{1,0:T(8,128)(2,1)S(1)}, bf16[128,512]{1,0:T(8,128)(2,1)S(1)}, u32[]{:S(2)}, u32[]{:S(2)}) %collective-permute-start.4) | collective-permute-done | bytes 131104 | tf_op jit(solution)/shard_map/ppermute | solution.py:58
  42.4 0.8 collective-permute-done.5
  43.3 0.1 convert_add_fusion.2
  43.4 0.1 reshape.563
  43.5 0.1 add_convert_fusion.2
  43.5 0.1 fusion.108
  43.7 6.1 %collective-permute-start.6 = (bf16[128,4,1]{2,1,0:T(4,128)(2,1)S(1)}, bf16[128,4,1]{2,1,0:T(4,128)(2,1)S(1)}, u32[]{:S(2)}, u32[]{:S(2)}) collective-permute-start(bf16[128,4,1]{2,1,0:T(4,128)(2,1)S(1)} %get-tuple-element.31), channel_id=1, source_target_pairs={{0,4},{4,8},{8,12},{12,0},{1,5},{5,9},{9,13},{13,1},{2,6},{6,10},{... | collective-permute-start | bytes 3080 | tf_op jit(solution)/shard_map/ppermute | solution.py:26
  49.8 1.1 collective-permute-start.7
  50.9 4.0 %collective-permute-done.6 = bf16[128,4,1]{2,1,0:T(4,128)(2,1)S(1)} collective-permute-done((bf16[128,4,1]{2,1,0:T(4,128)(2,1)S(1)}, bf16[128,4,1]{2,1,0:T(4,128)(2,1)S(1)}, u32[]{:S(2)}, u32[]{:S(2)}) %collective-permute-start.6) | collective-permute-done | bytes 1056 | tf_op jit(solution)/shard_map/ppermute | solution.py:26
  54.9 3.1 %collective-permute-done.7 = bf16[128,4,1]{2,1,0:T(4,128)(2,1)S(1)} collective-permute-done((bf16[128,4,1]{2,1,0:T(4,128)(2,1)S(1)}, bf16[128,4,1]{2,1,0:T(4,128)(2,1)S(1)}, u32[]{:S(2)}, u32[]{:S(2)}) %collective-permute-start.7) | collective-permute-done | bytes 1056 | tf_op jit(solution)/shard_map/ppermute | solution.py:27
  58.0 0.3 maximum_convert_fusion
  58.4 2.4 %fusion.93 = bf16[128,4,128]{2,1,0:T(4,128)(2,1)S(1)} fusion(f32[128,4,130]{2,1,0:T(4,128)S(1)} %maximum_convert_fusion, f32[128,4]{1,0:T(8,128)S(1)} %get-tuple-element.58, f32[128]{0:T(128)S(1)} %get-tuple-element.41, f32[128,4]{1,0:T(8,128)S(1)} %get-tuple-element.57, f32[128,4]{1,0:T(8,128)S(1)} %get-tuple-element.56, f32[128]{0:T(128)S(1)} %get-tuple-element.44, ...), kind=kLoop, calls=%fused_computation.134 | loop fusion | flops 1179648 | bytes 1836544 | tf_op jit(solution)/shard_map/convert_element_type | solution.py:111
  60.8 7.1 %all_gather.10 = bf16[512,4,128]{2,1,0:T(4,128)(2,1)S(1)} all-gather(bf16[128,4,128]{2,1,0:T(4,128)(2,1)S(1)} %fusion.93), channel_id=1, replica_groups=mesh['member'=2,'lon'=4,'lev'=4] {'lev'}, dimensions={0}, use_global_device_ids=true | all-gather | bytes 655360 | tf_op jit(solution)/shard_map/all_gather | solution.py:47
  67.8 0.5 fusion.7
  68.4 1.5 %fusion.9 = bf16[512,4,128]{2,1,0:T(4,128)(2,1)S(1)} fusion(bf16[512,4,128]{2,1,0:T(4,128)(2,1)S(1)} %all_gather.10, f32[512]{0:T(512)S(1)} %bitcast.154, f32[4,128]{1,0:T(4,128)S(1)} %add_rsqrt_fusion.3), kind=kLoop, calls=%fused_computation.37 | loop fusion | flops 1048576 | bytes 1052672 | tf_op jit(solution)/shard_map/convert_element_type | solution.py:113
  69.9 2.0 %convolution_convert_fusion.1 = bf16[512,512]{0,1:T(8,128)(2,1)S(1)} fusion(bf16[64,8,4,128]{3,2,1,0:T(4,128)(2,1)S(1)} %bitcast.150, bf16[2,512,512]{2,1,0:T(8,128)(2,1)S(1)} %copy-done.5, bf16[2,512,512]{2,1,0:T(8,128)(2,1)} %param.16), kind=kOutput, calls=%fused_computation.26 | convolution fusion | flops 539492352 | bytes 2097152 | tf_op jit(solution)/shard_map/dot_general | solution.py:63
  72.0 0.8 collective-permute-start.10
  72.9 1.2 %collective-permute-start.9 = (bf16[128,512]{1,0:T(8,128)(2,1)S(1)}, bf16[128,512]{1,0:T(8,128)(2,1)S(1)}, u32[]{:S(2)}, u32[]{:S(2)}) collective-permute-start(bf16[128,512]{1,0:T(8,128)(2,1)S(1)} %get-tuple-element.25), channel_id=1, source_target_pairs={{0,2},{1,3},{2,0},{3,1},{4,6},{5,7},{6,4},{7,5},{8,10},{9,11},{10,... | collective-permute-start | bytes 393224 | tf_op jit(solution)/shard_map/ppermute | solution.py:58
  74.1 2.1 %collective-permute-done.10 = bf16[128,512]{1,0:T(8,128)(2,1)S(1)} collective-permute-done((bf16[128,512]{1,0:T(8,128)(2,1)S(1)}, bf16[128,512]{1,0:T(8,128)(2,1)S(1)}, u32[]{:S(2)}, u32[]{:S(2)}) %collective-permute-start.10) | collective-permute-done | bytes 131104 | tf_op jit(solution)/shard_map/ppermute | solution.py:58
  76.2 2.5 %collective-permute-done.8 = bf16[128,512]{1,0:T(8,128)(2,1)S(1)} collective-permute-done((bf16[128,512]{1,0:T(8,128)(2,1)S(1)}, bf16[128,512]{1,0:T(8,128)(2,1)S(1)}, u32[]{:S(2)}, u32[]{:S(2)}) %collective-permute-start.8) | collective-permute-done | bytes 131104 | tf_op jit(solution)/shard_map/ppermute | solution.py:58
  78.7 2.3 %collective-permute-done.9 = bf16[128,512]{1,0:T(8,128)(2,1)S(1)} collective-permute-done((bf16[128,512]{1,0:T(8,128)(2,1)S(1)}, bf16[128,512]{1,0:T(8,128)(2,1)S(1)}, u32[]{:S(2)}, u32[]{:S(2)}) %collective-permute-start.9) | collective-permute-done | bytes 131104 | tf_op jit(solution)/shard_map/ppermute | solution.py:58
  81.0 0.1 convert_add_fusion.1
  81.0 0.1 reshape.566
  81.1 0.1 add_convert_fusion.1
  81.2 0.1 fusion.107
  81.4 0.5 collective-permute-start.11
  81.8 3.4 %collective-permute-start.12 = (bf16[128,4,1]{2,1,0:T(4,128)(2,1)S(1)}, bf16[128,4,1]{2,1,0:T(4,128)(2,1)S(1)}, u32[]{:S(2)}, u32[]{:S(2)}) collective-permute-start(bf16[128,4,1]{2,1,0:T(4,128)(2,1)S(1)} %get-tuple-element.30), channel_id=1, source_target_pairs={{4,0},{8,4},{12,8},{0,12},{5,1},{9,5},{13,9},{1,13},{6,2},{10,6},{... | collective-permute-start | bytes 3080 | tf_op jit(solution)/shard_map/ppermute | solution.py:27
  85.2 4.4 %collective-permute-done.11 = bf16[128,4,1]{2,1,0:T(4,128)(2,1)S(1)} collective-permute-done((bf16[128,4,1]{2,1,0:T(4,128)(2,1)S(1)}, bf16[128,4,1]{2,1,0:T(4,128)(2,1)S(1)}, u32[]{:S(2)}, u32[]{:S(2)}) %collective-permute-start.11) | collective-permute-done | bytes 1056 | tf_op jit(solution)/shard_map/ppermute | solution.py:26
  89.6 0.3 collective-permute-done.12
  89.9 0.4 maximum_convert_fusion.1
  90.3 2.3 %fusion.92 = bf16[128,4,128]{2,1,0:T(4,128)(2,1)S(1)} fusion(f32[128,4,130]{2,1,0:T(4,128)S(1)} %maximum_convert_fusion.1, f32[128,4]{1,0:T(8,128)S(1)} %get-tuple-element.63, f32[128]{0:T(128)S(1)} %get-tuple-element.50, f32[128,4]{1,0:T(8,128)S(1)} %get-tuple-element.62, f32[128,4]{1,0:T(8,128)S(1)} %get-tuple-element.61, f32[128]{0:T(128)S(1)} %get-tuple-element.36, ...), kind=kLoop, calls=%fused_computation.133 | loop fusion | flops 1179648 | bytes 1836544 | tf_op jit(solution)/shard_map/convert_element_type | solution.py:111
  92.6 6.8 %all_gather.11 = bf16[512,4,128]{2,1,0:T(4,128)(2,1)S(1)} all-gather(bf16[128,4,128]{2,1,0:T(4,128)(2,1)S(1)} %fusion.92), channel_id=1, replica_groups=mesh['member'=2,'lon'=4,'lev'=4] {'lev'}, dimensions={0}, use_global_device_ids=true | all-gather | bytes 655360 | tf_op jit(solution)/shard_map/all_gather | solution.py:47
  99.4 0.5 fusion.10
  100.0 1.5 %fusion.12 = bf16[512,4,128]{2,1,0:T(4,128)(2,1)S(1)} fusion(bf16[512,4,128]{2,1,0:T(4,128)(2,1)S(1)} %all_gather.11, f32[512]{0:T(512)S(1)} %bitcast.153, f32[4,128]{1,0:T(4,128)S(1)} %add_rsqrt_fusion.2), kind=kLoop, calls=%fused_computation.40 | loop fusion | flops 1048576 | bytes 1052672 | tf_op jit(solution)/shard_map/convert_element_type | solution.py:113
  101.5 2.1 %convolution_convert_fusion = bf16[512,512]{0,1:T(8,128)(2,1)S(1)} fusion(bf16[64,8,4,128]{3,2,1,0:T(4,128)(2,1)S(1)} %bitcast.151, bf16[2,512,512]{2,1,0:T(8,128)(2,1)S(1)} %copy-done.5, bf16[2,512,512]{2,1,0:T(8,128)(2,1)} %param.16), kind=kOutput, calls=%fused_computation.25 | convolution fusion | flops 539492352 | bytes 2097152 | tf_op jit(solution)/shard_map/dot_general | solution.py:63
  103.6 0.4 collective-permute-start.13
  104.0 1.1 collective-permute-start.14
  105.1 1.1 %collective-permute-start.15 = (bf16[128,512]{1,0:T(8,128)(2,1)S(1)}, bf16[128,512]{1,0:T(8,128)(2,1)S(1)}, u32[]{:S(2)}, u32[]{:S(2)}) collective-permute-start(bf16[128,512]{1,0:T(8,128)(2,1)S(1)} %get-tuple-element.21), channel_id=1, source_target_pairs={{0,3},{1,0},{2,1},{3,2},{4,7},{5,4},{6,5},{7,6},{8,11},{9,8},{10,9... | collective-permute-start | bytes 393224 | tf_op jit(solution)/shard_map/ppermute | solution.py:58
  106.2 2.3 %collective-permute-done.13 = bf16[128,512]{1,0:T(8,128)(2,1)S(1)} collective-permute-done((bf16[128,512]{1,0:T(8,128)(2,1)S(1)}, bf16[128,512]{1,0:T(8,128)(2,1)S(1)}, u32[]{:S(2)}, u32[]{:S(2)}) %collective-permute-start.13) | collective-permute-done | bytes 131104 | tf_op jit(solution)/shard_map/ppermute | solution.py:58
  108.5 1.8 %collective-permute-done.14 = bf16[128,512]{1,0:T(8,128)(2,1)S(1)} collective-permute-done((bf16[128,512]{1,0:T(8,128)(2,1)S(1)}, bf16[128,512]{1,0:T(8,128)(2,1)S(1)}, u32[]{:S(2)}, u32[]{:S(2)}) %collective-permute-start.14) | collective-permute-done | bytes 131104 | tf_op jit(solution)/shard_map/ppermute | solution.py:58
  110.4 0.5 collective-permute-done.15
  110.9 0.1 convert_add_fusion
  111.0 0.1 reshape.569
  111.1 0.7 add_convert_fusion
  (31 shorter events, 0.5 us)
Async XLA Ops:
  0.0 11.5 %copy-start = (bf16[3,128,512]{2,1,0:T(8,128)(2,1)S(1)}, bf16[3,128,512]{2,1,0:T(8,128)(2,1)}, u32[]{:S(2)}) copy-start(bf16[3,128,512]{2,1,0:T(8,128)(2,1)} %param.12) | copy-start | bytes 1179652
  11.5 6.3 %copy-start.3 = (f32[2,9,128]{2,0,1:T(2,128)S(1)}, f32[2,9,128]{2,0,1:T(2,128)}, u32[]{:S(2)}) copy-start(f32[2,9,128]{2,0,1:T(2,128)} %param.14) | copy-start | bytes 27652
  12.1 11.1 %collective-permute-start = (bf16[2,2,64,4,128]{4,2,3,1,0:T(8,128)(2,1)S(1)}, bf16[2,2,64,4,128]{4,2,3,1,0:T(8,128)(2,1)S(1)}, u32[]{:S(2)}, u32[]{:S(2)}) collective-permute-start(bf16[2,2,64,4,128]{4,2,3,1,0:T(8,128)(2,1)S(1)} %pad_maximum_fusion.1), channel_id=1, source_target_pairs={{0,4},{4,8},{8,12},{12,0},{1,5},{5,9},{9,13},{13,1},{2,6},{6,10},{... | collective-permute-start | bytes 786440 | tf_op jit(solution)/shard_map/ppermute | solution.py:74
  13.7 20.2 %collective-permute-start.1 = (bf16[2,2,64,4,128]{4,2,3,1,0:T(8,128)(2,1)S(1)}, bf16[2,2,64,4,128]{4,2,3,1,0:T(8,128)(2,1)S(1)}, u32[]{:S(2)}, u32[]{:S(2)}) collective-permute-start(bf16[2,2,64,4,128]{4,2,3,1,0:T(8,128)(2,1)S(1)} %pad_maximum_fusion.1), channel_id=1, source_target_pairs={{0,8},{4,12},{8,0},{12,4},{1,9},{5,13},{9,1},{13,5},{2,10},{6,14},... | collective-permute-start | bytes 786440 | tf_op jit(solution)/shard_map/ppermute | solution.py:74
  16.3 17.6 %collective-permute-start.2 = (bf16[2,2,64,4,128]{4,2,3,1,0:T(8,128)(2,1)S(1)}, bf16[2,2,64,4,128]{4,2,3,1,0:T(8,128)(2,1)S(1)}, u32[]{:S(2)}, u32[]{:S(2)}) collective-permute-start(bf16[2,2,64,4,128]{4,2,3,1,0:T(8,128)(2,1)S(1)} %pad_maximum_fusion.1), channel_id=1, source_target_pairs={{0,12},{4,0},{8,4},{12,8},{1,13},{5,1},{9,5},{13,9},{2,14},{6,2},{... | collective-permute-start | bytes 786440 | tf_op jit(solution)/shard_map/ppermute | solution.py:74
  34.7 0.9 copy-start.2
  35.2 8.3 %copy-start.1 = (bf16[128,4,128]{2,1,0:T(4,128)(2,1)S(1)}, bf16[128,4,128]{2,1,0:T(4,128)(2,1)}, u32[]{:S(2)}) copy-start(bf16[128,4,128]{2,1,0:T(4,128)(2,1)} %param.10) | copy-start | bytes 393220
  35.9 15.0 %copy-start.4 = (f32[2,512]{1,0:T(2,128)S(1)}, f32[2,512]{1,0:T(2,128)}, u32[]{:S(2)}) copy-start(f32[2,512]{1,0:T(2,128)} %param.15) | copy-start | bytes 12292
  36.0 5.2 %collective-permute-start.3 = (bf16[128,512]{1,0:T(8,128)(2,1)S(1)}, bf16[128,512]{1,0:T(8,128)(2,1)S(1)}, u32[]{:S(2)}, u32[]{:S(2)}) collective-permute-start(bf16[128,512]{1,0:T(8,128)(2,1)S(1)} %get-tuple-element.26), channel_id=1, source_target_pairs={{0,1},{1,2},{2,3},{3,0},{4,5},{5,6},{6,7},{7,4},{8,9},{9,10},{10,1... | collective-permute-start | bytes 393224 | tf_op jit(solution)/shard_map/ppermute | solution.py:58
  36.1 6.4 %collective-permute-start.4 = (bf16[128,512]{1,0:T(8,128)(2,1)S(1)}, bf16[128,512]{1,0:T(8,128)(2,1)S(1)}, u32[]{:S(2)}, u32[]{:S(2)}) collective-permute-start(bf16[128,512]{1,0:T(8,128)(2,1)S(1)} %get-tuple-element.28), channel_id=1, source_target_pairs={{0,2},{1,3},{2,0},{3,1},{4,6},{5,7},{6,4},{7,5},{8,10},{9,11},{10,... | collective-permute-start | bytes 393224 | tf_op jit(solution)/shard_map/ppermute | solution.py:58
  37.2 6.0 %collective-permute-start.5 = (bf16[128,512]{1,0:T(8,128)(2,1)S(1)}, bf16[128,512]{1,0:T(8,128)(2,1)S(1)}, u32[]{:S(2)}, u32[]{:S(2)}) collective-permute-start(bf16[128,512]{1,0:T(8,128)(2,1)S(1)} %get-tuple-element.27), channel_id=1, source_target_pairs={{0,3},{1,0},{2,1},{3,2},{4,7},{5,4},{6,5},{7,6},{8,11},{9,8},{10,9... | collective-permute-start | bytes 393224 | tf_op jit(solution)/shard_map/ppermute | solution.py:58
  43.7 11.2 %collective-permute-start.6 = (bf16[128,4,1]{2,1,0:T(4,128)(2,1)S(1)}, bf16[128,4,1]{2,1,0:T(4,128)(2,1)S(1)}, u32[]{:S(2)}, u32[]{:S(2)}) collective-permute-start(bf16[128,4,1]{2,1,0:T(4,128)(2,1)S(1)} %get-tuple-element.31), channel_id=1, source_target_pairs={{0,4},{4,8},{8,12},{12,0},{1,5},{5,9},{9,13},{13,1},{2,6},{6,10},{... | collective-permute-start | bytes 3080 | tf_op jit(solution)/shard_map/ppermute | solution.py:26
  49.8 8.2 %collective-permute-start.7 = (bf16[128,4,1]{2,1,0:T(4,128)(2,1)S(1)}, bf16[128,4,1]{2,1,0:T(4,128)(2,1)S(1)}, u32[]{:S(2)}, u32[]{:S(2)}) collective-permute-start(bf16[128,4,1]{2,1,0:T(4,128)(2,1)S(1)} %get-tuple-element.32), channel_id=1, source_target_pairs={{4,0},{8,4},{12,8},{0,12},{5,1},{9,5},{13,9},{1,13},{6,2},{10,6},{... | collective-permute-start | bytes 3080 | tf_op jit(solution)/shard_map/ppermute | solution.py:27
  58.4 11.5 %copy-start.5 = (bf16[2,512,512]{2,1,0:T(8,128)(2,1)S(1)}, bf16[2,512,512]{2,1,0:T(8,128)(2,1)}, u32[]{:S(2)}) copy-start(bf16[2,512,512]{2,1,0:T(8,128)(2,1)} %param.17) | copy-start | bytes 3145732
  72.0 4.1 %collective-permute-start.10 = (bf16[128,512]{1,0:T(8,128)(2,1)S(1)}, bf16[128,512]{1,0:T(8,128)(2,1)S(1)}, u32[]{:S(2)}, u32[]{:S(2)}) collective-permute-start(bf16[128,512]{1,0:T(8,128)(2,1)S(1)} %get-tuple-element.24), channel_id=1, source_target_pairs={{0,3},{1,0},{2,1},{3,2},{4,7},{5,4},{6,5},{7,6},{8,11},{9,8},{10,9... | collective-permute-start | bytes 393224 | tf_op jit(solution)/shard_map/ppermute | solution.py:58
  72.9 5.8 %collective-permute-start.8 = (bf16[128,512]{1,0:T(8,128)(2,1)S(1)}, bf16[128,512]{1,0:T(8,128)(2,1)S(1)}, u32[]{:S(2)}, u32[]{:S(2)}) collective-permute-start(bf16[128,512]{1,0:T(8,128)(2,1)S(1)} %get-tuple-element.23), channel_id=1, source_target_pairs={{0,1},{1,2},{2,3},{3,0},{4,5},{5,6},{6,7},{7,4},{8,9},{9,10},{10,1... | collective-permute-start | bytes 393224 | tf_op jit(solution)/shard_map/ppermute | solution.py:58
  72.9 8.1 %collective-permute-start.9 = (bf16[128,512]{1,0:T(8,128)(2,1)S(1)}, bf16[128,512]{1,0:T(8,128)(2,1)S(1)}, u32[]{:S(2)}, u32[]{:S(2)}) collective-permute-start(bf16[128,512]{1,0:T(8,128)(2,1)S(1)} %get-tuple-element.25), channel_id=1, source_target_pairs={{0,2},{1,3},{2,0},{3,1},{4,6},{5,7},{6,4},{7,5},{8,10},{9,11},{10,... | collective-permute-start | bytes 393224 | tf_op jit(solution)/shard_map/ppermute | solution.py:58
  81.4 8.2 %collective-permute-start.11 = (bf16[128,4,1]{2,1,0:T(4,128)(2,1)S(1)}, bf16[128,4,1]{2,1,0:T(4,128)(2,1)S(1)}, u32[]{:S(2)}, u32[]{:S(2)}) collective-permute-start(bf16[128,4,1]{2,1,0:T(4,128)(2,1)S(1)} %get-tuple-element.29), channel_id=1, source_target_pairs={{0,4},{4,8},{8,12},{12,0},{1,5},{5,9},{9,13},{13,1},{2,6},{6,10},{... | collective-permute-start | bytes 3080 | tf_op jit(solution)/shard_map/ppermute | solution.py:26
  81.8 8.1 %collective-permute-start.12 = (bf16[128,4,1]{2,1,0:T(4,128)(2,1)S(1)}, bf16[128,4,1]{2,1,0:T(4,128)(2,1)S(1)}, u32[]{:S(2)}, u32[]{:S(2)}) collective-permute-start(bf16[128,4,1]{2,1,0:T(4,128)(2,1)S(1)} %get-tuple-element.30), channel_id=1, source_target_pairs={{4,0},{8,4},{12,8},{0,12},{5,1},{9,5},{13,9},{1,13},{6,2},{10,6},{... | collective-permute-start | bytes 3080 | tf_op jit(solution)/shard_map/ppermute | solution.py:27
  103.6 4.9 %collective-permute-start.13 = (bf16[128,512]{1,0:T(8,128)(2,1)S(1)}, bf16[128,512]{1,0:T(8,128)(2,1)S(1)}, u32[]{:S(2)}, u32[]{:S(2)}) collective-permute-start(bf16[128,512]{1,0:T(8,128)(2,1)S(1)} %get-tuple-element.20), channel_id=1, source_target_pairs={{0,1},{1,2},{2,3},{3,0},{4,5},{5,6},{6,7},{7,4},{8,9},{9,10},{10,1... | collective-permute-start | bytes 393224 | tf_op jit(solution)/shard_map/ppermute | solution.py:58
  104.0 6.4 %collective-permute-start.14 = (bf16[128,512]{1,0:T(8,128)(2,1)S(1)}, bf16[128,512]{1,0:T(8,128)(2,1)S(1)}, u32[]{:S(2)}, u32[]{:S(2)}) collective-permute-start(bf16[128,512]{1,0:T(8,128)(2,1)S(1)} %get-tuple-element.22), channel_id=1, source_target_pairs={{0,2},{1,3},{2,0},{3,1},{4,6},{5,7},{6,4},{7,5},{8,10},{9,11},{10,... | collective-permute-start | bytes 393224 | tf_op jit(solution)/shard_map/ppermute | solution.py:58
  105.1 5.8 %collective-permute-start.15 = (bf16[128,512]{1,0:T(8,128)(2,1)S(1)}, bf16[128,512]{1,0:T(8,128)(2,1)S(1)}, u32[]{:S(2)}, u32[]{:S(2)}) collective-permute-start(bf16[128,512]{1,0:T(8,128)(2,1)S(1)} %get-tuple-element.21), channel_id=1, source_target_pairs={{0,3},{1,0},{2,1},{3,2},{4,7},{5,4},{6,5},{7,6},{8,11},{9,8},{10,9... | collective-permute-start | bytes 393224 | tf_op jit(solution)/shard_map/ppermute | solution.py:58

commit v2 on v1

--- a/solution.py
+++ b/solution.py
@@ -14,19 +14,6 @@
 band_start = 30.0
 grid_step = 0.25
 epsilon = 1e-06
-
-
-def with_halo(array, sides, width):
-    for axis, dim in sides:
-        devices, length = (lax.axis_size(axis), array.shape[dim])
-        up = [(i, (i + 1) % devices) for i in range(devices)]
-        down = [(j, i) for i, j in up]
-        last = lax.slice_in_dim(array, length - width, length, axis=dim)
-        leading = lax.slice_in_dim(array, 0, width, axis=dim)
-        before = lax.ppermute(last, axis, up)
-        after = lax.ppermute(leading, axis, down)
-        array = jnp.concatenate([before, array, after], axis=dim)
-    return array
 
 
 def secant_rows(count):
@@ -47,23 +34,43 @@
     return lax.all_gather(values, "lev", axis=0, tiled=True)
 
 
-def scatter_sum(partial, axis):
+def scatter_sum(partial, axis, halo=False):
     devices = lax.axis_size(axis)
     me = lax.axis_index(axis)
+    strips = lax.axis_size("lon")
     blocks = partial.reshape(devices, -1, *partial.shape[1:])
     total = jnp.take(blocks, me, axis=0).astype(jnp.float32)
-    for shift in range(1, devices):
-        pairs = [(i, (i + shift) % devices) for i in range(devices)]
+    before = jnp.zeros(total.shape[:-1] + (1,), jnp.float32)
+    after = jnp.zeros(total.shape[:-1] + (1,), jnp.float32)
+    for shift in range(devices):
         chunk = jnp.take(blocks, (me + shift) % devices, axis=0)
-        total = total + lax.ppermute(chunk, axis, pairs).astype(jnp.float32)
-    return total
+        if shift:
+            pairs = [(i, (i + shift) % devices) for i in range(devices)]
+            total = total + lax.ppermute(chunk, axis, pairs).astype(jnp.float32)
+        if halo:
+            for step, edge, sums in ((1, chunk[..., -1:], "before"), (-1, chunk[..., :1], "after")):
+                pairs = [
+                    (s * devices + i, ((s + step) % strips) * devices + (i + shift) % devices)
+                    for s in range(strips)
+                    for i in range(devices)
+                ]
+                got = lax.ppermute(edge, ("lon", axis), pairs).astype(jnp.float32)
+                if sums == "before":
+                    before = before + got
+                else:
+                    after = after + got
+    return total, before, after
 
 
-def spread_sum(weight, activation):
+def spread_sum(weight, activation, shape, halo=False):
     partial = lax.dot_general(
         weight, activation, (((0,), (0,)), ((), ())), preferred_element_type=jnp.float32
     ).astype(jnp.bfloat16)
-    return scatter_sum(partial, "lev")
+    return scatter_sum(partial.reshape(weight.shape[1], *shape), "lev", halo)
+
+
+def add_update(state, sums):
+    return tuple((s.astype(jnp.float32) + u).astype(jnp.bfloat16) for s, u in zip(state, sums))
 
 
 def gather_strips(values, axis):
@@ -91,7 +98,8 @@
     return (numerator, jnp.sum(weights, axis=3))
 
 
-def block_apply(extended, block_index, stencil_weight, block_gain, up_weight, down_weight):
+def block_apply(state, block_index, stencil_weight, block_gain, up_weight, down_weight, halo):
+    extended = jnp.concatenate([state[1], state[0], state[2]], axis=2)
     lat_rows = extended.shape[1]
     out_cols = extended.shape[2] - 2
     secants = secant_rows(lat_rows)[None, :, None]
@@ -117,9 +125,8 @@
     hidden = jax.nn.gelu(
         jnp.dot(up_weight[block_index], block_normed, preferred_element_type=jnp.float32)
     ).astype(jnp.bfloat16)
-    update = spread_sum(down_weight[block_index], hidden)
-    center = extended[:, :, 1:-1]
-    return (center.astype(jnp.float32) + update.reshape(center.shape)).astype(jnp.bfloat16)
+    sums = spread_sum(down_weight[block_index], hidden, state[0].shape[1:], halo)
+    return add_update(state, sums)
 
 
 def per_device(
@@ -138,15 +145,17 @@
     key_value = gather_strips(jnp.stack([key_rows, value_rows]), "lon")
     numerator, denominator = make_fold(queries, (key_value[0], key_value[1]))
     attended = (numerator / denominator[:, None]).astype(jnp.bfloat16)
-    update = spread_sum(out_weight, attended.reshape(ch_local, -1))
-    latent_state = (latent.astype(jnp.float32) + update.reshape(latent.shape)).astype(jnp.bfloat16)
-    current = latent_state
+    strips = lax.axis_size("lon")
+    latent_before = lax.ppermute(latent[..., -1:], "lon", [(i, (i + 1) % strips) for i in range(strips)])
+    latent_after = lax.ppermute(latent[..., :1], "lon", [(i, (i - 1) % strips) for i in range(strips)])
+    sums = spread_sum(out_weight, attended.reshape(ch_local, -1), latent.shape[1:], True)
+    current = add_update((latent, latent_before, latent_after), sums)
     for block_index in range(BLOCKS):
-        extended = with_halo(current, (("lon", 2),), 1)
         current = block_apply(
-            extended, block_index, stencil_weight, block_gain, up_weight, down_weight
+            current, block_index, stencil_weight, block_gain, up_weight, down_weight,
+            block_index < BLOCKS - 1,
         )
-    return current
+    return current[0]
 
 
 def solution(mesh):

time: 113 us -> 121 us (1.071)
  starting transfers between devices: 24 us -> 37.1 us
  waiting for transfers between devices: 43.8 us -> 37.7 us
  local copies, waits for them, and re-layouts: 1.01 us -> 6.3 us
  other arithmetic: 13.9 us -> 11.1 us
    ppermute x4 -> x18, starting transfers between devices: 11.1 us -> 24.5 us  [the longest x16 20.2 us: scatter_sum(): got = lax.ppermute(edge, ('lon', axis), pairs).astype(jnp.float32)]
    ppermute x4 -> x18, waiting for transfers between devices: 11.8 us -> 3.41 us  [the longest x16 3.41 us: scatter_sum(): got = lax.ppermute(edge, ('lon', axis), pairs).astype(jnp.float32)]
    another operation x0 -> x6, local copies, waits for them, and re-layouts: none -> 4.54 us  [the longest x3 4.17 us: scatter_sum(): total = jnp.take(blocks, me, axis=0).astype(jnp.float32)]
    convert_element_type x2, other arithmetic: 4.7 us -> 0.8 us  [block_apply(): smoothed = stencil_sum.astype(jnp.bfloat16)]
    ppermute x3, waiting for transfers between devices: 16.1 us -> 18.5 us  [gather_strips(): pieces.append(lax.ppermute(values, axis, pairs))]
    select_n x3 -> x11, other arithmetic: 0.14 us -> 2.04 us  [scatter_sum(): chunk = jnp.take(blocks, (me + shift) % devices, axis=0)]
  transfers between devices with their start and end apart: 16 -> 30, of which waited for: 15 -> 14; matrix products, arithmetic and copies ran while one was open for 0% -> 4% of each run, Pallas kernels for 0% -> 0%
where the time goes in v2:
time: 121 us
  waiting for transfers between devices  37.7 us (31%)
  starting transfers between devices  37.1 us (31%)
  blocking collectives  22.5 us (19%)
  other arithmetic  11.1 us (9%)
  local copies, waits for them, and re-layouts  6.3 us (5%)
  matrix products  5.77 us (5%)
    all_gather x3, blocking collectives, gather_channels(): return lax.all_gather(values, 'lev', axis=0, tiled=True)  22.5 us
    ppermute x16, starting transfers between devices, scatter_sum(): got = lax.ppermute(edge, ('lon', axis), pairs).astype(jnp.float32)  20.2 us
    ppermute x3, waiting for transfers between devices, gather_strips(): pieces.append(lax.ppermute(values, axis, pairs))  18.5 us
    ppermute x9, waiting for transfers between devices, scatter_sum(): total = total + lax.ppermute(chunk, axis, pairs).astype(jnp.float32)  15.8 us
    ppermute x9, starting transfers between devices, scatter_sum(): total = total + lax.ppermute(chunk, axis, pairs).astype(jnp.float32)  7.84 us
    ppermute x3, starting transfers between devices, gather_strips(): pieces.append(lax.ppermute(values, axis, pairs))  4.67 us
    dot_general x3, matrix products, spread_sum(): lax.dot_general(weight, activation, (((0,), (0,)), ((), ())), preferred_e...  4.29 us
    another operation x3, local copies, waits for them, and re-layouts, scatter_sum(): total = jnp.take(blocks, me, axis=0).astype(jnp.float32)  4.17 us
  transfers between devices with their start and end apart: 30, of which 14 were waited for; matrix products, arithmetic and copies ran while one was open for 4% of the time, Pallas kernels for 0%

profile of v2, /device:TPU:0, one launch (start us, length us, event | category | flops | bytes accessed | tf_op | source)
XLA Modules:
  0.0 121.0 jit_solution(17095749814816326519)
XLA Ops:
  0.0 8.9 %all_gather.9 = bf16[512,4,128]{2,1,0:T(4,128)(2,1)S(1)} all-gather(bf16[128,4,128]{2,1,0:T(4,128)(2,1)} %param.10), channel_id=1, replica_groups=mesh['member'=2,'lon'=4,'lev'=4] {'lev'}, dimensions={0}, use_global_device_ids=true | all-gather | bytes 655360 | tf_op jit(solution)/shard_map/all_gather | solution.py:34
  9.0 0.5 fusion.7
  9.5 1.9 %fusion.34 = bf16[512,4,128,1]{2,1,0,3:T(4,128)(2,1)S(1)} fusion(bf16[512,4,128]{2,1,0:T(4,128)(2,1)S(1)} %all_gather.9, f32[512]{0:T(512)} %param.11, f32[4,128]{1,0:T(4,128)S(1)} %add_rsqrt_fusion.4), kind=kLoop, calls=%fused_computation.62 | loop fusion | flops 1048576 | bytes 1052672 | tf_op jit(solution)/shard_map/convert_element_type | solution.py:139
  11.5 0.4 convolution_bitcast_fusion.2
  12.1 3.7 %collective-permute-start.2 = (bf16[2,2,64,4,128]{4,2,3,1,0:T(8,128)(2,1)S(1)}, bf16[2,2,64,4,128]{4,2,3,1,0:T(8,128)(2,1)S(1)}, u32[]{:S(2)}, u32[]{:S(2)}) collective-permute-start(bf16[2,2,64,4,128]{4,2,3,1,0:T(8,128)(2,1)S(1)} %pad_maximum_fusion.1), channel_id=1, source_target_pairs={{0,12},{4,0},{8,4},{12,8},{1,13},{5,1},{9,5},{13,9},{2,14},{6,2},{... | collective-permute-start | bytes 786440 | tf_op jit(solution)/shard_map/ppermute | solution.py:81
  15.8 1.0 collective-permute-start
  16.9 2.9 %collective-permute-start.11 = (bf16[128,4,1]{0,1,2:T(4,128)(2,1)S(1)}, bf16[128,4,1]{0,1,2:T(4,128)(2,1)S(1)}, u32[]{:S(2)}, u32[]{:S(2)}) collective-permute-start(bf16[128,4,1]{0,1,2:T(4,128)(2,1)S(1)} %get-tuple-element.43), channel_id=1, source_target_pairs={{0,12},{4,0},{8,4},{12,8},{1,13},{5,1},{9,5},{13,9},{2,14},{6,2},{... | collective-permute-start | bytes 3080 | tf_op jit(solution)/shard_map/ppermute | solution.py:150
  20.1 2.4 %collective-permute-done.2 = bf16[2,2,64,4,128]{4,2,3,1,0:T(8,128)(2,1)S(1)} collective-permute-done((bf16[2,2,64,4,128]{4,2,3,1,0:T(8,128)(2,1)S(1)}, bf16[2,2,64,4,128]{4,2,3,1,0:T(8,128)(2,1)S(1)}, u32[]{:S(2)}, u32[]{:S(2)}) %collective-permute-start.2) | collective-permute-done | bytes 262176 | tf_op jit(solution)/shard_map/ppermute | solution.py:81
  22.5 16.1 %collective-permute-done.1 = bf16[2,2,64,4,128]{4,2,3,1,0:T(8,128)(2,1)S(1)} collective-permute-done((bf16[2,2,64,4,128]{4,2,3,1,0:T(8,128)(2,1)S(1)}, bf16[2,2,64,4,128]{4,2,3,1,0:T(8,128)(2,1)S(1)}, u32[]{:S(2)}, u32[]{:S(2)}) %collective-permute-start.1) | collective-permute-done | bytes 262176 | tf_op jit(solution)/shard_map/ppermute | solution.py:81
  38.7 0.6 fusion
  39.4 0.5 fusion.6
  40.0 0.3 copy-done.2
  40.3 0.3 fusion.2
  40.7 1.4 %constant_dynamic-slice_fusion.12 = (bf16[1,128,4,128]{1,0,3,2:T(2,128)(2,1)S(1)}, bf16[1,128,4,128]{1,0,3,2:T(2,128)(2,1)S(1)}, bf16[1,128,4,128]{1,0,3,2:T(2,1...) fusion(bf16[4,128,4,128]{1,0,3,2:T(4,128)(2,1)S(1)} %reshape.765, s32[]{:T(128)S(6)} %select_n.83, ...), kind=kLoop, calls=%fused_computation.180 | loop fusion | bytes 1310740 | tf_op jit(solution)/shard_map/jit(_take) | solution.py:42
  42.4 0.2 fusion.110
  42.6 4.1 %collective-permute-start.14 = (bf16[128,4,1]{0,1,2:T(4,128)(2,1)S(1)}, bf16[128,4,1]{0,1,2:T(4,128)(2,1)S(1)}, u32[]{:S(2)}, u32[]{:S(2)}) collective-permute-start(bf16[128,4,1]{0,1,2:T(4,128)(2,1)S(1)} %get-tuple-element.49), channel_id=1, source_target_pairs={{0,14},{1,15},{2,12},{3,13},{4,2},{5,3},{6,0},{7,1},{8,6},{9,7},{1... | collective-permute-start | bytes 3080 | tf_op jit(solution)/shard_map/ppermute | solution.py:57
  47.0 0.2 fusion.108
  47.2 0.9 collective-permute-start.12
  48.1 1.4 %collective-permute-start.6 = (bf16[128,4,1]{0,1,2:T(4,128)(2,1)S(1)}, bf16[128,4,1]{0,1,2:T(4,128)(2,1)S(1)}, u32[]{:S(2)}, u32[]{:S(2)}) collective-permute-start(bf16[128,4,1]{0,1,2:T(4,128)(2,1)S(1)} %get-tuple-element.42), channel_id=1, source_target_pairs={{0,4},{4,8},{8,12},{12,0},{1,5},{5,9},{9,13},{13,1},{2,6},{6,10},{... | collective-permute-start | bytes 3080 | tf_op jit(solution)/shard_map/ppermute | solution.py:149
  49.5 1.9 %collective-permute-start.10 = (bf16[128,4,1]{0,1,2:T(4,128)(2,1)S(1)}, bf16[128,4,1]{0,1,2:T(4,128)(2,1)S(1)}, u32[]{:S(2)}, u32[]{:S(2)}) collective-permute-start(bf16[128,4,1]{0,1,2:T(4,128)(2,1)S(1)} %get-tuple-element.50), channel_id=1, source_target_pairs={{0,7},{1,4},{2,5},{3,6},{4,11},{5,8},{6,9},{7,10},{8,15},{9,12},{1... | collective-permute-start | bytes 3080 | tf_op jit(solution)/shard_map/ppermute | solution.py:57
  51.4 0.9 collective-permute-start.9
  52.3 0.6 collective-permute-start.8
  52.9 1.4 %collective-permute-start.7 = (bf16[128,4,1]{0,1,2:T(4,128)(2,1)S(1)}, bf16[128,4,1]{0,1,2:T(4,128)(2,1)S(1)}, u32[]{:S(2)}, u32[]{:S(2)}) collective-permute-start(bf16[128,4,1]{0,1,2:T(4,128)(2,1)S(1)} %get-tuple-element.44), channel_id=1, source_target_pairs={{0,4},{1,5},{2,6},{3,7},{4,8},{5,9},{6,10},{7,11},{8,12},{9,13},{1... | collective-permute-start | bytes 3080 | tf_op jit(solution)/shard_map/ppermute | solution.py:57
  54.3 2.1 %collective-permute-start.5 = (bf16[128,4,128]{0,1,2:T(4,128)(2,1)S(1)}, bf16[128,4,128]{0,1,2:T(4,128)(2,1)S(1)}, u32[]{:S(2)}, u32[]{:S(2)}) collective-permute-start(bf16[128,4,128]{0,1,2:T(4,128)(2,1)S(1)} %fusion.109), channel_id=1, source_target_pairs={{0,3},{1,0},{2,1},{3,2},{4,7},{5,4},{6,5},{7,6},{8,11},{9,8},{10,9... | collective-permute-start | bytes 393224 | tf_op jit(solution)/shard_map/ppermute | solution.py:49
  56.4 1.1 collective-permute-start.4
  57.7 0.3 collective-permute-done.8
  58.0 0.3 collective-permute-done.7
  58.3 1.9 %collective-permute-done.5 = bf16[128,4,128]{0,1,2:T(4,128)(2,1)S(1)} collective-permute-done((bf16[128,4,128]{0,1,2:T(4,128)(2,1)S(1)}, bf16[128,4,128]{0,1,2:T(4,128)(2,1)S(1)}, u32[]{:S(2)}, u32[]{:S(2)}) %collective-permute-start.5) | collective-permute-done | bytes 131104 | tf_op jit(solution)/shard_map/ppermute | solution.py:49
  60.2 4.0 %collective-permute-done.4 = bf16[128,4,128]{0,1,2:T(4,128)(2,1)S(1)} collective-permute-done((bf16[128,4,128]{0,1,2:T(4,128)(2,1)S(1)}, bf16[128,4,128]{0,1,2:T(4,128)(2,1)S(1)}, u32[]{:S(2)}, u32[]{:S(2)}) %collective-permute-start.4) | collective-permute-done | bytes 131104 | tf_op jit(solution)/shard_map/ppermute | solution.py:49
  64.2 0.3 add_convert_fusion.2
  64.6 0.4 fusion.96
  65.2 6.8 %all_gather.10 = bf16[512,4,128]{2,1,0:T(4,128)(2,1)S(1)} all-gather(bf16[128,4,128]{2,1,0:T(4,128)(2,1)S(1)} %copy.93), channel_id=1, replica_groups=mesh['member'=2,'lon'=4,'lev'=4] {'lev'}, dimensions={0}, use_global_device_ids=true | all-gather | bytes 655360 | tf_op jit(solution)/shard_map/all_gather | solution.py:34
  72.0 0.5 fusion.10
  72.5 1.5 %fusion.12 = bf16[512,4,128]{2,1,0:T(4,128)(2,1)S(1)} fusion(bf16[512,4,128]{2,1,0:T(4,128)(2,1)S(1)} %all_gather.10, f32[512]{0:T(512)S(1)} %bitcast.161, f32[4,128]{1,0:T(4,128)S(1)} %add_rsqrt_fusion.3), kind=kLoop, calls=%fused_computation.28 | loop fusion | flops 1048576 | bytes 1052672 | tf_op jit(solution)/shard_map/convert_element_type | solution.py:121
  74.0 2.0 %fusion.3 = bf16[512,512]{0,1:T(8,128)(2,1)S(1)} fusion(bf16[64,8,4,128]{3,2,1,0:T(4,128)(2,1)S(1)} %bitcast.157, bf16[2,512,512]{2,1,0:T(8,128)(2,1)S(1)} %copy-done.5, bf16[2,512,512]{2,1,0:T(8,128)(2,1)} %param.16), kind=kOutput, calls=%fused_computation.18 | convolution fusion | flops 539492352 | bytes 2097152 | tf_op jit(solution)/shard_map/dot_general | solution.py:66
  76.2 1.5 %constant_dynamic-slice_fusion.5 = (bf16[1,128,4,128]{1,0,3,2:T(2,128)(2,1)S(1)}, bf16[1,128,4,128]{1,0,3,2:T(2,128)(2,1)S(1)}, bf16[1,128,4,128]{1,0,3,2:T(2,12...) fusion(bf16[4,128,4,128]{1,0,3,2:T(4,128)(2,1)S(1)} %reshape.766, s32[]{:T(128)S(6)} %select_n.83, ...), kind=kLoop, calls=%fused_computation.173 | loop fusion | bytes 1310740 | tf_op jit(solution)/shard_map/jit(_take) | solution.py:42
  77.9 2.7 %collective-permute-start.26 = (bf16[128,4,1]{0,1,2:T(4,128)(2,1)S(1)}, bf16[128,4,1]{0,1,2:T(4,128)(2,1)S(1)}, u32[]{:S(2)}, u32[]{:S(2)}) collective-permute-start(bf16[128,4,1]{0,1,2:T(4,128)(2,1)S(1)} %get-tuple-element.41), channel_id=1, source_target_pairs={{0,15},{1,12},{2,13},{3,14},{4,3},{5,0},{6,1},{7,2},{8,7},{9,4},{1... | collective-permute-start | bytes 3080 | tf_op jit(solution)/shard_map/ppermute | solution.py:57
  80.8 1.0 collective-permute-start.25
  82.0 0.7 collective-permute-start.24
  82.9 1.1 collective-permute-start.23
  84.0 1.5 %collective-permute-start.18 = (bf16[128,4,128]{0,1,2:T(4,128)(2,1)S(1)}, bf16[128,4,128]{0,1,2:T(4,128)(2,1)S(1)}, u32[]{:S(2)}, u32[]{:S(2)}) collective-permute-start(bf16[128,4,128]{0,1,2:T(4,128)(2,1)S(1)} %fusion.104), channel_id=1, source_target_pairs={{0,3},{1,0},{2,1},{3,2},{4,7},{5,4},{6,5},{7,6},{8,11},{9,8},{10,9... | collective-permute-start | bytes 393224 | tf_op jit(solution)/shard_map/ppermute | solution.py:49
  85.4 0.9 collective-permute-start.22
  86.3 1.0 collective-permute-start.21
  87.3 1.3 %collective-permute-start.20 = (bf16[128,4,1]{0,1,2:T(4,128)(2,1)S(1)}, bf16[128,4,1]{0,1,2:T(4,128)(2,1)S(1)}, u32[]{:S(2)}, u32[]{:S(2)}) collective-permute-start(bf16[128,4,1]{0,1,2:T(4,128)(2,1)S(1)} %get-tuple-element.36), channel_id=1, source_target_pairs={{0,5},{1,6},{2,7},{3,4},{4,9},{5,10},{6,11},{7,8},{8,13},{9,14},{1... | collective-permute-start | bytes 3080 | tf_op jit(solution)/shard_map/ppermute | solution.py:57
  88.7 1.7 %collective-permute-start.19 = (bf16[128,4,1]{0,1,2:T(4,128)(2,1)S(1)}, bf16[128,4,1]{0,1,2:T(4,128)(2,1)S(1)}, u32[]{:S(2)}, u32[]{:S(2)}) collective-permute-start(bf16[128,4,1]{0,1,2:T(4,128)(2,1)S(1)} %get-tuple-element.34), channel_id=1, source_target_pairs={{0,4},{1,5},{2,6},{3,7},{4,8},{5,9},{6,10},{7,11},{8,12},{9,13},{1... | collective-permute-start | bytes 3080 | tf_op jit(solution)/shard_map/ppermute | solution.py:57
  90.4 1.0 collective-permute-start.17
  91.4 1.2 collective-permute-done.21
  92.6 0.4 collective-permute-done.20
  93.0 1.0 collective-permute-done.19
  94.1 2.4 %collective-permute-done.17 = bf16[128,4,128]{0,1,2:T(4,128)(2,1)S(1)} collective-permute-done((bf16[128,4,128]{0,1,2:T(4,128)(2,1)S(1)}, bf16[128,4,128]{0,1,2:T(4,128)(2,1)S(1)}, u32[]{:S(2)}, u32[]{:S(2)}) %collective-permute-start.17) | collective-permute-done | bytes 131104 | tf_op jit(solution)/shard_map/ppermute | solution.py:49
  96.5 1.0 collective-permute-done.16
  97.5 0.3 add_convert_fusion.1
  97.9 0.4 fusion.95
  98.4 6.8 %all_gather.11 = bf16[512,4,128]{2,1,0:T(4,128)(2,1)S(1)} all-gather(bf16[128,4,128]{2,1,0:T(4,128)(2,1)S(1)} %copy.100), channel_id=1, replica_groups=mesh['member'=2,'lon'=4,'lev'=4] {'lev'}, dimensions={0}, use_global_device_ids=true | all-gather | bytes 655360 | tf_op jit(solution)/shard_map/all_gather | solution.py:34
  105.2 0.5 fusion.13
  105.8 1.5 %fusion.15 = bf16[512,4,128]{2,1,0:T(4,128)(2,1)S(1)} fusion(bf16[512,4,128]{2,1,0:T(4,128)(2,1)S(1)} %all_gather.11, f32[512]{0:T(512)S(1)} %bitcast.160, f32[4,128]{1,0:T(4,128)S(1)} %add_rsqrt_fusion.2), kind=kLoop, calls=%fused_computation.31 | loop fusion | flops 1048576 | bytes 1052672 | tf_op jit(solution)/shard_map/convert_element_type | solution.py:121
  107.3 2.0 %fusion.4 = bf16[512,512]{0,1:T(8,128)(2,1)S(1)} fusion(bf16[64,8,4,128]{3,2,1,0:T(4,128)(2,1)S(1)} %bitcast.158, bf16[2,512,512]{2,1,0:T(8,128)(2,1)S(1)} %copy-done.5, bf16[2,512,512]{2,1,0:T(8,128)(2,1)} %param.16), kind=kOutput, calls=%fused_computation.19 | convolution fusion | flops 539492352 | bytes 2097152 | tf_op jit(solution)/shard_map/dot_general | solution.py:66
  109.4 1.2 %constant_dynamic-slice_fusion.13 = (bf16[1,128,4,128]{1,0,3,2:T(2,128)(2,1)S(1)}, bf16[1,128,4,128]{1,0,3,2:T(2,128)(2,1)S(1)}, bf16[1,128,4,128]{1,0,3,2:T(2,128)(2,1)S(1)}, bf16[1,128,4,128]{1,0,3,2:T(2,128)(2,1)S(1)}) fusion(bf16[4,128,4,128]{1,0,3,2:T(4,128)(2,1)S(1)} %reshape.767, s32[]{:T(128)S(6)} %select_n.83, s32[]{:T(128)S(6)} %select_n.87, ...), kind=kLoop, calls=%fused_computation.181 | loop fusion | bytes 1048592 | tf_op jit(solution)/shard_map/jit(_take) | solution.py:42
  110.8 0.9 collective-permute-start.29
  112.0 1.2 collective-permute-start.28
  113.4 2.3 %collective-permute-done.29 = bf16[128,4,128]{0,1,2:T(4,128)(2,1)S(1)} collective-permute-done((bf16[128,4,128]{0,1,2:T(4,128)(2,1)S(1)}, bf16[128,4,128]{0,1,2:T(4,128)(2,1)S(1)}, u32[]{:S(2)}, u32[]{:S(2)}) %collective-permute-start.29) | collective-permute-done | bytes 131104 | tf_op jit(solution)/shard_map/ppermute | solution.py:49
  115.7 4.2 %collective-permute-done.28 = bf16[128,4,128]{0,1,2:T(4,128)(2,1)S(1)} collective-permute-done((bf16[128,4,128]{0,1,2:T(4,128)(2,1)S(1)}, bf16[128,4,128]{0,1,2:T(4,128)(2,1)S(1)}, u32[]{:S(2)}, u32[]{:S(2)}) %collective-permute-start.28) | collective-permute-done | bytes 131104 | tf_op jit(solution)/shard_map/ppermute | solution.py:49
  119.9 0.3 add_convert_fusion
  120.2 0.8 copy.106
  (82 shorter events, 3.8 us)
Async XLA Ops:
  0.0 11.5 %copy-start = (bf16[3,128,512]{2,1,0:T(8,128)(2,1)S(1)}, bf16[3,128,512]{2,1,0:T(8,128)(2,1)}, u32[]{:S(2)}) copy-start(bf16[3,128,512]{2,1,0:T(8,128)(2,1)} %param.12) | copy-start | bytes 1179652
  11.5 5.3 %copy-start.1 = (bf16[128,4,128]{2,1,0:T(4,128)(2,1)S(1)}, bf16[128,4,128]{2,1,0:T(4,128)(2,1)}, u32[]{:S(2)}) copy-start(bf16[128,4,128]{2,1,0:T(4,128)(2,1)} %param.10) | copy-start | bytes 393220
  11.5 8.4 %copy-start.3 = (f32[2,9,128]{2,0,1:T(2,128)S(1)}, f32[2,9,128]{2,0,1:T(2,128)}, u32[]{:S(2)}) copy-start(f32[2,9,128]{2,0,1:T(2,128)} %param.14) | copy-start | bytes 27652
  12.1 10.4 %collective-permute-start.2 = (bf16[2,2,64,4,128]{4,2,3,1,0:T(8,128)(2,1)S(1)}, bf16[2,2,64,4,128]{4,2,3,1,0:T(8,128)(2,1)S(1)}, u32[]{:S(2)}, u32[]{:S(2)}) collective-permute-start(bf16[2,2,64,4,128]{4,2,3,1,0:T(8,128)(2,1)S(1)} %pad_maximum_fusion.1), channel_id=1, source_target_pairs={{0,12},{4,0},{8,4},{12,8},{1,13},{5,1},{9,5},{13,9},{2,14},{6,2},{... | collective-permute-start | bytes 786440 | tf_op jit(solution)/shard_map/ppermute | solution.py:81
  15.8 22.8 %collective-permute-start.1 = (bf16[2,2,64,4,128]{4,2,3,1,0:T(8,128)(2,1)S(1)}, bf16[2,2,64,4,128]{4,2,3,1,0:T(8,128)(2,1)S(1)}, u32[]{:S(2)}, u32[]{:S(2)}) collective-permute-start(bf16[2,2,64,4,128]{4,2,3,1,0:T(8,128)(2,1)S(1)} %pad_maximum_fusion.1), channel_id=1, source_target_pairs={{0,8},{4,12},{8,0},{12,4},{1,9},{5,13},{9,1},{13,5},{2,10},{6,14},... | collective-permute-start | bytes 786440 | tf_op jit(solution)/shard_map/ppermute | solution.py:81
  15.8 22.8 %collective-permute-start = (bf16[2,2,64,4,128]{4,2,3,1,0:T(8,128)(2,1)S(1)}, bf16[2,2,64,4,128]{4,2,3,1,0:T(8,128)(2,1)S(1)}, u32[]{:S(2)}, u32[]{:S(2)}) collective-permute-start(bf16[2,2,64,4,128]{4,2,3,1,0:T(8,128)(2,1)S(1)} %pad_maximum_fusion.1), channel_id=1, source_target_pairs={{0,4},{4,8},{8,12},{12,0},{1,5},{5,9},{9,13},{13,1},{2,6},{6,10},{... | collective-permute-start | bytes 786440 | tf_op jit(solution)/shard_map/ppermute | solution.py:81
  16.9 31.1 %collective-permute-start.11 = (bf16[128,4,1]{0,1,2:T(4,128)(2,1)S(1)}, bf16[128,4,1]{0,1,2:T(4,128)(2,1)S(1)}, u32[]{:S(2)}, u32[]{:S(2)}) collective-permute-start(bf16[128,4,1]{0,1,2:T(4,128)(2,1)S(1)} %get-tuple-element.43), channel_id=1, source_target_pairs={{0,12},{4,0},{8,4},{12,8},{1,13},{5,1},{9,5},{13,9},{2,14},{6,2},{... | collective-permute-start | bytes 3080 | tf_op jit(solution)/shard_map/ppermute | solution.py:150
  39.3 0.9 copy-start.2
  40.7 7.4 %copy-start.4 = (f32[2,512]{1,0:T(2,128)S(1)}, f32[2,512]{1,0:T(2,128)}, u32[]{:S(2)}) copy-start(f32[2,512]{1,0:T(2,128)} %param.15) | copy-start | bytes 12292
  42.3 7.2 %collective-permute-start.15 = (bf16[128,4,1]{0,1,2:T(4,128)(2,1)S(1)}, bf16[128,4,1]{0,1,2:T(4,128)(2,1)S(1)}, u32[]{:S(2)}, u32[]{:S(2)}) collective-permute-start(bf16[128,4,1]{0,1,2:T(4,128)(2,1)S(1)} %get-tuple-element.51), channel_id=1, source_target_pairs={{0,15},{1,12},{2,13},{3,14},{4,3},{5,0},{6,1},{7,2},{8,7},{9,4},{1... | collective-permute-start | bytes 3080 | tf_op jit(solution)/shard_map/ppermute | solution.py:57
  42.6 8.8 %collective-permute-start.14 = (bf16[128,4,1]{0,1,2:T(4,128)(2,1)S(1)}, bf16[128,4,1]{0,1,2:T(4,128)(2,1)S(1)}, u32[]{:S(2)}, u32[]{:S(2)}) collective-permute-start(bf16[128,4,1]{0,1,2:T(4,128)(2,1)S(1)} %get-tuple-element.49), channel_id=1, source_target_pairs={{0,14},{1,15},{2,12},{3,13},{4,2},{5,3},{6,0},{7,1},{8,6},{9,7},{1... | collective-permute-start | bytes 3080 | tf_op jit(solution)/shard_map/ppermute | solution.py:57
  46.9 5.4 %collective-permute-start.13 = (bf16[128,4,1]{0,1,2:T(4,128)(2,1)S(1)}, bf16[128,4,1]{0,1,2:T(4,128)(2,1)S(1)}, u32[]{:S(2)}, u32[]{:S(2)}) collective-permute-start(bf16[128,4,1]{0,1,2:T(4,128)(2,1)S(1)} %get-tuple-element.47), channel_id=1, source_target_pairs={{0,13},{1,14},{2,15},{3,12},{4,1},{5,2},{6,3},{7,0},{8,5},{9,6},{1... | collective-permute-start | bytes 3080 | tf_op jit(solution)/shard_map/ppermute | solution.py:57
  47.2 5.7 %collective-permute-start.12 = (bf16[128,4,1]{0,1,2:T(4,128)(2,1)S(1)}, bf16[128,4,1]{0,1,2:T(4,128)(2,1)S(1)}, u32[]{:S(2)}, u32[]{:S(2)}) collective-permute-start(bf16[128,4,1]{0,1,2:T(4,128)(2,1)S(1)} %get-tuple-element.45), channel_id=1, source_target_pairs={{0,12},{1,13},{2,14},{3,15},{4,0},{5,1},{6,2},{7,3},{8,4},{9,5},{1... | collective-permute-start | bytes 3080 | tf_op jit(solution)/shard_map/ppermute | solution.py:57
  48.1 6.2 %collective-permute-start.6 = (bf16[128,4,1]{0,1,2:T(4,128)(2,1)S(1)}, bf16[128,4,1]{0,1,2:T(4,128)(2,1)S(1)}, u32[]{:S(2)}, u32[]{:S(2)}) collective-permute-start(bf16[128,4,1]{0,1,2:T(4,128)(2,1)S(1)} %get-tuple-element.42), channel_id=1, source_target_pairs={{0,4},{4,8},{8,12},{12,0},{1,5},{5,9},{9,13},{13,1},{2,6},{6,10},{... | collective-permute-start | bytes 3080 | tf_op jit(solution)/shard_map/ppermute | solution.py:149
  49.5 6.9 %collective-permute-start.10 = (bf16[128,4,1]{0,1,2:T(4,128)(2,1)S(1)}, bf16[128,4,1]{0,1,2:T(4,128)(2,1)S(1)}, u32[]{:S(2)}, u32[]{:S(2)}) collective-permute-start(bf16[128,4,1]{0,1,2:T(4,128)(2,1)S(1)} %get-tuple-element.50), channel_id=1, source_target_pairs={{0,7},{1,4},{2,5},{3,6},{4,11},{5,8},{6,9},{7,10},{8,15},{9,12},{1... | collective-permute-start | bytes 3080 | tf_op jit(solution)/shard_map/ppermute | solution.py:57
  51.4 6.3 %collective-permute-start.9 = (bf16[128,4,1]{0,1,2:T(4,128)(2,1)S(1)}, bf16[128,4,1]{0,1,2:T(4,128)(2,1)S(1)}, u32[]{:S(2)}, u32[]{:S(2)}) collective-permute-start(bf16[128,4,1]{0,1,2:T(4,128)(2,1)S(1)} %get-tuple-element.48), channel_id=1, source_target_pairs={{0,6},{1,7},{2,4},{3,5},{4,10},{5,11},{6,8},{7,9},{8,14},{9,15},{1... | collective-permute-start | bytes 3080 | tf_op jit(solution)/shard_map/ppermute | solution.py:57
  52.3 5.7 %collective-permute-start.8 = (bf16[128,4,1]{0,1,2:T(4,128)(2,1)S(1)}, bf16[128,4,1]{0,1,2:T(4,128)(2,1)S(1)}, u32[]{:S(2)}, u32[]{:S(2)}) collective-permute-start(bf16[128,4,1]{0,1,2:T(4,128)(2,1)S(1)} %get-tuple-element.46), channel_id=1, source_target_pairs={{0,5},{1,6},{2,7},{3,4},{4,9},{5,10},{6,11},{7,8},{8,13},{9,14},{1... | collective-permute-start | bytes 3080 | tf_op jit(solution)/shard_map/ppermute | solution.py:57
  52.9 5.4 %collective-permute-start.7 = (bf16[128,4,1]{0,1,2:T(4,128)(2,1)S(1)}, bf16[128,4,1]{0,1,2:T(4,128)(2,1)S(1)}, u32[]{:S(2)}, u32[]{:S(2)}) collective-permute-start(bf16[128,4,1]{0,1,2:T(4,128)(2,1)S(1)} %get-tuple-element.44), channel_id=1, source_target_pairs={{0,4},{1,5},{2,6},{3,7},{4,8},{5,9},{6,10},{7,11},{8,12},{9,13},{1... | collective-permute-start | bytes 3080 | tf_op jit(solution)/shard_map/ppermute | solution.py:57
  54.3 5.9 %collective-permute-start.5 = (bf16[128,4,128]{0,1,2:T(4,128)(2,1)S(1)}, bf16[128,4,128]{0,1,2:T(4,128)(2,1)S(1)}, u32[]{:S(2)}, u32[]{:S(2)}) collective-permute-start(bf16[128,4,128]{0,1,2:T(4,128)(2,1)S(1)} %fusion.109), channel_id=1, source_target_pairs={{0,3},{1,0},{2,1},{3,2},{4,7},{5,4},{6,5},{7,6},{8,11},{9,8},{10,9... | collective-permute-start | bytes 393224 | tf_op jit(solution)/shard_map/ppermute | solution.py:49
  56.4 7.8 %collective-permute-start.4 = (bf16[128,4,128]{0,1,2:T(4,128)(2,1)S(1)}, bf16[128,4,128]{0,1,2:T(4,128)(2,1)S(1)}, u32[]{:S(2)}, u32[]{:S(2)}) collective-permute-start(bf16[128,4,128]{0,1,2:T(4,128)(2,1)S(1)} %fusion.110), channel_id=1, source_target_pairs={{0,2},{1,3},{2,0},{3,1},{4,6},{5,7},{6,4},{7,5},{8,10},{9,11},{10,... | collective-permute-start | bytes 393224 | tf_op jit(solution)/shard_map/ppermute | solution.py:49
  57.7 6.5 %collective-permute-start.3 = (bf16[128,4,128]{0,1,2:T(4,128)(2,1)S(1)}, bf16[128,4,128]{0,1,2:T(4,128)(2,1)S(1)}, u32[]{:S(2)}, u32[]{:S(2)}) collective-permute-start(bf16[128,4,128]{0,1,2:T(4,128)(2,1)S(1)} %fusion.111), channel_id=1, source_target_pairs={{0,1},{1,2},{2,3},{3,0},{4,5},{5,6},{6,7},{7,4},{8,9},{9,10},{10,1... | collective-permute-start | bytes 393224 | tf_op jit(solution)/shard_map/ppermute | solution.py:49
  64.5 9.6 %copy-start.5 = (bf16[2,512,512]{2,1,0:T(8,128)(2,1)S(1)}, bf16[2,512,512]{2,1,0:T(8,128)(2,1)}, u32[]{:S(2)}) copy-start(bf16[2,512,512]{2,1,0:T(8,128)(2,1)} %param.17) | copy-start | bytes 3145732
  77.9 7.5 %collective-permute-start.26 = (bf16[128,4,1]{0,1,2:T(4,128)(2,1)S(1)}, bf16[128,4,1]{0,1,2:T(4,128)(2,1)S(1)}, u32[]{:S(2)}, u32[]{:S(2)}) collective-permute-start(bf16[128,4,1]{0,1,2:T(4,128)(2,1)S(1)} %get-tuple-element.41), channel_id=1, source_target_pairs={{0,15},{1,12},{2,13},{3,14},{4,3},{5,0},{6,1},{7,2},{8,7},{9,4},{1... | collective-permute-start | bytes 3080 | tf_op jit(solution)/shard_map/ppermute | solution.py:57
  80.8 5.5 %collective-permute-start.25 = (bf16[128,4,1]{0,1,2:T(4,128)(2,1)S(1)}, bf16[128,4,1]{0,1,2:T(4,128)(2,1)S(1)}, u32[]{:S(2)}, u32[]{:S(2)}) collective-permute-start(bf16[128,4,1]{0,1,2:T(4,128)(2,1)S(1)} %get-tuple-element.39), channel_id=1, source_target_pairs={{0,14},{1,15},{2,12},{3,13},{4,2},{5,3},{6,0},{7,1},{8,6},{9,7},{1... | collective-permute-start | bytes 3080 | tf_op jit(solution)/shard_map/ppermute | solution.py:57
  82.0 5.3 %collective-permute-start.24 = (bf16[128,4,1]{0,1,2:T(4,128)(2,1)S(1)}, bf16[128,4,1]{0,1,2:T(4,128)(2,1)S(1)}, u32[]{:S(2)}, u32[]{:S(2)}) collective-permute-start(bf16[128,4,1]{0,1,2:T(4,128)(2,1)S(1)} %get-tuple-element.37), channel_id=1, source_target_pairs={{0,13},{1,14},{2,15},{3,12},{4,1},{5,2},{6,3},{7,0},{8,5},{9,6},{1... | collective-permute-start | bytes 3080 | tf_op jit(solution)/shard_map/ppermute | solution.py:57
  82.9 5.8 %collective-permute-start.23 = (bf16[128,4,1]{0,1,2:T(4,128)(2,1)S(1)}, bf16[128,4,1]{0,1,2:T(4,128)(2,1)S(1)}, u32[]{:S(2)}, u32[]{:S(2)}) collective-permute-start(bf16[128,4,1]{0,1,2:T(4,128)(2,1)S(1)} %get-tuple-element.35), channel_id=1, source_target_pairs={{0,12},{1,13},{2,14},{3,15},{4,0},{5,1},{6,2},{7,3},{8,4},{9,5},{1... | collective-permute-start | bytes 3080 | tf_op jit(solution)/shard_map/ppermute | solution.py:57
  84.0 10.1 %collective-permute-start.18 = (bf16[128,4,128]{0,1,2:T(4,128)(2,1)S(1)}, bf16[128,4,128]{0,1,2:T(4,128)(2,1)S(1)}, u32[]{:S(2)}, u32[]{:S(2)}) collective-permute-start(bf16[128,4,128]{0,1,2:T(4,128)(2,1)S(1)} %fusion.104), channel_id=1, source_target_pairs={{0,3},{1,0},{2,1},{3,2},{4,7},{5,4},{6,5},{7,6},{8,11},{9,8},{10,9... | collective-permute-start | bytes 393224 | tf_op jit(solution)/shard_map/ppermute | solution.py:49
  85.4 4.9 %collective-permute-start.22 = (bf16[128,4,1]{0,1,2:T(4,128)(2,1)S(1)}, bf16[128,4,1]{0,1,2:T(4,128)(2,1)S(1)}, u32[]{:S(2)}, u32[]{:S(2)}) collective-permute-start(bf16[128,4,1]{0,1,2:T(4,128)(2,1)S(1)} %get-tuple-element.40), channel_id=1, source_target_pairs={{0,7},{1,4},{2,5},{3,6},{4,11},{5,8},{6,9},{7,10},{8,15},{9,12},{1... | collective-permute-start | bytes 3080 | tf_op jit(solution)/shard_map/ppermute | solution.py:57
  86.3 6.3 %collective-permute-start.21 = (bf16[128,4,1]{0,1,2:T(4,128)(2,1)S(1)}, bf16[128,4,1]{0,1,2:T(4,128)(2,1)S(1)}, u32[]{:S(2)}, u32[]{:S(2)}) collective-permute-start(bf16[128,4,1]{0,1,2:T(4,128)(2,1)S(1)} %get-tuple-element.38), channel_id=1, source_target_pairs={{0,6},{1,7},{2,4},{3,5},{4,10},{5,11},{6,8},{7,9},{8,14},{9,15},{1... | collective-permute-start | bytes 3080 | tf_op jit(solution)/shard_map/ppermute | solution.py:57
  87.3 5.7 %collective-permute-start.20 = (bf16[128,4,1]{0,1,2:T(4,128)(2,1)S(1)}, bf16[128,4,1]{0,1,2:T(4,128)(2,1)S(1)}, u32[]{:S(2)}, u32[]{:S(2)}) collective-permute-start(bf16[128,4,1]{0,1,2:T(4,128)(2,1)S(1)} %get-tuple-element.36), channel_id=1, source_target_pairs={{0,5},{1,6},{2,7},{3,4},{4,9},{5,10},{6,11},{7,8},{8,13},{9,14},{1... | collective-permute-start | bytes 3080 | tf_op jit(solution)/shard_map/ppermute | solution.py:57
  88.7 5.4 %collective-permute-start.19 = (bf16[128,4,1]{0,1,2:T(4,128)(2,1)S(1)}, bf16[128,4,1]{0,1,2:T(4,128)(2,1)S(1)}, u32[]{:S(2)}, u32[]{:S(2)}) collective-permute-start(bf16[128,4,1]{0,1,2:T(4,128)(2,1)S(1)} %get-tuple-element.34), channel_id=1, source_target_pairs={{0,4},{1,5},{2,6},{3,7},{4,8},{5,9},{6,10},{7,11},{8,12},{9,13},{1... | collective-permute-start | bytes 3080 | tf_op jit(solution)/shard_map/ppermute | solution.py:57
  90.4 6.1 %collective-permute-start.17 = (bf16[128,4,128]{0,1,2:T(4,128)(2,1)S(1)}, bf16[128,4,128]{0,1,2:T(4,128)(2,1)S(1)}, u32[]{:S(2)}, u32[]{:S(2)}) collective-permute-start(bf16[128,4,128]{0,1,2:T(4,128)(2,1)S(1)} %fusion.105), channel_id=1, source_target_pairs={{0,2},{1,3},{2,0},{3,1},{4,6},{5,7},{6,4},{7,5},{8,10},{9,11},{10,... | collective-permute-start | bytes 393224 | tf_op jit(solution)/shard_map/ppermute | solution.py:49
  92.6 4.9 %collective-permute-start.16 = (bf16[128,4,128]{0,1,2:T(4,128)(2,1)S(1)}, bf16[128,4,128]{0,1,2:T(4,128)(2,1)S(1)}, u32[]{:S(2)}, u32[]{:S(2)}) collective-permute-start(bf16[128,4,128]{0,1,2:T(4,128)(2,1)S(1)} %fusion.106), channel_id=1, source_target_pairs={{0,1},{1,2},{2,3},{3,0},{4,5},{5,6},{6,7},{7,4},{8,9},{9,10},{10,1... | collective-permute-start | bytes 393224 | tf_op jit(solution)/shard_map/ppermute | solution.py:49
  110.8 4.8 %collective-permute-start.29 = (bf16[128,4,128]{0,1,2:T(4,128)(2,1)S(1)}, bf16[128,4,128]{0,1,2:T(4,128)(2,1)S(1)}, u32[]{:S(2)}, u32[]{:S(2)}) collective-permute-start(bf16[128,4,128]{0,1,2:T(4,128)(2,1)S(1)} %fusion.99), channel_id=1, source_target_pairs={{0,3},{1,0},{2,1},{3,2},{4,7},{5,4},{6,5},{7,6},{8,11},{9,8},{10,9... | collective-permute-start | bytes 393224 | tf_op jit(solution)/shard_map/ppermute | solution.py:49
  112.0 7.9 %collective-permute-start.28 = (bf16[128,4,128]{0,1,2:T(4,128)(2,1)S(1)}, bf16[128,4,128]{0,1,2:T(4,128)(2,1)S(1)}, u32[]{:S(2)}, u32[]{:S(2)}) collective-permute-start(bf16[128,4,128]{0,1,2:T(4,128)(2,1)S(1)} %fusion.100), channel_id=1, source_target_pairs={{0,2},{1,3},{2,0},{3,1},{4,6},{5,7},{6,4},{7,5},{8,10},{9,11},{10,... | collective-permute-start | bytes 393224 | tf_op jit(solution)/shard_map/ppermute | solution.py:49
  113.3 6.6 %collective-permute-start.27 = (bf16[128,4,128]{0,1,2:T(4,128)(2,1)S(1)}, bf16[128,4,128]{0,1,2:T(4,128)(2,1)S(1)}, u32[]{:S(2)}, u32[]{:S(2)}) collective-permute-start(bf16[128,4,128]{0,1,2:T(4,128)(2,1)S(1)} %fusion.101), channel_id=1, source_target_pairs={{0,1},{1,2},{2,3},{3,0},{4,5},{5,6},{6,7},{7,4},{8,9},{9,10},{10,1... | collective-permute-start | bytes 393224 | tf_op jit(solution)/shard_map/ppermute | solution.py:49

commit v3 on v1

--- a/solution.py
+++ b/solution.py
@@ -14,19 +14,6 @@
 band_start = 30.0
 grid_step = 0.25
 epsilon = 1e-06
-
-
-def with_halo(array, sides, width):
-    for axis, dim in sides:
-        devices, length = (lax.axis_size(axis), array.shape[dim])
-        up = [(i, (i + 1) % devices) for i in range(devices)]
-        down = [(j, i) for i, j in up]
-        last = lax.slice_in_dim(array, length - width, length, axis=dim)
-        leading = lax.slice_in_dim(array, 0, width, axis=dim)
-        before = lax.ppermute(last, axis, up)
-        after = lax.ppermute(leading, axis, down)
-        array = jnp.concatenate([before, array, after], axis=dim)
-    return array
 
 
 def secant_rows(count):
@@ -91,13 +78,13 @@
     return (numerator, jnp.sum(weights, axis=3))
 
 
-def block_apply(extended, block_index, stencil_weight, block_gain, up_weight, down_weight):
-    lat_rows = extended.shape[1]
-    out_cols = extended.shape[2] - 2
+def block_apply(state, block_index, stencil_weight, block_gain, up_weight, down_weight):
+    lat_rows = state.shape[1]
+    out_cols = state.shape[2] - 2
     secants = secant_rows(lat_rows)[None, :, None]
-    padded = jnp.pad(extended.astype(jnp.float32), ((0, 0), (1, 1), (0, 0)))
+    padded = jnp.pad(state.astype(jnp.float32), ((0, 0), (1, 1), (0, 0)))
     tap_weights = stencil_weight[block_index]
-    stencil_sum = jnp.zeros((extended.shape[0], lat_rows, out_cols), jnp.float32)
+    stencil_sum = jnp.zeros((state.shape[0], lat_rows, out_cols), jnp.float32)
     for row_step in (-1, 0, 1):
         for col_step in (-1, 0, 1):
             shifted = padded[
@@ -118,8 +105,12 @@
         jnp.dot(up_weight[block_index], block_normed, preferred_element_type=jnp.float32)
     ).astype(jnp.bfloat16)
     update = spread_sum(down_weight[block_index], hidden)
-    center = extended[:, :, 1:-1]
+    center = state[:, :, 1:-1]
     return (center.astype(jnp.float32) + update.reshape(center.shape)).astype(jnp.bfloat16)
+
+
+def edges(values, width):
+    return jnp.concatenate([values[..., :width], values[..., -width:]], axis=-1)
 
 
 def per_device(
@@ -128,6 +119,7 @@
     ch_local, lat_rows, columns = latent.shape
     head_size = C // H
     heads_local = qkv_weight.shape[1] // head_size
+    reach = BLOCKS
     gathered = gather_channels(latent)
     normed = norm_channels(gathered.astype(jnp.float32), att_gain).astype(jnp.bfloat16)
     projected = jnp.einsum("koc,crw->korw", qkv_weight, normed, preferred_element_type=jnp.float32)
@@ -135,16 +127,38 @@
     queries = unit_heads(projected[0]).astype(jnp.bfloat16)
     key_rows = unit_heads(projected[1]).astype(jnp.bfloat16)
     value_rows = projected[2].astype(jnp.bfloat16)
-    key_value = gather_strips(jnp.stack([key_rows, value_rows]), "lon")
-    numerator, denominator = make_fold(queries, (key_value[0], key_value[1]))
+
+    key_value = jnp.stack([key_rows, value_rows]).reshape(-1, lat_rows, columns)
+    rim = jnp.stack([edges(queries.reshape(ch_local, lat_rows, columns), reach), edges(latent, reach)])
+    rim_rows = rim.size // (lat_rows * columns)
+    payload = jnp.concatenate([key_value, rim.reshape(rim_rows, lat_rows, columns)], axis=0)
+    strips = lax.axis_size("lon")
+    pieces = [key_value]
+    from_left = from_right = None
+    for shift in range(1, strips):
+        pairs = [(i, (i + shift) % strips) for i in range(strips)]
+        sent = payload if shift in (1, strips - 1) else key_value
+        got = lax.ppermute(sent, "lon", pairs)
+        pieces.append(got[: key_value.shape[0]])
+        if shift == 1:
+            from_left = got[key_value.shape[0] :].reshape(rim.shape)[..., reach:]
+        if shift == strips - 1:
+            from_right = got[key_value.shape[0] :].reshape(rim.shape)[..., :reach]
+    all_keys = jnp.concatenate(pieces, axis=-1).reshape(2, heads_local, head_size, lat_rows, -1)
+    wide_queries = jnp.concatenate(
+        [from_left[0], queries.reshape(ch_local, lat_rows, columns), from_right[0]], axis=-1
+    ).reshape(heads_local, head_size, lat_rows, -1)
+    wide_latent = jnp.concatenate([from_left[1], latent, from_right[1]], axis=-1)
+
+    numerator, denominator = make_fold(wide_queries, (all_keys[0], all_keys[1]))
     attended = (numerator / denominator[:, None]).astype(jnp.bfloat16)
     update = spread_sum(out_weight, attended.reshape(ch_local, -1))
-    latent_state = (latent.astype(jnp.float32) + update.reshape(latent.shape)).astype(jnp.bfloat16)
-    current = latent_state
+    current = (wide_latent.astype(jnp.float32) + update.reshape(wide_latent.shape)).astype(
+        jnp.bfloat16
+    )
     for block_index in range(BLOCKS):
-        extended = with_halo(current, (("lon", 2),), 1)
         current = block_apply(
-            extended, block_index, stencil_weight, block_gain, up_weight, down_weight
+            current, block_index, stencil_weight, block_gain, up_weight, down_weight
         )
     return current
 

time: 113 us -> 91.9 us (0.81)
  the two profiles are of different devices: /device:TPU:0 before, /device:TPU:20 now
where the time goes in v3:
time: 91.9 us; the launch traced here: 91.6 us
  waiting for transfers between devices  40.2 us (44%)
  blocking collectives  22.2 us (24%)
  starting transfers between devices  9.74 us (11%)
  local copies, waits for them, and re-layouts  8.15 us (9%)
  matrix products  6.25 us (7%)
  other arithmetic  4.44 us (5%)
    all_gather x3, blocking collectives, gather_channels(): return lax.all_gather(values, 'lev', axis=0, tiled=True)  22.2 us
    ppermute x3, waiting for transfers between devices, per_device(): got = lax.ppermute(sent, 'lon', pairs)  21.4 us
    ppermute x9, waiting for transfers between devices, scatter_sum(): total = total + lax.ppermute(chunk, axis, pairs).astype(jnp.float32)  18.8 us
    ppermute x9, starting transfers between devices, scatter_sum(): total = total + lax.ppermute(chunk, axis, pairs).astype(jnp.float32)  6.88 us
    dot_general x3, matrix products, spread_sum(): lax.dot_general(weight, activation, (((0,), (0,)), ((), ())), preferred_e...  4.42 us
    ppermute x3, starting transfers between devices, per_device(): got = lax.ppermute(sent, 'lon', pairs)  2.86 us
    another operation x2, local copies, waits for them, and re-layouts, scatter_sum(): total = jnp.take(blocks, me, axis=0).astype(jnp.float32)  2.23 us
  transfers between devices with their start and end apart: 12, of which 11 were waited for; matrix products, arithmetic and copies ran while one was open for 3% of the time, Pallas kernels for 0%

profile of v3, /device:TPU:20, one launch (start us, length us, event | category | flops | bytes accessed | tf_op | source)
XLA Modules:
  0.0 91.6 jit_solution(15292610804997549383)
XLA Ops:
  0.0 7.5 %all_gather.9 = bf16[512,4,128]{2,1,0:T(4,128)(2,1)S(1)} all-gather(bf16[128,4,128]{2,1,0:T(4,128)(2,1)} %param.14), channel_id=1, replica_groups=mesh['member'=2,'lon'=4,'lev'=4] {'lev'}, dimensions={0}, use_global_device_ids=true | all-gather | bytes 655360 | tf_op jit(solution)/shard_map/all_gather | solution.py:34
  7.5 0.5 fusion.19
  8.1 1.5 %fusion.37 = bf16[512,4,128,1]{2,1,0,3:T(4,128)(2,1)S(1)} fusion(bf16[512,4,128]{2,1,0:T(4,128)(2,1)S(1)} %all_gather.9, f32[512]{0:T(512)S(1)} %copy-done.5, f32[4,128]{1,0:T(4,128)S(1)} %add_rsqrt_fusion.4), kind=kLoop, calls=%fused_computation.65 | loop fusion | flops 1048576 | bytes 1052672 | tf_op jit(solution)/shard_map/convert_element_type | solution.py:124
  9.6 0.4 convolution_bitcast_fusion.2
  10.2 0.4 collective-permute-start.2
  10.6 0.3 copy-done.1
  10.9 0.1 copy.62
  11.2 0.1 fusion.117
  11.3 0.1 copy.60
  11.4 0.1 copy.61
  11.6 0.2 copy.64
  11.8 0.3 reshape.592
  12.2 2.5 %collective-permute-start.1 = (bf16[264,4,128]{2,0,1:T(8,128)(2,1)S(1)}, bf16[264,4,128]{2,0,1:T(8,128)(2,1)S(1)}, u32[]{:S(2)}, u32[]{:S(2)}) collective-permute-start(bf16[264,4,128]{2,0,1:T(8,128)(2,1)S(1)} %pad_maximum_fusion.1), channel_id=1, source_target_pairs={{0,12},{4,0},{8,4},{12,8},{1,13},{5,1},{9,5},{13,9},{2,14},{6,2},{... | collective-permute-start | bytes 811016 | tf_op jit(solution)/shard_map/ppermute | solution.py:141
  14.9 19.1 %collective-permute-done.1 = bf16[264,4,128]{2,0,1:T(8,128)(2,1)S(1)} collective-permute-done((bf16[264,4,128]{2,0,1:T(8,128)(2,1)S(1)}, bf16[264,4,128]{2,0,1:T(8,128)(2,1)S(1)}, u32[]{:S(2)}, u32[]{:S(2)}) %collective-permute-start.1) | collective-permute-done | bytes 270368 | tf_op jit(solution)/shard_map/ppermute | solution.py:141
  34.0 0.6 reshape.594
  34.5 0.1 slice_bitcast_fusion
  34.7 2.3 %collective-permute-done = bf16[264,4,128]{2,0,1:T(8,128)(2,1)S(1)} collective-permute-done((bf16[264,4,128]{2,0,1:T(8,128)(2,1)S(1)}, bf16[264,4,128]{2,0,1:T(8,128)(2,1)S(1)}, u32[]{:S(2)}, u32[]{:S(2)}) %collective-permute-start) | collective-permute-done | bytes 270368 | tf_op jit(solution)/shard_map/ppermute | solution.py:141
  37.1 0.1 pad_maximum_fusion
  37.2 0.1 fusion.116
  37.3 0.6 reshape.593
  37.9 0.2 slice_bitcast_fusion.1
  38.1 0.9 fusion
  39.0 0.5 fusion.5
  39.6 0.3 copy.78
  39.9 0.2 reshape.595
  40.0 0.3 fusion.2
  40.3 0.1 reshape.596
  40.5 1.1 %constant_dynamic-slice_fusion.7 = (bf16[1,128,528]{1,0,2:T(2,128)(2,1)S(1)}, bf16[1,128,528]{1,0,2:T(2,128)(2,1)S(1)}, bf16[1,128,528]{1,0,2:T(2,128)(2,1)S(1)}, bf16[1,128,528]{1,0,2:T(2,128)(2,1)S(1)}) fusion(bf16[4,128,528]{1,0,2:T(4,128)(2,1)S(1)} %reshape.596, s32[]{:T(128)S(6)} %select_n.78, s32[]{:T(128)S(6)} %select_n.82, s32[]{:T(128)S(6)} %select_n.80, ...), kind=kLoop, calls=%fused_computation.173 | loop fusion | bytes 1081360 | tf_op jit(solution)/shard_map/jit(_take) | solution.py:41
  41.6 0.8 collective-permute-start.5
  42.6 1.0 %collective-permute-start.4 = (bf16[128,528]{0,1:T(8,128)(2,1)S(1)}, bf16[128,528]{0,1:T(8,128)(2,1)S(1)}, u32[]{:S(2)}, u32[]{:S(2)}) collective-permute-start(bf16[128,528]{0,1:T(8,128)(2,1)S(1)} %fusion.97), channel_id=1, source_target_pairs={{0,2},{1,3},{2,0},{3,1},{4,6},{5,7},{6,4},{7,5},{8,10},{9,11},{10,... | collective-permute-start | bytes 405512 | tf_op jit(solution)/shard_map/ppermute | solution.py:45
  43.6 0.1 copy.70
  43.7 0.1 copy.68
  43.8 2.3 %collective-permute-done.5 = bf16[128,528]{0,1:T(8,128)(2,1)S(1)} collective-permute-done((bf16[128,528]{0,1:T(8,128)(2,1)S(1)}, bf16[128,528]{0,1:T(8,128)(2,1)S(1)}, u32[]{:S(2)}, u32[]{:S(2)}) %collective-permute-start.5) | collective-permute-done | bytes 135200 | tf_op jit(solution)/shard_map/ppermute | solution.py:45
  46.1 2.3 %collective-permute-done.3 = bf16[128,528]{0,1:T(8,128)(2,1)S(1)} collective-permute-done((bf16[128,528]{0,1:T(8,128)(2,1)S(1)}, bf16[128,528]{0,1:T(8,128)(2,1)S(1)}, u32[]{:S(2)}, u32[]{:S(2)}) %collective-permute-start.3) | collective-permute-done | bytes 135200 | tf_op jit(solution)/shard_map/ppermute | solution.py:45
  48.3 1.8 %collective-permute-done.4 = bf16[128,528]{0,1:T(8,128)(2,1)S(1)} collective-permute-done((bf16[128,528]{0,1:T(8,128)(2,1)S(1)}, bf16[128,528]{0,1:T(8,128)(2,1)S(1)}, u32[]{:S(2)}, u32[]{:S(2)}) %collective-permute-start.4) | collective-permute-done | bytes 135200 | tf_op jit(solution)/shard_map/ppermute | solution.py:45
  50.2 0.1 convert_add_fusion
  50.3 0.2 fusion.68
  50.5 7.5 %all_gather.10 = bf16[512,4,130]{0,2,1:T(8,128)(2,1)S(1)} all-gather(bf16[128,4,130]{0,2,1:T(8,128)(2,1)S(1)} %fusion.68), channel_id=1, replica_groups=mesh['member'=2,'lon'=4,'lev'=4] {'lev'}, dimensions={0}, use_global_device_ids=true | all-gather | bytes 665600 | tf_op jit(solution)/shard_map/all_gather | solution.py:34
  58.0 0.2 fusion.6
  58.3 0.2 fusion.8
  58.5 0.1 reshape.598
  58.6 0.8 copy-done.6
  59.5 2.0 %fusion.3 = bf16[512,520]{0,1:T(8,128)(2,1)S(1)} fusion(bf16[512,520]{0,1:T(8,128)(2,1)S(1)} %reshape.598, bf16[2,512,512]{2,1,0:T(8,128)(2,1)S(1)} %copy-done.6, bf16[2,512,512]{2,1,0:T(8,128)(2,1)} %param.20), kind=kOutput, calls=%fused_computation.18 | convolution fusion | flops 547921920 | bytes 2113536 | tf_op jit(solution)/shard_map/dot_general | solution.py:50
  61.5 0.1 reshape.599
  61.6 1.1 %constant_dynamic-slice_fusion.2 = (bf16[1,128,520]{1,0,2:T(2,128)(2,1)S(1)}, bf16[1,128,520]{1,0,2:T(2,128)(2,1)S(1)}, bf16[1,128,520]{1,0,2:T(2,128)(2,1)S(1)}, bf16[1,128,520]{1,0,2:T(2,128)(2,1)S(1)}) fusion(bf16[4,128,520]{1,0,2:T(4,128)(2,1)S(1)} %reshape.599, s32[]{:T(128)S(6)} %select_n.78, s32[]{:T(128)S(6)} %select_n.82, s32[]{:T(128)S(6)} %select_n.80, ...), kind=kLoop, calls=%fused_computation.168 | loop fusion | bytes 1064976 | tf_op jit(solution)/shard_map/jit(_take) | solution.py:41
  62.9 1.1 %collective-permute-start.8 = (bf16[128,520]{0,1:T(8,128)(2,1)S(1)}, bf16[128,520]{0,1:T(8,128)(2,1)S(1)}, u32[]{:S(2)}, u32[]{:S(2)}) collective-permute-start(bf16[128,520]{0,1:T(8,128)(2,1)S(1)} %fusion.100), channel_id=1, source_target_pairs={{0,3},{1,0},{2,1},{3,2},{4,7},{5,4},{6,5},{7,6},{8,11},{9,8},{10,9... | collective-permute-start | bytes 399368 | tf_op jit(solution)/shard_map/ppermute | solution.py:45
  64.0 1.0 %collective-permute-start.7 = (bf16[128,520]{0,1:T(8,128)(2,1)S(1)}, bf16[128,520]{0,1:T(8,128)(2,1)S(1)}, u32[]{:S(2)}, u32[]{:S(2)}) collective-permute-start(bf16[128,520]{0,1:T(8,128)(2,1)S(1)} %fusion.101), channel_id=1, source_target_pairs={{0,2},{1,3},{2,0},{3,1},{4,6},{5,7},{6,4},{7,5},{8,10},{9,11},{10,... | collective-permute-start | bytes 399368 | tf_op jit(solution)/shard_map/ppermute | solution.py:45
  64.9 2.7 %collective-permute-done.8 = bf16[128,520]{0,1:T(8,128)(2,1)S(1)} collective-permute-done((bf16[128,520]{0,1:T(8,128)(2,1)S(1)}, bf16[128,520]{0,1:T(8,128)(2,1)S(1)}, u32[]{:S(2)}, u32[]{:S(2)}) %collective-permute-start.8) | collective-permute-done | bytes 133152 | tf_op jit(solution)/shard_map/ppermute | solution.py:45
  67.7 2.1 %collective-permute-done.6 = bf16[128,520]{0,1:T(8,128)(2,1)S(1)} collective-permute-done((bf16[128,520]{0,1:T(8,128)(2,1)S(1)}, bf16[128,520]{0,1:T(8,128)(2,1)S(1)}, u32[]{:S(2)}, u32[]{:S(2)}) %collective-permute-start.6) | collective-permute-done | bytes 133152 | tf_op jit(solution)/shard_map/ppermute | solution.py:45
  69.8 1.9 %collective-permute-done.7 = bf16[128,520]{0,1:T(8,128)(2,1)S(1)} collective-permute-done((bf16[128,520]{0,1:T(8,128)(2,1)S(1)}, bf16[128,520]{0,1:T(8,128)(2,1)S(1)}, u32[]{:S(2)}, u32[]{:S(2)}) %collective-permute-start.7) | collective-permute-done | bytes 133152 | tf_op jit(solution)/shard_map/ppermute | solution.py:45
  71.9 0.2 fusion.83
  72.1 7.2 %all_gather.11 = bf16[512,4,128]{0,2,1:T(8,128)(2,1)S(1)} all-gather(bf16[128,4,128]{0,2,1:T(8,128)(2,1)S(1)} %fusion.83), channel_id=1, replica_groups=mesh['member'=2,'lon'=4,'lev'=4] {'lev'}, dimensions={0}, use_global_device_ids=true | all-gather | bytes 655360 | tf_op jit(solution)/shard_map/all_gather | solution.py:34
  79.3 0.2 fusion.22
  79.5 0.2 fusion.24
  79.7 2.1 %convolution_convert_fusion.2 = bf16[512,512]{0,1:T(8,128)(2,1)S(1)} fusion(bf16[512,512]{0,1:T(8,128)(2,1)S(1)} %bitcast.168, bf16[2,512,512]{2,1,0:T(8,128)(2,1)S(1)} %copy-done.6, bf16[2,512,512]{2,1,0:T(8,128)(2,1)} %param.20), kind=kOutput, calls=%fused_computation.15 | convolution fusion | flops 539492352 | bytes 2097152 | tf_op jit(solution)/shard_map/dot_general | solution.py:50
  81.9 0.4 collective-permute-start.9
  82.3 1.4 %collective-permute-start.11 = (bf16[128,512]{1,0:T(8,128)(2,1)S(1)}, bf16[128,512]{1,0:T(8,128)(2,1)S(1)}, u32[]{:S(2)}, u32[]{:S(2)}) collective-permute-start(bf16[128,512]{1,0:T(8,128)(2,1)S(1)} %get-tuple-element.59), channel_id=1, source_target_pairs={{0,3},{1,0},{2,1},{3,2},{4,7},{5,4},{6,5},{7,6},{8,11},{9,8},{10,9... | collective-permute-start | bytes 393224 | tf_op jit(solution)/shard_map/ppermute | solution.py:45
  83.7 1.1 %collective-permute-start.10 = (bf16[128,512]{1,0:T(8,128)(2,1)S(1)}, bf16[128,512]{1,0:T(8,128)(2,1)S(1)}, u32[]{:S(2)}, u32[]{:S(2)}) collective-permute-start(bf16[128,512]{1,0:T(8,128)(2,1)S(1)} %get-tuple-element.60), channel_id=1, source_target_pairs={{0,2},{1,3},{2,0},{3,1},{4,6},{5,7},{6,4},{7,5},{8,10},{9,11},{10,... | collective-permute-start | bytes 393224 | tf_op jit(solution)/shard_map/ppermute | solution.py:45
  84.8 1.5 %collective-permute-done.9 = bf16[128,512]{1,0:T(8,128)(2,1)S(1)} collective-permute-done((bf16[128,512]{1,0:T(8,128)(2,1)S(1)}, bf16[128,512]{1,0:T(8,128)(2,1)S(1)}, u32[]{:S(2)}, u32[]{:S(2)}) %collective-permute-start.9) | collective-permute-done | bytes 131104 | tf_op jit(solution)/shard_map/ppermute | solution.py:45
  86.3 1.3 %collective-permute-done.11 = bf16[128,512]{1,0:T(8,128)(2,1)S(1)} collective-permute-done((bf16[128,512]{1,0:T(8,128)(2,1)S(1)}, bf16[128,512]{1,0:T(8,128)(2,1)S(1)}, u32[]{:S(2)}, u32[]{:S(2)}) %collective-permute-start.11) | collective-permute-done | bytes 131104 | tf_op jit(solution)/shard_map/ppermute | solution.py:45
  87.6 2.9 %collective-permute-done.10 = bf16[128,512]{1,0:T(8,128)(2,1)S(1)} collective-permute-done((bf16[128,512]{1,0:T(8,128)(2,1)S(1)}, bf16[128,512]{1,0:T(8,128)(2,1)S(1)}, u32[]{:S(2)}, u32[]{:S(2)}) %collective-permute-start.10) | collective-permute-done | bytes 131104 | tf_op jit(solution)/shard_map/ppermute | solution.py:45
  90.5 0.1 convert_add_fusion.2
  90.6 0.1 copy.87
  90.8 0.8 copy.88
  (60 shorter events, 1.2 us)
Async XLA Ops:
  0.0 9.6 %copy-start = (bf16[3,128,512]{2,1,0:T(8,128)(2,1)S(1)}, bf16[3,128,512]{2,1,0:T(8,128)(2,1)}, u32[]{:S(2)}) copy-start(bf16[3,128,512]{2,1,0:T(8,128)(2,1)} %param.16) | copy-start | bytes 1179652
  0.0 8.1 %copy-start.5 = (f32[512]{0:T(512)S(1)}, f32[512]{0:T(512)}, u32[]{:S(2)}) copy-start(f32[512]{0:T(512)} %param.15) | copy-start | bytes 6148
  10.0 0.9 copy-start.1
  10.2 26.8 %collective-permute-start.2 = (bf16[256,4,128]{2,0,1:T(8,128)(2,1)S(1)}, bf16[256,4,128]{2,0,1:T(8,128)(2,1)S(1)}, u32[]{:S(2)}, u32[]{:S(2)}) collective-permute-start(bf16[256,4,128]{2,0,1:T(8,128)(2,1)S(1)} %bitcast.159), channel_id=1, source_target_pairs={{0,8},{4,12},{8,0},{12,4},{1,9},{5,13},{9,1},{13,5},{2,10},{6,14},... | collective-permute-start | bytes 786440 | tf_op jit(solution)/shard_map/ppermute | solution.py:141
  11.1 3.5 %copy-start.3 = (f32[2,9,128]{2,0,1:T(2,128)S(1)}, f32[2,9,128]{2,0,1:T(2,128)}, u32[]{:S(2)}) copy-start(f32[2,9,128]{2,0,1:T(2,128)} %param.18) | copy-start | bytes 27652
  12.2 21.8 %collective-permute-start.1 = (bf16[264,4,128]{2,0,1:T(8,128)(2,1)S(1)}, bf16[264,4,128]{2,0,1:T(8,128)(2,1)S(1)}, u32[]{:S(2)}, u32[]{:S(2)}) collective-permute-start(bf16[264,4,128]{2,0,1:T(8,128)(2,1)S(1)} %pad_maximum_fusion.1), channel_id=1, source_target_pairs={{0,12},{4,0},{8,4},{12,8},{1,13},{5,1},{9,5},{13,9},{2,14},{6,2},{... | collective-permute-start | bytes 811016 | tf_op jit(solution)/shard_map/ppermute | solution.py:141
  14.6 22.4 %collective-permute-start = (bf16[264,4,128]{2,0,1:T(8,128)(2,1)S(1)}, bf16[264,4,128]{2,0,1:T(8,128)(2,1)S(1)}, u32[]{:S(2)}, u32[]{:S(2)}) collective-permute-start(bf16[264,4,128]{2,0,1:T(8,128)(2,1)S(1)} %pad_maximum_fusion.1), channel_id=1, source_target_pairs={{0,4},{4,8},{8,12},{12,0},{1,5},{5,9},{9,13},{13,1},{2,6},{6,10},{... | collective-permute-start | bytes 811016 | tf_op jit(solution)/shard_map/ppermute | solution.py:141
  39.0 1.0 %copy-start.2 = (bf16[128,512]{1,0:T(8,128)(2,1)S(1)}, bf16[128,512]{1,0:T(8,128)(2,1)}, u32[]{:S(2)}) copy-start(bf16[128,512]{1,0:T(8,128)(2,1)} %param.17) | copy-start | bytes 393220
  41.6 2.0 %copy-start.4 = (f32[2,512]{1,0:T(2,128)S(1)}, f32[2,512]{1,0:T(2,128)}, u32[]{:S(2)}) copy-start(f32[2,512]{1,0:T(2,128)} %param.19) | copy-start | bytes 12292
  41.6 4.4 %collective-permute-start.5 = (bf16[128,528]{0,1:T(8,128)(2,1)S(1)}, bf16[128,528]{0,1:T(8,128)(2,1)S(1)}, u32[]{:S(2)}, u32[]{:S(2)}) collective-permute-start(bf16[128,528]{0,1:T(8,128)(2,1)S(1)} %fusion.96), channel_id=1, source_target_pairs={{0,3},{1,0},{2,1},{3,2},{4,7},{5,4},{6,5},{7,6},{8,11},{9,8},{10,9... | collective-permute-start | bytes 405512 | tf_op jit(solution)/shard_map/ppermute | solution.py:45
  42.5 5.9 %collective-permute-start.3 = (bf16[128,528]{0,1:T(8,128)(2,1)S(1)}, bf16[128,528]{0,1:T(8,128)(2,1)S(1)}, u32[]{:S(2)}, u32[]{:S(2)}) collective-permute-start(bf16[128,528]{0,1:T(8,128)(2,1)S(1)} %fusion.98), channel_id=1, source_target_pairs={{0,1},{1,2},{2,3},{3,0},{4,5},{5,6},{6,7},{7,4},{8,9},{9,10},{10,1... | collective-permute-start | bytes 405512 | tf_op jit(solution)/shard_map/ppermute | solution.py:45
  42.6 7.6 %collective-permute-start.4 = (bf16[128,528]{0,1:T(8,128)(2,1)S(1)}, bf16[128,528]{0,1:T(8,128)(2,1)S(1)}, u32[]{:S(2)}, u32[]{:S(2)}) collective-permute-start(bf16[128,528]{0,1:T(8,128)(2,1)S(1)} %fusion.97), channel_id=1, source_target_pairs={{0,2},{1,3},{2,0},{3,1},{4,6},{5,7},{6,4},{7,5},{8,10},{9,11},{10,... | collective-permute-start | bytes 405512 | tf_op jit(solution)/shard_map/ppermute | solution.py:45
  58.3 1.2 %copy-start.6 = (bf16[2,512,512]{2,1,0:T(8,128)(2,1)S(1)}, bf16[2,512,512]{2,1,0:T(8,128)(2,1)}, u32[]{:S(2)}) copy-start(bf16[2,512,512]{2,1,0:T(8,128)(2,1)} %param.21) | copy-start | bytes 3145732
  62.9 4.8 %collective-permute-start.8 = (bf16[128,520]{0,1:T(8,128)(2,1)S(1)}, bf16[128,520]{0,1:T(8,128)(2,1)S(1)}, u32[]{:S(2)}, u32[]{:S(2)}) collective-permute-start(bf16[128,520]{0,1:T(8,128)(2,1)S(1)} %fusion.100), channel_id=1, source_target_pairs={{0,3},{1,0},{2,1},{3,2},{4,7},{5,4},{6,5},{7,6},{8,11},{9,8},{10,9... | collective-permute-start | bytes 399368 | tf_op jit(solution)/shard_map/ppermute | solution.py:45
  64.0 5.8 %collective-permute-start.6 = (bf16[128,520]{0,1:T(8,128)(2,1)S(1)}, bf16[128,520]{0,1:T(8,128)(2,1)S(1)}, u32[]{:S(2)}, u32[]{:S(2)}) collective-permute-start(bf16[128,520]{0,1:T(8,128)(2,1)S(1)} %fusion.102), channel_id=1, source_target_pairs={{0,1},{1,2},{2,3},{3,0},{4,5},{5,6},{6,7},{7,4},{8,9},{9,10},{10,1... | collective-permute-start | bytes 399368 | tf_op jit(solution)/shard_map/ppermute | solution.py:45
  64.0 7.7 %collective-permute-start.7 = (bf16[128,520]{0,1:T(8,128)(2,1)S(1)}, bf16[128,520]{0,1:T(8,128)(2,1)S(1)}, u32[]{:S(2)}, u32[]{:S(2)}) collective-permute-start(bf16[128,520]{0,1:T(8,128)(2,1)S(1)} %fusion.101), channel_id=1, source_target_pairs={{0,2},{1,3},{2,0},{3,1},{4,6},{5,7},{6,4},{7,5},{8,10},{9,11},{10,... | collective-permute-start | bytes 399368 | tf_op jit(solution)/shard_map/ppermute | solution.py:45
  81.9 4.4 %collective-permute-start.9 = (bf16[128,512]{1,0:T(8,128)(2,1)S(1)}, bf16[128,512]{1,0:T(8,128)(2,1)S(1)}, u32[]{:S(2)}, u32[]{:S(2)}) collective-permute-start(bf16[128,512]{1,0:T(8,128)(2,1)S(1)} %get-tuple-element.58), channel_id=1, source_target_pairs={{0,1},{1,2},{2,3},{3,0},{4,5},{5,6},{6,7},{7,4},{8,9},{9,10},{10,1... | collective-permute-start | bytes 393224 | tf_op jit(solution)/shard_map/ppermute | solution.py:45
  82.3 5.3 %collective-permute-start.11 = (bf16[128,512]{1,0:T(8,128)(2,1)S(1)}, bf16[128,512]{1,0:T(8,128)(2,1)S(1)}, u32[]{:S(2)}, u32[]{:S(2)}) collective-permute-start(bf16[128,512]{1,0:T(8,128)(2,1)S(1)} %get-tuple-element.59), channel_id=1, source_target_pairs={{0,3},{1,0},{2,1},{3,2},{4,7},{5,4},{6,5},{7,6},{8,11},{9,8},{10,9... | collective-permute-start | bytes 393224 | tf_op jit(solution)/shard_map/ppermute | solution.py:45
  83.7 6.9 %collective-permute-start.10 = (bf16[128,512]{1,0:T(8,128)(2,1)S(1)}, bf16[128,512]{1,0:T(8,128)(2,1)S(1)}, u32[]{:S(2)}, u32[]{:S(2)}) collective-permute-start(bf16[128,512]{1,0:T(8,128)(2,1)S(1)} %get-tuple-element.60), channel_id=1, source_target_pairs={{0,2},{1,3},{2,0},{3,1},{4,6},{5,7},{6,4},{7,5},{8,10},{9,11},{10,... | collective-permute-start | bytes 393224 | tf_op jit(solution)/shard_map/ppermute | solution.py:45

commit v4 on v3

--- a/solution.py
+++ b/solution.py
@@ -34,48 +34,40 @@
     return lax.all_gather(values, "lev", axis=0, tiled=True)
 
 
-def scatter_sum(partial, axis):
-    devices = lax.axis_size(axis)
-    me = lax.axis_index(axis)
-    blocks = partial.reshape(devices, -1, *partial.shape[1:])
-    total = jnp.take(blocks, me, axis=0).astype(jnp.float32)
+def spread_sum(weight, activation):
+    devices = lax.axis_size("lev")
+    me = lax.axis_index("lev")
+    width = weight.shape[1] // devices
+
+    def chunk(shift):
+        block = lax.dynamic_slice_in_dim(weight, ((me + shift) % devices) * width, width, axis=1)
+        return lax.dot_general(
+            block, activation, (((0,), (0,)), ((), ())), preferred_element_type=jnp.float32
+        ).astype(jnp.bfloat16)
+
+    total = chunk(0).astype(jnp.float32)
     for shift in range(1, devices):
         pairs = [(i, (i + shift) % devices) for i in range(devices)]
-        chunk = jnp.take(blocks, (me + shift) % devices, axis=0)
-        total = total + lax.ppermute(chunk, axis, pairs).astype(jnp.float32)
+        total = total + lax.ppermute(chunk(shift), "lev", pairs).astype(jnp.float32)
     return total
 
 
-def spread_sum(weight, activation):
-    partial = lax.dot_general(
-        weight, activation, (((0,), (0,)), ((), ())), preferred_element_type=jnp.float32
-    ).astype(jnp.bfloat16)
-    return scatter_sum(partial, "lev")
-
-
-def gather_strips(values, axis):
-    devices = lax.axis_size(axis)
-    pieces = [values]
-    for shift in range(1, devices):
-        pairs = [(i, (i + shift) % devices) for i in range(devices)]
-        pieces.append(lax.ppermute(values, axis, pairs))
-    return jnp.concatenate(pieces, axis=-1)
-
-
 def make_fold(queries, pieces):
-    key_part, value_part = pieces
-    scores = (
-        jnp.einsum("hdri,hdrj->hrij", queries, key_part, preferred_element_type=jnp.float32)
-        * attention_scale
-    )
-    weights = jnp.exp(scores)
-    numerator = jnp.einsum(
-        "hrij,hdrj->hdri",
-        weights.astype(jnp.bfloat16),
-        value_part,
-        preferred_element_type=jnp.float32,
-    )
-    return (numerator, jnp.sum(weights, axis=3))
+    numerator = denominator = 0.0
+    for key_part, value_part in pieces:
+        scores = (
+            jnp.einsum("hdri,hdrj->hrij", queries, key_part, preferred_element_type=jnp.float32)
+            * attention_scale
+        )
+        weights = jnp.exp(scores)
+        numerator = numerator + jnp.einsum(
+            "hrij,hdrj->hdri",
+            weights.astype(jnp.bfloat16),
+            value_part,
+            preferred_element_type=jnp.float32,
+        )
+        denominator = denominator + jnp.sum(weights, axis=3)
+    return (numerator, denominator)
 
 
 def block_apply(state, block_index, stencil_weight, block_gain, up_weight, down_weight):
@@ -133,24 +125,24 @@
     rim_rows = rim.size // (lat_rows * columns)
     payload = jnp.concatenate([key_value, rim.reshape(rim_rows, lat_rows, columns)], axis=0)
     strips = lax.axis_size("lon")
-    pieces = [key_value]
+    kv_shape = (2, heads_local, head_size, lat_rows, columns)
+    pieces = [(key_rows, value_rows)]
     from_left = from_right = None
     for shift in range(1, strips):
         pairs = [(i, (i + shift) % strips) for i in range(strips)]
-        sent = payload if shift in (1, strips - 1) else key_value
-        got = lax.ppermute(sent, "lon", pairs)
-        pieces.append(got[: key_value.shape[0]])
+        got = lax.ppermute(payload, "lon", pairs)
+        kv = got[: key_value.shape[0]].reshape(kv_shape)
+        pieces.append((kv[0], kv[1]))
         if shift == 1:
             from_left = got[key_value.shape[0] :].reshape(rim.shape)[..., reach:]
         if shift == strips - 1:
             from_right = got[key_value.shape[0] :].reshape(rim.shape)[..., :reach]
-    all_keys = jnp.concatenate(pieces, axis=-1).reshape(2, heads_local, head_size, lat_rows, -1)
     wide_queries = jnp.concatenate(
         [from_left[0], queries.reshape(ch_local, lat_rows, columns), from_right[0]], axis=-1
     ).reshape(heads_local, head_size, lat_rows, -1)
     wide_latent = jnp.concatenate([from_left[1], latent, from_right[1]], axis=-1)
 
-    numerator, denominator = make_fold(wide_queries, (all_keys[0], all_keys[1]))
+    numerator, denominator = make_fold(wide_queries, pieces)
     attended = (numerator / denominator[:, None]).astype(jnp.bfloat16)
     update = spread_sum(out_weight, attended.reshape(ch_local, -1))
     current = (wide_latent.astype(jnp.float32) + update.reshape(wide_latent.shape)).astype(

time: 91.9 us -> 98.5 us (1.072)
  the two profiles are of different devices: /device:TPU:20 before, /device:TPU:13 now
where the time goes in v4:
time: 98.5 us; the launch traced here: 98.1 us
  waiting for transfers between devices  39.2 us (40%)
  blocking collectives  23.7 us (24%)
  matrix products  10.4 us (11%)
  local copies, waits for them, and re-layouts  9.94 us (10%)
  starting transfers between devices  9.89 us (10%)
  other arithmetic  4.52 us (5%)
    all_gather x3, blocking collectives, gather_channels(): return lax.all_gather(values, 'lev', axis=0, tiled=True)  23.7 us
    ppermute x3, waiting for transfers between devices, per_device(): got = lax.ppermute(payload, 'lon', pairs)  21.5 us
    ppermute x9, waiting for transfers between devices, spread_sum(): total = total + lax.ppermute(chunk(shift), 'lev', pairs).astype(jnp.float32)  17.7 us
    ppermute x9, starting transfers between devices, spread_sum(): total = total + lax.ppermute(chunk(shift), 'lev', pairs).astype(jnp.float32)  6.13 us
    ppermute x3, starting transfers between devices, per_device(): got = lax.ppermute(payload, 'lon', pairs)  3.77 us
    dot_general x12, matrix products, chunk(): lax.dot_general(block, activation, (((0,), (0,)), ((), ())), preferred_el...  3.39 us
    dot_general x4, matrix products, make_fold(): jnp.einsum('hdri,hdrj->hrij', queries, key_part, preferred_element_type=j...  2.99 us
    slice x3, local copies, waits for them, and re-layouts, per_device(): pieces.append((kv[0], kv[1]))  2.98 us
  transfers between devices with their start and end apart: 12, of which 10 were waited for; matrix products, arithmetic and copies ran while one was open for 6% of the time, Pallas kernels for 0%

profile of v4, /device:TPU:13, one launch (start us, length us, event | category | flops | bytes accessed | tf_op | source)
XLA Modules:
  0.0 98.1 jit_solution(18137842938137636172)
XLA Ops:
  0.0 1.1 %copy.56 = bf16[128,4,128]{0,2,1:T(8,128)(2,1)S(1)} copy(bf16[128,4,128]{2,1,0:T(4,128)(2,1)} %param.8) | data formatting | bytes 262144 | tf_op args[0]
  1.1 7.9 %all_gather.9 = bf16[512,4,128]{2,1,0:T(4,128)(2,1)S(1)} all-gather(bf16[128,4,128]{2,1,0:T(4,128)(2,1)} %param.8), channel_id=1, replica_groups=mesh['member'=2,'lon'=4,'lev'=4] {'lev'}, dimensions={0}, use_global_device_ids=true | all-gather | bytes 655360 | tf_op jit(solution)/shard_map/all_gather | solution.py:34
  9.0 0.5 fusion.22
  9.6 1.5 %fusion.36 = bf16[512,4,128,1]{2,1,0,3:T(4,128)(2,1)S(1)} fusion(bf16[512,4,128]{2,1,0:T(4,128)(2,1)S(1)} %all_gather.9, f32[512]{0:T(512)S(1)} %copy-done.5, f32[4,128]{1,0:T(4,128)S(1)} %add_rsqrt_fusion.4), kind=kLoop, calls=%fused_computation.77 | loop fusion | flops 1048576 | bytes 1052672 | tf_op jit(solution)/shard_map/convert_element_type | solution.py:116
  11.1 0.4 convolution_bitcast_fusion.2
  12.1 0.2 copy.58
  12.4 0.3 reshape.608
  12.8 0.7 pad_maximum_fusion
  13.5 2.3 %collective-permute-start.2 = (bf16[264,4,128]{2,0,1:T(8,128)(2,1)}, bf16[264,4,128]{2,0,1:T(8,128)(2,1)}, u32[]{:S(2)}, u32[]{:S(2)}) collective-permute-start(bf16[264,4,128]{2,0,1:T(8,128)(2,1)} %pad_maximum_fusion), channel_id=1, source_target_pairs={{0,8},{4,12},{8,0},{12,4},{1,9},{5,13},{9,1},{13,5},{2,10},{6,14},... | collective-permute-start | bytes 811016 | tf_op jit(solution)/shard_map/ppermute | solution.py:133
  16.0 1.3 %collective-permute-start = (bf16[264,4,128]{2,0,1:T(8,128)(2,1)}, bf16[264,4,128]{2,0,1:T(8,128)(2,1)}, u32[]{:S(2)}, u32[]{:S(2)}) collective-permute-start(bf16[264,4,128]{2,0,1:T(8,128)(2,1)} %pad_maximum_fusion), channel_id=1, source_target_pairs={{0,4},{4,8},{8,12},{12,0},{1,5},{5,9},{9,13},{13,1},{2,6},{6,10},{... | collective-permute-start | bytes 811016 | tf_op jit(solution)/shard_map/ppermute | solution.py:133
  17.5 21.5 %collective-permute-done.1 = bf16[264,4,128]{2,0,1:T(8,128)(2,1)} collective-permute-done((bf16[264,4,128]{2,0,1:T(8,128)(2,1)}, bf16[264,4,128]{2,0,1:T(8,128)(2,1)}, u32[]{:S(2)}, u32[]{:S(2)}) %collective-permute-start.1) | collective-permute-done | bytes 270368 | tf_op jit(solution)/shard_map/ppermute | solution.py:133
  39.1 0.7 slice.329
  39.8 0.6 reshape.610
  40.5 0.7 slice.327
  41.2 0.6 reshape.609
  41.8 0.2 slice_bitcast_fusion.1
  42.0 1.0 %fusion.132 = (bf16[128,4,128]{2,0,1:T(8,128)(2,1)S(1)}, bf16[128,4,128]{2,0,1:T(8,128)(2,1)S(1)}) fusion(bf16[264,4,128]{2,0,1:T(8,128)(2,1)} %collective-permute-done), kind=kLoop, calls=%fused_computation.231 | loop fusion | bytes 524288 | tf_op jit(solution)/shard_map/slice | solution.py:135
  43.0 0.7 fusion.140
  43.8 0.8 fusion.139
  44.5 1.0 %fusion.131 = (bf16[128,4,128]{2,0,1:T(8,128)(2,1)S(1)}, bf16[128,4,128]{2,0,1:T(8,128)(2,1)S(1)}) fusion(bf16[264,4,128]{2,0,1:T(8,128)(2,1)} %collective-permute-done.2), kind=kLoop, calls=%fused_computation.230 | loop fusion | bytes 524288 | tf_op jit(solution)/shard_map/slice | solution.py:135
  45.5 0.7 fusion.138
  46.3 1.0 %fusion.133 = (bf16[128,4,128]{2,0,1:T(8,128)(2,1)S(1)}, bf16[128,4,128]{2,0,1:T(8,128)(2,1)S(1)}) fusion(bf16[264,4,128]{2,0,1:T(8,128)(2,1)} %collective-permute-done.1), kind=kLoop, calls=%fused_computation.232 | loop fusion | bytes 524288 | tf_op jit(solution)/shard_map/slice | solution.py:135
  47.3 0.7 fusion.137
  48.0 0.3 fusion.58
  48.3 0.3 fusion.62
  48.6 0.3 convolution_add_fusion.1
  49.0 0.3 fusion.7
  49.3 0.3 copy.78
  49.9 0.2 convolution_convert_fusion.2
  50.1 0.2 convolution_convert_fusion.1
  50.3 0.2 convolution_convert_fusion
  50.5 1.0 %collective-permute-start.5 = (bf16[128,528]{0,1:T(8,128)(2,1)S(1)}, bf16[128,528]{0,1:T(8,128)(2,1)S(1)}, u32[]{:S(2)}, u32[]{:S(2)}) collective-permute-start(bf16[128,528]{0,1:T(8,128)(2,1)S(1)} %convolution_convert_fusion), channel_id=1, source_target_pairs={{0,3},{1,0},{2,1},{3,2},{4,7},{5,4},{6,5},{7,6},{8,11},{9,8},{10,9... | collective-permute-start | bytes 405512 | tf_op jit(solution)/shard_map/ppermute | solution.py:51
  51.5 0.8 collective-permute-start.4
  52.4 1.0 %collective-permute-start.3 = (bf16[128,528]{0,1:T(8,128)(2,1)S(1)}, bf16[128,528]{0,1:T(8,128)(2,1)S(1)}, u32[]{:S(2)}, u32[]{:S(2)}) collective-permute-start(bf16[128,528]{0,1:T(8,128)(2,1)S(1)} %convolution_convert_fusion.2), channel_id=1, source_target_pairs={{0,1},{1,2},{2,3},{3,0},{4,5},{5,6},{6,7},{7,4},{8,9},{9,10},{10,1... | collective-permute-start | bytes 405512 | tf_op jit(solution)/shard_map/ppermute | solution.py:51
  53.6 2.6 %collective-permute-done.5 = bf16[128,528]{0,1:T(8,128)(2,1)S(1)} collective-permute-done((bf16[128,528]{0,1:T(8,128)(2,1)S(1)}, bf16[128,528]{0,1:T(8,128)(2,1)S(1)}, u32[]{:S(2)}, u32[]{:S(2)}) %collective-permute-start.5) | collective-permute-done | bytes 135200 | tf_op jit(solution)/shard_map/ppermute | solution.py:51
  56.2 0.8 collective-permute-done.4
  57.0 1.2 %collective-permute-done.3 = bf16[128,528]{0,1:T(8,128)(2,1)S(1)} collective-permute-done((bf16[128,528]{0,1:T(8,128)(2,1)S(1)}, bf16[128,528]{0,1:T(8,128)(2,1)S(1)}, u32[]{:S(2)}, u32[]{:S(2)}) %collective-permute-start.3) | collective-permute-done | bytes 135200 | tf_op jit(solution)/shard_map/ppermute | solution.py:51
  58.2 0.2 convert_add_fusion
  58.6 0.2 fusion.52
  58.8 8.6 %all_gather.10 = bf16[512,4,130]{0,2,1:T(8,128)(2,1)S(1)} all-gather(bf16[128,4,130]{0,2,1:T(8,128)(2,1)S(1)} %fusion.52), channel_id=1, replica_groups=mesh['member'=2,'lon'=4,'lev'=4] {'lev'}, dimensions={0}, use_global_device_ids=true | all-gather | bytes 665600 | tf_op jit(solution)/shard_map/all_gather | solution.py:34
  67.4 0.2 fusion.11
  67.6 0.2 fusion.13
  68.0 1.7 %fusion.21 = bf16[512,520]{0,1:T(8,128)(2,1)S(1)} fusion(bf16[512,520]{0,1:T(8,128)(2,1)S(1)} %reshape.613, bf16[2,512,512]{2,1,0:T(8,128)(2,1)} %param.14), kind=kOutput, calls=%fused_computation.50 | convolution fusion | flops 275025920 | bytes 1589248 | tf_op jit(solution)/shard_map/dot_general | solution.py:97
  69.7 0.3 convolution_convert_fusion.4
  70.0 0.3 convolution_convert_fusion.5
  70.3 0.3 convolution_convert_fusion.6
  70.6 0.8 collective-permute-start.6
  71.4 0.8 collective-permute-start.7
  72.2 1.6 %collective-permute-done.6 = bf16[128,520]{0,1:T(8,128)(2,1)S(1)} collective-permute-done((bf16[128,520]{0,1:T(8,128)(2,1)S(1)}, bf16[128,520]{0,1:T(8,128)(2,1)S(1)}, u32[]{:S(2)}, u32[]{:S(2)}) %collective-permute-start.6) | collective-permute-done | bytes 133152 | tf_op jit(solution)/shard_map/ppermute | solution.py:51
  73.9 4.1 %collective-permute-done.7 = bf16[128,520]{0,1:T(8,128)(2,1)S(1)} collective-permute-done((bf16[128,520]{0,1:T(8,128)(2,1)S(1)}, bf16[128,520]{0,1:T(8,128)(2,1)S(1)}, u32[]{:S(2)}, u32[]{:S(2)}) %collective-permute-start.7) | collective-permute-done | bytes 133152 | tf_op jit(solution)/shard_map/ppermute | solution.py:51
  77.9 0.9 collective-permute-done.8
  78.9 0.3 convert_add_fusion.1
  79.5 7.2 %all_gather.11 = bf16[512,4,128]{0,2,1:T(8,128)(2,1)S(1)} all-gather(bf16[128,4,128]{0,2,1:T(8,128)(2,1)S(1)} %fusion.73), channel_id=1, replica_groups=mesh['member'=2,'lon'=4,'lev'=4] {'lev'}, dimensions={0}, use_global_device_ids=true | all-gather | bytes 655360 | tf_op jit(solution)/shard_map/all_gather | solution.py:34
  87.0 0.7 fusion.35
  87.7 0.3 convolution_convert_fusion.8
  88.0 0.3 convolution_convert_fusion.9
  88.3 0.3 convolution_convert_fusion.10
  88.7 1.0 collective-permute-start.9
  89.6 0.6 collective-permute-start.10
  90.4 1.7 %collective-permute-done.9 = bf16[128,512]{1,0:T(8,128)(2,1)S(1)} collective-permute-done((bf16[128,512]{1,0:T(8,128)(2,1)S(1)}, bf16[128,512]{1,0:T(8,128)(2,1)S(1)}, u32[]{:S(2)}, u32[]{:S(2)}) %collective-permute-start.9) | collective-permute-done | bytes 131104 | tf_op jit(solution)/shard_map/ppermute | solution.py:51
  92.0 3.9 %collective-permute-done.10 = bf16[128,512]{1,0:T(8,128)(2,1)S(1)} collective-permute-done((bf16[128,512]{1,0:T(8,128)(2,1)S(1)}, bf16[128,512]{1,0:T(8,128)(2,1)S(1)}, u32[]{:S(2)}, u32[]{:S(2)}) %collective-permute-start.10) | collective-permute-done | bytes 131104 | tf_op jit(solution)/shard_map/ppermute | solution.py:51
  95.9 0.9 collective-permute-done.11
  96.8 0.3 convert_add_fusion.2
  97.3 0.8 copy.80
  (64 shorter events, 2.9 us)
Async XLA Ops:
  0.0 11.1 %copy-start = (bf16[3,128,512]{2,1,0:T(8,128)(2,1)S(1)}, bf16[3,128,512]{2,1,0:T(8,128)(2,1)}, u32[]{:S(2)}) copy-start(bf16[3,128,512]{2,1,0:T(8,128)(2,1)} %param.10) | copy-start | bytes 1179652
  0.0 9.6 %copy-start.5 = (f32[512]{0:T(512)S(1)}, f32[512]{0:T(512)}, u32[]{:S(2)}) copy-start(f32[512]{0:T(512)} %param.9) | copy-start | bytes 6148
  12.1 5.2 %copy-start.3 = (f32[2,9,128]{2,0,1:T(2,128)S(1)}, f32[2,9,128]{2,0,1:T(2,128)}, u32[]{:S(2)}) copy-start(f32[2,9,128]{2,0,1:T(2,128)} %param.12) | copy-start | bytes 27652
  12.4 5.0 %copy-start.1 = (bf16[2,512,512]{2,1,0:T(8,128)(2,1)S(1)}, bf16[2,512,512]{2,1,0:T(8,128)(2,1)}, u32[]{:S(2)}) copy-start(bf16[2,512,512]{2,1,0:T(8,128)(2,1)} %param.15) | copy-start | bytes 3145732
  13.5 31.0 %collective-permute-start.2 = (bf16[264,4,128]{2,0,1:T(8,128)(2,1)}, bf16[264,4,128]{2,0,1:T(8,128)(2,1)}, u32[]{:S(2)}, u32[]{:S(2)}) collective-permute-start(bf16[264,4,128]{2,0,1:T(8,128)(2,1)} %pad_maximum_fusion), channel_id=1, source_target_pairs={{0,8},{4,12},{8,0},{12,4},{1,9},{5,13},{9,1},{13,5},{2,10},{6,14},... | collective-permute-start | bytes 811016 | tf_op jit(solution)/shard_map/ppermute | solution.py:133
  15.8 23.3 %collective-permute-start.1 = (bf16[264,4,128]{2,0,1:T(8,128)(2,1)}, bf16[264,4,128]{2,0,1:T(8,128)(2,1)}, u32[]{:S(2)}, u32[]{:S(2)}) collective-permute-start(bf16[264,4,128]{2,0,1:T(8,128)(2,1)} %pad_maximum_fusion), channel_id=1, source_target_pairs={{0,12},{4,0},{8,4},{12,8},{1,13},{5,1},{9,5},{13,9},{2,14},{6,2},{... | collective-permute-start | bytes 811016 | tf_op jit(solution)/shard_map/ppermute | solution.py:133
  16.0 24.5 %collective-permute-start = (bf16[264,4,128]{2,0,1:T(8,128)(2,1)}, bf16[264,4,128]{2,0,1:T(8,128)(2,1)}, u32[]{:S(2)}, u32[]{:S(2)}) collective-permute-start(bf16[264,4,128]{2,0,1:T(8,128)(2,1)} %pad_maximum_fusion), channel_id=1, source_target_pairs={{0,4},{4,8},{8,12},{12,0},{1,5},{5,9},{9,13},{13,1},{2,6},{6,10},{... | collective-permute-start | bytes 811016 | tf_op jit(solution)/shard_map/ppermute | solution.py:133
  49.0 0.9 copy-start.2
  49.3 4.1 %copy-start.4 = (f32[2,512]{1,0:T(2,128)S(1)}, f32[2,512]{1,0:T(2,128)}, u32[]{:S(2)}) copy-start(f32[2,512]{1,0:T(2,128)} %param.13) | copy-start | bytes 12292
  50.5 5.7 %collective-permute-start.5 = (bf16[128,528]{0,1:T(8,128)(2,1)S(1)}, bf16[128,528]{0,1:T(8,128)(2,1)S(1)}, u32[]{:S(2)}, u32[]{:S(2)}) collective-permute-start(bf16[128,528]{0,1:T(8,128)(2,1)S(1)} %convolution_convert_fusion), channel_id=1, source_target_pairs={{0,3},{1,0},{2,1},{3,2},{4,7},{5,4},{6,5},{7,6},{8,11},{9,8},{10,9... | collective-permute-start | bytes 405512 | tf_op jit(solution)/shard_map/ppermute | solution.py:51
  51.5 5.5 %collective-permute-start.4 = (bf16[128,528]{0,1:T(8,128)(2,1)S(1)}, bf16[128,528]{0,1:T(8,128)(2,1)S(1)}, u32[]{:S(2)}, u32[]{:S(2)}) collective-permute-start(bf16[128,528]{0,1:T(8,128)(2,1)S(1)} %convolution_convert_fusion.1), channel_id=1, source_target_pairs={{0,2},{1,3},{2,0},{3,1},{4,6},{5,7},{6,4},{7,5},{8,10},{9,11},{10,... | collective-permute-start | bytes 405512 | tf_op jit(solution)/shard_map/ppermute | solution.py:51
  52.4 5.9 %collective-permute-start.3 = (bf16[128,528]{0,1:T(8,128)(2,1)S(1)}, bf16[128,528]{0,1:T(8,128)(2,1)S(1)}, u32[]{:S(2)}, u32[]{:S(2)}) collective-permute-start(bf16[128,528]{0,1:T(8,128)(2,1)S(1)} %convolution_convert_fusion.2), channel_id=1, source_target_pairs={{0,1},{1,2},{2,3},{3,0},{4,5},{5,6},{6,7},{7,4},{8,9},{9,10},{10,1... | collective-permute-start | bytes 405512 | tf_op jit(solution)/shard_map/ppermute | solution.py:51
  70.6 3.2 %collective-permute-start.6 = (bf16[128,520]{0,1:T(8,128)(2,1)S(1)}, bf16[128,520]{0,1:T(8,128)(2,1)S(1)}, u32[]{:S(2)}, u32[]{:S(2)}) collective-permute-start(bf16[128,520]{0,1:T(8,128)(2,1)S(1)} %convolution_convert_fusion.6), channel_id=1, source_target_pairs={{0,1},{1,2},{2,3},{3,0},{4,5},{5,6},{6,7},{7,4},{8,9},{9,10},{10,1... | collective-permute-start | bytes 399368 | tf_op jit(solution)/shard_map/ppermute | solution.py:51
  71.4 6.5 %collective-permute-start.7 = (bf16[128,520]{0,1:T(8,128)(2,1)S(1)}, bf16[128,520]{0,1:T(8,128)(2,1)S(1)}, u32[]{:S(2)}, u32[]{:S(2)}) collective-permute-start(bf16[128,520]{0,1:T(8,128)(2,1)S(1)} %convolution_convert_fusion.5), channel_id=1, source_target_pairs={{0,2},{1,3},{2,0},{3,1},{4,6},{5,7},{6,4},{7,5},{8,10},{9,11},{10,... | collective-permute-start | bytes 399368 | tf_op jit(solution)/shard_map/ppermute | solution.py:51
  72.2 6.7 %collective-permute-start.8 = (bf16[128,520]{0,1:T(8,128)(2,1)S(1)}, bf16[128,520]{0,1:T(8,128)(2,1)S(1)}, u32[]{:S(2)}, u32[]{:S(2)}) collective-permute-start(bf16[128,520]{0,1:T(8,128)(2,1)S(1)} %convolution_convert_fusion.4), channel_id=1, source_target_pairs={{0,3},{1,0},{2,1},{3,2},{4,7},{5,4},{6,5},{7,6},{8,11},{9,8},{10,9... | collective-permute-start | bytes 399368 | tf_op jit(solution)/shard_map/ppermute | solution.py:51
  79.5 7.6 %copy-start.6 = (bf16[2,512,512]{2,1,0:T(8,128)(2,1)S(1)}, bf16[2,512,512]{2,1,0:T(8,128)(2,1)}, u32[]{:S(2)}) copy-start(bf16[2,512,512]{2,1,0:T(8,128)(2,1)} %param.14) | copy-start | bytes 3145732
  88.7 3.4 %collective-permute-start.9 = (bf16[128,512]{1,0:T(8,128)(2,1)S(1)}, bf16[128,512]{1,0:T(8,128)(2,1)S(1)}, u32[]{:S(2)}, u32[]{:S(2)}) collective-permute-start(bf16[128,512]{1,0:T(8,128)(2,1)S(1)} %convolution_convert_fusion.10), channel_id=1, source_target_pairs={{0,1},{1,2},{2,3},{3,0},{4,5},{5,6},{6,7},{7,4},{8,9},{9,10},{10,1... | collective-permute-start | bytes 393224 | tf_op jit(solution)/shard_map/ppermute | solution.py:51
  89.6 6.3 %collective-permute-start.10 = (bf16[128,512]{1,0:T(8,128)(2,1)S(1)}, bf16[128,512]{1,0:T(8,128)(2,1)S(1)}, u32[]{:S(2)}, u32[]{:S(2)}) collective-permute-start(bf16[128,512]{1,0:T(8,128)(2,1)S(1)} %convolution_convert_fusion.9), channel_id=1, source_target_pairs={{0,2},{1,3},{2,0},{3,1},{4,6},{5,7},{6,4},{7,5},{8,10},{9,11},{10,... | collective-permute-start | bytes 393224 | tf_op jit(solution)/shard_map/ppermute | solution.py:51
  90.2 6.6 %collective-permute-start.11 = (bf16[128,512]{1,0:T(8,128)(2,1)S(1)}, bf16[128,512]{1,0:T(8,128)(2,1)S(1)}, u32[]{:S(2)}, u32[]{:S(2)}) collective-permute-start(bf16[128,512]{1,0:T(8,128)(2,1)S(1)} %convolution_convert_fusion.8), channel_id=1, source_target_pairs={{0,3},{1,0},{2,1},{3,2},{4,7},{5,4},{6,5},{7,6},{8,11},{9,8},{10,9... | collective-permute-start | bytes 393224 | tf_op jit(solution)/shard_map/ppermute | solution.py:51

commit v5 on v3

--- a/solution.py
+++ b/solution.py
@@ -34,23 +34,22 @@
     return lax.all_gather(values, "lev", axis=0, tiled=True)
 
 
-def scatter_sum(partial, axis):
-    devices = lax.axis_size(axis)
-    me = lax.axis_index(axis)
-    blocks = partial.reshape(devices, -1, *partial.shape[1:])
-    total = jnp.take(blocks, me, axis=0).astype(jnp.float32)
+def spread_sum(weight, activation):
+    devices = lax.axis_size("lev")
+    me = lax.axis_index("lev")
+    width = weight.shape[1] // devices
+
+    def chunk(shift):
+        block = lax.dynamic_slice_in_dim(weight, ((me + shift) % devices) * width, width, axis=1)
+        return lax.dot_general(
+            block, activation, (((0,), (0,)), ((), ())), preferred_element_type=jnp.float32
+        ).astype(jnp.bfloat16)
+
+    total = chunk(0).astype(jnp.float32)
     for shift in range(1, devices):
         pairs = [(i, (i + shift) % devices) for i in range(devices)]
-        chunk = jnp.take(blocks, (me + shift) % devices, axis=0)
-        total = total + lax.ppermute(chunk, axis, pairs).astype(jnp.float32)
+        total = total + lax.ppermute(chunk(shift), "lev", pairs).astype(jnp.float32)
     return total
-
-
-def spread_sum(weight, activation):
-    partial = lax.dot_general(
-        weight, activation, (((0,), (0,)), ((), ())), preferred_element_type=jnp.float32
-    ).astype(jnp.bfloat16)
-    return scatter_sum(partial, "lev")
 
 
 def gather_strips(values, axis):

time: 91.9 us -> 96.6 us (1.051)
  the two profiles are of different devices: /device:TPU:20 before, /device:TPU:0 now
where the time goes in v5:
time: 96.6 us; the launch traced here: 95.7 us
  waiting for transfers between devices  34.5 us (36%)
  blocking collectives  25.3 us (26%)
  starting transfers between devices  12.5 us (13%)
  local copies, waits for them, and re-layouts  9.69 us (10%)
  matrix products  7.55 us (8%)
  other arithmetic  5.62 us (6%)
    all_gather x3, blocking collectives, gather_channels(): return lax.all_gather(values, 'lev', axis=0, tiled=True)  25.3 us
    ppermute x3, waiting for transfers between devices, per_device(): got = lax.ppermute(sent, 'lon', pairs)  21.1 us
    ppermute x9, waiting for transfers between devices, spread_sum(): total = total + lax.ppermute(chunk(shift), 'lev', pairs).astype(jnp.float32)  13.4 us
    ppermute x9, starting transfers between devices, spread_sum(): total = total + lax.ppermute(chunk(shift), 'lev', pairs).astype(jnp.float32)  7.93 us
    ppermute x3, starting transfers between devices, per_device(): got = lax.ppermute(sent, 'lon', pairs)  4.61 us
    dot_general x12, matrix products, chunk(): lax.dot_general(block, activation, (((0,), (0,)), ((), ())), preferred_el...  3.38 us
    dot_general x2, matrix products, block_apply(): jnp.dot(up_weight[block_index], block_normed, preferred_element_type=jnp....  2.37 us
    slice x2, local copies, waits for them, and re-layouts, per_device(): pieces.append(got[:key_value.shape[0]])  1.94 us
  transfers between devices with their start and end apart: 12, of which 12 were waited for; matrix products, arithmetic and copies ran while one was open for 3% of the time, Pallas kernels for 0%

profile of v5, /device:TPU:0, one launch (start us, length us, event | category | flops | bytes accessed | tf_op | source)
XLA Modules:
  0.0 95.7 jit_solution(1949308154656329610)
XLA Ops:
  0.0 8.9 %all_gather.9 = bf16[512,4,128]{2,1,0:T(4,128)(2,1)S(1)} all-gather(bf16[128,4,128]{2,1,0:T(4,128)(2,1)} %param.8), channel_id=1, replica_groups=mesh['member'=2,'lon'=4,'lev'=4] {'lev'}, dimensions={0}, use_global_device_ids=true | all-gather | bytes 655360 | tf_op jit(solution)/shard_map/all_gather | solution.py:34
  9.0 1.0 %copy.48 = bf16[128,4,128]{0,2,1:T(8,128)(2,1)S(1)} copy(bf16[128,4,128]{2,1,0:T(4,128)(2,1)} %param.8) | data formatting | bytes 262144 | tf_op args[0]
  10.0 0.5 fusion.20
  10.6 1.5 %fusion.34 = bf16[512,4,128,1]{2,1,0,3:T(4,128)(2,1)S(1)} fusion(bf16[512,4,128]{2,1,0:T(4,128)(2,1)S(1)} %all_gather.9, f32[512]{0:T(512)S(1)} %copy-done.6, f32[4,128]{1,0:T(4,128)S(1)} %add_rsqrt_fusion.4), kind=kLoop, calls=%fused_computation.71 | loop fusion | flops 1048576 | bytes 1052672 | tf_op jit(solution)/shard_map/convert_element_type | solution.py:123
  12.1 0.4 convolution_bitcast_fusion.2
  13.1 0.2 copy.50
  13.3 0.3 reshape.588
  13.8 0.7 pad_maximum_fusion.1
  14.5 1.6 %collective-permute-start = (bf16[264,4,128]{2,0,1:T(8,128)(2,1)}, bf16[264,4,128]{2,0,1:T(8,128)(2,1)}, u32[]{:S(2)}, u32[]{:S(2)}) collective-permute-start(bf16[264,4,128]{2,0,1:T(8,128)(2,1)} %pad_maximum_fusion.1), channel_id=1, source_target_pairs={{0,4},{4,8},{8,12},{12,0},{1,5},{5,9},{9,13},{13,1},{2,6},{6,10},{... | collective-permute-start | bytes 811016 | tf_op jit(solution)/shard_map/ppermute | solution.py:140
  16.1 2.2 %collective-permute-start.1 = (bf16[264,4,128]{2,0,1:T(8,128)(2,1)}, bf16[264,4,128]{2,0,1:T(8,128)(2,1)}, u32[]{:S(2)}, u32[]{:S(2)}) collective-permute-start(bf16[264,4,128]{2,0,1:T(8,128)(2,1)} %pad_maximum_fusion.1), channel_id=1, source_target_pairs={{0,12},{4,0},{8,4},{12,8},{1,13},{5,1},{9,5},{13,9},{2,14},{6,2},{... | collective-permute-start | bytes 811016 | tf_op jit(solution)/shard_map/ppermute | solution.py:140
  18.3 0.8 collective-permute-start.2
  19.4 6.5 %collective-permute-done = bf16[264,4,128]{2,0,1:T(8,128)(2,1)} collective-permute-done((bf16[264,4,128]{2,0,1:T(8,128)(2,1)}, bf16[264,4,128]{2,0,1:T(8,128)(2,1)}, u32[]{:S(2)}, u32[]{:S(2)}) %collective-permute-start) | collective-permute-done | bytes 270368 | tf_op jit(solution)/shard_map/ppermute | solution.py:140
  25.9 1.0 %slice.311 = bf16[256,4,128]{2,0,1:T(8,128)(2,1)S(1)} slice(bf16[264,4,128]{2,0,1:T(8,128)(2,1)} %collective-permute-done), slice={[0:256], [0:4], [0:128]} | slice | bytes 524288 | tf_op jit(solution)/shard_map/slice | solution.py:141
  26.9 3.7 %collective-permute-done.1 = bf16[264,4,128]{2,0,1:T(8,128)(2,1)} collective-permute-done((bf16[264,4,128]{2,0,1:T(8,128)(2,1)}, bf16[264,4,128]{2,0,1:T(8,128)(2,1)}, u32[]{:S(2)}, u32[]{:S(2)}) %collective-permute-start.1) | collective-permute-done | bytes 270368 | tf_op jit(solution)/shard_map/ppermute | solution.py:140
  30.6 1.0 %slice.312 = bf16[256,4,128]{2,0,1:T(8,128)(2,1)S(1)} slice(bf16[264,4,128]{2,0,1:T(8,128)(2,1)} %collective-permute-done.1), slice={[0:256], [0:4], [0:128]} | slice | bytes 524288 | tf_op jit(solution)/shard_map/slice | solution.py:141
  31.6 10.8 %collective-permute-done.2 = bf16[256,4,128]{2,0,1:T(8,128)(2,1)} collective-permute-done((bf16[256,4,128]{2,0,1:T(8,128)(2,1)S(1)}, bf16[256,4,128]{2,0,1:T(8,128)(2,1)}, u32[]{:S(2)}, u32[]{:S(2)}) %collective-permute-start.2) | collective-permute-done | bytes 262176 | tf_op jit(solution)/shard_map/ppermute | solution.py:140
  42.4 1.1 %pad_maximum_fusion = bf16[256,4,512]{2,0,1:T(8,128)(2,1)S(1)} fusion(bf16[256,4,128]{2,0,1:T(8,128)(2,1)S(1)} %slice.312, bf16[256,4,128]{2,0,1:T(8,128)(2,1)} %collective-permute-done.2, bf16[256,4,128]{2,0,1:T(8,128)(2,1)S(1)} %slice.311, bf16[256,4,128]{2,0,1:T(8,128)(2,1)S(1)} %bitcast.148), kind=kLoop, calls=%fused_computation.58 | loop fusion | flops 4194304 | bytes 2097152 | tf_op jit(solution)/shard_map/concatenate | solution.py:146
  43.5 0.9 fusion.124
  44.4 0.7 slice.307
  45.1 0.6 reshape.589
  45.7 0.2 slice_bitcast_fusion.1
  45.9 0.7 slice.309
  46.7 0.6 reshape.590
  47.4 0.9 fusion
  48.4 0.5 fusion.3
  48.9 0.3 copy.64
  49.4 0.2 convolution_convert_fusion.2
  49.7 0.2 convolution_convert_fusion.1
  49.9 1.2 %collective-permute-start.4 = (bf16[128,528]{0,1:T(8,128)(2,1)S(1)}, bf16[128,528]{0,1:T(8,128)(2,1)S(1)}, u32[]{:S(2)}, u32[]{:S(2)}) collective-permute-start(bf16[128,528]{0,1:T(8,128)(2,1)S(1)} %convolution_convert_fusion.1), channel_id=1, source_target_pairs={{0,2},{1,3},{2,0},{3,1},{4,6},{5,7},{6,4},{7,5},{8,10},{9,11},{10,... | collective-permute-start | bytes 405512 | tf_op jit(solution)/shard_map/ppermute | solution.py:51
  51.1 0.2 convolution_convert_fusion
  51.3 1.5 %collective-permute-start.5 = (bf16[128,528]{0,1:T(8,128)(2,1)S(1)}, bf16[128,528]{0,1:T(8,128)(2,1)S(1)}, u32[]{:S(2)}, u32[]{:S(2)}) collective-permute-start(bf16[128,528]{0,1:T(8,128)(2,1)S(1)} %convolution_convert_fusion), channel_id=1, source_target_pairs={{0,3},{1,0},{2,1},{3,2},{4,7},{5,4},{6,5},{7,6},{8,11},{9,8},{10,9... | collective-permute-start | bytes 405512 | tf_op jit(solution)/shard_map/ppermute | solution.py:51
  53.0 1.7 %collective-permute-done.3 = bf16[128,528]{0,1:T(8,128)(2,1)S(1)} collective-permute-done((bf16[128,528]{0,1:T(8,128)(2,1)S(1)}, bf16[128,528]{0,1:T(8,128)(2,1)S(1)}, u32[]{:S(2)}, u32[]{:S(2)}) %collective-permute-start.3) | collective-permute-done | bytes 135200 | tf_op jit(solution)/shard_map/ppermute | solution.py:51
  54.7 1.7 %collective-permute-done.4 = bf16[128,528]{0,1:T(8,128)(2,1)S(1)} collective-permute-done((bf16[128,528]{0,1:T(8,128)(2,1)S(1)}, bf16[128,528]{0,1:T(8,128)(2,1)S(1)}, u32[]{:S(2)}, u32[]{:S(2)}) %collective-permute-start.4) | collective-permute-done | bytes 135200 | tf_op jit(solution)/shard_map/ppermute | solution.py:51
  56.4 0.7 collective-permute-done.5
  57.0 0.2 convert_add_fusion
  57.4 0.2 fusion.53
  57.6 8.3 %all_gather.10 = bf16[512,4,130]{0,2,1:T(8,128)(2,1)S(1)} all-gather(bf16[128,4,130]{0,2,1:T(8,128)(2,1)S(1)} %fusion.53), channel_id=1, replica_groups=mesh['member'=2,'lon'=4,'lev'=4] {'lev'}, dimensions={0}, use_global_device_ids=true | all-gather | bytes 665600 | tf_op jit(solution)/shard_map/all_gather | solution.py:34
  65.9 0.2 fusion.7
  66.1 0.2 fusion.9
  66.5 1.7 %fusion.19 = bf16[512,520]{0,1:T(8,128)(2,1)S(1)} fusion(bf16[512,520]{0,1:T(8,128)(2,1)S(1)} %reshape.593, bf16[2,512,512]{2,1,0:T(8,128)(2,1)} %param.14), kind=kOutput, calls=%fused_computation.43 | convolution fusion | flops 275025920 | bytes 1589248 | tf_op jit(solution)/shard_map/dot_general | solution.py:104
  68.2 0.3 convolution_convert_fusion.6
  68.5 0.3 convolution_convert_fusion.5
  68.8 0.3 convolution_convert_fusion.4
  69.2 0.4 collective-permute-start.6
  69.5 0.8 collective-permute-start.7
  70.3 1.1 %collective-permute-start.8 = (bf16[128,520]{0,1:T(8,128)(2,1)S(1)}, bf16[128,520]{0,1:T(8,128)(2,1)S(1)}, u32[]{:S(2)}, u32[]{:S(2)}) collective-permute-start(bf16[128,520]{0,1:T(8,128)(2,1)S(1)} %convolution_convert_fusion.4), channel_id=1, source_target_pairs={{0,3},{1,0},{2,1},{3,2},{4,7},{5,4},{6,5},{7,6},{8,11},{9,8},{10,9... | collective-permute-start | bytes 399368 | tf_op jit(solution)/shard_map/ppermute | solution.py:51
  71.5 2.7 %collective-permute-done.6 = bf16[128,520]{0,1:T(8,128)(2,1)S(1)} collective-permute-done((bf16[128,520]{0,1:T(8,128)(2,1)S(1)}, bf16[128,520]{0,1:T(8,128)(2,1)S(1)}, u32[]{:S(2)}, u32[]{:S(2)}) %collective-permute-start.6) | collective-permute-done | bytes 133152 | tf_op jit(solution)/shard_map/ppermute | solution.py:51
  74.1 1.8 %collective-permute-done.7 = bf16[128,520]{0,1:T(8,128)(2,1)S(1)} collective-permute-done((bf16[128,520]{0,1:T(8,128)(2,1)S(1)}, bf16[128,520]{0,1:T(8,128)(2,1)S(1)}, u32[]{:S(2)}, u32[]{:S(2)}) %collective-permute-start.7) | collective-permute-done | bytes 133152 | tf_op jit(solution)/shard_map/ppermute | solution.py:51
  75.9 0.3 collective-permute-done.8
  76.2 0.3 convert_add_fusion.1
  76.8 8.0 %all_gather.11 = bf16[512,4,128]{0,2,1:T(8,128)(2,1)S(1)} all-gather(bf16[128,4,128]{0,2,1:T(8,128)(2,1)S(1)} %fusion.68), channel_id=1, replica_groups=mesh['member'=2,'lon'=4,'lev'=4] {'lev'}, dimensions={0}, use_global_device_ids=true | all-gather | bytes 655360 | tf_op jit(solution)/shard_map/all_gather | solution.py:34
  85.0 0.2 fusion.25
  85.2 0.7 fusion.33
  85.9 0.3 convolution_convert_fusion.10
  86.2 0.3 convolution_convert_fusion.9
  86.5 0.3 convolution_convert_fusion.8
  86.8 0.4 collective-permute-start.9
  87.2 1.4 %collective-permute-start.10 = (bf16[128,512]{1,0:T(8,128)(2,1)S(1)}, bf16[128,512]{1,0:T(8,128)(2,1)S(1)}, u32[]{:S(2)}, u32[]{:S(2)}) collective-permute-start(bf16[128,512]{1,0:T(8,128)(2,1)S(1)} %convolution_convert_fusion.9), channel_id=1, source_target_pairs={{0,2},{1,3},{2,0},{3,1},{4,6},{5,7},{6,4},{7,5},{8,10},{9,11},{10,... | collective-permute-start | bytes 393224 | tf_op jit(solution)/shard_map/ppermute | solution.py:51
  88.6 1.1 %collective-permute-start.11 = (bf16[128,512]{1,0:T(8,128)(2,1)S(1)}, bf16[128,512]{1,0:T(8,128)(2,1)S(1)}, u32[]{:S(2)}, u32[]{:S(2)}) collective-permute-start(bf16[128,512]{1,0:T(8,128)(2,1)S(1)} %convolution_convert_fusion.8), channel_id=1, source_target_pairs={{0,3},{1,0},{2,1},{3,2},{4,7},{5,4},{6,5},{7,6},{8,11},{9,8},{10,9... | collective-permute-start | bytes 393224 | tf_op jit(solution)/shard_map/ppermute | solution.py:51
  89.8 2.0 %collective-permute-done.9 = bf16[128,512]{1,0:T(8,128)(2,1)S(1)} collective-permute-done((bf16[128,512]{1,0:T(8,128)(2,1)S(1)}, bf16[128,512]{1,0:T(8,128)(2,1)S(1)}, u32[]{:S(2)}, u32[]{:S(2)}) %collective-permute-start.9) | collective-permute-done | bytes 131104 | tf_op jit(solution)/shard_map/ppermute | solution.py:51
  91.8 1.8 %collective-permute-done.10 = bf16[128,512]{1,0:T(8,128)(2,1)S(1)} collective-permute-done((bf16[128,512]{1,0:T(8,128)(2,1)S(1)}, bf16[128,512]{1,0:T(8,128)(2,1)S(1)}, u32[]{:S(2)}, u32[]{:S(2)}) %collective-permute-start.10) | collective-permute-done | bytes 131104 | tf_op jit(solution)/shard_map/ppermute | solution.py:51
  93.6 0.8 collective-permute-done.11
  94.4 0.3 convert_add_fusion.2
  94.9 0.8 copy.66
  (60 shorter events, 2.5 us)
Async XLA Ops:
  0.0 12.1 %copy-start = (bf16[3,128,512]{2,1,0:T(8,128)(2,1)S(1)}, bf16[3,128,512]{2,1,0:T(8,128)(2,1)}, u32[]{:S(2)}) copy-start(bf16[3,128,512]{2,1,0:T(8,128)(2,1)} %param.10) | copy-start | bytes 1179652
  0.0 10.5 %copy-start.6 = (f32[512]{0:T(512)S(1)}, f32[512]{0:T(512)}, u32[]{:S(2)}) copy-start(f32[512]{0:T(512)} %param.9) | copy-start | bytes 6148
  13.6 5.6 %copy-start.4 = (f32[2,9,128]{2,0,1:T(2,128)S(1)}, f32[2,9,128]{2,0,1:T(2,128)}, u32[]{:S(2)}) copy-start(f32[2,9,128]{2,0,1:T(2,128)} %param.12) | copy-start | bytes 27652
  13.6 5.7 %copy-start.1 = (bf16[2,512,512]{2,1,0:T(8,128)(2,1)S(1)}, bf16[2,512,512]{2,1,0:T(8,128)(2,1)}, u32[]{:S(2)}) copy-start(bf16[2,512,512]{2,1,0:T(8,128)(2,1)} %param.15) | copy-start | bytes 3145732
  14.5 11.4 %collective-permute-start = (bf16[264,4,128]{2,0,1:T(8,128)(2,1)}, bf16[264,4,128]{2,0,1:T(8,128)(2,1)}, u32[]{:S(2)}, u32[]{:S(2)}) collective-permute-start(bf16[264,4,128]{2,0,1:T(8,128)(2,1)} %pad_maximum_fusion.1), channel_id=1, source_target_pairs={{0,4},{4,8},{8,12},{12,0},{1,5},{5,9},{9,13},{13,1},{2,6},{6,10},{... | collective-permute-start | bytes 811016 | tf_op jit(solution)/shard_map/ppermute | solution.py:140
  16.1 14.6 %collective-permute-start.1 = (bf16[264,4,128]{2,0,1:T(8,128)(2,1)}, bf16[264,4,128]{2,0,1:T(8,128)(2,1)}, u32[]{:S(2)}, u32[]{:S(2)}) collective-permute-start(bf16[264,4,128]{2,0,1:T(8,128)(2,1)} %pad_maximum_fusion.1), channel_id=1, source_target_pairs={{0,12},{4,0},{8,4},{12,8},{1,13},{5,1},{9,5},{13,9},{2,14},{6,2},{... | collective-permute-start | bytes 811016 | tf_op jit(solution)/shard_map/ppermute | solution.py:140
  18.3 24.1 %collective-permute-start.2 = (bf16[256,4,128]{2,0,1:T(8,128)(2,1)S(1)}, bf16[256,4,128]{2,0,1:T(8,128)(2,1)}, u32[]{:S(2)}, u32[]{:S(2)}) collective-permute-start(bf16[256,4,128]{2,0,1:T(8,128)(2,1)S(1)} %bitcast.147), channel_id=1, source_target_pairs={{0,8},{4,12},{8,0},{12,4},{1,9},{5,13},{9,1},{13,5},{2,10},{6,14},... | collective-permute-start | bytes 786440 | tf_op jit(solution)/shard_map/ppermute | solution.py:140
  47.4 1.0 %copy-start.2 = (bf16[128,4,512]{2,0,1:T(8,128)(2,1)S(1)}, bf16[128,4,512]{2,0,1:T(8,128)(2,1)}, u32[]{:S(2)}) copy-start(bf16[128,4,512]{2,0,1:T(8,128)(2,1)} %get-tuple-element.11) | copy-start | bytes 1572868
  48.4 1.0 %copy-start.3 = (bf16[128,512]{1,0:T(8,128)(2,1)S(1)}, bf16[128,512]{1,0:T(8,128)(2,1)}, u32[]{:S(2)}) copy-start(bf16[128,512]{1,0:T(8,128)(2,1)} %param.11) | copy-start | bytes 393220
  48.9 3.8 %copy-start.5 = (f32[2,512]{1,0:T(2,128)S(1)}, f32[2,512]{1,0:T(2,128)}, u32[]{:S(2)}) copy-start(f32[2,512]{1,0:T(2,128)} %param.13) | copy-start | bytes 12292
  49.6 5.1 %collective-permute-start.3 = (bf16[128,528]{0,1:T(8,128)(2,1)S(1)}, bf16[128,528]{0,1:T(8,128)(2,1)S(1)}, u32[]{:S(2)}, u32[]{:S(2)}) collective-permute-start(bf16[128,528]{0,1:T(8,128)(2,1)S(1)} %convolution_convert_fusion.2), channel_id=1, source_target_pairs={{0,1},{1,2},{2,3},{3,0},{4,5},{5,6},{6,7},{7,4},{8,9},{9,10},{10,1... | collective-permute-start | bytes 405512 | tf_op jit(solution)/shard_map/ppermute | solution.py:51
  49.9 6.5 %collective-permute-start.4 = (bf16[128,528]{0,1:T(8,128)(2,1)S(1)}, bf16[128,528]{0,1:T(8,128)(2,1)S(1)}, u32[]{:S(2)}, u32[]{:S(2)}) collective-permute-start(bf16[128,528]{0,1:T(8,128)(2,1)S(1)} %convolution_convert_fusion.1), channel_id=1, source_target_pairs={{0,2},{1,3},{2,0},{3,1},{4,6},{5,7},{6,4},{7,5},{8,10},{9,11},{10,... | collective-permute-start | bytes 405512 | tf_op jit(solution)/shard_map/ppermute | solution.py:51
  51.3 5.8 %collective-permute-start.5 = (bf16[128,528]{0,1:T(8,128)(2,1)S(1)}, bf16[128,528]{0,1:T(8,128)(2,1)S(1)}, u32[]{:S(2)}, u32[]{:S(2)}) collective-permute-start(bf16[128,528]{0,1:T(8,128)(2,1)S(1)} %convolution_convert_fusion), channel_id=1, source_target_pairs={{0,3},{1,0},{2,1},{3,2},{4,7},{5,4},{6,5},{7,6},{8,11},{9,8},{10,9... | collective-permute-start | bytes 405512 | tf_op jit(solution)/shard_map/ppermute | solution.py:51
  69.2 5.0 %collective-permute-start.6 = (bf16[128,520]{0,1:T(8,128)(2,1)S(1)}, bf16[128,520]{0,1:T(8,128)(2,1)S(1)}, u32[]{:S(2)}, u32[]{:S(2)}) collective-permute-start(bf16[128,520]{0,1:T(8,128)(2,1)S(1)} %convolution_convert_fusion.6), channel_id=1, source_target_pairs={{0,1},{1,2},{2,3},{3,0},{4,5},{5,6},{6,7},{7,4},{8,9},{9,10},{10,1... | collective-permute-start | bytes 399368 | tf_op jit(solution)/shard_map/ppermute | solution.py:51
  69.5 6.4 %collective-permute-start.7 = (bf16[128,520]{0,1:T(8,128)(2,1)S(1)}, bf16[128,520]{0,1:T(8,128)(2,1)S(1)}, u32[]{:S(2)}, u32[]{:S(2)}) collective-permute-start(bf16[128,520]{0,1:T(8,128)(2,1)S(1)} %convolution_convert_fusion.5), channel_id=1, source_target_pairs={{0,2},{1,3},{2,0},{3,1},{4,6},{5,7},{6,4},{7,5},{8,10},{9,11},{10,... | collective-permute-start | bytes 399368 | tf_op jit(solution)/shard_map/ppermute | solution.py:51
  70.3 5.9 %collective-permute-start.8 = (bf16[128,520]{0,1:T(8,128)(2,1)S(1)}, bf16[128,520]{0,1:T(8,128)(2,1)S(1)}, u32[]{:S(2)}, u32[]{:S(2)}) collective-permute-start(bf16[128,520]{0,1:T(8,128)(2,1)S(1)} %convolution_convert_fusion.4), channel_id=1, source_target_pairs={{0,3},{1,0},{2,1},{3,2},{4,7},{5,4},{6,5},{7,6},{8,11},{9,8},{10,9... | collective-permute-start | bytes 399368 | tf_op jit(solution)/shard_map/ppermute | solution.py:51
  76.8 8.4 %copy-start.7 = (bf16[2,512,512]{2,1,0:T(8,128)(2,1)S(1)}, bf16[2,512,512]{2,1,0:T(8,128)(2,1)}, u32[]{:S(2)}) copy-start(bf16[2,512,512]{2,1,0:T(8,128)(2,1)} %param.14) | copy-start | bytes 3145732
  86.8 4.9 %collective-permute-start.9 = (bf16[128,512]{1,0:T(8,128)(2,1)S(1)}, bf16[128,512]{1,0:T(8,128)(2,1)S(1)}, u32[]{:S(2)}, u32[]{:S(2)}) collective-permute-start(bf16[128,512]{1,0:T(8,128)(2,1)S(1)} %convolution_convert_fusion.10), channel_id=1, source_target_pairs={{0,1},{1,2},{2,3},{3,0},{4,5},{5,6},{6,7},{7,4},{8,9},{9,10},{10,1... | collective-permute-start | bytes 393224 | tf_op jit(solution)/shard_map/ppermute | solution.py:51
  87.2 6.4 %collective-permute-start.10 = (bf16[128,512]{1,0:T(8,128)(2,1)S(1)}, bf16[128,512]{1,0:T(8,128)(2,1)S(1)}, u32[]{:S(2)}, u32[]{:S(2)}) collective-permute-start(bf16[128,512]{1,0:T(8,128)(2,1)S(1)} %convolution_convert_fusion.9), channel_id=1, source_target_pairs={{0,2},{1,3},{2,0},{3,1},{4,6},{5,7},{6,4},{7,5},{8,10},{9,11},{10,... | collective-permute-start | bytes 393224 | tf_op jit(solution)/shard_map/ppermute | solution.py:51
  88.6 5.8 %collective-permute-start.11 = (bf16[128,512]{1,0:T(8,128)(2,1)S(1)}, bf16[128,512]{1,0:T(8,128)(2,1)S(1)}, u32[]{:S(2)}, u32[]{:S(2)}) collective-permute-start(bf16[128,512]{1,0:T(8,128)(2,1)S(1)} %convolution_convert_fusion.8), channel_id=1, source_target_pairs={{0,3},{1,0},{2,1},{3,2},{4,7},{5,4},{6,5},{7,6},{8,11},{9,8},{10,9... | collective-permute-start | bytes 393224 | tf_op jit(solution)/shard_map/ppermute | solution.py:51

commit v6 on v3

--- a/solution.py
+++ b/solution.py
@@ -128,34 +128,44 @@
     key_rows = unit_heads(projected[1]).astype(jnp.bfloat16)
     value_rows = projected[2].astype(jnp.bfloat16)
 
-    key_value = jnp.stack([key_rows, value_rows]).reshape(-1, lat_rows, columns)
-    rim = jnp.stack([edges(queries.reshape(ch_local, lat_rows, columns), reach), edges(latent, reach)])
-    rim_rows = rim.size // (lat_rows * columns)
-    payload = jnp.concatenate([key_value, rim.reshape(rim_rows, lat_rows, columns)], axis=0)
     strips = lax.axis_size("lon")
-    pieces = [key_value]
-    from_left = from_right = None
-    for shift in range(1, strips):
-        pairs = [(i, (i + shift) % strips) for i in range(strips)]
-        sent = payload if shift in (1, strips - 1) else key_value
-        got = lax.ppermute(sent, "lon", pairs)
-        pieces.append(got[: key_value.shape[0]])
-        if shift == 1:
-            from_left = got[key_value.shape[0] :].reshape(rim.shape)[..., reach:]
-        if shift == strips - 1:
-            from_right = got[key_value.shape[0] :].reshape(rim.shape)[..., :reach]
-    all_keys = jnp.concatenate(pieces, axis=-1).reshape(2, heads_local, head_size, lat_rows, -1)
-    wide_queries = jnp.concatenate(
-        [from_left[0], queries.reshape(ch_local, lat_rows, columns), from_right[0]], axis=-1
-    ).reshape(heads_local, head_size, lat_rows, -1)
-    wide_latent = jnp.concatenate([from_left[1], latent, from_right[1]], axis=-1)
-
-    numerator, denominator = make_fold(wide_queries, (all_keys[0], all_keys[1]))
-    attended = (numerator / denominator[:, None]).astype(jnp.bfloat16)
-    update = spread_sum(out_weight, attended.reshape(ch_local, -1))
-    current = (wide_latent.astype(jnp.float32) + update.reshape(wide_latent.shape)).astype(
-        jnp.bfloat16
-    )
+    split = lat_rows // 2
+    arrived = None
+    states = []
+    for low, high in ((0, split), (split, lat_rows)):
+        rows = high - low
+        key_value = jnp.stack([key_rows, value_rows])[:, :, :, low:high].reshape(-1, rows, columns)
+        own_queries = queries[:, :, low:high].reshape(ch_local, rows, columns)
+        own_latent = latent[:, low:high]
+        rim = jnp.stack([edges(own_queries, reach), edges(own_latent, reach)])
+        rim_rows = rim.size // (rows * columns)
+        payload = jnp.concatenate([key_value, rim.reshape(rim_rows, rows, columns)], axis=0)
+        if arrived is not None:
+            key_value, payload = lax.optimization_barrier((key_value, payload, arrived))[:2]
+        pieces = [key_value]
+        from_left = from_right = None
+        for shift in range(1, strips):
+            pairs = [(i, (i + shift) % strips) for i in range(strips)]
+            sent = payload if shift in (1, strips - 1) else key_value
+            got = lax.ppermute(sent, "lon", pairs)
+            pieces.append(got[: key_value.shape[0]])
+            if shift == 1:
+                from_left = got[key_value.shape[0] :].reshape(rim.shape)[..., reach:]
+            if shift == strips - 1:
+                from_right = got[key_value.shape[0] :].reshape(rim.shape)[..., :reach]
+        arrived = pieces[1:]
+        all_keys = jnp.concatenate(pieces, axis=-1).reshape(2, heads_local, head_size, rows, -1)
+        wide_queries = jnp.concatenate([from_left[0], own_queries, from_right[0]], axis=-1).reshape(
+            heads_local, head_size, rows, -1
+        )
+        wide_latent = jnp.concatenate([from_left[1], own_latent, from_right[1]], axis=-1)
+        numerator, denominator = make_fold(wide_queries, (all_keys[0], all_keys[1]))
+        attended = (numerator / denominator[:, None]).astype(jnp.bfloat16)
+        update = spread_sum(out_weight, attended.reshape(ch_local, -1))
+        states.append(
+            (wide_latent.astype(jnp.float32) + update.reshape(wide_latent.shape)).astype(jnp.bfloat16)
+        )
+    current = jnp.concatenate(states, axis=1)
     for block_index in range(BLOCKS):
         current = block_apply(
             current, block_index, stencil_weight, block_gain, up_weight, down_weight

time: 91.9 us -> 99.6 us (1.084)
  the two profiles are of different devices: /device:TPU:20 before, /device:TPU:0 now
where the time goes in v6:
time: 99.6 us; the launch traced here: 98.6 us
  waiting for transfers between devices  31 us (31%)
  blocking collectives  24.9 us (25%)
  starting transfers between devices  19.2 us (19%)
  local copies, waits for them, and re-layouts  11.2 us (11%)
  matrix products  6.89 us (7%)
  other arithmetic  4.51 us (5%)
    all_gather x3, blocking collectives, gather_channels(): return lax.all_gather(values, 'lev', axis=0, tiled=True)  24.9 us
    ppermute x6, waiting for transfers between devices, per_device(): got = lax.ppermute(sent, 'lon', pairs)  19.5 us
    ppermute x12, waiting for transfers between devices, scatter_sum(): total = total + lax.ppermute(chunk, axis, pairs).astype(jnp.float32)  11.5 us
    ppermute x12, starting transfers between devices, scatter_sum(): total = total + lax.ppermute(chunk, axis, pairs).astype(jnp.float32)  10.6 us
    ppermute x6, starting transfers between devices, per_device(): got = lax.ppermute(sent, 'lon', pairs)  8.61 us
    dot_general x4, matrix products, spread_sum(): lax.dot_general(weight, activation, (((0,), (0,)), ((), ())), preferred_e...  4.56 us
    another operation x3, local copies, waits for them, and re-layouts, scatter_sum(): total = jnp.take(blocks, me, axis=0).astype(jnp.float32)  2.24 us
    unnamed x22, local copies, waits for them, and re-layouts  2.04 us
  transfers between devices with their start and end apart: 18, of which 13 were waited for; matrix products, arithmetic and copies ran while one was open for 2% of the time, Pallas kernels for 0%

profile of v6, /device:TPU:0, one launch (start us, length us, event | category | flops | bytes accessed | tf_op | source)
XLA Modules:
  0.0 98.6 jit_solution(6540088279519049917)
XLA Ops:
  0.0 8.9 %all_gather.9 = bf16[512,4,128]{2,1,0:T(4,128)(2,1)S(1)} all-gather(bf16[128,4,128]{2,1,0:T(4,128)(2,1)} %param.14), channel_id=1, replica_groups=mesh['member'=2,'lon'=4,'lev'=4] {'lev'}, dimensions={0}, use_global_device_ids=true | all-gather | bytes 655360 | tf_op jit(solution)/shard_map/all_gather | solution.py:34
  9.0 1.4 %fusion.137 = (bf16[128,2,2]{2,1,0:T(2,128)(2,1)S(1)}, bf16[128,2,2]{2,1,0:T(2,128)(2,1)S(1)}, bf16[128,2,2]{2,1,0:T(2,128)(2,1)S(1)}, bf16[128,2,2]{2,1,0:T(2,128)(2,1)S(1)}) fusion(bf16[128,4,128]{2,1,0:T(4,128)(2,1)} %param.14), kind=kLoop, calls=%fused_computation.264 | loop fusion | bytes 8192 | tf_op jit(solution)/shard_map/slice | solution.py:113
  10.4 0.5 fusion.20
  10.9 1.5 %fusion.40 = bf16[512,4,128,1]{2,1,0,3:T(4,128)(2,1)S(1)} fusion(bf16[512,4,128]{2,1,0:T(4,128)(2,1)S(1)} %all_gather.9, f32[512]{0:T(512)S(1)} %copy-done.5, f32[4,128]{1,0:T(4,128)S(1)} %add_rsqrt_fusion.4), kind=kLoop, calls=%fused_computation.71 | loop fusion | flops 1048576 | bytes 1052672 | tf_op jit(solution)/shard_map/convert_element_type | solution.py:124
  12.5 0.4 convolution_bitcast_fusion.2
  13.6 0.2 copy.87
  13.8 0.2 reshape.629
  14.2 1.6 %collective-permute-start = (bf16[264,2,128]{2,0,1:T(8,128)(2,1)S(1)}, bf16[264,2,128]{2,0,1:T(8,128)(2,1)S(1)}, u32[]{:S(2)}, u32[]{:S(2)}) collective-permute-start(bf16[264,2,128]{2,0,1:T(8,128)(2,1)S(1)} %pad_maximum_fusion.3), channel_id=1, source_target_pairs={{0,4},{4,8},{8,12},{12,0},{1,5},{5,9},{9,13},{13,1},{2,6},{6,10},{... | collective-permute-start | bytes 405512 | tf_op jit(solution)/shard_map/ppermute | solution.py:150
  15.8 2.3 %collective-permute-start.1 = (bf16[264,2,128]{2,0,1:T(8,128)(2,1)S(1)}, bf16[264,2,128]{2,0,1:T(8,128)(2,1)S(1)}, u32[]{:S(2)}, u32[]{:S(2)}) collective-permute-start(bf16[264,2,128]{2,0,1:T(8,128)(2,1)S(1)} %pad_maximum_fusion.3), channel_id=1, source_target_pairs={{0,12},{4,0},{8,4},{12,8},{1,13},{5,1},{9,5},{13,9},{2,14},{6,2},{... | collective-permute-start | bytes 405512 | tf_op jit(solution)/shard_map/ppermute | solution.py:150
  18.1 0.8 collective-permute-start.2
  19.7 0.2 copy.110
  19.9 0.2 reshape.637
  20.4 2.1 %collective-permute-done = bf16[264,2,128]{2,0,1:T(8,128)(2,1)S(1)} collective-permute-done((bf16[264,2,128]{2,0,1:T(8,128)(2,1)S(1)}, bf16[264,2,128]{2,0,1:T(8,128)(2,1)S(1)}, u32[]{:S(2)}, u32[]{:S(2)}) %collective-permute-start) | collective-permute-done | bytes 135200 | tf_op jit(solution)/shard_map/ppermute | solution.py:150
  22.5 1.8 %collective-permute-done.1 = bf16[264,2,128]{2,0,1:T(8,128)(2,1)S(1)} collective-permute-done((bf16[264,2,128]{2,0,1:T(8,128)(2,1)S(1)}, bf16[264,2,128]{2,0,1:T(8,128)(2,1)S(1)}, u32[]{:S(2)}, u32[]{:S(2)}) %collective-permute-start.1) | collective-permute-done | bytes 135200 | tf_op jit(solution)/shard_map/ppermute | solution.py:150
  24.3 6.2 %collective-permute-done.2 = bf16[256,2,128]{2,0,1:T(8,128)(2,1)S(1)} collective-permute-done((bf16[256,2,128]{2,0,1:T(8,128)(2,1)S(1)}, bf16[256,2,128]{2,0,1:T(8,128)(2,1)S(1)}, u32[]{:S(2)}, u32[]{:S(2)}) %collective-permute-start.2) | collective-permute-done | bytes 131104 | tf_op jit(solution)/shard_map/ppermute | solution.py:150
  30.6 0.3 reshape.630
  30.9 0.2 slice_bitcast_fusion.1
  31.1 0.3 reshape.631
  31.6 0.7 fusion.142
  32.2 0.3 fusion.8
  32.8 0.3 copy-done.2
  33.1 0.2 fusion.3
  33.4 0.6 constant_dynamic-slice_fusion.11
  34.1 1.2 %collective-permute-start.4 = (bf16[128,264]{0,1:T(8,128)(2,1)S(1)}, bf16[128,264]{0,1:T(8,128)(2,1)S(1)}, u32[]{:S(2)}, u32[]{:S(2)}) collective-permute-start(bf16[128,264]{0,1:T(8,128)(2,1)S(1)} %fusion.116), channel_id=1, source_target_pairs={{0,2},{1,3},{2,0},{3,1},{4,6},{5,7},{6,4},{7,5},{8,10},{9,11},{10,... | collective-permute-start | bytes 202760 | tf_op jit(solution)/shard_map/ppermute | solution.py:45
  35.3 1.5 %collective-permute-start.5 = (bf16[128,264]{0,1:T(8,128)(2,1)S(1)}, bf16[128,264]{0,1:T(8,128)(2,1)S(1)}, u32[]{:S(2)}, u32[]{:S(2)}) collective-permute-start(bf16[128,264]{0,1:T(8,128)(2,1)S(1)} %fusion.115), channel_id=1, source_target_pairs={{0,3},{1,0},{2,1},{3,2},{4,7},{5,4},{6,5},{7,6},{8,11},{9,8},{10,9... | collective-permute-start | bytes 202760 | tf_op jit(solution)/shard_map/ppermute | solution.py:45
  36.9 3.8 %collective-permute-start.7 = (bf16[264,2,128]{2,0,1:T(8,128)(2,1)S(1)}, bf16[264,2,128]{2,0,1:T(8,128)(2,1)S(1)}, u32[]{:S(2)}, u32[]{:S(2)}) collective-permute-start(bf16[264,2,128]{2,0,1:T(8,128)(2,1)S(1)} %pad_maximum_fusion.4), channel_id=1, source_target_pairs={{0,12},{4,0},{8,4},{12,8},{1,13},{5,1},{9,5},{13,9},{2,14},{6,2},{... | collective-permute-start | bytes 405512 | tf_op jit(solution)/shard_map/ppermute | solution.py:150
  41.0 4.1 %collective-permute-done.6 = bf16[264,2,128]{2,0,1:T(8,128)(2,1)S(1)} collective-permute-done((bf16[264,2,128]{2,0,1:T(8,128)(2,1)S(1)}, bf16[264,2,128]{2,0,1:T(8,128)(2,1)S(1)}, u32[]{:S(2)}, u32[]{:S(2)}) %collective-permute-start.6) | collective-permute-done | bytes 135200 | tf_op jit(solution)/shard_map/ppermute | solution.py:150
  45.2 5.3 %collective-permute-done.8 = bf16[256,2,128]{2,0,1:T(8,128)(2,1)S(1)} collective-permute-done((bf16[256,2,128]{2,0,1:T(8,128)(2,1)S(1)}, bf16[256,2,128]{2,0,1:T(8,128)(2,1)S(1)}, u32[]{:S(2)}, u32[]{:S(2)}) %collective-permute-start.8) | collective-permute-done | bytes 131104 | tf_op jit(solution)/shard_map/ppermute | solution.py:150
  50.7 0.3 reshape.638
  51.0 0.2 fusion.134
  51.2 0.3 reshape.639
  51.6 0.7 fusion.141
  52.3 0.3 fusion.7
  52.9 0.2 fusion.4
  53.2 0.6 constant_dynamic-slice_fusion.6
  53.9 1.0 %collective-permute-start.10 = (bf16[128,264]{0,1:T(8,128)(2,1)S(1)}, bf16[128,264]{0,1:T(8,128)(2,1)S(1)}, u32[]{:S(2)}, u32[]{:S(2)}) collective-permute-start(bf16[128,264]{0,1:T(8,128)(2,1)S(1)} %fusion.112), channel_id=1, source_target_pairs={{0,2},{1,3},{2,0},{3,1},{4,6},{5,7},{6,4},{7,5},{8,10},{9,11},{10,... | collective-permute-start | bytes 202760 | tf_op jit(solution)/shard_map/ppermute | solution.py:45
  54.9 1.5 %collective-permute-start.11 = (bf16[128,264]{0,1:T(8,128)(2,1)S(1)}, bf16[128,264]{0,1:T(8,128)(2,1)S(1)}, u32[]{:S(2)}, u32[]{:S(2)}) collective-permute-start(bf16[128,264]{0,1:T(8,128)(2,1)S(1)} %fusion.111), channel_id=1, source_target_pairs={{0,3},{1,0},{2,1},{3,2},{4,7},{5,4},{6,5},{7,6},{8,11},{9,8},{10,9... | collective-permute-start | bytes 202760 | tf_op jit(solution)/shard_map/ppermute | solution.py:45
  56.6 1.0 %collective-permute-done.9 = bf16[128,264]{0,1:T(8,128)(2,1)S(1)} collective-permute-done((bf16[128,264]{0,1:T(8,128)(2,1)S(1)}, bf16[128,264]{0,1:T(8,128)(2,1)S(1)}, u32[]{:S(2)}, u32[]{:S(2)}) %collective-permute-start.9) | collective-permute-done | bytes 67616 | tf_op jit(solution)/shard_map/ppermute | solution.py:45
  57.7 1.3 %collective-permute-done.10 = bf16[128,264]{0,1:T(8,128)(2,1)S(1)} collective-permute-done((bf16[128,264]{0,1:T(8,128)(2,1)S(1)}, bf16[128,264]{0,1:T(8,128)(2,1)S(1)}, u32[]{:S(2)}, u32[]{:S(2)}) %collective-permute-start.10) | collective-permute-done | bytes 67616 | tf_op jit(solution)/shard_map/ppermute | solution.py:45
  59.1 0.2 fusion.68
  59.3 8.0 %all_gather.10 = bf16[512,4,130]{0,2,1:T(8,128)(2,1)S(1)} all-gather(bf16[128,4,130]{0,2,1:T(8,128)(2,1)S(1)} %fusion.68), channel_id=1, replica_groups=mesh['member'=2,'lon'=4,'lev'=4] {'lev'}, dimensions={0}, use_global_device_ids=true | all-gather | bytes 665600 | tf_op jit(solution)/shard_map/all_gather | solution.py:34
  67.2 0.2 fusion.9
  67.5 0.2 fusion.11
  67.9 0.9 copy-done.6
  68.7 2.0 %fusion.2 = bf16[512,520]{0,1:T(8,128)(2,1)S(1)} fusion(bf16[512,520]{0,1:T(8,128)(2,1)S(1)} %reshape.643, bf16[2,512,512]{2,1,0:T(8,128)(2,1)S(1)} %copy-done.6, bf16[2,512,512]{2,1,0:T(8,128)(2,1)} %param.20), kind=kOutput, calls=%fused_computation.17 | convolution fusion | flops 547921920 | bytes 2113536 | tf_op jit(solution)/shard_map/dot_general | solution.py:50
  70.9 1.1 %constant_dynamic-slice_fusion.4 = (bf16[1,128,520]{1,0,2:T(2,128)(2,1)S(1)}, bf16[1,128,520]{1,0,2:T(2,128)(2,1)S(1)}, bf16[1,128,520]{1,0,2:T(2,128)(2,1)S(1)}, bf16[1,128,520]{1,0,2:T(2,128)(2,1)S(1)}) fusion(bf16[4,128,520]{1,0,2:T(4,128)(2,1)S(1)} %reshape.644, s32[]{:T(128)S(6)} %select_n.96, s32[]{:T(128)S(6)} %select_n.100, s32[]{:T(128)S(6)} %select_n.98, ...), kind=kLoop, calls=%fused_computation.198 | loop fusion | bytes 1064976 | tf_op jit(solution)/shard_map/jit(_take) | solution.py:41
  72.0 0.4 collective-permute-start.12
  72.4 1.0 %collective-permute-start.13 = (bf16[128,520]{0,1:T(8,128)(2,1)S(1)}, bf16[128,520]{0,1:T(8,128)(2,1)S(1)}, u32[]{:S(2)}, u32[]{:S(2)}) collective-permute-start(bf16[128,520]{0,1:T(8,128)(2,1)S(1)} %fusion.97), channel_id=1, source_target_pairs={{0,2},{1,3},{2,0},{3,1},{4,6},{5,7},{6,4},{7,5},{8,10},{9,11},{10,... | collective-permute-start | bytes 399368 | tf_op jit(solution)/shard_map/ppermute | solution.py:45
  73.5 1.2 %collective-permute-start.14 = (bf16[128,520]{0,1:T(8,128)(2,1)S(1)}, bf16[128,520]{0,1:T(8,128)(2,1)S(1)}, u32[]{:S(2)}, u32[]{:S(2)}) collective-permute-start(bf16[128,520]{0,1:T(8,128)(2,1)S(1)} %fusion.96), channel_id=1, source_target_pairs={{0,3},{1,0},{2,1},{3,2},{4,7},{5,4},{6,5},{7,6},{8,11},{9,8},{10,9... | collective-permute-start | bytes 399368 | tf_op jit(solution)/shard_map/ppermute | solution.py:45
  74.6 2.2 %collective-permute-done.12 = bf16[128,520]{0,1:T(8,128)(2,1)S(1)} collective-permute-done((bf16[128,520]{0,1:T(8,128)(2,1)S(1)}, bf16[128,520]{0,1:T(8,128)(2,1)S(1)}, u32[]{:S(2)}, u32[]{:S(2)}) %collective-permute-start.12) | collective-permute-done | bytes 133152 | tf_op jit(solution)/shard_map/ppermute | solution.py:45
  76.9 2.0 %collective-permute-done.13 = bf16[128,520]{0,1:T(8,128)(2,1)S(1)} collective-permute-done((bf16[128,520]{0,1:T(8,128)(2,1)S(1)}, bf16[128,520]{0,1:T(8,128)(2,1)S(1)}, u32[]{:S(2)}, u32[]{:S(2)}) %collective-permute-start.13) | collective-permute-done | bytes 133152 | tf_op jit(solution)/shard_map/ppermute | solution.py:45
  78.9 0.3 collective-permute-done.14
  79.4 0.2 fusion.83
  79.6 8.0 %all_gather.11 = bf16[512,4,128]{0,2,1:T(8,128)(2,1)S(1)} all-gather(bf16[128,4,128]{0,2,1:T(8,128)(2,1)S(1)} %fusion.83), channel_id=1, replica_groups=mesh['member'=2,'lon'=4,'lev'=4] {'lev'}, dimensions={0}, use_global_device_ids=true | all-gather | bytes 655360 | tf_op jit(solution)/shard_map/all_gather | solution.py:34
  87.6 0.2 fusion.23
  87.8 0.2 fusion.25
  88.0 2.1 %convolution_convert_fusion.1 = bf16[512,512]{0,1:T(8,128)(2,1)S(1)} fusion(bf16[512,512]{0,1:T(8,128)(2,1)S(1)} %bitcast.203, bf16[2,512,512]{2,1,0:T(8,128)(2,1)S(1)} %copy-done.6, bf16[2,512,512]{2,1,0:T(8,128)(2,1)} %param.20), kind=kOutput, calls=%fused_computation.15 | convolution fusion | flops 539492352 | bytes 2097152 | tf_op jit(solution)/shard_map/dot_general | solution.py:50
  90.2 0.4 collective-permute-start.15
  90.6 1.2 %collective-permute-start.16 = (bf16[128,512]{1,0:T(8,128)(2,1)S(1)}, bf16[128,512]{1,0:T(8,128)(2,1)S(1)}, u32[]{:S(2)}, u32[]{:S(2)}) collective-permute-start(bf16[128,512]{1,0:T(8,128)(2,1)S(1)} %get-tuple-element.56), channel_id=1, source_target_pairs={{0,2},{1,3},{2,0},{3,1},{4,6},{5,7},{6,4},{7,5},{8,10},{9,11},{10,... | collective-permute-start | bytes 393224 | tf_op jit(solution)/shard_map/ppermute | solution.py:45
  91.8 1.1 %collective-permute-start.17 = (bf16[128,512]{1,0:T(8,128)(2,1)S(1)}, bf16[128,512]{1,0:T(8,128)(2,1)S(1)}, u32[]{:S(2)}, u32[]{:S(2)}) collective-permute-start(bf16[128,512]{1,0:T(8,128)(2,1)S(1)} %get-tuple-element.55), channel_id=1, source_target_pairs={{0,3},{1,0},{2,1},{3,2},{4,7},{5,4},{6,5},{7,6},{8,11},{9,8},{10,9... | collective-permute-start | bytes 393224 | tf_op jit(solution)/shard_map/ppermute | solution.py:45
  92.9 2.2 %collective-permute-done.15 = bf16[128,512]{1,0:T(8,128)(2,1)S(1)} collective-permute-done((bf16[128,512]{1,0:T(8,128)(2,1)S(1)}, bf16[128,512]{1,0:T(8,128)(2,1)S(1)}, u32[]{:S(2)}, u32[]{:S(2)}) %collective-permute-start.15) | collective-permute-done | bytes 131104 | tf_op jit(solution)/shard_map/ppermute | solution.py:45
  95.1 1.8 %collective-permute-done.16 = bf16[128,512]{1,0:T(8,128)(2,1)S(1)} collective-permute-done((bf16[128,512]{1,0:T(8,128)(2,1)S(1)}, bf16[128,512]{1,0:T(8,128)(2,1)S(1)}, u32[]{:S(2)}, u32[]{:S(2)}) %collective-permute-start.16) | collective-permute-done | bytes 131104 | tf_op jit(solution)/shard_map/ppermute | solution.py:45
  96.9 0.7 collective-permute-done.17
  97.8 0.8 copy.133
  (119 shorter events, 4.8 us)
Async XLA Ops:
  0.0 12.5 %copy-start = (bf16[3,128,512]{2,1,0:T(8,128)(2,1)S(1)}, bf16[3,128,512]{2,1,0:T(8,128)(2,1)}, u32[]{:S(2)}) copy-start(bf16[3,128,512]{2,1,0:T(8,128)(2,1)} %param.16) | copy-start | bytes 1179652
  0.0 10.9 %copy-start.5 = (f32[512]{0:T(512)S(1)}, f32[512]{0:T(512)}, u32[]{:S(2)}) copy-start(f32[512]{0:T(512)} %param.15) | copy-start | bytes 6148
  13.3 5.6 %copy-start.1 = (bf16[128,4,128]{2,1,0:T(4,128)(2,1)S(1)}, bf16[128,4,128]{2,1,0:T(4,128)(2,1)}, u32[]{:S(2)}) copy-start(bf16[128,4,128]{2,1,0:T(4,128)(2,1)} %param.14) | copy-start | bytes 393220
  14.1 6.1 %copy-start.3 = (f32[2,9,128]{2,0,1:T(2,128)S(1)}, f32[2,9,128]{2,0,1:T(2,128)}, u32[]{:S(2)}) copy-start(f32[2,9,128]{2,0,1:T(2,128)} %param.18) | copy-start | bytes 27652
  14.2 6.2 %copy-start.4 = (f32[2,512]{1,0:T(2,128)S(1)}, f32[2,512]{1,0:T(2,128)}, u32[]{:S(2)}) copy-start(f32[2,512]{1,0:T(2,128)} %param.19) | copy-start | bytes 12292
  14.2 8.3 %collective-permute-start = (bf16[264,2,128]{2,0,1:T(8,128)(2,1)S(1)}, bf16[264,2,128]{2,0,1:T(8,128)(2,1)S(1)}, u32[]{:S(2)}, u32[]{:S(2)}) collective-permute-start(bf16[264,2,128]{2,0,1:T(8,128)(2,1)S(1)} %pad_maximum_fusion.3), channel_id=1, source_target_pairs={{0,4},{4,8},{8,12},{12,0},{1,5},{5,9},{9,13},{13,1},{2,6},{6,10},{... | collective-permute-start | bytes 405512 | tf_op jit(solution)/shard_map/ppermute | solution.py:150
  15.8 8.5 %collective-permute-start.1 = (bf16[264,2,128]{2,0,1:T(8,128)(2,1)S(1)}, bf16[264,2,128]{2,0,1:T(8,128)(2,1)S(1)}, u32[]{:S(2)}, u32[]{:S(2)}) collective-permute-start(bf16[264,2,128]{2,0,1:T(8,128)(2,1)S(1)} %pad_maximum_fusion.3), channel_id=1, source_target_pairs={{0,12},{4,0},{8,4},{12,8},{1,13},{5,1},{9,5},{13,9},{2,14},{6,2},{... | collective-permute-start | bytes 405512 | tf_op jit(solution)/shard_map/ppermute | solution.py:150
  18.1 12.4 %collective-permute-start.2 = (bf16[256,2,128]{2,0,1:T(8,128)(2,1)S(1)}, bf16[256,2,128]{2,0,1:T(8,128)(2,1)S(1)}, u32[]{:S(2)}, u32[]{:S(2)}) collective-permute-start(bf16[256,2,128]{2,0,1:T(8,128)(2,1)S(1)} %bitcast.194), channel_id=1, source_target_pairs={{0,8},{4,12},{8,0},{12,4},{1,9},{5,13},{9,1},{13,5},{2,10},{6,14},... | collective-permute-start | bytes 393224 | tf_op jit(solution)/shard_map/ppermute | solution.py:150
  32.2 0.9 copy-start.2
  34.0 6.8 %collective-permute-start.3 = (bf16[128,264]{0,1:T(8,128)(2,1)S(1)}, bf16[128,264]{0,1:T(8,128)(2,1)S(1)}, u32[]{:S(2)}, u32[]{:S(2)}) collective-permute-start(bf16[128,264]{0,1:T(8,128)(2,1)S(1)} %fusion.117), channel_id=1, source_target_pairs={{0,1},{1,2},{2,3},{3,0},{4,5},{5,6},{6,7},{7,4},{8,9},{9,10},{10,1... | collective-permute-start | bytes 202760 | tf_op jit(solution)/shard_map/ppermute | solution.py:45
  34.1 6.8 %collective-permute-start.4 = (bf16[128,264]{0,1:T(8,128)(2,1)S(1)}, bf16[128,264]{0,1:T(8,128)(2,1)S(1)}, u32[]{:S(2)}, u32[]{:S(2)}) collective-permute-start(bf16[128,264]{0,1:T(8,128)(2,1)S(1)} %fusion.116), channel_id=1, source_target_pairs={{0,2},{1,3},{2,0},{3,1},{4,6},{5,7},{6,4},{7,5},{8,10},{9,11},{10,... | collective-permute-start | bytes 202760 | tf_op jit(solution)/shard_map/ppermute | solution.py:45
  35.3 5.7 %collective-permute-start.5 = (bf16[128,264]{0,1:T(8,128)(2,1)S(1)}, bf16[128,264]{0,1:T(8,128)(2,1)S(1)}, u32[]{:S(2)}, u32[]{:S(2)}) collective-permute-start(bf16[128,264]{0,1:T(8,128)(2,1)S(1)} %fusion.115), channel_id=1, source_target_pairs={{0,3},{1,0},{2,1},{3,2},{4,7},{5,4},{6,5},{7,6},{8,11},{9,8},{10,9... | collective-permute-start | bytes 202760 | tf_op jit(solution)/shard_map/ppermute | solution.py:45
  36.8 8.4 %collective-permute-start.6 = (bf16[264,2,128]{2,0,1:T(8,128)(2,1)S(1)}, bf16[264,2,128]{2,0,1:T(8,128)(2,1)S(1)}, u32[]{:S(2)}, u32[]{:S(2)}) collective-permute-start(bf16[264,2,128]{2,0,1:T(8,128)(2,1)S(1)} %pad_maximum_fusion.4), channel_id=1, source_target_pairs={{0,4},{4,8},{8,12},{12,0},{1,5},{5,9},{9,13},{13,1},{2,6},{6,10},{... | collective-permute-start | bytes 405512 | tf_op jit(solution)/shard_map/ppermute | solution.py:150
  36.9 8.3 %collective-permute-start.7 = (bf16[264,2,128]{2,0,1:T(8,128)(2,1)S(1)}, bf16[264,2,128]{2,0,1:T(8,128)(2,1)S(1)}, u32[]{:S(2)}, u32[]{:S(2)}) collective-permute-start(bf16[264,2,128]{2,0,1:T(8,128)(2,1)S(1)} %pad_maximum_fusion.4), channel_id=1, source_target_pairs={{0,12},{4,0},{8,4},{12,8},{1,13},{5,1},{9,5},{13,9},{2,14},{6,2},{... | collective-permute-start | bytes 405512 | tf_op jit(solution)/shard_map/ppermute | solution.py:150
  40.9 9.7 %collective-permute-start.8 = (bf16[256,2,128]{2,0,1:T(8,128)(2,1)S(1)}, bf16[256,2,128]{2,0,1:T(8,128)(2,1)S(1)}, u32[]{:S(2)}, u32[]{:S(2)}) collective-permute-start(bf16[256,2,128]{2,0,1:T(8,128)(2,1)S(1)} %bitcast.191), channel_id=1, source_target_pairs={{0,8},{4,12},{8,0},{12,4},{1,9},{5,13},{9,1},{13,5},{2,10},{6,14},... | collective-permute-start | bytes 393224 | tf_op jit(solution)/shard_map/ppermute | solution.py:150
  53.8 3.9 %collective-permute-start.9 = (bf16[128,264]{0,1:T(8,128)(2,1)S(1)}, bf16[128,264]{0,1:T(8,128)(2,1)S(1)}, u32[]{:S(2)}, u32[]{:S(2)}) collective-permute-start(bf16[128,264]{0,1:T(8,128)(2,1)S(1)} %fusion.113), channel_id=1, source_target_pairs={{0,1},{1,2},{2,3},{3,0},{4,5},{5,6},{6,7},{7,4},{8,9},{9,10},{10,1... | collective-permute-start | bytes 202760 | tf_op jit(solution)/shard_map/ppermute | solution.py:45
  53.9 5.0 %collective-permute-start.10 = (bf16[128,264]{0,1:T(8,128)(2,1)S(1)}, bf16[128,264]{0,1:T(8,128)(2,1)S(1)}, u32[]{:S(2)}, u32[]{:S(2)}) collective-permute-start(bf16[128,264]{0,1:T(8,128)(2,1)S(1)} %fusion.112), channel_id=1, source_target_pairs={{0,2},{1,3},{2,0},{3,1},{4,6},{5,7},{6,4},{7,5},{8,10},{9,11},{10,... | collective-permute-start | bytes 202760 | tf_op jit(solution)/shard_map/ppermute | solution.py:45
  54.9 4.0 %collective-permute-start.11 = (bf16[128,264]{0,1:T(8,128)(2,1)S(1)}, bf16[128,264]{0,1:T(8,128)(2,1)S(1)}, u32[]{:S(2)}, u32[]{:S(2)}) collective-permute-start(bf16[128,264]{0,1:T(8,128)(2,1)S(1)} %fusion.111), channel_id=1, source_target_pairs={{0,3},{1,0},{2,1},{3,2},{4,7},{5,4},{6,5},{7,6},{8,11},{9,8},{10,9... | collective-permute-start | bytes 202760 | tf_op jit(solution)/shard_map/ppermute | solution.py:45
  67.5 1.2 %copy-start.6 = (bf16[2,512,512]{2,1,0:T(8,128)(2,1)S(1)}, bf16[2,512,512]{2,1,0:T(8,128)(2,1)}, u32[]{:S(2)}) copy-start(bf16[2,512,512]{2,1,0:T(8,128)(2,1)} %param.21) | copy-start | bytes 3145732
  72.0 4.9 %collective-permute-start.12 = (bf16[128,520]{0,1:T(8,128)(2,1)S(1)}, bf16[128,520]{0,1:T(8,128)(2,1)S(1)}, u32[]{:S(2)}, u32[]{:S(2)}) collective-permute-start(bf16[128,520]{0,1:T(8,128)(2,1)S(1)} %fusion.98), channel_id=1, source_target_pairs={{0,1},{1,2},{2,3},{3,0},{4,5},{5,6},{6,7},{7,4},{8,9},{9,10},{10,1... | collective-permute-start | bytes 399368 | tf_op jit(solution)/shard_map/ppermute | solution.py:45
  72.4 6.5 %collective-permute-start.13 = (bf16[128,520]{0,1:T(8,128)(2,1)S(1)}, bf16[128,520]{0,1:T(8,128)(2,1)S(1)}, u32[]{:S(2)}, u32[]{:S(2)}) collective-permute-start(bf16[128,520]{0,1:T(8,128)(2,1)S(1)} %fusion.97), channel_id=1, source_target_pairs={{0,2},{1,3},{2,0},{3,1},{4,6},{5,7},{6,4},{7,5},{8,10},{9,11},{10,... | collective-permute-start | bytes 399368 | tf_op jit(solution)/shard_map/ppermute | solution.py:45
  73.5 5.7 %collective-permute-start.14 = (bf16[128,520]{0,1:T(8,128)(2,1)S(1)}, bf16[128,520]{0,1:T(8,128)(2,1)S(1)}, u32[]{:S(2)}, u32[]{:S(2)}) collective-permute-start(bf16[128,520]{0,1:T(8,128)(2,1)S(1)} %fusion.96), channel_id=1, source_target_pairs={{0,3},{1,0},{2,1},{3,2},{4,7},{5,4},{6,5},{7,6},{8,11},{9,8},{10,9... | collective-permute-start | bytes 399368 | tf_op jit(solution)/shard_map/ppermute | solution.py:45
  90.2 4.9 %collective-permute-start.15 = (bf16[128,512]{1,0:T(8,128)(2,1)S(1)}, bf16[128,512]{1,0:T(8,128)(2,1)S(1)}, u32[]{:S(2)}, u32[]{:S(2)}) collective-permute-start(bf16[128,512]{1,0:T(8,128)(2,1)S(1)} %get-tuple-element.54), channel_id=1, source_target_pairs={{0,1},{1,2},{2,3},{3,0},{4,5},{5,6},{6,7},{7,4},{8,9},{9,10},{10,1... | collective-permute-start | bytes 393224 | tf_op jit(solution)/shard_map/ppermute | solution.py:45
  90.6 6.4 %collective-permute-start.16 = (bf16[128,512]{1,0:T(8,128)(2,1)S(1)}, bf16[128,512]{1,0:T(8,128)(2,1)S(1)}, u32[]{:S(2)}, u32[]{:S(2)}) collective-permute-start(bf16[128,512]{1,0:T(8,128)(2,1)S(1)} %get-tuple-element.56), channel_id=1, source_target_pairs={{0,2},{1,3},{2,0},{3,1},{4,6},{5,7},{6,4},{7,5},{8,10},{9,11},{10,... | collective-permute-start | bytes 393224 | tf_op jit(solution)/shard_map/ppermute | solution.py:45
  91.8 5.8 %collective-permute-start.17 = (bf16[128,512]{1,0:T(8,128)(2,1)S(1)}, bf16[128,512]{1,0:T(8,128)(2,1)S(1)}, u32[]{:S(2)}, u32[]{:S(2)}) collective-permute-start(bf16[128,512]{1,0:T(8,128)(2,1)S(1)} %get-tuple-element.55), channel_id=1, source_target_pairs={{0,3},{1,0},{2,1},{3,2},{4,7},{5,4},{6,5},{7,6},{8,11},{9,8},{10,9... | collective-permute-start | bytes 393224 | tf_op jit(solution)/shard_map/ppermute | solution.py:45

commit v7 on v3

--- a/solution.py
+++ b/solution.py
@@ -129,25 +129,20 @@
     value_rows = projected[2].astype(jnp.bfloat16)
 
     key_value = jnp.stack([key_rows, value_rows]).reshape(-1, lat_rows, columns)
-    rim = jnp.stack([edges(queries.reshape(ch_local, lat_rows, columns), reach), edges(latent, reach)])
-    rim_rows = rim.size // (lat_rows * columns)
-    payload = jnp.concatenate([key_value, rim.reshape(rim_rows, lat_rows, columns)], axis=0)
     strips = lax.axis_size("lon")
     pieces = [key_value]
-    from_left = from_right = None
     for shift in range(1, strips):
         pairs = [(i, (i + shift) % strips) for i in range(strips)]
-        sent = payload if shift in (1, strips - 1) else key_value
-        got = lax.ppermute(sent, "lon", pairs)
-        pieces.append(got[: key_value.shape[0]])
-        if shift == 1:
-            from_left = got[key_value.shape[0] :].reshape(rim.shape)[..., reach:]
-        if shift == strips - 1:
-            from_right = got[key_value.shape[0] :].reshape(rim.shape)[..., :reach]
+        pieces.append(lax.ppermute(key_value, "lon", pairs))
     all_keys = jnp.concatenate(pieces, axis=-1).reshape(2, heads_local, head_size, lat_rows, -1)
-    wide_queries = jnp.concatenate(
-        [from_left[0], queries.reshape(ch_local, lat_rows, columns), from_right[0]], axis=-1
-    ).reshape(heads_local, head_size, lat_rows, -1)
+    flat_queries = queries.reshape(ch_local, lat_rows, columns)
+    rim_right = jnp.stack([flat_queries[..., -reach:], latent[..., -reach:]])
+    rim_left = jnp.stack([flat_queries[..., :reach], latent[..., :reach]])
+    from_left = lax.ppermute(rim_right, "lon", [(i, (i + 1) % strips) for i in range(strips)])
+    from_right = lax.ppermute(rim_left, "lon", [(i, (i - 1) % strips) for i in range(strips)])
+    wide_queries = jnp.concatenate([from_left[0], flat_queries, from_right[0]], axis=-1).reshape(
+        heads_local, head_size, lat_rows, -1
+    )
     wide_latent = jnp.concatenate([from_left[1], latent, from_right[1]], axis=-1)
 
     numerator, denominator = make_fold(wide_queries, (all_keys[0], all_keys[1]))

time: 91.9 us -> 103 us (1.12)
  waiting for transfers between devices: 40.2 us -> 48.6 us
  starting transfers between devices: 9.74 us -> 12.7 us
    ppermute x3 -> x5, waiting for transfers between devices: 21.4 us -> 29.7 us  [the longest x1 26.5 us: per_device(): lax.ppermute(rim_left, 'lon', [(i, (i - 1) % strips) for i in range(strip...]
    ppermute x3 -> x5, starting transfers between devices: 2.86 us -> 6.13 us  [the longest x3 3.99 us: per_device(): pieces.append(lax.ppermute(key_value, 'lon', pairs))]
    reshape x4 -> x0, local copies, waits for them, and re-layouts: 1.48 us -> none  [the longest x1 0.57 us: per_device(): from_right = got[key_value.shape[0]:].reshape(rim.shape)[..., :reach]]
    unnamed x15 -> x45, local copies, waits for them, and re-layouts: 1.33 us -> 2.06 us
  transfers between devices with their start and end apart: 12 -> 14, of which waited for: 11 -> 11; matrix products, arithmetic and copies ran while one was open for 3% -> 2% of each run, Pallas kernels for 0% -> 0%
where the time goes in v7:
time: 103 us; the launch traced here: 102 us
  waiting for transfers between devices  48.6 us (47%)
  blocking collectives  22 us (21%)
  starting transfers between devices  12.7 us (12%)
  local copies, waits for them, and re-layouts  7.24 us (7%)
  matrix products  6.22 us (6%)
  other arithmetic  5.1 us (5%)
    ppermute x1, waiting for transfers between devices, per_device(): lax.ppermute(rim_left, 'lon', [(i, (i - 1) % strips) for i in range(strip...  26.5 us
    all_gather x3, blocking collectives, gather_channels(): return lax.all_gather(values, 'lev', axis=0, tiled=True)  22 us
    ppermute x9, waiting for transfers between devices, scatter_sum(): total = total + lax.ppermute(chunk, axis, pairs).astype(jnp.float32)  18.9 us
    ppermute x9, starting transfers between devices, scatter_sum(): total = total + lax.ppermute(chunk, axis, pairs).astype(jnp.float32)  6.55 us
    dot_general x3, matrix products, spread_sum(): lax.dot_general(weight, activation, (((0,), (0,)), ((), ())), preferred_e...  4.42 us
    ppermute x3, starting transfers between devices, per_device(): pieces.append(lax.ppermute(key_value, 'lon', pairs))  3.99 us
    ppermute x1, waiting for transfers between devices, per_device(): lax.ppermute(rim_right, 'lon', [(i, (i + 1) % strips) for i in range(stri...  3.28 us
    another operation x2, local copies, waits for them, and re-layouts, scatter_sum(): total = jnp.take(blocks, me, axis=0).astype(jnp.float32)  2.23 us
  transfers between devices with their start and end apart: 14, of which 11 were waited for; matrix products, arithmetic and copies ran while one was open for 2% of the time, Pallas kernels for 0%

profile of v7, /device:TPU:20, one launch (start us, length us, event | category | flops | bytes accessed | tf_op | source)
XLA Modules:
  0.0 102.4 jit_solution(2722582913871713772)
XLA Ops:
  0.0 7.5 %all_gather.9 = bf16[512,4,128]{2,1,0:T(4,128)(2,1)S(1)} all-gather(bf16[128,4,128]{2,1,0:T(4,128)(2,1)} %param.14), channel_id=1, replica_groups=mesh['member'=2,'lon'=4,'lev'=4] {'lev'}, dimensions={0}, use_global_device_ids=true | all-gather | bytes 655360 | tf_op jit(solution)/shard_map/all_gather | solution.py:34
  7.5 0.5 fusion.19
  8.1 1.5 %fusion.37 = bf16[512,4,128,1]{2,1,0,3:T(4,128)(2,1)S(1)} fusion(bf16[512,4,128]{2,1,0:T(4,128)(2,1)S(1)} %all_gather.9, f32[512]{0:T(512)S(1)} %copy-done.16, f32[4,128]{1,0:T(4,128)S(1)} %add_rsqrt_fusion.4), kind=kLoop, calls=%fused_computation.65 | loop fusion | flops 1048576 | bytes 1052672 | tf_op jit(solution)/shard_map/convert_element_type | solution.py:124
  9.6 0.4 convolution_bitcast_fusion.2
  10.2 0.5 collective-permute-start.4
  10.7 3.5 %collective-permute-start.3 = (bf16[256,4,128]{2,0,1:T(8,128)(2,1)S(1)}, bf16[256,4,128]{2,0,1:T(8,128)(2,1)S(1)}, u32[]{:S(2)}, u32[]{:S(2)}) collective-permute-start(bf16[256,4,128]{2,0,1:T(8,128)(2,1)S(1)} %bitcast.170), channel_id=1, source_target_pairs={{0,8},{4,12},{8,0},{12,4},{1,9},{5,13},{9,1},{13,5},{2,10},{6,14},... | collective-permute-start | bytes 786440 | tf_op jit(solution)/shard_map/ppermute | solution.py:136
  14.2 0.1 fusion.118
  14.5 0.1 slice_bitcast_fusion.3
  14.7 2.1 %collective-permute-start.1 = (bf16[2,128,4,2]{3,1,2,0:T(8,128)(2,1)S(1)}, bf16[2,128,4,2]{3,1,2,0:T(8,128)(2,1)S(1)}, u32[]{:S(2)}, u32[]{:S(2)}) collective-permute-start(bf16[2,128,4,2]{3,1,2,0:T(8,128)(2,1)S(1)} %pad_maximum_fusion.2), channel_id=1, source_target_pairs={{0,12},{4,0},{8,4},{12,8},{1,13},{5,1},{9,5},{13,9},{2,14},{6,2},{... | collective-permute-start | bytes 12296 | tf_op jit(solution)/shard_map/ppermute | solution.py:142
  17.0 0.6 slice_bitcast_fusion.12
  17.6 0.7 broadcast_multiply_fusion.5
  18.3 0.1 copy.113
  18.4 26.5 %collective-permute-done.1 = bf16[2,128,4,2]{3,1,2,0:T(8,128)(2,1)S(1)} collective-permute-done((bf16[2,128,4,2]{3,1,2,0:T(8,128)(2,1)S(1)}, bf16[2,128,4,2]{3,1,2,0:T(8,128)(2,1)S(1)}, u32[]{:S(2)}, u32[]{:S(2)}) %collective-permute-start.1) | collective-permute-done | bytes 4128 | tf_op jit(solution)/shard_map/ppermute | solution.py:142
  44.9 3.3 %collective-permute-done = bf16[2,128,4,2]{3,1,2,0:T(8,128)(2,1)S(1)} collective-permute-done((bf16[2,128,4,2]{3,1,2,0:T(8,128)(2,1)S(1)}, bf16[2,128,4,2]{3,1,2,0:T(8,128)(2,1)S(1)}, u32[]{:S(2)}, u32[]{:S(2)}) %collective-permute-start) | collective-permute-done | bytes 4128 | tf_op jit(solution)/shard_map/ppermute | solution.py:141
  48.2 0.1 pad_maximum_fusion
  48.4 0.1 fusion.116
  48.5 0.9 fusion
  49.4 0.5 fusion.5
  49.9 0.3 copy.124
  50.2 0.1 reshape.582
  50.3 0.3 fusion.2
  50.6 0.1 reshape.583
  50.7 1.1 %constant_dynamic-slice_fusion.7 = (bf16[1,128,528]{1,0,2:T(2,128)(2,1)S(1)}, bf16[1,128,528]{1,0,2:T(2,128)(2,1)S(1)}, bf16[1,128,528]{1,0,2:T(2,128)(2,1)S(1)}, bf16[1,128,528]{1,0,2:T(2,128)(2,1)S(1)}) fusion(bf16[4,128,528]{1,0,2:T(4,128)(2,1)S(1)} %reshape.583, s32[]{:T(128)S(6)} %select_n.78, s32[]{:T(128)S(6)} %select_n.82, s32[]{:T(128)S(6)} %select_n.80, ...), kind=kLoop, calls=%fused_computation.175 | loop fusion | bytes 1081360 | tf_op jit(solution)/shard_map/jit(_take) | solution.py:41
  51.9 0.1 collective-permute-start.7
  52.0 0.5 collective-permute-start.5
  52.6 1.2 %collective-permute-start.6 = (bf16[128,528]{0,1:T(8,128)(2,1)S(1)}, bf16[128,528]{0,1:T(8,128)(2,1)S(1)}, u32[]{:S(2)}, u32[]{:S(2)}) collective-permute-start(bf16[128,528]{0,1:T(8,128)(2,1)S(1)} %fusion.97), channel_id=1, source_target_pairs={{0,2},{1,3},{2,0},{3,1},{4,6},{5,7},{6,4},{7,5},{8,10},{9,11},{10,... | collective-permute-start | bytes 405512 | tf_op jit(solution)/shard_map/ppermute | solution.py:45
  53.8 0.1 copy.114
  53.9 0.1 copy.112
  54.0 1.4 %collective-permute-done.7 = bf16[128,528]{0,1:T(8,128)(2,1)S(1)} collective-permute-done((bf16[128,528]{0,1:T(8,128)(2,1)S(1)}, bf16[128,528]{0,1:T(8,128)(2,1)S(1)}, u32[]{:S(2)}, u32[]{:S(2)}) %collective-permute-start.7) | collective-permute-done | bytes 135200 | tf_op jit(solution)/shard_map/ppermute | solution.py:45
  55.4 2.5 %collective-permute-done.5 = bf16[128,528]{0,1:T(8,128)(2,1)S(1)} collective-permute-done((bf16[128,528]{0,1:T(8,128)(2,1)S(1)}, bf16[128,528]{0,1:T(8,128)(2,1)S(1)}, u32[]{:S(2)}, u32[]{:S(2)}) %collective-permute-start.5) | collective-permute-done | bytes 135200 | tf_op jit(solution)/shard_map/ppermute | solution.py:45
  57.9 2.2 %collective-permute-done.6 = bf16[128,528]{0,1:T(8,128)(2,1)S(1)} collective-permute-done((bf16[128,528]{0,1:T(8,128)(2,1)S(1)}, bf16[128,528]{0,1:T(8,128)(2,1)S(1)}, u32[]{:S(2)}, u32[]{:S(2)}) %collective-permute-start.6) | collective-permute-done | bytes 135200 | tf_op jit(solution)/shard_map/ppermute | solution.py:45
  60.1 0.1 convert_add_fusion
  60.2 0.1 fusion.115
  60.3 0.4 copy-done.6
  60.8 0.2 fusion.68
  61.0 7.3 %all_gather.10 = bf16[512,4,130]{0,2,1:T(8,128)(2,1)S(1)} all-gather(bf16[128,4,130]{0,2,1:T(8,128)(2,1)S(1)} %fusion.68), channel_id=1, replica_groups=mesh['member'=2,'lon'=4,'lev'=4] {'lev'}, dimensions={0}, use_global_device_ids=true | all-gather | bytes 665600 | tf_op jit(solution)/shard_map/all_gather | solution.py:34
  68.3 0.2 fusion.6
  68.6 0.2 fusion.8
  68.8 0.1 reshape.585
  68.9 0.8 copy-done.20
  69.8 2.0 %fusion.3 = bf16[512,520]{0,1:T(8,128)(2,1)S(1)} fusion(bf16[512,520]{0,1:T(8,128)(2,1)S(1)} %reshape.585, bf16[2,512,512]{2,1,0:T(8,128)(2,1)S(1)} %copy-done.20, bf16[2,512,512]{2,1,0:T(8,128)(2,1)} %param.20), kind=kOutput, calls=%fused_computation.18 | convolution fusion | flops 547921920 | bytes 2113536 | tf_op jit(solution)/shard_map/dot_general | solution.py:50
  71.8 0.1 reshape.586
  71.9 1.1 %constant_dynamic-slice_fusion.2 = (bf16[1,128,520]{1,0,2:T(2,128)(2,1)S(1)}, bf16[1,128,520]{1,0,2:T(2,128)(2,1)S(1)}, bf16[1,128,520]{1,0,2:T(2,128)(2,1)S(1)}, bf16[1,128,520]{1,0,2:T(2,128)(2,1)S(1)}) fusion(bf16[4,128,520]{1,0,2:T(4,128)(2,1)S(1)} %reshape.586, s32[]{:T(128)S(6)} %select_n.78, s32[]{:T(128)S(6)} %select_n.82, s32[]{:T(128)S(6)} %select_n.80, ...), kind=kLoop, calls=%fused_computation.170 | loop fusion | bytes 1064976 | tf_op jit(solution)/shard_map/jit(_take) | solution.py:41
  73.2 0.9 collective-permute-start.10
  74.1 1.1 %collective-permute-start.9 = (bf16[128,520]{0,1:T(8,128)(2,1)S(1)}, bf16[128,520]{0,1:T(8,128)(2,1)S(1)}, u32[]{:S(2)}, u32[]{:S(2)}) collective-permute-start(bf16[128,520]{0,1:T(8,128)(2,1)S(1)} %fusion.101), channel_id=1, source_target_pairs={{0,2},{1,3},{2,0},{3,1},{4,6},{5,7},{6,4},{7,5},{8,10},{9,11},{10,... | collective-permute-start | bytes 399368 | tf_op jit(solution)/shard_map/ppermute | solution.py:45
  75.2 2.3 %collective-permute-done.10 = bf16[128,520]{0,1:T(8,128)(2,1)S(1)} collective-permute-done((bf16[128,520]{0,1:T(8,128)(2,1)S(1)}, bf16[128,520]{0,1:T(8,128)(2,1)S(1)}, u32[]{:S(2)}, u32[]{:S(2)}) %collective-permute-start.10) | collective-permute-done | bytes 133152 | tf_op jit(solution)/shard_map/ppermute | solution.py:45
  77.6 2.4 %collective-permute-done.8 = bf16[128,520]{0,1:T(8,128)(2,1)S(1)} collective-permute-done((bf16[128,520]{0,1:T(8,128)(2,1)S(1)}, bf16[128,520]{0,1:T(8,128)(2,1)S(1)}, u32[]{:S(2)}, u32[]{:S(2)}) %collective-permute-start.8) | collective-permute-done | bytes 133152 | tf_op jit(solution)/shard_map/ppermute | solution.py:45
  79.9 2.2 %collective-permute-done.9 = bf16[128,520]{0,1:T(8,128)(2,1)S(1)} collective-permute-done((bf16[128,520]{0,1:T(8,128)(2,1)S(1)}, bf16[128,520]{0,1:T(8,128)(2,1)S(1)}, u32[]{:S(2)}, u32[]{:S(2)}) %collective-permute-start.9) | collective-permute-done | bytes 133152 | tf_op jit(solution)/shard_map/ppermute | solution.py:45
  82.1 0.1 convert_add_fusion.1
  82.3 0.5 copy-done.4
  82.8 0.2 fusion.83
  83.0 7.1 %all_gather.11 = bf16[512,4,128]{0,2,1:T(8,128)(2,1)S(1)} all-gather(bf16[128,4,128]{0,2,1:T(8,128)(2,1)S(1)} %fusion.83), channel_id=1, replica_groups=mesh['member'=2,'lon'=4,'lev'=4] {'lev'}, dimensions={0}, use_global_device_ids=true | all-gather | bytes 655360 | tf_op jit(solution)/shard_map/all_gather | solution.py:34
  90.1 0.2 fusion.22
  90.3 0.2 fusion.24
  90.5 2.1 %convolution_convert_fusion.2 = bf16[512,512]{0,1:T(8,128)(2,1)S(1)} fusion(bf16[512,512]{0,1:T(8,128)(2,1)S(1)} %bitcast.175, bf16[2,512,512]{2,1,0:T(8,128)(2,1)S(1)} %copy-done.20, bf16[2,512,512]{2,1,0:T(8,128)(2,1)} %param.20), kind=kOutput, calls=%fused_computation.15 | convolution fusion | flops 539492352 | bytes 2097152 | tf_op jit(solution)/shard_map/dot_general | solution.py:50
  92.7 0.4 collective-permute-start.11
  93.1 1.4 %collective-permute-start.13 = (bf16[128,512]{1,0:T(8,128)(2,1)S(1)}, bf16[128,512]{1,0:T(8,128)(2,1)S(1)}, u32[]{:S(2)}, u32[]{:S(2)}) collective-permute-start(bf16[128,512]{1,0:T(8,128)(2,1)S(1)} %get-tuple-element.59), channel_id=1, source_target_pairs={{0,3},{1,0},{2,1},{3,2},{4,7},{5,4},{6,5},{7,6},{8,11},{9,8},{10,9... | collective-permute-start | bytes 393224 | tf_op jit(solution)/shard_map/ppermute | solution.py:45
  94.5 0.9 collective-permute-start.12
  95.4 1.9 %collective-permute-done.11 = bf16[128,512]{1,0:T(8,128)(2,1)S(1)} collective-permute-done((bf16[128,512]{1,0:T(8,128)(2,1)S(1)}, bf16[128,512]{1,0:T(8,128)(2,1)S(1)}, u32[]{:S(2)}, u32[]{:S(2)}) %collective-permute-start.11) | collective-permute-done | bytes 131104 | tf_op jit(solution)/shard_map/ppermute | solution.py:45
  97.3 1.1 %collective-permute-done.13 = bf16[128,512]{1,0:T(8,128)(2,1)S(1)} collective-permute-done((bf16[128,512]{1,0:T(8,128)(2,1)S(1)}, bf16[128,512]{1,0:T(8,128)(2,1)S(1)}, u32[]{:S(2)}, u32[]{:S(2)}) %collective-permute-start.13) | collective-permute-done | bytes 131104 | tf_op jit(solution)/shard_map/ppermute | solution.py:45
  98.4 3.0 %collective-permute-done.12 = bf16[128,512]{1,0:T(8,128)(2,1)S(1)} collective-permute-done((bf16[128,512]{1,0:T(8,128)(2,1)S(1)}, bf16[128,512]{1,0:T(8,128)(2,1)S(1)}, u32[]{:S(2)}, u32[]{:S(2)}) %collective-permute-start.12) | collective-permute-done | bytes 131104 | tf_op jit(solution)/shard_map/ppermute | solution.py:45
  101.4 0.1 convert_add_fusion.2
  101.4 0.1 copy.133
  101.6 0.8 copy.134
  (78 shorter events, 1.1 us)
Async XLA Ops:
  0.0 9.6 %copy-start = (bf16[3,128,512]{2,1,0:T(8,128)(2,1)S(1)}, bf16[3,128,512]{2,1,0:T(8,128)(2,1)}, u32[]{:S(2)}) copy-start(bf16[3,128,512]{2,1,0:T(8,128)(2,1)} %param.16) | copy-start | bytes 1179652
  0.0 8.1 %copy-start.16 = (f32[512]{0:T(512)S(1)}, f32[512]{0:T(512)}, u32[]{:S(2)}) copy-start(f32[512]{0:T(512)} %param.15) | copy-start | bytes 6148
  10.0 4.2 %copy-start.1 = (bf16[128,4,128]{2,1,0:T(4,128)(2,1)S(1)}, bf16[128,4,128]{2,1,0:T(4,128)(2,1)}, u32[]{:S(2)}) copy-start(bf16[128,4,128]{2,1,0:T(4,128)(2,1)} %param.14) | copy-start | bytes 393220
  10.2 38.0 %collective-permute-start.4 = (bf16[256,4,128]{2,0,1:T(8,128)(2,1)S(1)}, bf16[256,4,128]{2,0,1:T(8,128)(2,1)S(1)}, u32[]{:S(2)}, u32[]{:S(2)}) collective-permute-start(bf16[256,4,128]{2,0,1:T(8,128)(2,1)S(1)} %bitcast.169), channel_id=1, source_target_pairs={{0,12},{4,0},{8,4},{12,8},{1,13},{5,1},{9,5},{13,9},{2,14},{6,2},{... | collective-permute-start | bytes 786440 | tf_op jit(solution)/shard_map/ppermute | solution.py:136
  10.7 37.5 %collective-permute-start.3 = (bf16[256,4,128]{2,0,1:T(8,128)(2,1)S(1)}, bf16[256,4,128]{2,0,1:T(8,128)(2,1)S(1)}, u32[]{:S(2)}, u32[]{:S(2)}) collective-permute-start(bf16[256,4,128]{2,0,1:T(8,128)(2,1)S(1)} %bitcast.170), channel_id=1, source_target_pairs={{0,8},{4,12},{8,0},{12,4},{1,9},{5,13},{9,1},{13,5},{2,10},{6,14},... | collective-permute-start | bytes 786440 | tf_op jit(solution)/shard_map/ppermute | solution.py:136
  14.2 34.0 %collective-permute-start.2 = (bf16[256,4,128]{2,0,1:T(8,128)(2,1)S(1)}, bf16[256,4,128]{2,0,1:T(8,128)(2,1)S(1)}, u32[]{:S(2)}, u32[]{:S(2)}) collective-permute-start(bf16[256,4,128]{2,0,1:T(8,128)(2,1)S(1)} %bitcast.171), channel_id=1, source_target_pairs={{0,4},{4,8},{8,12},{12,0},{1,5},{5,9},{9,13},{13,1},{2,6},{6,10},{... | collective-permute-start | bytes 786440 | tf_op jit(solution)/shard_map/ppermute | solution.py:136
  14.4 2.5 %copy-start.3 = (f32[2,9,128]{2,0,1:T(2,128)S(1)}, f32[2,9,128]{2,0,1:T(2,128)}, u32[]{:S(2)}) copy-start(f32[2,9,128]{2,0,1:T(2,128)} %param.18) | copy-start | bytes 27652
  14.7 30.2 %collective-permute-start.1 = (bf16[2,128,4,2]{3,1,2,0:T(8,128)(2,1)S(1)}, bf16[2,128,4,2]{3,1,2,0:T(8,128)(2,1)S(1)}, u32[]{:S(2)}, u32[]{:S(2)}) collective-permute-start(bf16[2,128,4,2]{3,1,2,0:T(8,128)(2,1)S(1)} %pad_maximum_fusion.2), channel_id=1, source_target_pairs={{0,12},{4,0},{8,4},{12,8},{1,13},{5,1},{9,5},{13,9},{2,14},{6,2},{... | collective-permute-start | bytes 12296 | tf_op jit(solution)/shard_map/ppermute | solution.py:142
  16.8 31.4 %collective-permute-start = (bf16[2,128,4,2]{3,1,2,0:T(8,128)(2,1)S(1)}, bf16[2,128,4,2]{3,1,2,0:T(8,128)(2,1)S(1)}, u32[]{:S(2)}, u32[]{:S(2)}) collective-permute-start(bf16[2,128,4,2]{3,1,2,0:T(8,128)(2,1)S(1)} %pad_maximum_fusion.1), channel_id=1, source_target_pairs={{0,4},{4,8},{8,12},{12,0},{1,5},{5,9},{9,13},{13,1},{2,6},{6,10},{... | collective-permute-start | bytes 12296 | tf_op jit(solution)/shard_map/ppermute | solution.py:141
  49.4 1.0 copy-start.2
  51.9 1.9 %copy-start.12 = (f32[2,512]{1,0:T(2,128)S(1)}, f32[2,512]{1,0:T(2,128)}, u32[]{:S(2)}) copy-start(f32[2,512]{1,0:T(2,128)} %param.19) | copy-start | bytes 12292
  51.9 3.5 %collective-permute-start.7 = (bf16[128,528]{0,1:T(8,128)(2,1)S(1)}, bf16[128,528]{0,1:T(8,128)(2,1)S(1)}, u32[]{:S(2)}, u32[]{:S(2)}) collective-permute-start(bf16[128,528]{0,1:T(8,128)(2,1)S(1)} %fusion.96), channel_id=1, source_target_pairs={{0,3},{1,0},{2,1},{3,2},{4,7},{5,4},{6,5},{7,6},{8,11},{9,8},{10,9... | collective-permute-start | bytes 405512 | tf_op jit(solution)/shard_map/ppermute | solution.py:45
  52.0 5.9 %collective-permute-start.5 = (bf16[128,528]{0,1:T(8,128)(2,1)S(1)}, bf16[128,528]{0,1:T(8,128)(2,1)S(1)}, u32[]{:S(2)}, u32[]{:S(2)}) collective-permute-start(bf16[128,528]{0,1:T(8,128)(2,1)S(1)} %fusion.98), channel_id=1, source_target_pairs={{0,1},{1,2},{2,3},{3,0},{4,5},{5,6},{6,7},{7,4},{8,9},{9,10},{10,1... | collective-permute-start | bytes 405512 | tf_op jit(solution)/shard_map/ppermute | solution.py:45
  52.6 7.5 %collective-permute-start.6 = (bf16[128,528]{0,1:T(8,128)(2,1)S(1)}, bf16[128,528]{0,1:T(8,128)(2,1)S(1)}, u32[]{:S(2)}, u32[]{:S(2)}) collective-permute-start(bf16[128,528]{0,1:T(8,128)(2,1)S(1)} %fusion.97), channel_id=1, source_target_pairs={{0,2},{1,3},{2,0},{3,1},{4,6},{5,7},{6,4},{7,5},{8,10},{9,11},{10,... | collective-permute-start | bytes 405512 | tf_op jit(solution)/shard_map/ppermute | solution.py:45
  60.1 0.7 copy-start.6
  60.1 0.7 copy-start.7
  60.1 0.7 copy-start.8
  60.1 0.7 copy-start.9
  60.1 0.7 copy-start.10
  60.1 0.7 copy-start.11
  60.1 0.7 copy-start.17
  60.1 0.7 copy-start.18
  60.1 0.7 copy-start.19
  68.6 1.2 %copy-start.20 = (bf16[2,512,512]{2,1,0:T(8,128)(2,1)S(1)}, bf16[2,512,512]{2,1,0:T(8,128)(2,1)}, u32[]{:S(2)}) copy-start(bf16[2,512,512]{2,1,0:T(8,128)(2,1)} %param.21) | copy-start | bytes 3145732
  73.2 4.4 %collective-permute-start.10 = (bf16[128,520]{0,1:T(8,128)(2,1)S(1)}, bf16[128,520]{0,1:T(8,128)(2,1)S(1)}, u32[]{:S(2)}, u32[]{:S(2)}) collective-permute-start(bf16[128,520]{0,1:T(8,128)(2,1)S(1)} %fusion.100), channel_id=1, source_target_pairs={{0,3},{1,0},{2,1},{3,2},{4,7},{5,4},{6,5},{7,6},{8,11},{9,8},{10,9... | collective-permute-start | bytes 399368 | tf_op jit(solution)/shard_map/ppermute | solution.py:45
  74.1 5.8 %collective-permute-start.8 = (bf16[128,520]{0,1:T(8,128)(2,1)S(1)}, bf16[128,520]{0,1:T(8,128)(2,1)S(1)}, u32[]{:S(2)}, u32[]{:S(2)}) collective-permute-start(bf16[128,520]{0,1:T(8,128)(2,1)S(1)} %fusion.102), channel_id=1, source_target_pairs={{0,1},{1,2},{2,3},{3,0},{4,5},{5,6},{6,7},{7,4},{8,9},{9,10},{10,1... | collective-permute-start | bytes 399368 | tf_op jit(solution)/shard_map/ppermute | solution.py:45
  74.1 8.0 %collective-permute-start.9 = (bf16[128,520]{0,1:T(8,128)(2,1)S(1)}, bf16[128,520]{0,1:T(8,128)(2,1)S(1)}, u32[]{:S(2)}, u32[]{:S(2)}) collective-permute-start(bf16[128,520]{0,1:T(8,128)(2,1)S(1)} %fusion.101), channel_id=1, source_target_pairs={{0,2},{1,3},{2,0},{3,1},{4,6},{5,7},{6,4},{7,5},{8,10},{9,11},{10,... | collective-permute-start | bytes 399368 | tf_op jit(solution)/shard_map/ppermute | solution.py:45
  82.1 0.7 copy-start.4
  82.1 0.7 copy-start.5
  82.1 0.7 copy-start.13
  82.1 0.7 copy-start.14
  82.1 0.7 copy-start.15
  92.7 4.6 %collective-permute-start.11 = (bf16[128,512]{1,0:T(8,128)(2,1)S(1)}, bf16[128,512]{1,0:T(8,128)(2,1)S(1)}, u32[]{:S(2)}, u32[]{:S(2)}) collective-permute-start(bf16[128,512]{1,0:T(8,128)(2,1)S(1)} %get-tuple-element.58), channel_id=1, source_target_pairs={{0,1},{1,2},{2,3},{3,0},{4,5},{5,6},{6,7},{7,4},{8,9},{9,10},{10,1... | collective-permute-start | bytes 393224 | tf_op jit(solution)/shard_map/ppermute | solution.py:45
  93.1 5.3 %collective-permute-start.13 = (bf16[128,512]{1,0:T(8,128)(2,1)S(1)}, bf16[128,512]{1,0:T(8,128)(2,1)S(1)}, u32[]{:S(2)}, u32[]{:S(2)}) collective-permute-start(bf16[128,512]{1,0:T(8,128)(2,1)S(1)} %get-tuple-element.59), channel_id=1, source_target_pairs={{0,3},{1,0},{2,1},{3,2},{4,7},{5,4},{6,5},{7,6},{8,11},{9,8},{10,9... | collective-permute-start | bytes 393224 | tf_op jit(solution)/shard_map/ppermute | solution.py:45
  94.5 6.9 %collective-permute-start.12 = (bf16[128,512]{1,0:T(8,128)(2,1)S(1)}, bf16[128,512]{1,0:T(8,128)(2,1)S(1)}, u32[]{:S(2)}, u32[]{:S(2)}) collective-permute-start(bf16[128,512]{1,0:T(8,128)(2,1)S(1)} %get-tuple-element.60), channel_id=1, source_target_pairs={{0,2},{1,3},{2,0},{3,1},{4,6},{5,7},{6,4},{7,5},{8,10},{9,11},{10,... | collective-permute-start | bytes 393224 | tf_op jit(solution)/shard_map/ppermute | solution.py:45

commit v8 on v3

--- a/solution.py
+++ b/solution.py
@@ -65,17 +65,17 @@
 def make_fold(queries, pieces):
     key_part, value_part = pieces
     scores = (
-        jnp.einsum("hdri,hdrj->hrij", queries, key_part, preferred_element_type=jnp.float32)
+        jnp.einsum("hdri,phdrj->hripj", queries, key_part, preferred_element_type=jnp.float32)
         * attention_scale
     )
     weights = jnp.exp(scores)
     numerator = jnp.einsum(
-        "hrij,hdrj->hdri",
+        "hripj,phdrj->hdri",
         weights.astype(jnp.bfloat16),
         value_part,
         preferred_element_type=jnp.float32,
     )
-    return (numerator, jnp.sum(weights, axis=3))
+    return (numerator, jnp.sum(weights, axis=(3, 4)))
 
 
 def block_apply(state, block_index, stencil_weight, block_gain, up_weight, down_weight):
@@ -144,13 +144,13 @@
             from_left = got[key_value.shape[0] :].reshape(rim.shape)[..., reach:]
         if shift == strips - 1:
             from_right = got[key_value.shape[0] :].reshape(rim.shape)[..., :reach]
-    all_keys = jnp.concatenate(pieces, axis=-1).reshape(2, heads_local, head_size, lat_rows, -1)
+    all_keys = jnp.stack(pieces).reshape(strips, 2, heads_local, head_size, lat_rows, columns)
     wide_queries = jnp.concatenate(
         [from_left[0], queries.reshape(ch_local, lat_rows, columns), from_right[0]], axis=-1
     ).reshape(heads_local, head_size, lat_rows, -1)
     wide_latent = jnp.concatenate([from_left[1], latent, from_right[1]], axis=-1)
 
-    numerator, denominator = make_fold(wide_queries, (all_keys[0], all_keys[1]))
+    numerator, denominator = make_fold(wide_queries, (all_keys[:, 0], all_keys[:, 1]))
     attended = (numerator / denominator[:, None]).astype(jnp.bfloat16)
     update = spread_sum(out_weight, attended.reshape(ch_local, -1))
     current = (wide_latent.astype(jnp.float32) + update.reshape(wide_latent.shape)).astype(

time: 91.9 us -> 91.8 us (level)
  the two profiles are of different devices: /device:TPU:20 before, /device:TPU:16 now
where the time goes in v8:
time: 91.8 us; the launch traced here: 91.5 us
  waiting for transfers between devices  40.2 us (44%)
  blocking collectives  22.2 us (24%)
  starting transfers between devices  9.74 us (11%)
  local copies, waits for them, and re-layouts  8.06 us (9%)
  matrix products  6.22 us (7%)
  other arithmetic  4.41 us (5%)
    all_gather x3, blocking collectives, gather_channels(): return lax.all_gather(values, 'lev', axis=0, tiled=True)  22.2 us
    ppermute x3, waiting for transfers between devices, per_device(): got = lax.ppermute(sent, 'lon', pairs)  21.4 us
    ppermute x9, waiting for transfers between devices, scatter_sum(): total = total + lax.ppermute(chunk, axis, pairs).astype(jnp.float32)  18.8 us
    ppermute x9, starting transfers between devices, scatter_sum(): total = total + lax.ppermute(chunk, axis, pairs).astype(jnp.float32)  6.89 us
    dot_general x3, matrix products, spread_sum(): lax.dot_general(weight, activation, (((0,), (0,)), ((), ())), preferred_e...  4.42 us
    ppermute x3, starting transfers between devices, per_device(): got = lax.ppermute(sent, 'lon', pairs)  2.85 us
    another operation x2, local copies, waits for them, and re-layouts, scatter_sum(): total = jnp.take(blocks, me, axis=0).astype(jnp.float32)  2.23 us
  transfers between devices with their start and end apart: 12, of which 11 were waited for; matrix products, arithmetic and copies ran while one was open for 3% of the time, Pallas kernels for 0%

profile of v8, /device:TPU:16, one launch (start us, length us, event | category | flops | bytes accessed | tf_op | source)
XLA Modules:
  0.0 91.5 jit_solution(4199462890208673837)
XLA Ops:
  0.0 7.5 %all_gather.9 = bf16[512,4,128]{2,1,0:T(4,128)(2,1)S(1)} all-gather(bf16[128,4,128]{2,1,0:T(4,128)(2,1)} %param.14), channel_id=1, replica_groups=mesh['member'=2,'lon'=4,'lev'=4] {'lev'}, dimensions={0}, use_global_device_ids=true | all-gather | bytes 655360 | tf_op jit(solution)/shard_map/all_gather | solution.py:34
  7.5 0.5 fusion.17
  8.1 1.5 %fusion.44 = bf16[512,4,128,1]{2,1,0,3:T(4,128)(2,1)S(1)} fusion(bf16[512,4,128]{2,1,0:T(4,128)(2,1)S(1)} %all_gather.9, f32[512]{0:T(512)S(1)} %copy-done.5, f32[4,128]{1,0:T(4,128)S(1)} %add_rsqrt_fusion.2), kind=kLoop, calls=%fused_computation.66 | loop fusion | flops 1048576 | bytes 1052672 | tf_op jit(solution)/shard_map/convert_element_type | solution.py:124
  9.6 0.4 convolution_bitcast_fusion.2
  10.3 0.4 collective-permute-start.2
  10.7 0.3 copy-done.1
  11.0 0.1 copy.103
  11.3 0.1 fusion.124
  11.4 0.1 copy.101
  11.5 0.1 copy.102
  11.7 0.2 copy.105
  11.9 0.3 reshape.596
  12.3 2.5 %collective-permute-start.1 = (bf16[264,4,128]{2,0,1:T(8,128)(2,1)S(1)}, bf16[264,4,128]{2,0,1:T(8,128)(2,1)S(1)}, u32[]{:S(2)}, u32[]{:S(2)}) collective-permute-start(bf16[264,4,128]{2,0,1:T(8,128)(2,1)S(1)} %pad_maximum_fusion.1), channel_id=1, source_target_pairs={{0,12},{4,0},{8,4},{12,8},{1,13},{5,1},{9,5},{13,9},{2,14},{6,2},{... | collective-permute-start | bytes 811016 | tf_op jit(solution)/shard_map/ppermute | solution.py:141
  14.8 0.1 broadcast_multiply_fusion.5
  14.9 19.1 %collective-permute-done.1 = bf16[264,4,128]{2,0,1:T(8,128)(2,1)S(1)} collective-permute-done((bf16[264,4,128]{2,0,1:T(8,128)(2,1)S(1)}, bf16[264,4,128]{2,0,1:T(8,128)(2,1)S(1)}, u32[]{:S(2)}, u32[]{:S(2)}) %collective-permute-start.1) | collective-permute-done | bytes 270368 | tf_op jit(solution)/shard_map/ppermute | solution.py:141
  34.0 0.6 reshape.598
  34.6 0.1 slice_bitcast_fusion.4
  34.7 2.3 %collective-permute-done = bf16[264,4,128]{2,0,1:T(8,128)(2,1)S(1)} collective-permute-done((bf16[264,4,128]{2,0,1:T(8,128)(2,1)S(1)}, bf16[264,4,128]{2,0,1:T(8,128)(2,1)S(1)}, u32[]{:S(2)}, u32[]{:S(2)}) %collective-permute-start) | collective-permute-done | bytes 270368 | tf_op jit(solution)/shard_map/ppermute | solution.py:141
  37.1 0.6 reshape.597
  37.7 0.2 slice_bitcast_fusion.5
  38.0 0.9 fusion
  39.0 0.5 fusion.37
  39.5 0.3 copy.120
  39.8 0.1 reshape.599
  39.9 0.3 fusion.2
  40.2 0.1 reshape.600
  40.3 1.1 %constant_dynamic-slice_fusion.7 = (bf16[1,128,528]{1,0,2:T(2,128)(2,1)S(1)}, bf16[1,128,528]{1,0,2:T(2,128)(2,1)S(1)}, bf16[1,128,528]{1,0,2:T(2,128)(2,1)S(1)}, bf16[1,128,528]{1,0,2:T(2,128)(2,1)S(1)}) fusion(bf16[4,128,528]{1,0,2:T(4,128)(2,1)S(1)} %reshape.600, s32[]{:T(128)S(6)} %select_n.78, s32[]{:T(128)S(6)} %select_n.82, s32[]{:T(128)S(6)} %select_n.80, ...), kind=kLoop, calls=%fused_computation.177 | loop fusion | bytes 1081360 | tf_op jit(solution)/shard_map/jit(_take) | solution.py:41
  41.5 0.8 collective-permute-start.5
  42.4 1.0 %collective-permute-start.4 = (bf16[128,528]{0,1:T(8,128)(2,1)S(1)}, bf16[128,528]{0,1:T(8,128)(2,1)S(1)}, u32[]{:S(2)}, u32[]{:S(2)}) collective-permute-start(bf16[128,528]{0,1:T(8,128)(2,1)S(1)} %fusion.102), channel_id=1, source_target_pairs={{0,2},{1,3},{2,0},{3,1},{4,6},{5,7},{6,4},{7,5},{8,10},{9,11},{10,... | collective-permute-start | bytes 405512 | tf_op jit(solution)/shard_map/ppermute | solution.py:45
  43.5 0.1 copy.111
  43.6 0.1 copy.109
  43.7 2.3 %collective-permute-done.5 = bf16[128,528]{0,1:T(8,128)(2,1)S(1)} collective-permute-done((bf16[128,528]{0,1:T(8,128)(2,1)S(1)}, bf16[128,528]{0,1:T(8,128)(2,1)S(1)}, u32[]{:S(2)}, u32[]{:S(2)}) %collective-permute-start.5) | collective-permute-done | bytes 135200 | tf_op jit(solution)/shard_map/ppermute | solution.py:45
  45.9 2.3 %collective-permute-done.3 = bf16[128,528]{0,1:T(8,128)(2,1)S(1)} collective-permute-done((bf16[128,528]{0,1:T(8,128)(2,1)S(1)}, bf16[128,528]{0,1:T(8,128)(2,1)S(1)}, u32[]{:S(2)}, u32[]{:S(2)}) %collective-permute-start.3) | collective-permute-done | bytes 135200 | tf_op jit(solution)/shard_map/ppermute | solution.py:45
  48.2 1.8 %collective-permute-done.4 = bf16[128,528]{0,1:T(8,128)(2,1)S(1)} collective-permute-done((bf16[128,528]{0,1:T(8,128)(2,1)S(1)}, bf16[128,528]{0,1:T(8,128)(2,1)S(1)}, u32[]{:S(2)}, u32[]{:S(2)}) %collective-permute-start.4) | collective-permute-done | bytes 135200 | tf_op jit(solution)/shard_map/ppermute | solution.py:45
  50.1 0.1 convert_add_fusion
  50.2 0.2 fusion.73
  50.4 7.5 %all_gather.10 = bf16[512,4,130]{0,2,1:T(8,128)(2,1)S(1)} all-gather(bf16[128,4,130]{0,2,1:T(8,128)(2,1)S(1)} %fusion.73), channel_id=1, replica_groups=mesh['member'=2,'lon'=4,'lev'=4] {'lev'}, dimensions={0}, use_global_device_ids=true | all-gather | bytes 665600 | tf_op jit(solution)/shard_map/all_gather | solution.py:34
  57.9 0.2 fusion.4
  58.2 0.2 fusion.6
  58.4 0.1 reshape.602
  58.5 0.8 copy-done.6
  59.4 2.0 %fusion.3 = bf16[512,520]{0,1:T(8,128)(2,1)S(1)} fusion(bf16[512,520]{0,1:T(8,128)(2,1)S(1)} %reshape.602, bf16[2,512,512]{2,1,0:T(8,128)(2,1)S(1)} %copy-done.6, bf16[2,512,512]{2,1,0:T(8,128)(2,1)} %param.20), kind=kOutput, calls=%fused_computation.18 | convolution fusion | flops 547921920 | bytes 2113536 | tf_op jit(solution)/shard_map/dot_general | solution.py:50
  61.4 0.1 reshape.603
  61.5 1.1 %constant_dynamic-slice_fusion.2 = (bf16[1,128,520]{1,0,2:T(2,128)(2,1)S(1)}, bf16[1,128,520]{1,0,2:T(2,128)(2,1)S(1)}, bf16[1,128,520]{1,0,2:T(2,128)(2,1)S(1)}, bf16[1,128,520]{1,0,2:T(2,128)(2,1)S(1)}) fusion(bf16[4,128,520]{1,0,2:T(4,128)(2,1)S(1)} %reshape.603, s32[]{:T(128)S(6)} %select_n.78, s32[]{:T(128)S(6)} %select_n.82, s32[]{:T(128)S(6)} %select_n.80, ...), kind=kLoop, calls=%fused_computation.172 | loop fusion | bytes 1064976 | tf_op jit(solution)/shard_map/jit(_take) | solution.py:41
  62.8 1.1 %collective-permute-start.8 = (bf16[128,520]{0,1:T(8,128)(2,1)S(1)}, bf16[128,520]{0,1:T(8,128)(2,1)S(1)}, u32[]{:S(2)}, u32[]{:S(2)}) collective-permute-start(bf16[128,520]{0,1:T(8,128)(2,1)S(1)} %fusion.105), channel_id=1, source_target_pairs={{0,3},{1,0},{2,1},{3,2},{4,7},{5,4},{6,5},{7,6},{8,11},{9,8},{10,9... | collective-permute-start | bytes 399368 | tf_op jit(solution)/shard_map/ppermute | solution.py:45
  63.9 1.0 %collective-permute-start.7 = (bf16[128,520]{0,1:T(8,128)(2,1)S(1)}, bf16[128,520]{0,1:T(8,128)(2,1)S(1)}, u32[]{:S(2)}, u32[]{:S(2)}) collective-permute-start(bf16[128,520]{0,1:T(8,128)(2,1)S(1)} %fusion.106), channel_id=1, source_target_pairs={{0,2},{1,3},{2,0},{3,1},{4,6},{5,7},{6,4},{7,5},{8,10},{9,11},{10,... | collective-permute-start | bytes 399368 | tf_op jit(solution)/shard_map/ppermute | solution.py:45
  64.8 2.7 %collective-permute-done.8 = bf16[128,520]{0,1:T(8,128)(2,1)S(1)} collective-permute-done((bf16[128,520]{0,1:T(8,128)(2,1)S(1)}, bf16[128,520]{0,1:T(8,128)(2,1)S(1)}, u32[]{:S(2)}, u32[]{:S(2)}) %collective-permute-start.8) | collective-permute-done | bytes 133152 | tf_op jit(solution)/shard_map/ppermute | solution.py:45
  67.6 2.1 %collective-permute-done.6 = bf16[128,520]{0,1:T(8,128)(2,1)S(1)} collective-permute-done((bf16[128,520]{0,1:T(8,128)(2,1)S(1)}, bf16[128,520]{0,1:T(8,128)(2,1)S(1)}, u32[]{:S(2)}, u32[]{:S(2)}) %collective-permute-start.6) | collective-permute-done | bytes 133152 | tf_op jit(solution)/shard_map/ppermute | solution.py:45
  69.7 1.9 %collective-permute-done.7 = bf16[128,520]{0,1:T(8,128)(2,1)S(1)} collective-permute-done((bf16[128,520]{0,1:T(8,128)(2,1)S(1)}, bf16[128,520]{0,1:T(8,128)(2,1)S(1)}, u32[]{:S(2)}, u32[]{:S(2)}) %collective-permute-start.7) | collective-permute-done | bytes 133152 | tf_op jit(solution)/shard_map/ppermute | solution.py:45
  71.6 0.1 convert_add_fusion.1
  71.8 0.2 fusion.88
  71.9 7.2 %all_gather.11 = bf16[512,4,128]{0,2,1:T(8,128)(2,1)S(1)} all-gather(bf16[128,4,128]{0,2,1:T(8,128)(2,1)S(1)} %fusion.88), channel_id=1, replica_groups=mesh['member'=2,'lon'=4,'lev'=4] {'lev'}, dimensions={0}, use_global_device_ids=true | all-gather | bytes 655360 | tf_op jit(solution)/shard_map/all_gather | solution.py:34
  79.2 0.2 fusion.20
  79.4 0.2 fusion.22
  79.6 2.1 %convolution_convert_fusion.2 = bf16[512,512]{0,1:T(8,128)(2,1)S(1)} fusion(bf16[512,512]{0,1:T(8,128)(2,1)S(1)} %bitcast.191, bf16[2,512,512]{2,1,0:T(8,128)(2,1)S(1)} %copy-done.6, bf16[2,512,512]{2,1,0:T(8,128)(2,1)} %param.20), kind=kOutput, calls=%fused_computation.15 | convolution fusion | flops 539492352 | bytes 2097152 | tf_op jit(solution)/shard_map/dot_general | solution.py:50
  81.8 0.4 collective-permute-start.9
  82.2 1.4 %collective-permute-start.11 = (bf16[128,512]{1,0:T(8,128)(2,1)S(1)}, bf16[128,512]{1,0:T(8,128)(2,1)S(1)}, u32[]{:S(2)}, u32[]{:S(2)}) collective-permute-start(bf16[128,512]{1,0:T(8,128)(2,1)S(1)} %get-tuple-element.57), channel_id=1, source_target_pairs={{0,3},{1,0},{2,1},{3,2},{4,7},{5,4},{6,5},{7,6},{8,11},{9,8},{10,9... | collective-permute-start | bytes 393224 | tf_op jit(solution)/shard_map/ppermute | solution.py:45
  83.6 1.2 %collective-permute-start.10 = (bf16[128,512]{1,0:T(8,128)(2,1)S(1)}, bf16[128,512]{1,0:T(8,128)(2,1)S(1)}, u32[]{:S(2)}, u32[]{:S(2)}) collective-permute-start(bf16[128,512]{1,0:T(8,128)(2,1)S(1)} %get-tuple-element.58), channel_id=1, source_target_pairs={{0,2},{1,3},{2,0},{3,1},{4,6},{5,7},{6,4},{7,5},{8,10},{9,11},{10,... | collective-permute-start | bytes 393224 | tf_op jit(solution)/shard_map/ppermute | solution.py:45
  84.7 1.5 %collective-permute-done.9 = bf16[128,512]{1,0:T(8,128)(2,1)S(1)} collective-permute-done((bf16[128,512]{1,0:T(8,128)(2,1)S(1)}, bf16[128,512]{1,0:T(8,128)(2,1)S(1)}, u32[]{:S(2)}, u32[]{:S(2)}) %collective-permute-start.9) | collective-permute-done | bytes 131104 | tf_op jit(solution)/shard_map/ppermute | solution.py:45
  86.2 1.3 %collective-permute-done.11 = bf16[128,512]{1,0:T(8,128)(2,1)S(1)} collective-permute-done((bf16[128,512]{1,0:T(8,128)(2,1)S(1)}, bf16[128,512]{1,0:T(8,128)(2,1)S(1)}, u32[]{:S(2)}, u32[]{:S(2)}) %collective-permute-start.11) | collective-permute-done | bytes 131104 | tf_op jit(solution)/shard_map/ppermute | solution.py:45
  87.5 2.9 %collective-permute-done.10 = bf16[128,512]{1,0:T(8,128)(2,1)S(1)} collective-permute-done((bf16[128,512]{1,0:T(8,128)(2,1)S(1)}, bf16[128,512]{1,0:T(8,128)(2,1)S(1)}, u32[]{:S(2)}, u32[]{:S(2)}) %collective-permute-start.10) | collective-permute-done | bytes 131104 | tf_op jit(solution)/shard_map/ppermute | solution.py:45
  90.4 0.1 convert_add_fusion.2
  90.5 0.1 copy.129
  90.7 0.8 copy.130
  (60 shorter events, 1.2 us)
Async XLA Ops:
  0.0 9.6 %copy-start = (bf16[3,128,512]{2,1,0:T(8,128)(2,1)S(1)}, bf16[3,128,512]{2,1,0:T(8,128)(2,1)}, u32[]{:S(2)}) copy-start(bf16[3,128,512]{2,1,0:T(8,128)(2,1)} %param.16) | copy-start | bytes 1179652
  0.0 8.1 %copy-start.5 = (f32[512]{0:T(512)S(1)}, f32[512]{0:T(512)}, u32[]{:S(2)}) copy-start(f32[512]{0:T(512)} %param.15) | copy-start | bytes 6148
  10.1 0.9 copy-start.1
  10.3 27.7 %collective-permute-start.2 = (bf16[256,4,128]{2,0,1:T(8,128)(2,1)S(1)}, bf16[256,4,128]{2,0,1:T(8,128)(2,1)S(1)}, u32[]{:S(2)}, u32[]{:S(2)}) collective-permute-start(bf16[256,4,128]{2,0,1:T(8,128)(2,1)S(1)} %bitcast.184), channel_id=1, source_target_pairs={{0,8},{4,12},{8,0},{12,4},{1,9},{5,13},{9,1},{13,5},{2,10},{6,14},... | collective-permute-start | bytes 786440 | tf_op jit(solution)/shard_map/ppermute | solution.py:141
  11.3 3.5 %copy-start.3 = (f32[2,9,128]{2,0,1:T(2,128)S(1)}, f32[2,9,128]{2,0,1:T(2,128)}, u32[]{:S(2)}) copy-start(f32[2,9,128]{2,0,1:T(2,128)} %param.18) | copy-start | bytes 27652
  12.3 21.8 %collective-permute-start.1 = (bf16[264,4,128]{2,0,1:T(8,128)(2,1)S(1)}, bf16[264,4,128]{2,0,1:T(8,128)(2,1)S(1)}, u32[]{:S(2)}, u32[]{:S(2)}) collective-permute-start(bf16[264,4,128]{2,0,1:T(8,128)(2,1)S(1)} %pad_maximum_fusion.1), channel_id=1, source_target_pairs={{0,12},{4,0},{8,4},{12,8},{1,13},{5,1},{9,5},{13,9},{2,14},{6,2},{... | collective-permute-start | bytes 811016 | tf_op jit(solution)/shard_map/ppermute | solution.py:141
  14.7 22.4 %collective-permute-start = (bf16[264,4,128]{2,0,1:T(8,128)(2,1)S(1)}, bf16[264,4,128]{2,0,1:T(8,128)(2,1)S(1)}, u32[]{:S(2)}, u32[]{:S(2)}) collective-permute-start(bf16[264,4,128]{2,0,1:T(8,128)(2,1)S(1)} %pad_maximum_fusion.1), channel_id=1, source_target_pairs={{0,4},{4,8},{8,12},{12,0},{1,5},{5,9},{9,13},{13,1},{2,6},{6,10},{... | collective-permute-start | bytes 811016 | tf_op jit(solution)/shard_map/ppermute | solution.py:141
  38.9 1.0 %copy-start.2 = (bf16[128,512]{1,0:T(8,128)(2,1)S(1)}, bf16[128,512]{1,0:T(8,128)(2,1)}, u32[]{:S(2)}) copy-start(bf16[128,512]{1,0:T(8,128)(2,1)} %param.17) | copy-start | bytes 393220
  41.5 2.0 %copy-start.4 = (f32[2,512]{1,0:T(2,128)S(1)}, f32[2,512]{1,0:T(2,128)}, u32[]{:S(2)}) copy-start(f32[2,512]{1,0:T(2,128)} %param.19) | copy-start | bytes 12292
  41.5 4.4 %collective-permute-start.5 = (bf16[128,528]{0,1:T(8,128)(2,1)S(1)}, bf16[128,528]{0,1:T(8,128)(2,1)S(1)}, u32[]{:S(2)}, u32[]{:S(2)}) collective-permute-start(bf16[128,528]{0,1:T(8,128)(2,1)S(1)} %fusion.101), channel_id=1, source_target_pairs={{0,3},{1,0},{2,1},{3,2},{4,7},{5,4},{6,5},{7,6},{8,11},{9,8},{10,9... | collective-permute-start | bytes 405512 | tf_op jit(solution)/shard_map/ppermute | solution.py:45
  42.4 5.9 %collective-permute-start.3 = (bf16[128,528]{0,1:T(8,128)(2,1)S(1)}, bf16[128,528]{0,1:T(8,128)(2,1)S(1)}, u32[]{:S(2)}, u32[]{:S(2)}) collective-permute-start(bf16[128,528]{0,1:T(8,128)(2,1)S(1)} %fusion.103), channel_id=1, source_target_pairs={{0,1},{1,2},{2,3},{3,0},{4,5},{5,6},{6,7},{7,4},{8,9},{9,10},{10,1... | collective-permute-start | bytes 405512 | tf_op jit(solution)/shard_map/ppermute | solution.py:45
  42.4 7.6 %collective-permute-start.4 = (bf16[128,528]{0,1:T(8,128)(2,1)S(1)}, bf16[128,528]{0,1:T(8,128)(2,1)S(1)}, u32[]{:S(2)}, u32[]{:S(2)}) collective-permute-start(bf16[128,528]{0,1:T(8,128)(2,1)S(1)} %fusion.102), channel_id=1, source_target_pairs={{0,2},{1,3},{2,0},{3,1},{4,6},{5,7},{6,4},{7,5},{8,10},{9,11},{10,... | collective-permute-start | bytes 405512 | tf_op jit(solution)/shard_map/ppermute | solution.py:45
  58.2 1.2 %copy-start.6 = (bf16[2,512,512]{2,1,0:T(8,128)(2,1)S(1)}, bf16[2,512,512]{2,1,0:T(8,128)(2,1)}, u32[]{:S(2)}) copy-start(bf16[2,512,512]{2,1,0:T(8,128)(2,1)} %param.21) | copy-start | bytes 3145732
  62.8 4.8 %collective-permute-start.8 = (bf16[128,520]{0,1:T(8,128)(2,1)S(1)}, bf16[128,520]{0,1:T(8,128)(2,1)S(1)}, u32[]{:S(2)}, u32[]{:S(2)}) collective-permute-start(bf16[128,520]{0,1:T(8,128)(2,1)S(1)} %fusion.105), channel_id=1, source_target_pairs={{0,3},{1,0},{2,1},{3,2},{4,7},{5,4},{6,5},{7,6},{8,11},{9,8},{10,9... | collective-permute-start | bytes 399368 | tf_op jit(solution)/shard_map/ppermute | solution.py:45
  63.9 5.8 %collective-permute-start.6 = (bf16[128,520]{0,1:T(8,128)(2,1)S(1)}, bf16[128,520]{0,1:T(8,128)(2,1)S(1)}, u32[]{:S(2)}, u32[]{:S(2)}) collective-permute-start(bf16[128,520]{0,1:T(8,128)(2,1)S(1)} %fusion.107), channel_id=1, source_target_pairs={{0,1},{1,2},{2,3},{3,0},{4,5},{5,6},{6,7},{7,4},{8,9},{9,10},{10,1... | collective-permute-start | bytes 399368 | tf_op jit(solution)/shard_map/ppermute | solution.py:45
  63.9 7.7 %collective-permute-start.7 = (bf16[128,520]{0,1:T(8,128)(2,1)S(1)}, bf16[128,520]{0,1:T(8,128)(2,1)S(1)}, u32[]{:S(2)}, u32[]{:S(2)}) collective-permute-start(bf16[128,520]{0,1:T(8,128)(2,1)S(1)} %fusion.106), channel_id=1, source_target_pairs={{0,2},{1,3},{2,0},{3,1},{4,6},{5,7},{6,4},{7,5},{8,10},{9,11},{10,... | collective-permute-start | bytes 399368 | tf_op jit(solution)/shard_map/ppermute | solution.py:45
  81.8 4.4 %collective-permute-start.9 = (bf16[128,512]{1,0:T(8,128)(2,1)S(1)}, bf16[128,512]{1,0:T(8,128)(2,1)S(1)}, u32[]{:S(2)}, u32[]{:S(2)}) collective-permute-start(bf16[128,512]{1,0:T(8,128)(2,1)S(1)} %get-tuple-element.56), channel_id=1, source_target_pairs={{0,1},{1,2},{2,3},{3,0},{4,5},{5,6},{6,7},{7,4},{8,9},{9,10},{10,1... | collective-permute-start | bytes 393224 | tf_op jit(solution)/shard_map/ppermute | solution.py:45
  82.2 5.3 %collective-permute-start.11 = (bf16[128,512]{1,0:T(8,128)(2,1)S(1)}, bf16[128,512]{1,0:T(8,128)(2,1)S(1)}, u32[]{:S(2)}, u32[]{:S(2)}) collective-permute-start(bf16[128,512]{1,0:T(8,128)(2,1)S(1)} %get-tuple-element.57), channel_id=1, source_target_pairs={{0,3},{1,0},{2,1},{3,2},{4,7},{5,4},{6,5},{7,6},{8,11},{9,8},{10,9... | collective-permute-start | bytes 393224 | tf_op jit(solution)/shard_map/ppermute | solution.py:45
  83.6 6.9 %collective-permute-start.10 = (bf16[128,512]{1,0:T(8,128)(2,1)S(1)}, bf16[128,512]{1,0:T(8,128)(2,1)S(1)}, u32[]{:S(2)}, u32[]{:S(2)}) collective-permute-start(bf16[128,512]{1,0:T(8,128)(2,1)S(1)} %get-tuple-element.58), channel_id=1, source_target_pairs={{0,2},{1,3},{2,0},{3,1},{4,6},{5,7},{6,4},{7,5},{8,10},{9,11},{10,... | collective-permute-start | bytes 393224 | tf_op jit(solution)/shard_map/ppermute | solution.py:45

commit v9 on v8

--- a/solution.py
+++ b/solution.py
@@ -129,7 +129,8 @@
     value_rows = projected[2].astype(jnp.bfloat16)
 
     key_value = jnp.stack([key_rows, value_rows]).reshape(-1, lat_rows, columns)
-    rim = jnp.stack([edges(queries.reshape(ch_local, lat_rows, columns), reach), edges(latent, reach)])
+    flat_queries = queries.reshape(ch_local, lat_rows, columns)
+    rim = jnp.stack([edges(flat_queries, reach), edges(latent, reach)]).transpose(0, 3, 2, 1)
     rim_rows = rim.size // (lat_rows * columns)
     payload = jnp.concatenate([key_value, rim.reshape(rim_rows, lat_rows, columns)], axis=0)
     strips = lax.axis_size("lon")
@@ -141,13 +142,13 @@
         got = lax.ppermute(sent, "lon", pairs)
         pieces.append(got[: key_value.shape[0]])
         if shift == 1:
-            from_left = got[key_value.shape[0] :].reshape(rim.shape)[..., reach:]
+            from_left = got[key_value.shape[0] :].reshape(rim.shape)[:, reach:].transpose(0, 3, 2, 1)
         if shift == strips - 1:
-            from_right = got[key_value.shape[0] :].reshape(rim.shape)[..., :reach]
+            from_right = got[key_value.shape[0] :].reshape(rim.shape)[:, :reach].transpose(0, 3, 2, 1)
     all_keys = jnp.stack(pieces).reshape(strips, 2, heads_local, head_size, lat_rows, columns)
-    wide_queries = jnp.concatenate(
-        [from_left[0], queries.reshape(ch_local, lat_rows, columns), from_right[0]], axis=-1
-    ).reshape(heads_local, head_size, lat_rows, -1)
+    wide_queries = jnp.concatenate([from_left[0], flat_queries, from_right[0]], axis=-1).reshape(
+        heads_local, head_size, lat_rows, -1
+    )
     wide_latent = jnp.concatenate([from_left[1], latent, from_right[1]], axis=-1)
 
     numerator, denominator = make_fold(wide_queries, (all_keys[:, 0], all_keys[:, 1]))

time: 91.8 us -> 92.8 us (1.011)
  the two profiles are of different devices: /device:TPU:16 before, /device:TPU:0 now
where the time goes in v9:
time: 92.8 us; the launch traced here: 92.5 us
  waiting for transfers between devices  37.5 us (40%)
  blocking collectives  25.1 us (27%)
  starting transfers between devices  11.8 us (13%)
  local copies, waits for them, and re-layouts  6.88 us (7%)
  matrix products  6.22 us (7%)
  other arithmetic  4.46 us (5%)
    all_gather x3, blocking collectives, gather_channels(): return lax.all_gather(values, 'lev', axis=0, tiled=True)  25.1 us
    ppermute x3, waiting for transfers between devices, per_device(): got = lax.ppermute(sent, 'lon', pairs)  22.2 us
    ppermute x9, waiting for transfers between devices, scatter_sum(): total = total + lax.ppermute(chunk, axis, pairs).astype(jnp.float32)  15.3 us
    ppermute x9, starting transfers between devices, scatter_sum(): total = total + lax.ppermute(chunk, axis, pairs).astype(jnp.float32)  7.11 us
    ppermute x3, starting transfers between devices, per_device(): got = lax.ppermute(sent, 'lon', pairs)  4.67 us
    dot_general x3, matrix products, spread_sum(): lax.dot_general(weight, activation, (((0,), (0,)), ((), ())), preferred_e...  4.42 us
    another operation x2, local copies, waits for them, and re-layouts, scatter_sum(): total = jnp.take(blocks, me, axis=0).astype(jnp.float32)  2.23 us
    unnamed x14, local copies, waits for them, and re-layouts  1.91 us
  transfers between devices with their start and end apart: 12, of which 12 were waited for; matrix products, arithmetic and copies ran while one was open for 1% of the time, Pallas kernels for 0%

profile of v9, /device:TPU:0, one launch (start us, length us, event | category | flops | bytes accessed | tf_op | source)
XLA Modules:
  0.0 92.5 jit_solution(4037177854688358332)
XLA Ops:
  0.0 8.9 %all_gather.9 = bf16[512,4,128]{2,1,0:T(4,128)(2,1)S(1)} all-gather(bf16[128,4,128]{2,1,0:T(4,128)(2,1)} %param.14), channel_id=1, replica_groups=mesh['member'=2,'lon'=4,'lev'=4] {'lev'}, dimensions={0}, use_global_device_ids=true | all-gather | bytes 655360 | tf_op jit(solution)/shard_map/all_gather | solution.py:34
  9.0 1.0 %copy.89 = bf16[128,4,128]{0,2,1:T(8,128)(2,1)S(1)} copy(bf16[128,4,128]{2,1,0:T(4,128)(2,1)} %param.14) | data formatting | bytes 262144 | tf_op args[0]
  10.0 0.5 fusion.17
  10.6 1.5 %fusion.44 = bf16[512,4,128,1]{2,1,0,3:T(4,128)(2,1)S(1)} fusion(bf16[512,4,128]{2,1,0:T(4,128)(2,1)S(1)} %all_gather.9, f32[512]{0:T(512)S(1)} %copy-done.4, f32[4,128]{1,0:T(4,128)S(1)} %add_rsqrt_fusion.2), kind=kLoop, calls=%fused_computation.66 | loop fusion | flops 1048576 | bytes 1052672 | tf_op jit(solution)/shard_map/convert_element_type | solution.py:124
  12.1 0.4 convolution_bitcast_fusion.2
  12.7 0.1 fusion.124
  12.8 0.1 copy.87
  12.9 0.1 copy.88
  13.2 0.1 fusion.121
  13.4 1.6 %collective-permute-start = (bf16[264,4,128]{2,0,1:T(8,128)(2,1)S(1)}, bf16[264,4,128]{2,0,1:T(8,128)(2,1)S(1)}, u32[]{:S(2)}, u32[]{:S(2)}) collective-permute-start(bf16[264,4,128]{2,0,1:T(8,128)(2,1)S(1)} %pad_maximum_fusion.1), channel_id=1, source_target_pairs={{0,4},{4,8},{8,12},{12,0},{1,5},{5,9},{9,13},{13,1},{2,6},{6,10},{... | collective-permute-start | bytes 811016 | tf_op jit(solution)/shard_map/ppermute | solution.py:142
  15.0 2.2 %collective-permute-start.1 = (bf16[264,4,128]{2,0,1:T(8,128)(2,1)S(1)}, bf16[264,4,128]{2,0,1:T(8,128)(2,1)S(1)}, u32[]{:S(2)}, u32[]{:S(2)}) collective-permute-start(bf16[264,4,128]{2,0,1:T(8,128)(2,1)S(1)} %pad_maximum_fusion.1), channel_id=1, source_target_pairs={{0,12},{4,0},{8,4},{12,8},{1,13},{5,1},{9,5},{13,9},{2,14},{6,2},{... | collective-permute-start | bytes 811016 | tf_op jit(solution)/shard_map/ppermute | solution.py:142
  17.2 0.8 collective-permute-start.2
  18.1 0.1 broadcast_multiply_fusion.5
  18.2 6.3 %collective-permute-done = bf16[264,4,128]{2,0,1:T(8,128)(2,1)S(1)} collective-permute-done((bf16[264,4,128]{2,0,1:T(8,128)(2,1)S(1)}, bf16[264,4,128]{2,0,1:T(8,128)(2,1)S(1)}, u32[]{:S(2)}, u32[]{:S(2)}) %collective-permute-start) | collective-permute-done | bytes 270368 | tf_op jit(solution)/shard_map/ppermute | solution.py:142
  24.6 4.7 %collective-permute-done.1 = bf16[264,4,128]{2,0,1:T(8,128)(2,1)S(1)} collective-permute-done((bf16[264,4,128]{2,0,1:T(8,128)(2,1)S(1)}, bf16[264,4,128]{2,0,1:T(8,128)(2,1)S(1)}, u32[]{:S(2)}, u32[]{:S(2)}) %collective-permute-start.1) | collective-permute-done | bytes 270368 | tf_op jit(solution)/shard_map/ppermute | solution.py:142
  29.3 0.1 concatenate.25
  29.4 0.2 copy.97
  29.5 0.1 concatenate.26
  29.6 0.2 copy.98
  29.8 11.2 %collective-permute-done.2 = bf16[256,4,128]{2,0,1:T(8,128)(2,1)S(1)} collective-permute-done((bf16[256,4,128]{2,0,1:T(8,128)(2,1)S(1)}, bf16[256,4,128]{2,0,1:T(8,128)(2,1)S(1)}, u32[]{:S(2)}, u32[]{:S(2)}) %collective-permute-start.2) | collective-permute-done | bytes 262176 | tf_op jit(solution)/shard_map/ppermute | solution.py:142
  41.1 0.1 pad_maximum_fusion
  41.1 0.9 fusion
  42.1 0.5 fusion.37
  42.6 0.3 copy.99
  42.8 0.2 reshape.598
  43.0 0.3 fusion.2
  43.3 0.1 reshape.599
  43.4 1.1 %constant_dynamic-slice_fusion.7 = (bf16[1,128,528]{1,0,2:T(2,128)(2,1)S(1)}, bf16[1,128,528]{1,0,2:T(2,128)(2,1)S(1)}, bf16[1,128,528]{1,0,2:T(2,128)(2,1)S(1)}, bf16[1,128,528]{1,0,2:T(2,128)(2,1)S(1)}) fusion(bf16[4,128,528]{1,0,2:T(4,128)(2,1)S(1)} %reshape.599, s32[]{:T(128)S(6)} %select_n.78, s32[]{:T(128)S(6)} %select_n.82, s32[]{:T(128)S(6)} %select_n.80, ...), kind=kLoop, calls=%fused_computation.177 | loop fusion | bytes 1081360 | tf_op jit(solution)/shard_map/jit(_take) | solution.py:41
  44.7 1.2 %collective-permute-start.4 = (bf16[128,528]{0,1:T(8,128)(2,1)S(1)}, bf16[128,528]{0,1:T(8,128)(2,1)S(1)}, u32[]{:S(2)}, u32[]{:S(2)}) collective-permute-start(bf16[128,528]{0,1:T(8,128)(2,1)S(1)} %fusion.102), channel_id=1, source_target_pairs={{0,2},{1,3},{2,0},{3,1},{4,6},{5,7},{6,4},{7,5},{8,10},{9,11},{10,... | collective-permute-start | bytes 405512 | tf_op jit(solution)/shard_map/ppermute | solution.py:45
  45.9 1.5 %collective-permute-start.5 = (bf16[128,528]{0,1:T(8,128)(2,1)S(1)}, bf16[128,528]{0,1:T(8,128)(2,1)S(1)}, u32[]{:S(2)}, u32[]{:S(2)}) collective-permute-start(bf16[128,528]{0,1:T(8,128)(2,1)S(1)} %fusion.101), channel_id=1, source_target_pairs={{0,3},{1,0},{2,1},{3,2},{4,7},{5,4},{6,5},{7,6},{8,11},{9,8},{10,9... | collective-permute-start | bytes 405512 | tf_op jit(solution)/shard_map/ppermute | solution.py:45
  47.4 2.5 %collective-permute-done.3 = bf16[128,528]{0,1:T(8,128)(2,1)S(1)} collective-permute-done((bf16[128,528]{0,1:T(8,128)(2,1)S(1)}, bf16[128,528]{0,1:T(8,128)(2,1)S(1)}, u32[]{:S(2)}, u32[]{:S(2)}) %collective-permute-start.3) | collective-permute-done | bytes 135200 | tf_op jit(solution)/shard_map/ppermute | solution.py:45
  49.9 1.3 %collective-permute-done.4 = bf16[128,528]{0,1:T(8,128)(2,1)S(1)} collective-permute-done((bf16[128,528]{0,1:T(8,128)(2,1)S(1)}, bf16[128,528]{0,1:T(8,128)(2,1)S(1)}, u32[]{:S(2)}, u32[]{:S(2)}) %collective-permute-start.4) | collective-permute-done | bytes 135200 | tf_op jit(solution)/shard_map/ppermute | solution.py:45
  51.2 0.9 collective-permute-done.5
  52.1 0.1 convert_add_fusion
  52.2 0.2 fusion.73
  52.4 8.3 %all_gather.10 = bf16[512,4,130]{0,2,1:T(8,128)(2,1)S(1)} all-gather(bf16[128,4,130]{0,2,1:T(8,128)(2,1)S(1)} %fusion.73), channel_id=1, replica_groups=mesh['member'=2,'lon'=4,'lev'=4] {'lev'}, dimensions={0}, use_global_device_ids=true | all-gather | bytes 665600 | tf_op jit(solution)/shard_map/all_gather | solution.py:34
  60.8 0.2 fusion.4
  61.0 0.2 fusion.6
  61.2 0.1 reshape.601
  61.4 0.8 copy-done.5
  62.2 2.0 %fusion.3 = bf16[512,520]{0,1:T(8,128)(2,1)S(1)} fusion(bf16[512,520]{0,1:T(8,128)(2,1)S(1)} %reshape.601, bf16[2,512,512]{2,1,0:T(8,128)(2,1)S(1)} %copy-done.5, bf16[2,512,512]{2,1,0:T(8,128)(2,1)} %param.20), kind=kOutput, calls=%fused_computation.18 | convolution fusion | flops 547921920 | bytes 2113536 | tf_op jit(solution)/shard_map/dot_general | solution.py:50
  64.3 0.1 reshape.602
  64.4 1.1 %constant_dynamic-slice_fusion.2 = (bf16[1,128,520]{1,0,2:T(2,128)(2,1)S(1)}, bf16[1,128,520]{1,0,2:T(2,128)(2,1)S(1)}, bf16[1,128,520]{1,0,2:T(2,128)(2,1)S(1)}, bf16[1,128,520]{1,0,2:T(2,128)(2,1)S(1)}) fusion(bf16[4,128,520]{1,0,2:T(4,128)(2,1)S(1)} %reshape.602, s32[]{:T(128)S(6)} %select_n.78, s32[]{:T(128)S(6)} %select_n.82, s32[]{:T(128)S(6)} %select_n.80, ...), kind=kLoop, calls=%fused_computation.172 | loop fusion | bytes 1064976 | tf_op jit(solution)/shard_map/jit(_take) | solution.py:41
  65.5 0.4 collective-permute-start.6
  66.0 0.9 collective-permute-start.7
  66.9 1.2 %collective-permute-start.8 = (bf16[128,520]{0,1:T(8,128)(2,1)S(1)}, bf16[128,520]{0,1:T(8,128)(2,1)S(1)}, u32[]{:S(2)}, u32[]{:S(2)}) collective-permute-start(bf16[128,520]{0,1:T(8,128)(2,1)S(1)} %fusion.105), channel_id=1, source_target_pairs={{0,3},{1,0},{2,1},{3,2},{4,7},{5,4},{6,5},{7,6},{8,11},{9,8},{10,9... | collective-permute-start | bytes 399368 | tf_op jit(solution)/shard_map/ppermute | solution.py:45
  68.0 2.4 %collective-permute-done.6 = bf16[128,520]{0,1:T(8,128)(2,1)S(1)} collective-permute-done((bf16[128,520]{0,1:T(8,128)(2,1)S(1)}, bf16[128,520]{0,1:T(8,128)(2,1)S(1)}, u32[]{:S(2)}, u32[]{:S(2)}) %collective-permute-start.6) | collective-permute-done | bytes 133152 | tf_op jit(solution)/shard_map/ppermute | solution.py:45
  70.4 2.0 %collective-permute-done.7 = bf16[128,520]{0,1:T(8,128)(2,1)S(1)} collective-permute-done((bf16[128,520]{0,1:T(8,128)(2,1)S(1)}, bf16[128,520]{0,1:T(8,128)(2,1)S(1)}, u32[]{:S(2)}, u32[]{:S(2)}) %collective-permute-start.7) | collective-permute-done | bytes 133152 | tf_op jit(solution)/shard_map/ppermute | solution.py:45
  72.4 0.1 collective-permute-done.8
  72.6 0.1 convert_add_fusion.1
  72.8 0.2 fusion.88
  72.9 7.9 %all_gather.11 = bf16[512,4,128]{0,2,1:T(8,128)(2,1)S(1)} all-gather(bf16[128,4,128]{0,2,1:T(8,128)(2,1)S(1)} %fusion.88), channel_id=1, replica_groups=mesh['member'=2,'lon'=4,'lev'=4] {'lev'}, dimensions={0}, use_global_device_ids=true | all-gather | bytes 655360 | tf_op jit(solution)/shard_map/all_gather | solution.py:34
  80.8 0.2 fusion.20
  81.0 0.2 fusion.22
  81.2 2.1 %convolution_convert_fusion.2 = bf16[512,512]{0,1:T(8,128)(2,1)S(1)} fusion(bf16[512,512]{0,1:T(8,128)(2,1)S(1)} %bitcast.202, bf16[2,512,512]{2,1,0:T(8,128)(2,1)S(1)} %copy-done.5, bf16[2,512,512]{2,1,0:T(8,128)(2,1)} %param.20), kind=kOutput, calls=%fused_computation.15 | convolution fusion | flops 539492352 | bytes 2097152 | tf_op jit(solution)/shard_map/dot_general | solution.py:50
  83.4 1.5 %collective-permute-start.10 = (bf16[128,512]{1,0:T(8,128)(2,1)S(1)}, bf16[128,512]{1,0:T(8,128)(2,1)S(1)}, u32[]{:S(2)}, u32[]{:S(2)}) collective-permute-start(bf16[128,512]{1,0:T(8,128)(2,1)S(1)} %get-tuple-element.58), channel_id=1, source_target_pairs={{0,2},{1,3},{2,0},{3,1},{4,6},{5,7},{6,4},{7,5},{8,10},{9,11},{10,... | collective-permute-start | bytes 393224 | tf_op jit(solution)/shard_map/ppermute | solution.py:45
  84.8 0.3 collective-permute-start.11
  85.2 0.2 collective-permute-start.9
  85.3 4.4 %collective-permute-done.10 = bf16[128,512]{1,0:T(8,128)(2,1)S(1)} collective-permute-done((bf16[128,512]{1,0:T(8,128)(2,1)S(1)}, bf16[128,512]{1,0:T(8,128)(2,1)S(1)}, u32[]{:S(2)}, u32[]{:S(2)}) %collective-permute-start.10) | collective-permute-done | bytes 131104 | tf_op jit(solution)/shard_map/ppermute | solution.py:45
  89.8 1.2 %collective-permute-done.11 = bf16[128,512]{1,0:T(8,128)(2,1)S(1)} collective-permute-done((bf16[128,512]{1,0:T(8,128)(2,1)S(1)}, bf16[128,512]{1,0:T(8,128)(2,1)S(1)}, u32[]{:S(2)}, u32[]{:S(2)}) %collective-permute-start.11) | collective-permute-done | bytes 131104 | tf_op jit(solution)/shard_map/ppermute | solution.py:45
  90.9 0.5 collective-permute-done.9
  91.4 0.1 convert_add_fusion.2
  91.5 0.1 copy.108
  91.7 0.8 copy.109
  (54 shorter events, 1.0 us)
Async XLA Ops:
  0.0 12.1 %copy-start = (bf16[3,128,512]{2,1,0:T(8,128)(2,1)S(1)}, bf16[3,128,512]{2,1,0:T(8,128)(2,1)}, u32[]{:S(2)}) copy-start(bf16[3,128,512]{2,1,0:T(8,128)(2,1)} %param.16) | copy-start | bytes 1179652
  0.0 10.5 %copy-start.4 = (f32[512]{0:T(512)S(1)}, f32[512]{0:T(512)}, u32[]{:S(2)}) copy-start(f32[512]{0:T(512)} %param.15) | copy-start | bytes 6148
  13.2 4.9 %copy-start.2 = (f32[2,9,128]{2,0,1:T(2,128)S(1)}, f32[2,9,128]{2,0,1:T(2,128)}, u32[]{:S(2)}) copy-start(f32[2,9,128]{2,0,1:T(2,128)} %param.18) | copy-start | bytes 27652
  13.4 11.2 %collective-permute-start = (bf16[264,4,128]{2,0,1:T(8,128)(2,1)S(1)}, bf16[264,4,128]{2,0,1:T(8,128)(2,1)S(1)}, u32[]{:S(2)}, u32[]{:S(2)}) collective-permute-start(bf16[264,4,128]{2,0,1:T(8,128)(2,1)S(1)} %pad_maximum_fusion.1), channel_id=1, source_target_pairs={{0,4},{4,8},{8,12},{12,0},{1,5},{5,9},{9,13},{13,1},{2,6},{6,10},{... | collective-permute-start | bytes 811016 | tf_op jit(solution)/shard_map/ppermute | solution.py:142
  15.0 14.2 %collective-permute-start.1 = (bf16[264,4,128]{2,0,1:T(8,128)(2,1)S(1)}, bf16[264,4,128]{2,0,1:T(8,128)(2,1)S(1)}, u32[]{:S(2)}, u32[]{:S(2)}) collective-permute-start(bf16[264,4,128]{2,0,1:T(8,128)(2,1)S(1)} %pad_maximum_fusion.1), channel_id=1, source_target_pairs={{0,12},{4,0},{8,4},{12,8},{1,13},{5,1},{9,5},{13,9},{2,14},{6,2},{... | collective-permute-start | bytes 811016 | tf_op jit(solution)/shard_map/ppermute | solution.py:142
  17.2 23.8 %collective-permute-start.2 = (bf16[256,4,128]{2,0,1:T(8,128)(2,1)S(1)}, bf16[256,4,128]{2,0,1:T(8,128)(2,1)S(1)}, u32[]{:S(2)}, u32[]{:S(2)}) collective-permute-start(bf16[256,4,128]{2,0,1:T(8,128)(2,1)S(1)} %bitcast.196), channel_id=1, source_target_pairs={{0,8},{4,12},{8,0},{12,4},{1,9},{5,13},{9,1},{13,5},{2,10},{6,14},... | collective-permute-start | bytes 786440 | tf_op jit(solution)/shard_map/ppermute | solution.py:142
  42.0 1.0 %copy-start.1 = (bf16[128,512]{1,0:T(8,128)(2,1)S(1)}, bf16[128,512]{1,0:T(8,128)(2,1)}, u32[]{:S(2)}) copy-start(bf16[128,512]{1,0:T(8,128)(2,1)} %param.17) | copy-start | bytes 393220
  44.6 2.8 %copy-start.3 = (f32[2,512]{1,0:T(2,128)S(1)}, f32[2,512]{1,0:T(2,128)}, u32[]{:S(2)}) copy-start(f32[2,512]{1,0:T(2,128)} %param.19) | copy-start | bytes 12292
  44.6 5.3 %collective-permute-start.3 = (bf16[128,528]{0,1:T(8,128)(2,1)S(1)}, bf16[128,528]{0,1:T(8,128)(2,1)S(1)}, u32[]{:S(2)}, u32[]{:S(2)}) collective-permute-start(bf16[128,528]{0,1:T(8,128)(2,1)S(1)} %fusion.103), channel_id=1, source_target_pairs={{0,1},{1,2},{2,3},{3,0},{4,5},{5,6},{6,7},{7,4},{8,9},{9,10},{10,1... | collective-permute-start | bytes 405512 | tf_op jit(solution)/shard_map/ppermute | solution.py:45
  44.7 6.5 %collective-permute-start.4 = (bf16[128,528]{0,1:T(8,128)(2,1)S(1)}, bf16[128,528]{0,1:T(8,128)(2,1)S(1)}, u32[]{:S(2)}, u32[]{:S(2)}) collective-permute-start(bf16[128,528]{0,1:T(8,128)(2,1)S(1)} %fusion.102), channel_id=1, source_target_pairs={{0,2},{1,3},{2,0},{3,1},{4,6},{5,7},{6,4},{7,5},{8,10},{9,11},{10,... | collective-permute-start | bytes 405512 | tf_op jit(solution)/shard_map/ppermute | solution.py:45
  45.9 6.2 %collective-permute-start.5 = (bf16[128,528]{0,1:T(8,128)(2,1)S(1)}, bf16[128,528]{0,1:T(8,128)(2,1)S(1)}, u32[]{:S(2)}, u32[]{:S(2)}) collective-permute-start(bf16[128,528]{0,1:T(8,128)(2,1)S(1)} %fusion.101), channel_id=1, source_target_pairs={{0,3},{1,0},{2,1},{3,2},{4,7},{5,4},{6,5},{7,6},{8,11},{9,8},{10,9... | collective-permute-start | bytes 405512 | tf_op jit(solution)/shard_map/ppermute | solution.py:45
  61.0 1.2 %copy-start.5 = (bf16[2,512,512]{2,1,0:T(8,128)(2,1)S(1)}, bf16[2,512,512]{2,1,0:T(8,128)(2,1)}, u32[]{:S(2)}) copy-start(bf16[2,512,512]{2,1,0:T(8,128)(2,1)} %param.21) | copy-start | bytes 3145732
  65.5 4.9 %collective-permute-start.6 = (bf16[128,520]{0,1:T(8,128)(2,1)S(1)}, bf16[128,520]{0,1:T(8,128)(2,1)S(1)}, u32[]{:S(2)}, u32[]{:S(2)}) collective-permute-start(bf16[128,520]{0,1:T(8,128)(2,1)S(1)} %fusion.107), channel_id=1, source_target_pairs={{0,1},{1,2},{2,3},{3,0},{4,5},{5,6},{6,7},{7,4},{8,9},{9,10},{10,1... | collective-permute-start | bytes 399368 | tf_op jit(solution)/shard_map/ppermute | solution.py:45
  66.0 6.5 %collective-permute-start.7 = (bf16[128,520]{0,1:T(8,128)(2,1)S(1)}, bf16[128,520]{0,1:T(8,128)(2,1)S(1)}, u32[]{:S(2)}, u32[]{:S(2)}) collective-permute-start(bf16[128,520]{0,1:T(8,128)(2,1)S(1)} %fusion.106), channel_id=1, source_target_pairs={{0,2},{1,3},{2,0},{3,1},{4,6},{5,7},{6,4},{7,5},{8,10},{9,11},{10,... | collective-permute-start | bytes 399368 | tf_op jit(solution)/shard_map/ppermute | solution.py:45
  66.9 5.7 %collective-permute-start.8 = (bf16[128,520]{0,1:T(8,128)(2,1)S(1)}, bf16[128,520]{0,1:T(8,128)(2,1)S(1)}, u32[]{:S(2)}, u32[]{:S(2)}) collective-permute-start(bf16[128,520]{0,1:T(8,128)(2,1)S(1)} %fusion.105), channel_id=1, source_target_pairs={{0,3},{1,0},{2,1},{3,2},{4,7},{5,4},{6,5},{7,6},{8,11},{9,8},{10,9... | collective-permute-start | bytes 399368 | tf_op jit(solution)/shard_map/ppermute | solution.py:45
  83.4 6.4 %collective-permute-start.10 = (bf16[128,512]{1,0:T(8,128)(2,1)S(1)}, bf16[128,512]{1,0:T(8,128)(2,1)S(1)}, u32[]{:S(2)}, u32[]{:S(2)}) collective-permute-start(bf16[128,512]{1,0:T(8,128)(2,1)S(1)} %get-tuple-element.58), channel_id=1, source_target_pairs={{0,2},{1,3},{2,0},{3,1},{4,6},{5,7},{6,4},{7,5},{8,10},{9,11},{10,... | collective-permute-start | bytes 393224 | tf_op jit(solution)/shard_map/ppermute | solution.py:45
  84.8 6.1 %collective-permute-start.11 = (bf16[128,512]{1,0:T(8,128)(2,1)S(1)}, bf16[128,512]{1,0:T(8,128)(2,1)S(1)}, u32[]{:S(2)}, u32[]{:S(2)}) collective-permute-start(bf16[128,512]{1,0:T(8,128)(2,1)S(1)} %get-tuple-element.57), channel_id=1, source_target_pairs={{0,3},{1,0},{2,1},{3,2},{4,7},{5,4},{6,5},{7,6},{8,11},{9,8},{10,9... | collective-permute-start | bytes 393224 | tf_op jit(solution)/shard_map/ppermute | solution.py:45
  85.2 6.3 %collective-permute-start.9 = (bf16[128,512]{1,0:T(8,128)(2,1)S(1)}, bf16[128,512]{1,0:T(8,128)(2,1)S(1)}, u32[]{:S(2)}, u32[]{:S(2)}) collective-permute-start(bf16[128,512]{1,0:T(8,128)(2,1)S(1)} %get-tuple-element.56), channel_id=1, source_target_pairs={{0,1},{1,2},{2,3},{3,0},{4,5},{5,6},{6,7},{7,4},{8,9},{9,10},{10,1... | collective-permute-start | bytes 393224 | tf_op jit(solution)/shard_map/ppermute | solution.py:45

commit v10 on v8

--- a/solution.py
+++ b/solution.py
@@ -37,12 +37,17 @@
 def scatter_sum(partial, axis):
     devices = lax.axis_size(axis)
     me = lax.axis_index(axis)
-    blocks = partial.reshape(devices, -1, *partial.shape[1:])
-    total = jnp.take(blocks, me, axis=0).astype(jnp.float32)
-    for shift in range(1, devices):
-        pairs = [(i, (i + shift) % devices) for i in range(devices)]
-        chunk = jnp.take(blocks, (me + shift) % devices, axis=0)
-        total = total + lax.ppermute(chunk, axis, pairs).astype(jnp.float32)
+    chips, core = devices // 2, me % 2
+    chip = me // 2
+    blocks = partial.reshape(chips, 2, -1, *partial.shape[1:])
+    mine = jnp.take(blocks, core, axis=1).astype(jnp.float32)
+    theirs = jnp.take(blocks, 1 - core, axis=1)
+    pair = mine + lax.ppermute(theirs, axis, [(i, i ^ 1) for i in range(devices)]).astype(jnp.float32)
+    total = jnp.take(pair, chip, axis=0)
+    for shift in range(1, chips):
+        pairs = [(i, ((i // 2 + shift) % chips) * 2 + i % 2) for i in range(devices)]
+        sent = jnp.take(pair, (chip + shift) % chips, axis=0).astype(jnp.bfloat16)
+        total = total + lax.ppermute(sent, axis, pairs).astype(jnp.float32)
     return total
 
 

time: 91.8 us -> 86.7 us (0.944)
  starting transfers between devices: 9.74 us -> 7.18 us
  waiting for transfers between devices: 40.2 us -> 39 us
    ppermute x9 -> x6, starting transfers between devices: 6.89 us -> 4.28 us  [the longest x3 3.33 us: scatter_sum(): total = total + lax.ppermute(sent, axis, pairs).astype(jnp.float32)]
    ppermute x9 -> x6, waiting for transfers between devices: 18.8 us -> 17.5 us  [the longest x3 13.8 us: scatter_sum(): total = total + lax.ppermute(sent, axis, pairs).astype(jnp.float32)]
  transfers between devices with their start and end apart: 12 -> 9, of which waited for: 11 -> 8; matrix products, arithmetic and copies ran while one was open for 3% -> 4% of each run, Pallas kernels for 0% -> 0%
where the time goes in v10:
time: 86.7 us; the launch traced here: 86.4 us
  waiting for transfers between devices  39 us (45%)
  blocking collectives  21.5 us (25%)
  local copies, waits for them, and re-layouts  7.18 us (8%)
  starting transfers between devices  7.18 us (8%)
  matrix products  6.37 us (7%)
  other arithmetic  4.59 us (5%)
    ppermute x3, waiting for transfers between devices, per_device(): got = lax.ppermute(sent, 'lon', pairs)  21.5 us
    all_gather x3, blocking collectives, gather_channels(): return lax.all_gather(values, 'lev', axis=0, tiled=True)  21.5 us
    ppermute x3, waiting for transfers between devices, scatter_sum(): total = total + lax.ppermute(sent, axis, pairs).astype(jnp.float32)  13.8 us
    dot_general x3, matrix products, spread_sum(): lax.dot_general(weight, activation, (((0,), (0,)), ((), ())), preferred_e...  4.58 us
    ppermute x3, waiting for transfers between devices, scatter_sum(): lax.ppermute(theirs, axis, [(i, i ^ 1) for i in range(devices)])  3.68 us
    ppermute x3, starting transfers between devices, scatter_sum(): total = total + lax.ppermute(sent, axis, pairs).astype(jnp.float32)  3.33 us
    ppermute x3, starting transfers between devices, per_device(): got = lax.ppermute(sent, 'lon', pairs)  2.9 us
    another operation x2, local copies, waits for them, and re-layouts, scatter_sum(): mine = jnp.take(blocks, core, axis=1).astype(jnp.float32)  2.23 us
  transfers between devices with their start and end apart: 9, of which 8 were waited for; matrix products, arithmetic and copies ran while one was open for 4% of the time, Pallas kernels for 0%

profile of v10, /device:TPU:16, one launch (start us, length us, event | category | flops | bytes accessed | tf_op | source)
XLA Modules:
  0.0 86.4 jit_solution(8553692904996933168)
XLA Ops:
  0.0 7.5 %all_gather.9 = bf16[512,4,128]{2,1,0:T(4,128)(2,1)S(1)} all-gather(bf16[128,4,128]{2,1,0:T(4,128)(2,1)} %param.20), channel_id=1, replica_groups=mesh['member'=2,'lon'=4,'lev'=4] {'lev'}, dimensions={0}, use_global_device_ids=true | all-gather | bytes 655360 | tf_op jit(solution)/shard_map/all_gather | solution.py:34
  7.5 0.5 fusion.17
  8.1 1.5 %fusion.44 = bf16[512,4,128,1]{2,1,0,3:T(4,128)(2,1)S(1)} fusion(bf16[512,4,128]{2,1,0:T(4,128)(2,1)S(1)} %all_gather.9, f32[512]{0:T(512)S(1)} %copy-done.5, f32[4,128]{1,0:T(4,128)S(1)} %add_rsqrt_fusion.2), kind=kLoop, calls=%fused_computation.68 | loop fusion | flops 1048576 | bytes 1052672 | tf_op jit(solution)/shard_map/convert_element_type | solution.py:129
  9.6 0.4 convolution_bitcast_fusion.2
  10.0 0.1 slice_multiply_fusion.6
  10.2 0.1 fusion.118
  10.3 0.4 collective-permute-start.2
  10.7 0.3 copy-done.1
  11.0 0.1 copy.96
  11.3 0.1 fusion.121
  11.4 0.1 copy.94
  11.5 0.1 copy.95
  11.7 0.2 copy.98
  11.9 0.3 reshape.599
  12.3 2.5 %collective-permute-start.1 = (bf16[264,4,128]{2,0,1:T(8,128)(2,1)S(1)}, bf16[264,4,128]{2,0,1:T(8,128)(2,1)S(1)}, u32[]{:S(2)}, u32[]{:S(2)}) collective-permute-start(bf16[264,4,128]{2,0,1:T(8,128)(2,1)S(1)} %pad_maximum_fusion.1), channel_id=1, source_target_pairs={{0,12},{4,0},{8,4},{12,8},{1,13},{5,1},{9,5},{13,9},{2,14},{6,2},{... | collective-permute-start | bytes 811016 | tf_op jit(solution)/shard_map/ppermute | solution.py:146
  14.9 19.2 %collective-permute-done.1 = bf16[264,4,128]{2,0,1:T(8,128)(2,1)S(1)} collective-permute-done((bf16[264,4,128]{2,0,1:T(8,128)(2,1)S(1)}, bf16[264,4,128]{2,0,1:T(8,128)(2,1)S(1)}, u32[]{:S(2)}, u32[]{:S(2)}) %collective-permute-start.1) | collective-permute-done | bytes 270368 | tf_op jit(solution)/shard_map/ppermute | solution.py:146
  34.1 0.6 reshape.601
  34.7 0.1 slice_bitcast_fusion.4
  34.8 2.3 %collective-permute-done = bf16[264,4,128]{2,0,1:T(8,128)(2,1)S(1)} collective-permute-done((bf16[264,4,128]{2,0,1:T(8,128)(2,1)S(1)}, bf16[264,4,128]{2,0,1:T(8,128)(2,1)S(1)}, u32[]{:S(2)}, u32[]{:S(2)}) %collective-permute-start) | collective-permute-done | bytes 270368 | tf_op jit(solution)/shard_map/ppermute | solution.py:146
  37.1 0.6 reshape.600
  37.7 0.2 slice_bitcast_fusion.5
  38.0 0.1 pad_maximum_fusion
  38.1 0.9 %fusion = (f32[2,4,132]{2,1,0:T(4,128)S(1)}, f32[2,4,132,4,128]{4,2,3,1,0:T(8,128)S(1)}) fusion(bf16[4,2,2,64,4,128]{5,3,0,4,2,1:T(8,128)(2,1)S(1)} %pad_maximum_fusion, bf16[2,64,4,2]{3,1,2,0:T(8,128)(2,1)S(1)} %copy.112, bf16[2,64,4,128]{3,1,2,0:T(8,128)(2,1)S(1)} %fusion.104, bf16[2,64,4,2]{3,1,2,0:T(8,128)(2,1)S(1)} %copy.111), kind=kOutput, calls=%fused_computation.1 | convolution fusion | flops 70691808 | bytes 3084416 | tf_op jit(solution)/shard_map/hdri,phdrj->hripj/dot_general | solution.py:73
  39.0 0.5 fusion.37
  39.5 0.3 copy.113
  39.8 0.2 reshape.602
  40.0 0.3 fusion.2
  40.3 0.1 reshape.603
  40.4 1.1 %constant_dynamic-slice_fusion.3 = (bf16[2,1,128,528]{2,1,0,3:T(2,128)(2,1)S(1)}, bf16[2,1,128,528]{2,1,0,3:T(2,128)(2,1)S(1)}) fusion(bf16[2,2,128,528]{2,1,0,3:T(2,128)(2,1)S(1)} %reshape.603, s32[]{:T(128)S(6)} %select_n.94, s32[]{:T(128)S(6)} %select_n.96), kind=kLoop, calls=%fused_computation.171 | loop fusion | bytes 1081352 | tf_op jit(solution)/shard_map/jit(_take) | solution.py:43
  41.6 0.1 collective-permute-start.3
  41.8 0.1 broadcast_multiply_fusion.5
  41.9 1.3 %collective-permute-done.3 = bf16[2,128,528]{1,2,0:T(8,128)(2,1)S(1)} collective-permute-done((bf16[2,128,528]{1,2,0:T(8,128)(2,1)S(1)}, bf16[2,128,528]{1,2,0:T(8,128)(2,1)S(1)}, u32[]{:S(2)}, u32[]{:S(2)}) %collective-permute-start.3) | collective-permute-done | bytes 270368 | tf_op jit(solution)/shard_map/ppermute | solution.py:45
  43.2 0.1 convert_add_fusion
  43.3 1.2 %collective-permute-start.4 = (bf16[128,528]{0,1:T(8,128)(2,1)S(1)}, bf16[128,528]{0,1:T(8,128)(2,1)S(1)}, u32[]{:S(2)}, u32[]{:S(2)}) collective-permute-start(bf16[128,528]{0,1:T(8,128)(2,1)S(1)} %bitcast_convert_fusion), channel_id=1, source_target_pairs={{0,2},{1,3},{2,0},{3,1},{4,6},{5,7},{6,4},{7,5},{8,10},{9,11},{10,... | collective-permute-start | bytes 405512 | tf_op jit(solution)/shard_map/ppermute | solution.py:50
  44.5 0.1 copy.104
  44.6 0.1 copy.102
  44.8 4.3 %collective-permute-done.4 = bf16[128,528]{0,1:T(8,128)(2,1)S(1)} collective-permute-done((bf16[128,528]{0,1:T(8,128)(2,1)S(1)}, bf16[128,528]{0,1:T(8,128)(2,1)S(1)}, u32[]{:S(2)}, u32[]{:S(2)}) %collective-permute-start.4) | collective-permute-done | bytes 135200 | tf_op jit(solution)/shard_map/ppermute | solution.py:50
  49.1 0.1 fusion.120
  49.1 0.2 fusion.73
  49.3 7.2 %all_gather.10 = bf16[512,4,130]{0,2,1:T(8,128)(2,1)S(1)} all-gather(bf16[128,4,130]{0,2,1:T(8,128)(2,1)S(1)} %fusion.73), channel_id=1, replica_groups=mesh['member'=2,'lon'=4,'lev'=4] {'lev'}, dimensions={0}, use_global_device_ids=true | all-gather | bytes 665600 | tf_op jit(solution)/shard_map/all_gather | solution.py:34
  56.5 0.2 fusion.4
  56.8 0.2 fusion.6
  57.0 0.1 reshape.605
  57.1 2.2 %fusion.3 = bf16[512,520]{0,1:T(8,128)(2,1)S(1)} fusion(bf16[512,520]{0,1:T(8,128)(2,1)S(1)} %reshape.605, bf16[2,512,512]{2,1,0:T(8,128)(2,1)} %param.27, bf16[2,512,512]{2,1,0:T(8,128)(2,1)} %param.26), kind=kOutput, calls=%fused_computation.18 | convolution fusion | flops 547921920 | bytes 2113536 | tf_op jit(solution)/shard_map/dot_general | solution.py:55
  59.3 0.1 reshape.606
  59.4 1.1 %constant_dynamic-slice_fusion.1 = (bf16[2,1,128,520]{2,1,0,3:T(2,128)(2,1)S(1)}, bf16[2,1,128,520]{2,1,0,3:T(2,128)(2,1)S(1)}) fusion(bf16[2,2,128,520]{2,1,0,3:T(2,128)(2,1)S(1)} %reshape.606, s32[]{:T(128)S(6)} %select_n.94, s32[]{:T(128)S(6)} %select_n.96), kind=kLoop, calls=%fused_computation.169 | loop fusion | bytes 1064968 | tf_op jit(solution)/shard_map/jit(_take) | solution.py:43
  60.6 0.4 collective-permute-start.5
  61.0 1.2 %collective-permute-done.5 = bf16[2,128,520]{1,2,0:T(8,128)(2,1)S(1)} collective-permute-done((bf16[2,128,520]{1,2,0:T(8,128)(2,1)S(1)}, bf16[2,128,520]{1,2,0:T(8,128)(2,1)S(1)}, u32[]{:S(2)}, u32[]{:S(2)}) %collective-permute-start.5) | collective-permute-done | bytes 266272 | tf_op jit(solution)/shard_map/ppermute | solution.py:45
  62.2 0.1 convert_add_fusion.1
  62.3 1.0 %collective-permute-start.6 = (bf16[128,520]{0,1:T(8,128)(2,1)S(1)}, bf16[128,520]{0,1:T(8,128)(2,1)S(1)}, u32[]{:S(2)}, u32[]{:S(2)}) collective-permute-start(bf16[128,520]{0,1:T(8,128)(2,1)S(1)} %bitcast_convert_fusion.1), channel_id=1, source_target_pairs={{0,2},{1,3},{2,0},{3,1},{4,6},{5,7},{6,4},{7,5},{8,10},{9,11},{10,... | collective-permute-start | bytes 399368 | tf_op jit(solution)/shard_map/ppermute | solution.py:50
  63.3 4.9 %collective-permute-done.6 = bf16[128,520]{0,1:T(8,128)(2,1)S(1)} collective-permute-done((bf16[128,520]{0,1:T(8,128)(2,1)S(1)}, bf16[128,520]{0,1:T(8,128)(2,1)S(1)}, u32[]{:S(2)}, u32[]{:S(2)}) %collective-permute-start.6) | collective-permute-done | bytes 133152 | tf_op jit(solution)/shard_map/ppermute | solution.py:50
  68.3 0.1 fusion.119
  68.3 0.2 fusion.92
  68.5 6.8 %all_gather.11 = bf16[512,4,128]{0,2,1:T(8,128)(2,1)S(1)} all-gather(bf16[128,4,128]{0,2,1:T(8,128)(2,1)S(1)} %fusion.92), channel_id=1, replica_groups=mesh['member'=2,'lon'=4,'lev'=4] {'lev'}, dimensions={0}, use_global_device_ids=true | all-gather | bytes 655360 | tf_op jit(solution)/shard_map/all_gather | solution.py:34
  75.3 0.2 fusion.20
  75.5 0.2 fusion.22
  75.7 2.1 %convolution_convert_fusion.2 = bf16[512,512]{0,1:T(8,128)(2,1)S(1)} fusion(bf16[512,512]{0,1:T(8,128)(2,1)S(1)} %bitcast.199, bf16[2,512,512]{2,1,0:T(8,128)(2,1)S(1)} %copy-done.6, bf16[2,512,512]{2,1,0:T(8,128)(2,1)} %param.26), kind=kOutput, calls=%fused_computation.15 | convolution fusion | flops 539492352 | bytes 2097152 | tf_op jit(solution)/shard_map/dot_general | solution.py:55
  77.9 0.4 collective-permute-start.7
  78.3 1.2 %collective-permute-done.7 = bf16[2,128,512]{2,1,0:T(8,128)(2,1)S(1)} collective-permute-done((bf16[2,128,512]{2,1,0:T(8,128)(2,1)S(1)}, bf16[2,128,512]{2,1,0:T(8,128)(2,1)S(1)}, u32[]{:S(2)}, u32[]{:S(2)}) %collective-permute-start.7) | collective-permute-done | bytes 262176 | tf_op jit(solution)/shard_map/ppermute | solution.py:45
  79.5 0.1 convert_add_fusion.2
  79.6 1.2 %collective-permute-start.8 = (bf16[128,512]{1,0:T(8,128)(2,1)S(1)}, bf16[128,512]{1,0:T(8,128)(2,1)S(1)}, u32[]{:S(2)}, u32[]{:S(2)}) collective-permute-start(bf16[128,512]{1,0:T(8,128)(2,1)S(1)} %bitcast_convert_fusion.2), channel_id=1, source_target_pairs={{0,2},{1,3},{2,0},{3,1},{4,6},{5,7},{6,4},{7,5},{8,10},{9,11},{10,... | collective-permute-start | bytes 393224 | tf_op jit(solution)/shard_map/ppermute | solution.py:50
  80.8 4.7 %collective-permute-done.8 = bf16[128,512]{1,0:T(8,128)(2,1)S(1)} collective-permute-done((bf16[128,512]{1,0:T(8,128)(2,1)S(1)}, bf16[128,512]{1,0:T(8,128)(2,1)S(1)}, u32[]{:S(2)}, u32[]{:S(2)}) %collective-permute-start.8) | collective-permute-done | bytes 131104 | tf_op jit(solution)/shard_map/ppermute | solution.py:50
  85.5 0.1 copy.119
  85.7 0.8 copy.120
  (56 shorter events, 0.9 us)
Async XLA Ops:
  0.0 9.6 %copy-start = (bf16[3,128,512]{2,1,0:T(8,128)(2,1)S(1)}, bf16[3,128,512]{2,1,0:T(8,128)(2,1)}, u32[]{:S(2)}) copy-start(bf16[3,128,512]{2,1,0:T(8,128)(2,1)} %param.22) | copy-start | bytes 1179652
  0.0 8.1 %copy-start.5 = (f32[512]{0:T(512)S(1)}, f32[512]{0:T(512)}, u32[]{:S(2)}) copy-start(f32[512]{0:T(512)} %param.21) | copy-start | bytes 6148
  10.1 0.9 %copy-start.1 = (bf16[128,4,128]{2,1,0:T(4,128)(2,1)S(1)}, bf16[128,4,128]{2,1,0:T(4,128)(2,1)}, u32[]{:S(2)}) copy-start(bf16[128,4,128]{2,1,0:T(4,128)(2,1)} %param.20) | copy-start | bytes 393220
  10.3 27.7 %collective-permute-start.2 = (bf16[256,4,128]{2,0,1:T(8,128)(2,1)S(1)}, bf16[256,4,128]{2,0,1:T(8,128)(2,1)S(1)}, u32[]{:S(2)}, u32[]{:S(2)}) collective-permute-start(bf16[256,4,128]{2,0,1:T(8,128)(2,1)S(1)} %bitcast.192), channel_id=1, source_target_pairs={{0,8},{4,12},{8,0},{12,4},{1,9},{5,13},{9,1},{13,5},{2,10},{6,14},... | collective-permute-start | bytes 786440 | tf_op jit(solution)/shard_map/ppermute | solution.py:146
  11.3 3.5 %copy-start.3 = (f32[2,9,128]{2,0,1:T(2,128)S(1)}, f32[2,9,128]{2,0,1:T(2,128)}, u32[]{:S(2)}) copy-start(f32[2,9,128]{2,0,1:T(2,128)} %param.24) | copy-start | bytes 27652
  12.3 21.8 %collective-permute-start.1 = (bf16[264,4,128]{2,0,1:T(8,128)(2,1)S(1)}, bf16[264,4,128]{2,0,1:T(8,128)(2,1)S(1)}, u32[]{:S(2)}, u32[]{:S(2)}) collective-permute-start(bf16[264,4,128]{2,0,1:T(8,128)(2,1)S(1)} %pad_maximum_fusion.1), channel_id=1, source_target_pairs={{0,12},{4,0},{8,4},{12,8},{1,13},{5,1},{9,5},{13,9},{2,14},{6,2},{... | collective-permute-start | bytes 811016 | tf_op jit(solution)/shard_map/ppermute | solution.py:146
  14.8 22.3 %collective-permute-start = (bf16[264,4,128]{2,0,1:T(8,128)(2,1)S(1)}, bf16[264,4,128]{2,0,1:T(8,128)(2,1)S(1)}, u32[]{:S(2)}, u32[]{:S(2)}) collective-permute-start(bf16[264,4,128]{2,0,1:T(8,128)(2,1)S(1)} %pad_maximum_fusion.1), channel_id=1, source_target_pairs={{0,4},{4,8},{8,12},{12,0},{1,5},{5,9},{9,13},{13,1},{2,6},{6,10},{... | collective-permute-start | bytes 811016 | tf_op jit(solution)/shard_map/ppermute | solution.py:146
  39.0 1.0 %copy-start.2 = (bf16[128,512]{1,0:T(8,128)(2,1)S(1)}, bf16[128,512]{1,0:T(8,128)(2,1)}, u32[]{:S(2)}) copy-start(bf16[128,512]{1,0:T(8,128)(2,1)} %param.23) | copy-start | bytes 393220
  41.5 3.0 %copy-start.4 = (f32[2,512]{1,0:T(2,128)S(1)}, f32[2,512]{1,0:T(2,128)}, u32[]{:S(2)}) copy-start(f32[2,512]{1,0:T(2,128)} %param.25) | copy-start | bytes 12292
  41.6 1.6 %collective-permute-start.3 = (bf16[2,128,528]{1,2,0:T(8,128)(2,1)S(1)}, bf16[2,128,528]{1,2,0:T(8,128)(2,1)S(1)}, u32[]{:S(2)}, u32[]{:S(2)}) collective-permute-start(bf16[2,128,528]{1,2,0:T(8,128)(2,1)S(1)} %fusion.79), channel_id=1, source_target_pairs={{0,1},{1,0},{2,3},{3,2},{4,5},{5,4},{6,7},{7,6},{8,9},{9,8},{10,11... | collective-permute-start | bytes 811016 | tf_op jit(solution)/shard_map/ppermute | solution.py:45
  43.3 5.7 %collective-permute-start.4 = (bf16[128,528]{0,1:T(8,128)(2,1)S(1)}, bf16[128,528]{0,1:T(8,128)(2,1)S(1)}, u32[]{:S(2)}, u32[]{:S(2)}) collective-permute-start(bf16[128,528]{0,1:T(8,128)(2,1)S(1)} %bitcast_convert_fusion), channel_id=1, source_target_pairs={{0,2},{1,3},{2,0},{3,1},{4,6},{5,7},{6,4},{7,5},{8,10},{9,11},{10,... | collective-permute-start | bytes 405512 | tf_op jit(solution)/shard_map/ppermute | solution.py:50
  60.6 1.6 %collective-permute-start.5 = (bf16[2,128,520]{1,2,0:T(8,128)(2,1)S(1)}, bf16[2,128,520]{1,2,0:T(8,128)(2,1)S(1)}, u32[]{:S(2)}, u32[]{:S(2)}) collective-permute-start(bf16[2,128,520]{1,2,0:T(8,128)(2,1)S(1)} %fusion.81), channel_id=1, source_target_pairs={{0,1},{1,0},{2,3},{3,2},{4,5},{5,4},{6,7},{7,6},{8,9},{9,8},{10,11... | collective-permute-start | bytes 798728 | tf_op jit(solution)/shard_map/ppermute | solution.py:45
  62.3 5.9 %collective-permute-start.6 = (bf16[128,520]{0,1:T(8,128)(2,1)S(1)}, bf16[128,520]{0,1:T(8,128)(2,1)S(1)}, u32[]{:S(2)}, u32[]{:S(2)}) collective-permute-start(bf16[128,520]{0,1:T(8,128)(2,1)S(1)} %bitcast_convert_fusion.1), channel_id=1, source_target_pairs={{0,2},{1,3},{2,0},{3,1},{4,6},{5,7},{6,4},{7,5},{8,10},{9,11},{10,... | collective-permute-start | bytes 399368 | tf_op jit(solution)/shard_map/ppermute | solution.py:50
  68.5 7.2 %copy-start.6 = (bf16[2,512,512]{2,1,0:T(8,128)(2,1)S(1)}, bf16[2,512,512]{2,1,0:T(8,128)(2,1)}, u32[]{:S(2)}) copy-start(bf16[2,512,512]{2,1,0:T(8,128)(2,1)} %param.27) | copy-start | bytes 3145732
  77.9 1.6 %collective-permute-start.7 = (bf16[2,128,512]{2,1,0:T(8,128)(2,1)S(1)}, bf16[2,128,512]{2,1,0:T(8,128)(2,1)S(1)}, u32[]{:S(2)}, u32[]{:S(2)}) collective-permute-start(bf16[2,128,512]{2,1,0:T(8,128)(2,1)S(1)} %select_bitcast_fusion), channel_id=1, source_target_pairs={{0,1},{1,0},{2,3},{3,2},{4,5},{5,4},{6,7},{7,6},{8,9},{9,8},{10,11... | collective-permute-start | bytes 786440 | tf_op jit(solution)/shard_map/ppermute | solution.py:45
  79.6 5.8 %collective-permute-start.8 = (bf16[128,512]{1,0:T(8,128)(2,1)S(1)}, bf16[128,512]{1,0:T(8,128)(2,1)S(1)}, u32[]{:S(2)}, u32[]{:S(2)}) collective-permute-start(bf16[128,512]{1,0:T(8,128)(2,1)S(1)} %bitcast_convert_fusion.2), channel_id=1, source_target_pairs={{0,2},{1,3},{2,0},{3,1},{4,6},{5,7},{6,4},{7,5},{8,10},{9,11},{10,... | collective-permute-start | bytes 393224 | tf_op jit(solution)/shard_map/ppermute | solution.py:50

commit v11 on v10

--- a/solution.py
+++ b/solution.py
@@ -31,7 +31,18 @@
 
 
 def gather_channels(values):
-    return lax.all_gather(values, "lev", axis=0, tiled=True)
+    devices = lax.axis_size("lev")
+    me = lax.axis_index("lev")
+    chips, core = devices // 2, me % 2
+    chip = me // 2
+    stacked = [values]
+    for shift in range(1, chips):
+        pairs = [(i, ((i // 2 - shift) % chips) * 2 + i % 2) for i in range(devices)]
+        stacked.append(lax.ppermute(values, "lev", pairs))
+    mine = jnp.roll(jnp.stack(stacked), chip, axis=0)
+    theirs = lax.ppermute(mine, "lev", [(i, i ^ 1) for i in range(devices)])
+    both = jnp.where(core == 0, jnp.stack([mine, theirs], axis=1), jnp.stack([theirs, mine], axis=1))
+    return both.reshape(devices * values.shape[0], *values.shape[1:])
 
 
 def scatter_sum(partial, axis):

time: 86.7 us -> 95 us (1.096)
  the two profiles are of different devices: /device:TPU:16 before, /device:TPU:0 now
where the time goes in v11:
time: 95 us; the launch traced here: 94.7 us
  waiting for transfers between devices  51.2 us (54%)
  starting transfers between devices  16.4 us (17%)
  local copies, waits for them, and re-layouts  10.9 us (11%)
  other arithmetic  9.32 us (10%)
  matrix products  6.16 us (6%)
    ppermute x3, waiting for transfers between devices, per_device(): got = lax.ppermute(sent, 'lon', pairs)  21.5 us
    ppermute x3, waiting for transfers between devices, scatter_sum(): total = total + lax.ppermute(sent, axis, pairs).astype(jnp.float32)  12.2 us
    ppermute x3, waiting for transfers between devices, gather_channels(): stacked.append(lax.ppermute(values, 'lev', pairs))  10.8 us
    ppermute x3, starting transfers between devices, gather_channels(): stacked.append(lax.ppermute(values, 'lev', pairs))  6.11 us
    ppermute x3, starting transfers between devices, per_device(): got = lax.ppermute(sent, 'lon', pairs)  4.92 us
    ppermute x3, starting transfers between devices, scatter_sum(): total = total + lax.ppermute(sent, axis, pairs).astype(jnp.float32)  4.66 us
    dot_general x3, matrix products, spread_sum(): lax.dot_general(weight, activation, (((0,), (0,)), ((), ())), preferred_e...  4.36 us
    ppermute x3, waiting for transfers between devices, scatter_sum(): lax.ppermute(theirs, axis, [(i, i ^ 1) for i in range(devices)])  4.01 us
  transfers between devices with their start and end apart: 15, of which 14 were waited for; matrix products, arithmetic and copies ran while one was open for 7% of the time, Pallas kernels for 0%

profile of v11, /device:TPU:0, one launch (start us, length us, event | category | flops | bytes accessed | tf_op | source)
XLA Modules:
  0.0 94.7 jit_solution(3690561136955837571)
XLA Ops:
  0.0 1.0 %copy.248 = bf16[128,4,128]{2,0,1:T(8,128)(2,1)S(1)} copy(bf16[128,4,128]{2,1,0:T(4,128)(2,1)} %param.22) | data formatting | bytes 262144 | tf_op args[0]
  1.0 3.0 %collective-permute-start = (bf16[128,4,128]{2,0,1:T(8,128)(2,1)S(1)}, bf16[128,4,128]{2,0,1:T(8,128)(2,1)S(1)}, u32[]{:S(2)}, u32[]{:S(2)}) collective-permute-start(bf16[128,4,128]{2,0,1:T(8,128)(2,1)S(1)} %copy.248), channel_id=1, source_target_pairs={{0,2},{1,3},{2,0},{3,1},{4,6},{5,7},{6,4},{7,5},{8,10},{9,11},{10,... | collective-permute-start | bytes 393224 | tf_op jit(solution)/shard_map/ppermute | solution.py:41
  4.0 3.5 %collective-permute-done = bf16[128,4,128]{2,0,1:T(8,128)(2,1)S(1)} collective-permute-done((bf16[128,4,128]{2,0,1:T(8,128)(2,1)S(1)}, bf16[128,4,128]{2,0,1:T(8,128)(2,1)S(1)}, u32[]{:S(2)}, u32[]{:S(2)}) %collective-permute-start) | collective-permute-done | bytes 131104 | tf_op jit(solution)/shard_map/ppermute | solution.py:41
  7.5 0.2 fusion.93
  7.8 1.1 %fusion.136 = (bf16[128,4,2]{2,1,0:T(4,128)(2,1)S(1)}, bf16[128,4,2]{2,1,0:T(4,128)(2,1)S(1)}) fusion(bf16[128,4,128]{2,1,0:T(4,128)(2,1)} %param.22), kind=kLoop, calls=%fused_computation.249 | loop fusion | bytes 8192 | tf_op jit(solution)/shard_map/slice | solution.py:129
  9.1 0.2 fusion.145
  9.6 0.2 fusion.29
  9.8 0.4 convolution_bitcast_fusion.2
  10.7 0.2 copy.152
  11.0 0.3 reshape.734
  11.5 1.9 %collective-permute-start.2 = (bf16[264,4,128]{2,0,1:T(8,128)(2,1)S(1)}, bf16[264,4,128]{2,0,1:T(8,128)(2,1)S(1)}, u32[]{:S(2)}, u32[]{:S(2)}) collective-permute-start(bf16[264,4,128]{2,0,1:T(8,128)(2,1)S(1)} %pad_maximum_fusion.1), channel_id=1, source_target_pairs={{0,4},{4,8},{8,12},{12,0},{1,5},{5,9},{9,13},{13,1},{2,6},{6,10},{... | collective-permute-start | bytes 811016 | tf_op jit(solution)/shard_map/ppermute | solution.py:157
  13.4 2.1 %collective-permute-start.3 = (bf16[264,4,128]{2,0,1:T(8,128)(2,1)S(1)}, bf16[264,4,128]{2,0,1:T(8,128)(2,1)S(1)}, u32[]{:S(2)}, u32[]{:S(2)}) collective-permute-start(bf16[264,4,128]{2,0,1:T(8,128)(2,1)S(1)} %pad_maximum_fusion.1), channel_id=1, source_target_pairs={{0,12},{4,0},{8,4},{12,8},{1,13},{5,1},{9,5},{13,9},{2,14},{6,2},{... | collective-permute-start | bytes 811016 | tf_op jit(solution)/shard_map/ppermute | solution.py:157
  15.5 0.9 collective-permute-start.4
  16.5 6.3 %collective-permute-done.2 = bf16[264,4,128]{2,0,1:T(8,128)(2,1)S(1)} collective-permute-done((bf16[264,4,128]{2,0,1:T(8,128)(2,1)S(1)}, bf16[264,4,128]{2,0,1:T(8,128)(2,1)S(1)}, u32[]{:S(2)}, u32[]{:S(2)}) %collective-permute-start.2) | collective-permute-done | bytes 270368 | tf_op jit(solution)/shard_map/ppermute | solution.py:157
  22.8 0.6 reshape.735
  23.4 0.2 fusion.132
  23.6 4.2 %collective-permute-done.3 = bf16[264,4,128]{2,0,1:T(8,128)(2,1)S(1)} collective-permute-done((bf16[264,4,128]{2,0,1:T(8,128)(2,1)S(1)}, bf16[264,4,128]{2,0,1:T(8,128)(2,1)S(1)}, u32[]{:S(2)}, u32[]{:S(2)}) %collective-permute-start.3) | collective-permute-done | bytes 270368 | tf_op jit(solution)/shard_map/ppermute | solution.py:157
  27.8 0.6 reshape.736
  28.6 11.0 %collective-permute-done.4 = bf16[256,4,128]{2,0,1:T(8,128)(2,1)S(1)} collective-permute-done((bf16[256,4,128]{2,0,1:T(8,128)(2,1)S(1)}, bf16[256,4,128]{2,0,1:T(8,128)(2,1)S(1)}, u32[]{:S(2)}, u32[]{:S(2)}) %collective-permute-start.4) | collective-permute-done | bytes 262176 | tf_op jit(solution)/shard_map/ppermute | solution.py:157
  39.7 0.9 fusion.3
  40.6 0.5 fusion.36
  41.1 0.3 copy.167
  41.6 0.3 fusion.5
  42.0 1.1 %constant_dynamic-slice_fusion.3 = (bf16[2,1,128,528]{2,1,0,3:T(2,128)(2,1)S(1)}, bf16[2,1,128,528]{2,1,0,3:T(2,128)(2,1)S(1)}) fusion(bf16[2,2,128,528]{2,1,0,3:T(2,128)(2,1)S(1)} %reshape.738, s32[]{:T(128)S(6)} %select_n.176, s32[]{:T(128)S(6)} %select_n.178), kind=kLoop, calls=%fused_computation.187 | loop fusion | bytes 1081352 | tf_op jit(solution)/shard_map/jit(_take) | solution.py:54
  43.4 1.4 %collective-permute-done.5 = bf16[2,128,528]{1,2,0:T(8,128)(2,1)S(1)} collective-permute-done((bf16[2,128,528]{1,2,0:T(8,128)(2,1)S(1)}, bf16[2,128,528]{1,2,0:T(8,128)(2,1)S(1)}, u32[]{:S(2)}, u32[]{:S(2)}) %collective-permute-start.5) | collective-permute-done | bytes 270368 | tf_op jit(solution)/shard_map/ppermute | solution.py:56
  44.9 1.6 %collective-permute-start.6 = (bf16[128,528]{0,1:T(8,128)(2,1)S(1)}, bf16[128,528]{0,1:T(8,128)(2,1)S(1)}, u32[]{:S(2)}, u32[]{:S(2)}) collective-permute-start(bf16[128,528]{0,1:T(8,128)(2,1)S(1)} %bitcast_convert_fusion), channel_id=1, source_target_pairs={{0,2},{1,3},{2,0},{3,1},{4,6},{5,7},{6,4},{7,5},{8,10},{9,11},{10,... | collective-permute-start | bytes 405512 | tf_op jit(solution)/shard_map/ppermute | solution.py:61
  46.6 4.0 %collective-permute-done.6 = bf16[128,528]{0,1:T(8,128)(2,1)S(1)} collective-permute-done((bf16[128,528]{0,1:T(8,128)(2,1)S(1)}, bf16[128,528]{0,1:T(8,128)(2,1)S(1)}, u32[]{:S(2)}, u32[]{:S(2)}) %collective-permute-start.6) | collective-permute-done | bytes 135200 | tf_op jit(solution)/shard_map/ppermute | solution.py:61
  50.7 0.2 copy.170
  50.9 0.2 fusion.131
  51.1 1.6 %fusion.55 = bf16[128,4,130]{2,0,1:T(8,128)(2,1)S(1)} fusion(f32[128,4,132]{2,0,1:T(8,128)S(1)} %get-tuple-element.80, f32[128,4]{0,1:T(4,128)S(1)} %get-tuple-element.128, f32[128]{0:T(128)S(1)} %get-tuple-element.111, f32[128,4]{0,1:T(4,128)S(1)} %get-tuple-element.127, f32[128,4]{0,1:T(4,128)S(1)} %get-tuple-element.126, f32[128]{0:T(128)S(1)} %get-tuple-element.114, ...), kind=kLoop, calls=%fused_computation.84 | loop fusion | flops 1198080 | bytes 2244096 | tf_op jit(solution)/shard_map/convert_element_type | solution.py:114
  52.7 1.6 %collective-permute-start.7 = (bf16[128,4,130]{2,0,1:T(8,128)(2,1)S(1)}, bf16[128,4,130]{2,0,1:T(8,128)(2,1)S(1)}, u32[]{:S(2)}, u32[]{:S(2)}) collective-permute-start(bf16[128,4,130]{2,0,1:T(8,128)(2,1)S(1)} %fusion.55), channel_id=1, source_target_pairs={{0,2},{1,3},{2,0},{3,1},{4,6},{5,7},{6,4},{7,5},{8,10},{9,11},{10,... | collective-permute-start | bytes 399368 | tf_op jit(solution)/shard_map/ppermute | solution.py:41
  54.2 1.4 %fusion.144 = bf16[1,128,4,130]{3,1,2,0:T(8,128)(2,1)S(1)} fusion(f32[128,4]{0,1:T(4,128)S(1)} %get-tuple-element.128, f32[128]{0:T(128)S(1)} %get-tuple-element.111, f32[128,4]{0,1:T(4,128)S(1)} %get-tuple-element.127, f32[128,4,132]{2,0,1:T(8,128)S(1)} %get-tuple-element.80, f32[128,4]{0,1:T(4,128)S(1)} %get-tuple-element.126, ...), kind=kLoop, calls=%fused_computation.254 | loop fusion | flops 1198080 | bytes 2244096 | tf_op jit(solution)/shard_map/stack | solution.py:42
  55.6 4.7 %collective-permute-done.7 = bf16[128,4,130]{2,0,1:T(8,128)(2,1)S(1)} collective-permute-done((bf16[128,4,130]{2,0,1:T(8,128)(2,1)S(1)}, bf16[128,4,130]{2,0,1:T(8,128)(2,1)S(1)}, u32[]{:S(2)}, u32[]{:S(2)}) %collective-permute-start.7) | collective-permute-done | bytes 133152 | tf_op jit(solution)/shard_map/ppermute | solution.py:41
  60.3 0.4 fusion.45
  60.8 0.4 fusion.143
  61.3 1.4 %collective-permute-done.8 = bf16[2,128,4,130]{3,1,2,0:T(8,128)(2,1)S(1)} collective-permute-done((bf16[2,128,4,130]{3,1,2,0:T(8,128)(2,1)S(1)}, bf16[2,128,4,130]{3,1,2,0:T(8,128)(2,1)S(1)}, u32[]{:S(2)}, u32[]{:S(2)}) %collective-permute-start.8) | collective-permute-done | bytes 266272 | tf_op jit(solution)/shard_map/ppermute | solution.py:43
  62.7 0.4 fusion
  63.1 0.4 fusion.2
  63.4 0.8 copy.172
  64.2 0.2 convert_element_type.248
  64.4 2.0 %fusion.6 = bf16[512,520]{0,1:T(8,128)(2,1)S(1)} fusion(bf16[512,520]{0,1:T(8,128)(2,1)S(1)} %convert_element_type.248, bf16[2,512,512]{2,1,0:T(8,128)(2,1)S(1)} %copy-done.5, bf16[2,512,512]{2,1,0:T(8,128)(2,1)} %param.28), kind=kOutput, calls=%fused_computation.19 | convolution fusion | flops 547921920 | bytes 2113536 | tf_op jit(solution)/shard_map/dot_general | solution.py:66
  66.6 1.1 %constant_dynamic-slice_fusion.1 = (bf16[2,1,128,520]{2,1,0,3:T(2,128)(2,1)S(1)}, bf16[2,1,128,520]{2,1,0,3:T(2,128)(2,1)S(1)}) fusion(bf16[2,2,128,520]{2,1,0,3:T(2,128)(2,1)S(1)} %reshape.740, s32[]{:T(128)S(6)} %select_n.176, s32[]{:T(128)S(6)} %select_n.178), kind=kLoop, calls=%fused_computation.185 | loop fusion | bytes 1064968 | tf_op jit(solution)/shard_map/jit(_take) | solution.py:54
  67.8 0.2 collective-permute-start.9
  68.0 1.4 %collective-permute-done.9 = bf16[2,128,520]{1,2,0:T(8,128)(2,1)S(1)} collective-permute-done((bf16[2,128,520]{1,2,0:T(8,128)(2,1)S(1)}, bf16[2,128,520]{1,2,0:T(8,128)(2,1)S(1)}, u32[]{:S(2)}, u32[]{:S(2)}) %collective-permute-start.9) | collective-permute-done | bytes 266272 | tf_op jit(solution)/shard_map/ppermute | solution.py:56
  69.5 1.6 %collective-permute-start.10 = (bf16[128,520]{0,1:T(8,128)(2,1)S(1)}, bf16[128,520]{0,1:T(8,128)(2,1)S(1)}, u32[]{:S(2)}, u32[]{:S(2)}) collective-permute-start(bf16[128,520]{0,1:T(8,128)(2,1)S(1)} %bitcast_convert_fusion.1), channel_id=1, source_target_pairs={{0,2},{1,3},{2,0},{3,1},{4,6},{5,7},{6,4},{7,5},{8,10},{9,11},{10,... | collective-permute-start | bytes 399368 | tf_op jit(solution)/shard_map/ppermute | solution.py:61
  71.0 4.1 %collective-permute-done.10 = bf16[128,520]{0,1:T(8,128)(2,1)S(1)} collective-permute-done((bf16[128,520]{0,1:T(8,128)(2,1)S(1)}, bf16[128,520]{0,1:T(8,128)(2,1)S(1)}, u32[]{:S(2)}, u32[]{:S(2)}) %collective-permute-start.10) | collective-permute-done | bytes 133152 | tf_op jit(solution)/shard_map/ppermute | solution.py:61
  75.2 0.2 copy.175
  75.5 0.9 fusion.116
  76.4 1.6 %collective-permute-start.11 = (bf16[128,4,128]{2,0,1:T(8,128)(2,1)S(1)}, bf16[128,4,128]{2,0,1:T(8,128)(2,1)S(1)}, u32[]{:S(2)}, u32[]{:S(2)}) collective-permute-start(bf16[128,4,128]{2,0,1:T(8,128)(2,1)S(1)} %fusion.116), channel_id=1, source_target_pairs={{0,2},{1,3},{2,0},{3,1},{4,6},{5,7},{6,4},{7,5},{8,10},{9,11},{10,... | collective-permute-start | bytes 393224 | tf_op jit(solution)/shard_map/ppermute | solution.py:41
  78.0 0.9 fusion.142
  78.8 2.6 %collective-permute-done.11 = bf16[128,4,128]{2,0,1:T(8,128)(2,1)S(1)} collective-permute-done((bf16[128,4,128]{2,0,1:T(8,128)(2,1)S(1)}, bf16[128,4,128]{2,0,1:T(8,128)(2,1)S(1)}, u32[]{:S(2)}, u32[]{:S(2)}) %collective-permute-start.11) | collective-permute-done | bytes 131104 | tf_op jit(solution)/shard_map/ppermute | solution.py:41
  81.5 0.2 fusion.90
  81.7 0.2 fusion.141
  81.9 1.3 %collective-permute-done.12 = bf16[2,128,4,128]{3,1,0,2:T(8,128)(2,1)S(1)} collective-permute-done((bf16[2,128,4,128]{3,1,0,2:T(8,128)(2,1)S(1)}, bf16[2,128,4,128]{3,1,0,2:T(8,128)(2,1)S(1)}, u32[]{:S(2)}, u32[]{:S(2)}) %collective-permute-start.12) | collective-permute-done | bytes 262176 | tf_op jit(solution)/shard_map/ppermute | solution.py:43
  83.4 0.2 fusion.19
  83.6 0.4 copy.177
  84.0 2.1 %convolution_convert_fusion.2 = bf16[512,512]{0,1:T(8,128)(2,1)S(1)} fusion(bf16[64,8,4,128]{3,2,1,0:T(4,128)(2,1)S(1)} %bitcast.239, bf16[2,512,512]{2,1,0:T(8,128)(2,1)S(1)} %copy-done.5, bf16[2,512,512]{2,1,0:T(8,128)(2,1)} %param.28), kind=kOutput, calls=%fused_computation.16 | convolution fusion | flops 539492352 | bytes 2097152 | tf_op jit(solution)/shard_map/dot_general | solution.py:66
  86.2 0.2 copy.198
  86.4 0.2 collective-permute-start.13
  86.6 0.2 copy.197
  86.8 1.2 %collective-permute-done.13 = bf16[2,128,512]{1,2,0:T(8,128)(2,1)S(1)} collective-permute-done((bf16[2,128,512]{1,2,0:T(8,128)(2,1)S(1)}, bf16[2,128,512]{1,2,0:T(8,128)(2,1)S(1)}, u32[]{:S(2)}, u32[]{:S(2)}) %collective-permute-start.13) | collective-permute-done | bytes 262176 | tf_op jit(solution)/shard_map/ppermute | solution.py:56
  88.1 1.6 %collective-permute-start.14 = (bf16[128,512]{0,1:T(8,128)(2,1)S(1)}, bf16[128,512]{0,1:T(8,128)(2,1)S(1)}, u32[]{:S(2)}, u32[]{:S(2)}) collective-permute-start(bf16[128,512]{0,1:T(8,128)(2,1)S(1)} %bitcast_convert_fusion.2), channel_id=1, source_target_pairs={{0,2},{1,3},{2,0},{3,1},{4,6},{5,7},{6,4},{7,5},{8,10},{9,11},{10,... | collective-permute-start | bytes 393224 | tf_op jit(solution)/shard_map/ppermute | solution.py:61
  89.7 4.1 %collective-permute-done.14 = bf16[128,512]{0,1:T(8,128)(2,1)S(1)} collective-permute-done((bf16[128,512]{0,1:T(8,128)(2,1)S(1)}, bf16[128,512]{0,1:T(8,128)(2,1)S(1)}, u32[]{:S(2)}, u32[]{:S(2)}) %collective-permute-start.14) | collective-permute-done | bytes 131104 | tf_op jit(solution)/shard_map/ppermute | solution.py:61
  94.0 0.8 copy.181
  (82 shorter events, 3.6 us)
Async XLA Ops:
  0.0 9.8 %copy-start = (bf16[3,128,512]{2,1,0:T(8,128)(2,1)S(1)}, bf16[3,128,512]{2,1,0:T(8,128)(2,1)}, u32[]{:S(2)}) copy-start(bf16[3,128,512]{2,1,0:T(8,128)(2,1)} %param.24) | copy-start | bytes 1179652
  0.0 9.6 %copy-start.4 = (f32[512]{0:T(512)S(1)}, f32[512]{0:T(512)}, u32[]{:S(2)}) copy-start(f32[512]{0:T(512)} %param.23) | copy-start | bytes 6148
  1.0 6.5 %collective-permute-start = (bf16[128,4,128]{2,0,1:T(8,128)(2,1)S(1)}, bf16[128,4,128]{2,0,1:T(8,128)(2,1)S(1)}, u32[]{:S(2)}, u32[]{:S(2)}) collective-permute-start(bf16[128,4,128]{2,0,1:T(8,128)(2,1)S(1)} %copy.248), channel_id=1, source_target_pairs={{0,2},{1,3},{2,0},{3,1},{4,6},{5,7},{6,4},{7,5},{8,10},{9,11},{10,... | collective-permute-start | bytes 393224 | tf_op jit(solution)/shard_map/ppermute | solution.py:41
  7.7 1.6 %collective-permute-start.1 = (bf16[2,128,4,128]{3,1,0,2:T(8,128)(2,1)S(1)}, bf16[2,128,4,128]{3,1,0,2:T(8,128)(2,1)S(1)}, u32[]{:S(2)}, u32[]{:S(2)}) collective-permute-start(bf16[2,128,4,128]{3,1,0,2:T(8,128)(2,1)S(1)} %fusion.93), channel_id=1, source_target_pairs={{0,1},{1,0},{2,3},{3,2},{4,5},{5,4},{6,7},{7,6},{8,9},{9,8},{10,11... | collective-permute-start | bytes 786440 | tf_op jit(solution)/shard_map/ppermute | solution.py:43
  11.5 11.3 %collective-permute-start.2 = (bf16[264,4,128]{2,0,1:T(8,128)(2,1)S(1)}, bf16[264,4,128]{2,0,1:T(8,128)(2,1)S(1)}, u32[]{:S(2)}, u32[]{:S(2)}) collective-permute-start(bf16[264,4,128]{2,0,1:T(8,128)(2,1)S(1)} %pad_maximum_fusion.1), channel_id=1, source_target_pairs={{0,4},{4,8},{8,12},{12,0},{1,5},{5,9},{9,13},{13,1},{2,6},{6,10},{... | collective-permute-start | bytes 811016 | tf_op jit(solution)/shard_map/ppermute | solution.py:157
  13.4 14.4 %collective-permute-start.3 = (bf16[264,4,128]{2,0,1:T(8,128)(2,1)S(1)}, bf16[264,4,128]{2,0,1:T(8,128)(2,1)S(1)}, u32[]{:S(2)}, u32[]{:S(2)}) collective-permute-start(bf16[264,4,128]{2,0,1:T(8,128)(2,1)S(1)} %pad_maximum_fusion.1), channel_id=1, source_target_pairs={{0,12},{4,0},{8,4},{12,8},{1,13},{5,1},{9,5},{13,9},{2,14},{6,2},{... | collective-permute-start | bytes 811016 | tf_op jit(solution)/shard_map/ppermute | solution.py:157
  15.5 24.1 %collective-permute-start.4 = (bf16[256,4,128]{2,0,1:T(8,128)(2,1)S(1)}, bf16[256,4,128]{2,0,1:T(8,128)(2,1)S(1)}, u32[]{:S(2)}, u32[]{:S(2)}) collective-permute-start(bf16[256,4,128]{2,0,1:T(8,128)(2,1)S(1)} %bitcast.225), channel_id=1, source_target_pairs={{0,8},{4,12},{8,0},{12,4},{1,9},{5,13},{9,1},{13,5},{2,10},{6,14},... | collective-permute-start | bytes 786440 | tf_op jit(solution)/shard_map/ppermute | solution.py:157
  40.6 1.0 %copy-start.1 = (bf16[128,512]{1,0:T(8,128)(2,1)S(1)}, bf16[128,512]{1,0:T(8,128)(2,1)}, u32[]{:S(2)}) copy-start(bf16[128,512]{1,0:T(8,128)(2,1)} %param.25) | copy-start | bytes 393220
  41.9 1.5 %copy-start.2 = (f32[2,9,128]{2,0,1:T(2,128)S(1)}, f32[2,9,128]{2,0,1:T(2,128)}, u32[]{:S(2)}) copy-start(f32[2,9,128]{2,0,1:T(2,128)} %param.26) | copy-start | bytes 27652
  43.2 1.6 %collective-permute-start.5 = (bf16[2,128,528]{1,2,0:T(8,128)(2,1)S(1)}, bf16[2,128,528]{1,2,0:T(8,128)(2,1)S(1)}, u32[]{:S(2)}, u32[]{:S(2)}) collective-permute-start(bf16[2,128,528]{1,2,0:T(8,128)(2,1)S(1)} %fusion.85), channel_id=1, source_target_pairs={{0,1},{1,0},{2,3},{3,2},{4,5},{5,4},{6,7},{7,6},{8,9},{9,8},{10,11... | collective-permute-start | bytes 811016 | tf_op jit(solution)/shard_map/ppermute | solution.py:56
  44.9 5.7 %collective-permute-start.6 = (bf16[128,528]{0,1:T(8,128)(2,1)S(1)}, bf16[128,528]{0,1:T(8,128)(2,1)S(1)}, u32[]{:S(2)}, u32[]{:S(2)}) collective-permute-start(bf16[128,528]{0,1:T(8,128)(2,1)S(1)} %bitcast_convert_fusion), channel_id=1, source_target_pairs={{0,2},{1,3},{2,0},{3,1},{4,6},{5,7},{6,4},{7,5},{8,10},{9,11},{10,... | collective-permute-start | bytes 405512 | tf_op jit(solution)/shard_map/ppermute | solution.py:61
  52.7 8.1 %copy-start.3 = (f32[2,512]{1,0:T(2,128)S(1)}, f32[2,512]{1,0:T(2,128)}, u32[]{:S(2)}) copy-start(f32[2,512]{1,0:T(2,128)} %param.27) | copy-start | bytes 12292
  52.7 7.6 %collective-permute-start.7 = (bf16[128,4,130]{2,0,1:T(8,128)(2,1)S(1)}, bf16[128,4,130]{2,0,1:T(8,128)(2,1)S(1)}, u32[]{:S(2)}, u32[]{:S(2)}) collective-permute-start(bf16[128,4,130]{2,0,1:T(8,128)(2,1)S(1)} %fusion.55), channel_id=1, source_target_pairs={{0,2},{1,3},{2,0},{3,1},{4,6},{5,7},{6,4},{7,5},{8,10},{9,11},{10,... | collective-permute-start | bytes 399368 | tf_op jit(solution)/shard_map/ppermute | solution.py:41
  60.7 2.0 %collective-permute-start.8 = (bf16[2,128,4,130]{3,1,2,0:T(8,128)(2,1)S(1)}, bf16[2,128,4,130]{3,1,2,0:T(8,128)(2,1)S(1)}, u32[]{:S(2)}, u32[]{:S(2)}) collective-permute-start(bf16[2,128,4,130]{3,1,2,0:T(8,128)(2,1)S(1)} %fusion.45), channel_id=1, source_target_pairs={{0,1},{1,0},{2,3},{3,2},{4,5},{5,4},{6,7},{7,6},{8,9},{9,8},{10,11... | collective-permute-start | bytes 798728 | tf_op jit(solution)/shard_map/ppermute | solution.py:43
  63.0 1.4 %copy-start.5 = (bf16[2,512,512]{2,1,0:T(8,128)(2,1)S(1)}, bf16[2,512,512]{2,1,0:T(8,128)(2,1)}, u32[]{:S(2)}) copy-start(bf16[2,512,512]{2,1,0:T(8,128)(2,1)} %param.29) | copy-start | bytes 3145732
  67.8 1.6 %collective-permute-start.9 = (bf16[2,128,520]{1,2,0:T(8,128)(2,1)S(1)}, bf16[2,128,520]{1,2,0:T(8,128)(2,1)S(1)}, u32[]{:S(2)}, u32[]{:S(2)}) collective-permute-start(bf16[2,128,520]{1,2,0:T(8,128)(2,1)S(1)} %fusion.87), channel_id=1, source_target_pairs={{0,1},{1,0},{2,3},{3,2},{4,5},{5,4},{6,7},{7,6},{8,9},{9,8},{10,11... | collective-permute-start | bytes 798728 | tf_op jit(solution)/shard_map/ppermute | solution.py:56
  69.5 5.7 %collective-permute-start.10 = (bf16[128,520]{0,1:T(8,128)(2,1)S(1)}, bf16[128,520]{0,1:T(8,128)(2,1)S(1)}, u32[]{:S(2)}, u32[]{:S(2)}) collective-permute-start(bf16[128,520]{0,1:T(8,128)(2,1)S(1)} %bitcast_convert_fusion.1), channel_id=1, source_target_pairs={{0,2},{1,3},{2,0},{3,1},{4,6},{5,7},{6,4},{7,5},{8,10},{9,11},{10,... | collective-permute-start | bytes 399368 | tf_op jit(solution)/shard_map/ppermute | solution.py:61
  76.4 5.0 %collective-permute-start.11 = (bf16[128,4,128]{2,0,1:T(8,128)(2,1)S(1)}, bf16[128,4,128]{2,0,1:T(8,128)(2,1)S(1)}, u32[]{:S(2)}, u32[]{:S(2)}) collective-permute-start(bf16[128,4,128]{2,0,1:T(8,128)(2,1)S(1)} %fusion.116), channel_id=1, source_target_pairs={{0,2},{1,3},{2,0},{3,1},{4,6},{5,7},{6,4},{7,5},{8,10},{9,11},{10,... | collective-permute-start | bytes 393224 | tf_op jit(solution)/shard_map/ppermute | solution.py:41
  81.6 1.6 %collective-permute-start.12 = (bf16[2,128,4,128]{3,1,0,2:T(8,128)(2,1)S(1)}, bf16[2,128,4,128]{3,1,0,2:T(8,128)(2,1)S(1)}, u32[]{:S(2)}, u32[]{:S(2)}) collective-permute-start(bf16[2,128,4,128]{3,1,0,2:T(8,128)(2,1)S(1)} %fusion.90), channel_id=1, source_target_pairs={{0,1},{1,0},{2,3},{3,2},{4,5},{5,4},{6,7},{7,6},{8,9},{9,8},{10,11... | collective-permute-start | bytes 786440 | tf_op jit(solution)/shard_map/ppermute | solution.py:43
  86.4 1.6 %collective-permute-start.13 = (bf16[2,128,512]{1,2,0:T(8,128)(2,1)S(1)}, bf16[2,128,512]{1,2,0:T(8,128)(2,1)S(1)}, u32[]{:S(2)}, u32[]{:S(2)}) collective-permute-start(bf16[2,128,512]{1,2,0:T(8,128)(2,1)S(1)} %select_bitcast_fusion), channel_id=1, source_target_pairs={{0,1},{1,0},{2,3},{3,2},{4,5},{5,4},{6,7},{7,6},{8,9},{9,8},{10,11... | collective-permute-start | bytes 786440 | tf_op jit(solution)/shard_map/ppermute | solution.py:56
  88.1 5.6 %collective-permute-start.14 = (bf16[128,512]{0,1:T(8,128)(2,1)S(1)}, bf16[128,512]{0,1:T(8,128)(2,1)S(1)}, u32[]{:S(2)}, u32[]{:S(2)}) collective-permute-start(bf16[128,512]{0,1:T(8,128)(2,1)S(1)} %bitcast_convert_fusion.2), channel_id=1, source_target_pairs={{0,2},{1,3},{2,0},{3,1},{4,6},{5,7},{6,4},{7,5},{8,10},{9,11},{10,... | collective-permute-start | bytes 393224 | tf_op jit(solution)/shard_map/ppermute | solution.py:61

commit v12 on v10

--- a/solution.py
+++ b/solution.py
@@ -51,11 +51,54 @@
     return total
 
 
-def spread_sum(weight, activation):
-    partial = lax.dot_general(
+def core_half(values, axis=0):
+    devices = lax.axis_size("lev")
+    grouped = values.reshape(*values.shape[:axis], devices // 2, 2, -1, *values.shape[axis + 1 :])
+    taken = jnp.take(grouped, lax.axis_index("lev") % 2, axis=axis + 1)
+    return taken.reshape(*values.shape[:axis], -1, *values.shape[axis + 1 :])
+
+
+def reduce_half(partial):
+    devices = lax.axis_size("lev")
+    me = lax.axis_index("lev")
+    chips, core = devices // 2, me % 2
+    blocks = partial.reshape(chips, 2, -1, *partial.shape[1:])
+    mine = jnp.take(blocks, core, axis=1).astype(jnp.float32)
+    theirs = jnp.take(blocks, 1 - core, axis=1)
+    pair = mine + lax.ppermute(theirs, "lev", [(i, i ^ 1) for i in range(devices)]).astype(jnp.float32)
+    pair = pair.astype(jnp.bfloat16)
+    total = pair.astype(jnp.float32)
+    for shift in range(1, chips):
+        pairs = [(i, ((i // 2 + shift) % chips) * 2 + i % 2) for i in range(devices)]
+        total = total + lax.ppermute(pair, "lev", pairs).astype(jnp.float32)
+    return total.reshape(-1, *partial.shape[1:])
+
+
+def gather_half(values):
+    devices = lax.axis_size("lev")
+    core = lax.axis_index("lev") % 2
+    mine = values.reshape(devices // 2, -1, *values.shape[1:])
+    theirs = lax.ppermute(mine, "lev", [(i, i ^ 1) for i in range(devices)])
+    both = jnp.where(core == 0, jnp.stack([mine, theirs], axis=1), jnp.stack([theirs, mine], axis=1))
+    return both.reshape(-1, *values.shape[1:])
+
+
+def half_weights(weights):
+    devices = lax.axis_size("lev")
+    chips = devices // 2
+    chip = lax.axis_index("lev") // 2
+    stacked = [weights]
+    for shift in range(1, chips):
+        pairs = [(i, ((i // 2 - shift) % chips) * 2 + i % 2) for i in range(devices)]
+        stacked.append(lax.ppermute(weights, "lev", pairs))
+    ordered = jnp.roll(jnp.stack(stacked), chip, axis=0)
+    return jnp.moveaxis(ordered, 0, -2).reshape(*weights.shape[:-1], -1)
+
+
+def group_partial(weight, activation):
+    return lax.dot_general(
         weight, activation, (((0,), (0,)), ((), ())), preferred_element_type=jnp.float32
     ).astype(jnp.bfloat16)
-    return scatter_sum(partial, "lev")
 
 
 def gather_strips(values, axis):
@@ -83,12 +126,11 @@
     return (numerator, jnp.sum(weights, axis=(3, 4)))
 
 
-def block_apply(state, block_index, stencil_weight, block_gain, up_weight, down_weight):
+def block_apply(state, block_index, tap_weights, block_gain, up_weight, down_weight, last):
     lat_rows = state.shape[1]
     out_cols = state.shape[2] - 2
     secants = secant_rows(lat_rows)[None, :, None]
     padded = jnp.pad(state.astype(jnp.float32), ((0, 0), (1, 1), (0, 0)))
-    tap_weights = stencil_weight[block_index]
     stencil_sum = jnp.zeros((state.shape[0], lat_rows, out_cols), jnp.float32)
     for row_step in (-1, 0, 1):
         for col_step in (-1, 0, 1):
@@ -101,7 +143,7 @@
             else:
                 stencil_sum = stencil_sum + tap_row * shifted
     smoothed = stencil_sum.astype(jnp.bfloat16)
-    full_channels = gather_channels(smoothed)
+    full_channels = gather_half(smoothed)
     block_normed = norm_channels(full_channels.astype(jnp.float32), block_gain[block_index]).astype(
         jnp.bfloat16
     )
@@ -109,8 +151,15 @@
     hidden = jax.nn.gelu(
         jnp.dot(up_weight[block_index], block_normed, preferred_element_type=jnp.float32)
     ).astype(jnp.bfloat16)
-    update = spread_sum(down_weight[block_index], hidden)
+    partial = group_partial(down_weight[block_index], hidden)
     center = state[:, :, 1:-1]
+    if last:
+        chips = lax.axis_size("lev") // 2
+        chip = lax.axis_index("lev") // 2
+        center = jnp.take(center.reshape(chips, -1, *center.shape[1:]), chip, axis=0)
+        update = scatter_sum(partial, "lev")
+    else:
+        update = reduce_half(partial)
     return (center.astype(jnp.float32) + update.reshape(center.shape)).astype(jnp.bfloat16)
 
 
@@ -126,6 +175,8 @@
     heads_local = qkv_weight.shape[1] // head_size
     reach = BLOCKS
     gathered = gather_channels(latent)
+    taps = half_weights(stencil_weight)
+    own_latent = core_half(gathered)
     normed = norm_channels(gathered.astype(jnp.float32), att_gain).astype(jnp.bfloat16)
     projected = jnp.einsum("koc,crw->korw", qkv_weight, normed, preferred_element_type=jnp.float32)
     projected = projected.reshape(3, heads_local, head_size, lat_rows, columns)
@@ -134,7 +185,7 @@
     value_rows = projected[2].astype(jnp.bfloat16)
 
     key_value = jnp.stack([key_rows, value_rows]).reshape(-1, lat_rows, columns)
-    rim = jnp.stack([edges(queries.reshape(ch_local, lat_rows, columns), reach), edges(latent, reach)])
+    rim = jnp.concatenate([edges(queries.reshape(ch_local, lat_rows, columns), reach), edges(own_latent, reach)])
     rim_rows = rim.size // (lat_rows * columns)
     payload = jnp.concatenate([key_value, rim.reshape(rim_rows, lat_rows, columns)], axis=0)
     strips = lax.axis_size("lon")
@@ -151,19 +202,20 @@
             from_right = got[key_value.shape[0] :].reshape(rim.shape)[..., :reach]
     all_keys = jnp.stack(pieces).reshape(strips, 2, heads_local, head_size, lat_rows, columns)
     wide_queries = jnp.concatenate(
-        [from_left[0], queries.reshape(ch_local, lat_rows, columns), from_right[0]], axis=-1
+        [from_left[:ch_local], queries.reshape(ch_local, lat_rows, columns), from_right[:ch_local]], axis=-1
     ).reshape(heads_local, head_size, lat_rows, -1)
-    wide_latent = jnp.concatenate([from_left[1], latent, from_right[1]], axis=-1)
+    wide_latent = jnp.concatenate([from_left[ch_local:], own_latent, from_right[ch_local:]], axis=-1)
 
     numerator, denominator = make_fold(wide_queries, (all_keys[:, 0], all_keys[:, 1]))
     attended = (numerator / denominator[:, None]).astype(jnp.bfloat16)
-    update = spread_sum(out_weight, attended.reshape(ch_local, -1))
+    update = reduce_half(group_partial(out_weight, attended.reshape(ch_local, -1)))
     current = (wide_latent.astype(jnp.float32) + update.reshape(wide_latent.shape)).astype(
         jnp.bfloat16
     )
     for block_index in range(BLOCKS):
         current = block_apply(
-            current, block_index, stencil_weight, block_gain, up_weight, down_weight
+            current, block_index, taps[block_index], block_gain, up_weight, down_weight,
+            block_index == BLOCKS - 1,
         )
     return current
 

time: 86.7 us -> 95 us (1.096)
  the two profiles are of different devices: /device:TPU:16 before, /device:TPU:0 now
where the time goes in v12:
time: 95 us; the launch traced here: 94.7 us
  waiting for transfers between devices  46 us (48%)
  other arithmetic  12.4 us (13%)
  local copies, waits for them, and re-layouts  10.5 us (11%)
  starting transfers between devices  9.92 us (10%)
  blocking collectives  8.95 us (9%)
  matrix products  6.33 us (7%)
    ppermute x3, waiting for transfers between devices, per_device(): got = lax.ppermute(sent, 'lon', pairs)  20.5 us
    ppermute x2, waiting for transfers between devices, reduce_half(): total = total + lax.ppermute(pair, 'lev', pairs).astype(jnp.float32)  13.2 us
    all_gather x1, blocking collectives, gather_channels(): return lax.all_gather(values, 'lev', axis=0, tiled=True)  8.95 us
    reduce_sum x3, other arithmetic, norm_channels(): jnp.mean(values * values, axis=0, keepdims=True) + epsilon  5.28 us
    ppermute x3, starting transfers between devices, per_device(): got = lax.ppermute(sent, 'lon', pairs)  4.67 us
    dot_general x3, matrix products, group_partial(): lax.dot_general(weight, activation, (((0,), (0,)), ((), ())), preferred_e...  4.53 us
    ppermute x1, waiting for transfers between devices, scatter_sum(): total = total + lax.ppermute(sent, axis, pairs).astype(jnp.float32)  4.19 us
    ppermute x2, waiting for transfers between devices, gather_half(): theirs = lax.ppermute(mine, 'lev', [(i, i ^ 1) for i in range(devices)])  2.83 us
  transfers between devices with their start and end apart: 12, of which 11 were waited for; matrix products, arithmetic and copies ran while one was open for 3% of the time, Pallas kernels for 0%

profile of v12, /device:TPU:0, one launch (start us, length us, event | category | flops | bytes accessed | tf_op | source)
XLA Modules:
  0.0 94.7 jit_solution(6074446387788465346)
XLA Ops:
  0.0 8.9 %all_gather.3 = bf16[512,4,128]{2,1,0:T(4,128)(2,1)S(1)} all-gather(bf16[128,4,128]{2,1,0:T(4,128)(2,1)} %param.16), channel_id=1, replica_groups=mesh['member'=2,'lon'=4,'lev'=4] {'lev'}, dimensions={0}, use_global_device_ids=true | all-gather | bytes 655360 | tf_op jit(solution)/shard_map/all_gather | solution.py:34
  9.0 0.5 fusion.17
  9.5 1.5 %fusion.59 = bf16[512,4,128,1]{2,1,0,3:T(4,128)(2,1)S(1)} fusion(bf16[512,4,128]{2,1,0:T(4,128)(2,1)S(1)} %all_gather.3, f32[512]{0:T(512)S(1)} %copy-done.4, f32[4,128]{1,0:T(4,128)S(1)} %add_rsqrt_fusion.2), kind=kLoop, calls=%fused_computation.91 | loop fusion | flops 1048576 | bytes 1052672 | tf_op jit(solution)/shard_map/convert_element_type | solution.py:180
  11.1 0.4 convolution_bitcast_fusion.2
  11.6 0.2 copy.189
  11.9 0.2 broadcast_select_fusion.1
  12.1 0.2 select_n.124
  12.7 0.1 copy.144
  13.0 0.3 copy.146
  13.2 0.5 reshape.742
  13.8 3.7 %collective-permute-start.1 = (bf16[268,4,128]{2,0,1:T(8,128)(2,1)S(1)}, bf16[268,4,128]{2,0,1:T(8,128)(2,1)S(1)}, u32[]{:S(2)}, u32[]{:S(2)}) collective-permute-start(bf16[268,4,128]{2,0,1:T(8,128)(2,1)S(1)} %pad_maximum_fusion.1), channel_id=1, source_target_pairs={{0,12},{4,0},{8,4},{12,8},{1,13},{5,1},{9,5},{13,9},{2,14},{6,2},{... | collective-permute-start | bytes 823304 | tf_op jit(solution)/shard_map/ppermute | solution.py:197
  17.5 1.0 %collective-permute-start.2 = (bf16[256,4,128]{2,0,1:T(8,128)(2,1)S(1)}, bf16[256,4,128]{2,0,1:T(8,128)(2,1)}, u32[]{:S(2)}, u32[]{:S(2)}) collective-permute-start(bf16[256,4,128]{2,0,1:T(8,128)(2,1)S(1)} %bitcast.185), channel_id=1, source_target_pairs={{0,8},{4,12},{8,0},{12,4},{1,9},{5,13},{9,1},{13,5},{2,10},{6,14},... | collective-permute-start | bytes 786440 | tf_op jit(solution)/shard_map/ppermute | solution.py:197
  18.5 6.0 %collective-permute-done.1 = bf16[268,4,128]{2,0,1:T(8,128)(2,1)S(1)} collective-permute-done((bf16[268,4,128]{2,0,1:T(8,128)(2,1)S(1)}, bf16[268,4,128]{2,0,1:T(8,128)(2,1)S(1)}, u32[]{:S(2)}, u32[]{:S(2)}) %collective-permute-start.1) | collective-permute-done | bytes 274464 | tf_op jit(solution)/shard_map/ppermute | solution.py:197
  24.5 6.9 %collective-permute-done = bf16[268,4,128]{2,0,1:T(8,128)(2,1)S(1)} collective-permute-done((bf16[268,4,128]{2,0,1:T(8,128)(2,1)S(1)}, bf16[268,4,128]{2,0,1:T(8,128)(2,1)S(1)}, u32[]{:S(2)}, u32[]{:S(2)}) %collective-permute-start) | collective-permute-done | bytes 274464 | tf_op jit(solution)/shard_map/ppermute | solution.py:197
  31.5 0.8 reshape.743
  32.3 0.1 slice.380
  32.5 0.8 reshape.744
  33.5 7.6 %collective-permute-done.2 = bf16[256,4,128]{2,0,1:T(8,128)(2,1)} collective-permute-done((bf16[256,4,128]{2,0,1:T(8,128)(2,1)S(1)}, bf16[256,4,128]{2,0,1:T(8,128)(2,1)}, u32[]{:S(2)}, u32[]{:S(2)}) %collective-permute-start.2) | collective-permute-done | bytes 262176 | tf_op jit(solution)/shard_map/ppermute | solution.py:197
  41.1 1.1 %pad_maximum_fusion = bf16[4,2,2,64,4,128]{5,3,0,4,2,1:T(8,128)(2,1)S(1)} fusion(bf16[1,2,2,64,4,128]{5,3,0,4,2,1:T(8,128)(2,1)S(1)} %get-tuple-element.90, bf16[1,2,2,64,4,128]{5,3,2,1,4,0:T(8,128)(2,1)S(1)} %bitcast.189, bf16[1,2,2,64,4,128]{5,3,2,1,4,0:T(8,128)(2,1)} %bitcast.13, bf16[1,2,2,64,4,128]{5,3,2,1,4,0:T(8,128)(2,1)S(1)} %bitcast.188), kind=kLoop, calls=%fused_computation.59 | loop fusion | flops 4194304 | bytes 2097152 | tf_op jit(solution)/shard_map/stack | solution.py:203
  42.2 0.9 fusion
  43.1 0.5 fusion.37
  43.6 0.3 copy.160
  43.9 0.1 reshape.745
  44.0 0.3 fusion.2
  44.3 0.1 reshape.746
  44.5 1.1 %constant_dynamic-slice_fusion.3 = (bf16[2,1,128,528]{2,1,0,3:T(2,128)(2,1)S(1)}, bf16[2,1,128,528]{2,1,0,3:T(2,128)(2,1)S(1)}) fusion(bf16[2,2,128,528]{2,1,0,3:T(2,128)(2,1)S(1)} %reshape.746, s32[]{:T(128)S(6)} %select_n.122, s32[]{:T(128)S(6)} %select_n.160), kind=kLoop, calls=%fused_computation.180 | loop fusion | bytes 1081352 | tf_op jit(solution)/shard_map/jit(_take) | solution.py:66
  45.7 1.2 %collective-permute-start.5 = (f32[2,9,128]{2,0,1:T(2,128)S(1)}, f32[2,9,128]{2,0,1:T(2,128)S(1)}, u32[]{:S(2)}, u32[]{:S(2)}) collective-permute-start(f32[2,9,128]{2,0,1:T(2,128)S(1)} %copy-done.2), channel_id=1, source_target_pairs={{0,2},{1,3},{2,0},{3,1},{4,6},{5,7},{6,4},{7,5},{8,10},{9,11},{10,... | collective-permute-start | bytes 27656 | tf_op jit(solution)/shard_map/ppermute | solution.py:93
  47.0 2.5 %collective-permute-done.5 = f32[2,9,128]{2,0,1:T(2,128)S(1)} collective-permute-done((f32[2,9,128]{2,0,1:T(2,128)S(1)}, f32[2,9,128]{2,0,1:T(2,128)S(1)}, u32[]{:S(2)}, u32[]{:S(2)}) %collective-permute-start.5) | collective-permute-done | bytes 9248 | tf_op jit(solution)/shard_map/ppermute | solution.py:93
  49.6 1.2 %collective-permute-start.4 = (bf16[2,128,528]{1,2,0:T(8,128)(2,1)S(1)}, bf16[2,128,528]{1,2,0:T(8,128)(2,1)S(1)}, u32[]{:S(2)}, u32[]{:S(2)}) collective-permute-start(bf16[2,128,528]{1,2,0:T(8,128)(2,1)S(1)} %add_convert_fusion.2), channel_id=1, source_target_pairs={{0,2},{1,3},{2,0},{3,1},{4,6},{5,7},{6,4},{7,5},{8,10},{9,11},{10,... | collective-permute-start | bytes 811016 | tf_op jit(solution)/shard_map/ppermute | solution.py:73
  50.9 0.2 slice.374
  51.2 0.2 copy.150
  51.4 0.2 copy.151
  51.6 5.8 %collective-permute-done.4 = bf16[2,128,528]{1,2,0:T(8,128)(2,1)S(1)} collective-permute-done((bf16[2,128,528]{1,2,0:T(8,128)(2,1)S(1)}, bf16[2,128,528]{1,2,0:T(8,128)(2,1)S(1)}, u32[]{:S(2)}, u32[]{:S(2)}) %collective-permute-start.4) | collective-permute-done | bytes 270368 | tf_op jit(solution)/shard_map/ppermute | solution.py:73
  57.4 0.3 copy.163
  57.7 0.4 reshape_reshape.6
  58.3 0.4 fusion.49
  58.8 0.1 copy-done.3
  59.0 1.3 %collective-permute-done.6 = bf16[2,128,4,130]{1,0,3,2:T(2,128)(2,1)S(1)} collective-permute-done((bf16[2,128,4,130]{1,0,3,2:T(2,128)(2,1)S(1)}, bf16[2,128,4,130]{1,0,3,2:T(2,128)(2,1)S(1)}, u32[]{:S(2)}, u32[]{:S(2)}) %collective-permute-start.6) | collective-permute-done | bytes 266272 | tf_op jit(solution)/shard_map/ppermute | solution.py:81
  60.4 0.2 copy.165
  60.6 4.2 %fusion.6 = (f32[4,130]{1,0:T(4,128)S(1)}, bf16[2,2,128,4,130]{2,0,4,3,1:T(2,128)(2,1)S(1)}) fusion(bf16[2,1,128,4,130]{2,0,4,3,1:T(2,128)(2,1)S(1)} %stack_reshape.4, bf16[2,1,128,4,130]{2,0,4,3,1:T(2,128)(2,1)S(1)} %copy.165, pred[]{:T(512)S(6)} %eq.15), kind=kLoop, calls=%fused_computation.33 | loop fusion | flops 1596920 | bytes 1067041 | tf_op jit(solution)/shard_map/reduce_sum | solution.py:25
  64.8 0.7 fusion.8
  65.6 0.5 copy.168
  66.1 0.2 convert_element_type.247
  66.3 2.2 %fusion.3 = bf16[512,520]{0,1:T(8,128)(2,1)S(1)} fusion(bf16[512,520]{0,1:T(8,128)(2,1)S(1)} %convert_element_type.247, bf16[2,512,512]{2,1,0:T(8,128)(2,1)} %param.23, bf16[2,512,512]{2,1,0:T(8,128)(2,1)} %param.22), kind=kOutput, calls=%fused_computation.30 | convolution fusion | flops 547921920 | bytes 2113536 | tf_op jit(solution)/shard_map/dot_general | solution.py:99
  68.5 0.1 reshape.748
  68.6 1.1 %constant_dynamic-slice_fusion.1 = (bf16[2,1,128,520]{2,1,0,3:T(2,128)(2,1)S(1)}, bf16[2,1,128,520]{2,1,0,3:T(2,128)(2,1)S(1)}) fusion(bf16[2,2,128,520]{2,1,0,3:T(2,128)(2,1)S(1)} %reshape.748, s32[]{:T(128)S(6)} %select_n.122, s32[]{:T(128)S(6)} %select_n.160), kind=kLoop, calls=%fused_computation.178 | loop fusion | bytes 1064968 | tf_op jit(solution)/shard_map/jit(_take) | solution.py:66
  69.8 0.2 collective-permute-start.7
  70.0 1.4 %collective-permute-done.7 = bf16[2,128,520]{1,2,0:T(8,128)(2,1)S(1)} collective-permute-done((bf16[2,128,520]{1,2,0:T(8,128)(2,1)S(1)}, bf16[2,128,520]{1,2,0:T(8,128)(2,1)S(1)}, u32[]{:S(2)}, u32[]{:S(2)}) %collective-permute-start.7) | collective-permute-done | bytes 266272 | tf_op jit(solution)/shard_map/ppermute | solution.py:68
  71.5 1.2 %collective-permute-start.8 = (bf16[2,128,520]{1,2,0:T(8,128)(2,1)S(1)}, bf16[2,128,520]{1,2,0:T(8,128)(2,1)S(1)}, u32[]{:S(2)}, u32[]{:S(2)}) collective-permute-start(bf16[2,128,520]{1,2,0:T(8,128)(2,1)S(1)} %add_convert_fusion.3), channel_id=1, source_target_pairs={{0,2},{1,3},{2,0},{3,1},{4,6},{5,7},{6,4},{7,5},{8,10},{9,11},{10,... | collective-permute-start | bytes 798728 | tf_op jit(solution)/shard_map/ppermute | solution.py:73
  72.7 7.3 %collective-permute-done.8 = bf16[2,128,520]{1,2,0:T(8,128)(2,1)S(1)} collective-permute-done((bf16[2,128,520]{1,2,0:T(8,128)(2,1)S(1)}, bf16[2,128,520]{1,2,0:T(8,128)(2,1)S(1)}, u32[]{:S(2)}, u32[]{:S(2)}) %collective-permute-start.8) | collective-permute-done | bytes 266272 | tf_op jit(solution)/shard_map/ppermute | solution.py:73
  80.1 0.3 copy.171
  80.4 0.4 reshape_reshape.7
  80.9 0.4 fusion.69
  81.3 0.2 copy.188
  81.6 1.5 %collective-permute-done.9 = bf16[2,128,4,128]{3,2,1,0:T(4,128)(2,1)S(1)} collective-permute-done((bf16[2,128,4,128]{3,2,1,0:T(4,128)(2,1)S(1)}, bf16[2,128,4,128]{3,2,1,0:T(4,128)(2,1)S(1)}, u32[]{:S(2)}, u32[]{:S(2)}) %collective-permute-start.9) | collective-permute-done | bytes 262176 | tf_op jit(solution)/shard_map/ppermute | solution.py:81
  83.1 0.6 fusion.20
  83.7 0.7 fusion.22
  84.4 2.1 %convolution_convert_fusion.2 = bf16[512,512]{0,1:T(8,128)(2,1)S(1)} fusion(bf16[64,8,4,128]{3,2,1,0:T(4,128)(2,1)S(1)} %bitcast.193, bf16[2,512,512]{2,1,0:T(8,128)(2,1)S(1)} %copy-done.5, bf16[2,512,512]{2,1,0:T(8,128)(2,1)} %param.22), kind=kOutput, calls=%fused_computation.15 | convolution fusion | flops 539492352 | bytes 2097152 | tf_op jit(solution)/shard_map/dot_general | solution.py:99
  86.5 0.2 collective-permute-start.10
  86.7 1.4 %collective-permute-done.10 = bf16[2,128,512]{2,1,0:T(8,128)(2,1)S(1)} collective-permute-done((bf16[2,128,512]{2,1,0:T(8,128)(2,1)S(1)}, bf16[2,128,512]{2,1,0:T(8,128)(2,1)S(1)}, u32[]{:S(2)}, u32[]{:S(2)}) %collective-permute-start.10) | collective-permute-done | bytes 262176 | tf_op jit(solution)/shard_map/ppermute | solution.py:45
  88.2 1.2 %collective-permute-start.11 = (bf16[128,512]{1,0:T(8,128)(2,1)S(1)}, bf16[128,512]{1,0:T(8,128)(2,1)S(1)}, u32[]{:S(2)}, u32[]{:S(2)}) collective-permute-start(bf16[128,512]{1,0:T(8,128)(2,1)S(1)} %bitcast_convert_fusion), channel_id=1, source_target_pairs={{0,2},{1,3},{2,0},{3,1},{4,6},{5,7},{6,4},{7,5},{8,10},{9,11},{10,... | collective-permute-start | bytes 393224 | tf_op jit(solution)/shard_map/ppermute | solution.py:50
  89.4 0.2 copy.186
  89.6 4.2 %collective-permute-done.11 = bf16[128,512]{1,0:T(8,128)(2,1)S(1)} collective-permute-done((bf16[128,512]{1,0:T(8,128)(2,1)S(1)}, bf16[128,512]{1,0:T(8,128)(2,1)S(1)}, u32[]{:S(2)}, u32[]{:S(2)}) %collective-permute-start.11) | collective-permute-done | bytes 131104 | tf_op jit(solution)/shard_map/ppermute | solution.py:50
  94.0 0.7 fusion.107
  (71 shorter events, 2.6 us)
Async XLA Ops:
  0.0 11.0 %copy-start = (bf16[3,128,512]{2,1,0:T(8,128)(2,1)S(1)}, bf16[3,128,512]{2,1,0:T(8,128)(2,1)}, u32[]{:S(2)}) copy-start(bf16[3,128,512]{2,1,0:T(8,128)(2,1)} %param.18) | copy-start | bytes 1179652
  0.0 9.5 %copy-start.4 = (f32[512]{0:T(512)S(1)}, f32[512]{0:T(512)}, u32[]{:S(2)}) copy-start(f32[512]{0:T(512)} %param.17) | copy-start | bytes 6148
  13.8 10.7 %collective-permute-start.1 = (bf16[268,4,128]{2,0,1:T(8,128)(2,1)S(1)}, bf16[268,4,128]{2,0,1:T(8,128)(2,1)S(1)}, u32[]{:S(2)}, u32[]{:S(2)}) collective-permute-start(bf16[268,4,128]{2,0,1:T(8,128)(2,1)S(1)} %pad_maximum_fusion.1), channel_id=1, source_target_pairs={{0,12},{4,0},{8,4},{12,8},{1,13},{5,1},{9,5},{13,9},{2,14},{6,2},{... | collective-permute-start | bytes 823304 | tf_op jit(solution)/shard_map/ppermute | solution.py:197
  17.5 14.0 %collective-permute-start = (bf16[268,4,128]{2,0,1:T(8,128)(2,1)S(1)}, bf16[268,4,128]{2,0,1:T(8,128)(2,1)S(1)}, u32[]{:S(2)}, u32[]{:S(2)}) collective-permute-start(bf16[268,4,128]{2,0,1:T(8,128)(2,1)S(1)} %pad_maximum_fusion.1), channel_id=1, source_target_pairs={{0,4},{4,8},{8,12},{12,0},{1,5},{5,9},{9,13},{13,1},{2,6},{6,10},{... | collective-permute-start | bytes 823304 | tf_op jit(solution)/shard_map/ppermute | solution.py:197
  17.5 23.6 %collective-permute-start.2 = (bf16[256,4,128]{2,0,1:T(8,128)(2,1)S(1)}, bf16[256,4,128]{2,0,1:T(8,128)(2,1)}, u32[]{:S(2)}, u32[]{:S(2)}) collective-permute-start(bf16[256,4,128]{2,0,1:T(8,128)(2,1)S(1)} %bitcast.185), channel_id=1, source_target_pairs={{0,8},{4,12},{8,0},{12,4},{1,9},{5,13},{9,1},{13,5},{2,10},{6,14},... | collective-permute-start | bytes 786440 | tf_op jit(solution)/shard_map/ppermute | solution.py:197
  43.1 1.0 %copy-start.1 = (bf16[128,512]{1,0:T(8,128)(2,1)S(1)}, bf16[128,512]{1,0:T(8,128)(2,1)}, u32[]{:S(2)}) copy-start(bf16[128,512]{1,0:T(8,128)(2,1)} %param.19) | copy-start | bytes 393220
  44.5 1.3 %copy-start.2 = (f32[2,9,128]{2,0,1:T(2,128)S(1)}, f32[2,9,128]{2,0,1:T(2,128)}, u32[]{:S(2)}) copy-start(f32[2,9,128]{2,0,1:T(2,128)} %param.20) | copy-start | bytes 27652
  45.7 3.9 %collective-permute-start.3 = (bf16[2,128,528]{1,2,0:T(8,128)(2,1)S(1)}, bf16[2,128,528]{1,2,0:T(8,128)(2,1)S(1)}, u32[]{:S(2)}, u32[]{:S(2)}) collective-permute-start(bf16[2,128,528]{1,2,0:T(8,128)(2,1)S(1)} %fusion.98), channel_id=1, source_target_pairs={{0,1},{1,0},{2,3},{3,2},{4,5},{5,4},{6,7},{7,6},{8,9},{9,8},{10,11... | collective-permute-start | bytes 811016 | tf_op jit(solution)/shard_map/ppermute | solution.py:68
  45.7 3.7 %collective-permute-start.5 = (f32[2,9,128]{2,0,1:T(2,128)S(1)}, f32[2,9,128]{2,0,1:T(2,128)S(1)}, u32[]{:S(2)}, u32[]{:S(2)}) collective-permute-start(f32[2,9,128]{2,0,1:T(2,128)S(1)} %copy-done.2), channel_id=1, source_target_pairs={{0,2},{1,3},{2,0},{3,1},{4,6},{5,7},{6,4},{7,5},{8,10},{9,11},{10,... | collective-permute-start | bytes 27656 | tf_op jit(solution)/shard_map/ppermute | solution.py:93
  49.6 7.7 %collective-permute-start.4 = (bf16[2,128,528]{1,2,0:T(8,128)(2,1)S(1)}, bf16[2,128,528]{1,2,0:T(8,128)(2,1)S(1)}, u32[]{:S(2)}, u32[]{:S(2)}) collective-permute-start(bf16[2,128,528]{1,2,0:T(8,128)(2,1)S(1)} %add_convert_fusion.2), channel_id=1, source_target_pairs={{0,2},{1,3},{2,0},{3,1},{4,6},{5,7},{6,4},{7,5},{8,10},{9,11},{10,... | collective-permute-start | bytes 811016 | tf_op jit(solution)/shard_map/ppermute | solution.py:73
  58.3 0.7 copy-start.3
  58.8 1.6 %collective-permute-start.6 = (bf16[2,128,4,130]{1,0,3,2:T(2,128)(2,1)S(1)}, bf16[2,128,4,130]{1,0,3,2:T(2,128)(2,1)S(1)}, u32[]{:S(2)}, u32[]{:S(2)}) collective-permute-start(bf16[2,128,4,130]{1,0,3,2:T(2,128)(2,1)S(1)} %reshape.747), channel_id=1, source_target_pairs={{0,1},{1,0},{2,3},{3,2},{4,5},{5,4},{6,7},{7,6},{8,9},{9,8},{10,11... | collective-permute-start | bytes 798728 | tf_op jit(solution)/shard_map/ppermute | solution.py:81
  69.8 1.6 %collective-permute-start.7 = (bf16[2,128,520]{1,2,0:T(8,128)(2,1)S(1)}, bf16[2,128,520]{1,2,0:T(8,128)(2,1)S(1)}, u32[]{:S(2)}, u32[]{:S(2)}) collective-permute-start(bf16[2,128,520]{1,2,0:T(8,128)(2,1)S(1)} %fusion.100), channel_id=1, source_target_pairs={{0,1},{1,0},{2,3},{3,2},{4,5},{5,4},{6,7},{7,6},{8,9},{9,8},{10,11... | collective-permute-start | bytes 798728 | tf_op jit(solution)/shard_map/ppermute | solution.py:68
  71.5 8.5 %collective-permute-start.8 = (bf16[2,128,520]{1,2,0:T(8,128)(2,1)S(1)}, bf16[2,128,520]{1,2,0:T(8,128)(2,1)S(1)}, u32[]{:S(2)}, u32[]{:S(2)}) collective-permute-start(bf16[2,128,520]{1,2,0:T(8,128)(2,1)S(1)} %add_convert_fusion.3), channel_id=1, source_target_pairs={{0,2},{1,3},{2,0},{3,1},{4,6},{5,7},{6,4},{7,5},{8,10},{9,11},{10,... | collective-permute-start | bytes 798728 | tf_op jit(solution)/shard_map/ppermute | solution.py:73
  81.5 2.9 %copy-start.5 = (bf16[2,512,512]{2,1,0:T(8,128)(2,1)S(1)}, bf16[2,512,512]{2,1,0:T(8,128)(2,1)}, u32[]{:S(2)}) copy-start(bf16[2,512,512]{2,1,0:T(8,128)(2,1)} %param.23) | copy-start | bytes 3145732
  81.5 1.6 %collective-permute-start.9 = (bf16[2,128,4,128]{3,2,1,0:T(4,128)(2,1)S(1)}, bf16[2,128,4,128]{3,2,1,0:T(4,128)(2,1)S(1)}, u32[]{:S(2)}, u32[]{:S(2)}) collective-permute-start(bf16[2,128,4,128]{3,2,1,0:T(4,128)(2,1)S(1)} %bitcast.186), channel_id=1, source_target_pairs={{0,1},{1,0},{2,3},{3,2},{4,5},{5,4},{6,7},{7,6},{8,9},{9,8},{10,11... | collective-permute-start | bytes 786440 | tf_op jit(solution)/shard_map/ppermute | solution.py:81
  86.5 1.6 %collective-permute-start.10 = (bf16[2,128,512]{2,1,0:T(8,128)(2,1)S(1)}, bf16[2,128,512]{2,1,0:T(8,128)(2,1)S(1)}, u32[]{:S(2)}, u32[]{:S(2)}) collective-permute-start(bf16[2,128,512]{2,1,0:T(8,128)(2,1)S(1)} %select_bitcast_fusion), channel_id=1, source_target_pairs={{0,1},{1,0},{2,3},{3,2},{4,5},{5,4},{6,7},{7,6},{8,9},{9,8},{10,11... | collective-permute-start | bytes 786440 | tf_op jit(solution)/shard_map/ppermute | solution.py:45
  88.2 5.6 %collective-permute-start.11 = (bf16[128,512]{1,0:T(8,128)(2,1)S(1)}, bf16[128,512]{1,0:T(8,128)(2,1)S(1)}, u32[]{:S(2)}, u32[]{:S(2)}) collective-permute-start(bf16[128,512]{1,0:T(8,128)(2,1)S(1)} %bitcast_convert_fusion), channel_id=1, source_target_pairs={{0,2},{1,3},{2,0},{3,1},{4,6},{5,7},{6,4},{7,5},{8,10},{9,11},{10,... | collective-permute-start | bytes 393224 | tf_op jit(solution)/shard_map/ppermute | solution.py:50

commit v13 on v10

--- a/solution.py
+++ b/solution.py
@@ -34,14 +34,20 @@
     return lax.all_gather(values, "lev", axis=0, tiled=True)
 
 
-def scatter_sum(partial, axis):
+def scatter_sum(weight, activation, axis):
     devices = lax.axis_size(axis)
     me = lax.axis_index(axis)
     chips, core = devices // 2, me % 2
     chip = me // 2
-    blocks = partial.reshape(chips, 2, -1, *partial.shape[1:])
-    mine = jnp.take(blocks, core, axis=1).astype(jnp.float32)
-    theirs = jnp.take(blocks, 1 - core, axis=1)
+    grouped = weight.reshape(weight.shape[0], chips, 2, -1)
+
+    def part(which):
+        columns = jnp.take(grouped, which, axis=2).reshape(weight.shape[0], -1)
+        product = jnp.dot(columns.T, activation, preferred_element_type=jnp.float32)
+        return product.astype(jnp.bfloat16).reshape(chips, -1, activation.shape[1])
+
+    mine = part(core).astype(jnp.float32)
+    theirs = part(1 - core)
     pair = mine + lax.ppermute(theirs, axis, [(i, i ^ 1) for i in range(devices)]).astype(jnp.float32)
     total = jnp.take(pair, chip, axis=0)
     for shift in range(1, chips):
@@ -52,10 +58,7 @@
 
 
 def spread_sum(weight, activation):
-    partial = lax.dot_general(
-        weight, activation, (((0,), (0,)), ((), ())), preferred_element_type=jnp.float32
-    ).astype(jnp.bfloat16)
-    return scatter_sum(partial, "lev")
+    return scatter_sum(weight, activation, "lev")
 
 
 def gather_strips(values, axis):
@@ -125,6 +128,7 @@
     head_size = C // H
     heads_local = qkv_weight.shape[1] // head_size
     reach = BLOCKS
+    wide_source, latent = lax.optimization_barrier((latent.astype(jnp.float32), latent))
     gathered = gather_channels(latent)
     normed = norm_channels(gathered.astype(jnp.float32), att_gain).astype(jnp.bfloat16)
     projected = jnp.einsum("koc,crw->korw", qkv_weight, normed, preferred_element_type=jnp.float32)
@@ -134,7 +138,9 @@
     value_rows = projected[2].astype(jnp.bfloat16)
 
     key_value = jnp.stack([key_rows, value_rows]).reshape(-1, lat_rows, columns)
-    rim = jnp.stack([edges(queries.reshape(ch_local, lat_rows, columns), reach), edges(latent, reach)])
+    rim = jnp.stack(
+        [edges(queries.reshape(ch_local, lat_rows, columns), reach), edges(wide_source, reach).astype(jnp.bfloat16)]
+    )
     rim_rows = rim.size // (lat_rows * columns)
     payload = jnp.concatenate([key_value, rim.reshape(rim_rows, lat_rows, columns)], axis=0)
     strips = lax.axis_size("lon")
@@ -153,7 +159,9 @@
     wide_queries = jnp.concatenate(
         [from_left[0], queries.reshape(ch_local, lat_rows, columns), from_right[0]], axis=-1
     ).reshape(heads_local, head_size, lat_rows, -1)
-    wide_latent = jnp.concatenate([from_left[1], latent, from_right[1]], axis=-1)
+    wide_latent = jnp.concatenate(
+        [from_left[1].astype(jnp.float32), wide_source, from_right[1].astype(jnp.float32)], axis=-1
+    )
 
     numerator, denominator = make_fold(wide_queries, (all_keys[:, 0], all_keys[:, 1]))
     attended = (numerator / denominator[:, None]).astype(jnp.bfloat16)

time: 86.7 us -> 91.8 us (1.059)
  the two profiles are of different devices: /device:TPU:16 before, /device:TPU:0 now
where the time goes in v13:
time: 91.8 us; the launch traced here: 91.4 us
  waiting for transfers between devices  30.2 us (33%)
  blocking collectives  22.5 us (25%)
  local copies, waits for them, and re-layouts  12.3 us (13%)
  other arithmetic  11.6 us (13%)
  starting transfers between devices  8.85 us (10%)
  matrix products  4.9 us (5%)
    all_gather x3, blocking collectives, gather_channels(): return lax.all_gather(values, 'lev', axis=0, tiled=True)  22.5 us
    ppermute x3, waiting for transfers between devices, per_device(): got = lax.ppermute(sent, 'lon', pairs)  15 us
    ppermute x3, waiting for transfers between devices, scatter_sum(): total = total + lax.ppermute(sent, axis, pairs).astype(jnp.float32)  12.9 us
    ppermute x3, starting transfers between devices, per_device(): got = lax.ppermute(sent, 'lon', pairs)  4.61 us
    ppermute x3, starting transfers between devices, scatter_sum(): total = total + lax.ppermute(sent, axis, pairs).astype(jnp.float32)  3.32 us
    unnamed x71, local copies, waits for them, and re-layouts  2.9 us
    ppermute x3, waiting for transfers between devices, scatter_sum(): lax.ppermute(theirs, axis, [(i, i ^ 1) for i in range(devices)])  2.26 us
    slice x2, local copies, waits for them, and re-layouts, per_device(): pieces.append(got[:key_value.shape[0]])  1.95 us
  transfers between devices with their start and end apart: 9, of which 9 were waited for; matrix products, arithmetic and copies ran while one was open for 12% of the time, Pallas kernels for 0%

profile of v13, /device:TPU:0, one launch (start us, length us, event | category | flops | bytes accessed | tf_op | source)
XLA Modules:
  0.0 91.4 jit_solution(15769088189958031544)
XLA Ops:
  0.0 1.1 %copy.144 = bf16[128,4,128]{0,2,1:T(8,128)(2,1)S(1)} copy(bf16[128,4,128]{2,1,0:T(4,128)(2,1)} %param.18) | data formatting | bytes 262144 | tf_op args[0]
  1.1 8.8 %all_gather.9 = bf16[512,4,128]{2,1,0:T(4,128)(2,1)S(1)} all-gather(bf16[128,4,128]{2,1,0:T(4,128)(2,1)} %param.18), channel_id=1, replica_groups=mesh['member'=2,'lon'=4,'lev'=4] {'lev'}, dimensions={0}, use_global_device_ids=true | all-gather | bytes 655360 | tf_op jit(solution)/shard_map/all_gather | solution.py:34
  10.0 0.5 fusion.21
  10.5 1.5 %fusion.44 = bf16[512,4,128,1]{2,1,0,3:T(4,128)(2,1)S(1)} fusion(bf16[512,4,128]{2,1,0:T(4,128)(2,1)S(1)} %all_gather.9, f32[512]{0:T(512)S(1)} %copy-done.28, f32[4,128]{1,0:T(4,128)S(1)} %add_rsqrt_fusion.2), kind=kLoop, calls=%fused_computation.71 | loop fusion | flops 1048576 | bytes 1052672 | tf_op jit(solution)/shard_map/convert_element_type | solution.py:133
  12.1 0.4 convolution_bitcast_fusion.2
  13.1 0.2 copy.154
  13.3 0.3 reshape.663
  13.8 0.8 fusion.96
  14.6 0.7 copy.149
  15.3 1.7 %pad_maximum_fusion.1 = bf16[264,4,128]{2,0,1:T(8,128)(2,1)} fusion(bf16[8,4,128]{2,0,1:T(8,128)(2,1)S(1)} %copy.155, bf16[256,4,128]{2,0,1:T(8,128)(2,1)} %bitcast.6), kind=kLoop, calls=%fused_computation.104 | loop fusion | flops 540672 | bytes 540672 | tf_op jit(solution)/shard_map/concatenate | solution.py:145
  16.9 1.6 %collective-permute-start = (bf16[264,4,128]{2,0,1:T(8,128)(2,1)}, bf16[264,4,128]{2,0,1:T(8,128)(2,1)}, u32[]{:S(2)}, u32[]{:S(2)}) collective-permute-start(bf16[264,4,128]{2,0,1:T(8,128)(2,1)} %pad_maximum_fusion.1), channel_id=1, source_target_pairs={{0,4},{4,8},{8,12},{12,0},{1,5},{5,9},{9,13},{13,1},{2,6},{6,10},{... | collective-permute-start | bytes 811016 | tf_op jit(solution)/shard_map/ppermute | solution.py:152
  18.5 2.2 %collective-permute-start.1 = (bf16[264,4,128]{2,0,1:T(8,128)(2,1)}, bf16[264,4,128]{2,0,1:T(8,128)(2,1)}, u32[]{:S(2)}, u32[]{:S(2)}) collective-permute-start(bf16[264,4,128]{2,0,1:T(8,128)(2,1)} %pad_maximum_fusion.1), channel_id=1, source_target_pairs={{0,12},{4,0},{8,4},{12,8},{1,13},{5,1},{9,5},{13,9},{2,14},{6,2},{... | collective-permute-start | bytes 811016 | tf_op jit(solution)/shard_map/ppermute | solution.py:152
  20.8 0.8 collective-permute-start.2
  21.6 0.7 fusion.88
  22.4 0.6 slice_bitcast_fusion.16
  23.1 0.7 broadcast_multiply_fusion.5
  23.8 0.7 dynamic-slice_select_fusion.4
  24.5 0.2 copy.206
  24.7 0.2 copy.207
  25.0 3.4 %collective-permute-done = bf16[264,4,128]{2,0,1:T(8,128)(2,1)} collective-permute-done((bf16[264,4,128]{2,0,1:T(8,128)(2,1)}, bf16[264,4,128]{2,0,1:T(8,128)(2,1)}, u32[]{:S(2)}, u32[]{:S(2)}) %collective-permute-start) | collective-permute-done | bytes 270368 | tf_op jit(solution)/shard_map/ppermute | solution.py:152
  28.4 0.7 slice.356
  29.1 0.6 reshape.664
  29.7 0.2 fusion.91
  29.9 3.1 %collective-permute-done.1 = bf16[264,4,128]{2,0,1:T(8,128)(2,1)} collective-permute-done((bf16[264,4,128]{2,0,1:T(8,128)(2,1)}, bf16[264,4,128]{2,0,1:T(8,128)(2,1)}, u32[]{:S(2)}, u32[]{:S(2)}) %collective-permute-start.1) | collective-permute-done | bytes 270368 | tf_op jit(solution)/shard_map/ppermute | solution.py:152
  33.1 0.7 slice.358
  33.8 0.6 reshape.665
  34.5 1.0 %slice.360 = bf16[256,4,128]{2,0,1:T(8,128)(2,1)S(1)} slice(bf16[264,4,128]{2,0,1:T(8,128)(2,1)} %collective-permute-done), slice={[0:256], [0:4], [0:128]} | slice | bytes 524288 | tf_op jit(solution)/shard_map/slice | solution.py:153
  35.4 1.0 %slice.361 = bf16[256,4,128]{2,0,1:T(8,128)(2,1)S(1)} slice(bf16[264,4,128]{2,0,1:T(8,128)(2,1)} %collective-permute-done.1), slice={[0:256], [0:4], [0:128]} | slice | bytes 524288 | tf_op jit(solution)/shard_map/slice | solution.py:153
  36.4 8.5 %collective-permute-done.2 = bf16[256,4,128]{2,0,1:T(8,128)(2,1)} collective-permute-done((bf16[256,4,128]{2,0,1:T(8,128)(2,1)}, bf16[256,4,128]{2,0,1:T(8,128)(2,1)}, u32[]{:S(2)}, u32[]{:S(2)}) %collective-permute-start.2) | collective-permute-done | bytes 262176 | tf_op jit(solution)/shard_map/ppermute | solution.py:152
  44.9 1.0 %pad_maximum_fusion = bf16[4,2,2,64,4,128]{5,3,0,4,2,1:T(8,128)(2,1)S(1)} fusion(bf16[1,2,2,64,4,128]{5,3,0,4,2,1:T(8,128)(2,1)S(1)} %copy-done.4, bf16[1,2,2,64,4,128]{5,3,2,1,4,0:T(8,128)(2,1)S(1)} %bitcast.214, bf16[1,2,2,64,4,128]{5,3,2,1,4,0:T(8,128)(2,1)} %bitcast.20, bf16[1,2,2,64,4,128]{5,3,2,1,4,0:T(8,128)(2,1)S(1)} %bitcast.215), kind=kLoop, calls=%fused_computation.53 | loop fusion | flops 4194304 | bytes 2097152 | tf_op jit(solution)/shard_map/stack | solution.py:158
  45.9 0.9 fusion
  46.8 0.5 fusion.41
  47.4 0.3 copy.171
  47.8 0.2 fusion.6
  48.2 0.6 fusion.102
  48.8 0.2 fusion.3
  49.0 0.7 collective-permute-done.3
  49.8 1.2 %collective-permute-start.4 = (bf16[128,528]{0,1:T(8,128)(2,1)S(1)}, bf16[128,528]{0,1:T(8,128)(2,1)}, u32[]{:S(2)}, u32[]{:S(2)}) collective-permute-start(bf16[128,528]{0,1:T(8,128)(2,1)S(1)} %bitcast_convert_fusion), channel_id=1, source_target_pairs={{0,2},{1,3},{2,0},{3,1},{4,6},{5,7},{6,4},{7,5},{8,10},{9,11},{10,... | collective-permute-start | bytes 405512 | tf_op jit(solution)/shard_map/ppermute | solution.py:56
  51.0 0.9 dynamic-slice_select_fusion
  52.2 3.4 %collective-permute-done.4 = bf16[128,528]{0,1:T(8,128)(2,1)} collective-permute-done((bf16[128,528]{0,1:T(8,128)(2,1)S(1)}, bf16[128,528]{0,1:T(8,128)(2,1)}, u32[]{:S(2)}, u32[]{:S(2)}) %collective-permute-start.4) | collective-permute-done | bytes 135200 | tf_op jit(solution)/shard_map/ppermute | solution.py:56
  55.6 0.9 %bitcast_add_fusion.2 = f32[128,528]{0,1:T(8,128)S(1)} fusion(f32[2,128,528]{1,2,0:T(8,128)S(1)} %bitcast_add_fusion, s32[]{:T(128)S(6)} %select_n.94, bf16[128,528]{0,1:T(8,128)(2,1)} %collective-permute-done.4, pred[]{:T(512)S(6)} %and.60), kind=kLoop, calls=%fused_computation.106 | loop fusion | flops 202752 | bytes 675845 | tf_op jit(solution)/shard_map/add | solution.py:56
  56.7 0.2 fusion.61
  56.9 7.0 %all_gather.10 = bf16[512,4,130]{0,2,1:T(8,128)(2,1)S(1)} all-gather(bf16[128,4,130]{0,2,1:T(8,128)(2,1)S(1)} %fusion.61), channel_id=1, replica_groups=mesh['member'=2,'lon'=4,'lev'=4] {'lev'}, dimensions={0}, use_global_device_ids=true | all-gather | bytes 665600 | tf_op jit(solution)/shard_map/all_gather | solution.py:34
  63.9 0.2 fusion.8
  64.2 0.2 fusion.10
  64.5 0.8 copy-done.32
  65.4 0.7 fusion.20
  66.1 0.3 copy-done.3
  66.3 0.3 fusion.7
  66.7 0.4 collective-permute-start.5
  67.1 0.3 fusion.5
  67.5 0.8 collective-permute-done.5
  68.5 1.0 %collective-permute-start.6 = (bf16[128,520]{0,1:T(8,128)(2,1)S(1)}, bf16[128,520]{0,1:T(8,128)(2,1)S(1)}, u32[]{:S(2)}, u32[]{:S(2)}) collective-permute-start(bf16[128,520]{0,1:T(8,128)(2,1)S(1)} %bitcast_convert_fusion.1), channel_id=1, source_target_pairs={{0,2},{1,3},{2,0},{3,1},{4,6},{5,7},{6,4},{7,5},{8,10},{9,11},{10,... | collective-permute-start | bytes 399368 | tf_op jit(solution)/shard_map/ppermute | solution.py:56
  69.5 4.9 %collective-permute-done.6 = bf16[128,520]{0,1:T(8,128)(2,1)S(1)} collective-permute-done((bf16[128,520]{0,1:T(8,128)(2,1)S(1)}, bf16[128,520]{0,1:T(8,128)(2,1)S(1)}, u32[]{:S(2)}, u32[]{:S(2)}) %collective-permute-start.6) | collective-permute-done | bytes 133152 | tf_op jit(solution)/shard_map/ppermute | solution.py:56
  74.6 0.2 fusion.77
  74.8 6.6 %all_gather.11 = bf16[512,4,128]{0,2,1:T(8,128)(2,1)S(1)} all-gather(bf16[128,4,128]{0,2,1:T(8,128)(2,1)S(1)} %fusion.77), channel_id=1, replica_groups=mesh['member'=2,'lon'=4,'lev'=4] {'lev'}, dimensions={0}, use_global_device_ids=true | all-gather | bytes 655360 | tf_op jit(solution)/shard_map/all_gather | solution.py:34
  81.8 0.7 fusion.34
  82.5 0.3 convolution_convert_fusion.4
  83.0 0.4 collective-permute-start.7
  83.4 0.3 convolution_convert_fusion.5
  83.9 0.7 collective-permute-done.7
  84.7 1.2 %collective-permute-start.8 = (bf16[128,512]{0,1:T(8,128)(2,1)S(1)}, bf16[128,512]{0,1:T(8,128)(2,1)S(1)}, u32[]{:S(2)}, u32[]{:S(2)}) collective-permute-start(bf16[128,512]{0,1:T(8,128)(2,1)S(1)} %bitcast_convert_fusion.2), channel_id=1, source_target_pairs={{0,2},{1,3},{2,0},{3,1},{4,6},{5,7},{6,4},{7,5},{8,10},{9,11},{10,... | collective-permute-start | bytes 393224 | tf_op jit(solution)/shard_map/ppermute | solution.py:56
  85.8 4.6 %collective-permute-done.8 = bf16[128,512]{0,1:T(8,128)(2,1)S(1)} collective-permute-done((bf16[128,512]{0,1:T(8,128)(2,1)S(1)}, bf16[128,512]{0,1:T(8,128)(2,1)S(1)}, u32[]{:S(2)}, u32[]{:S(2)}) %collective-permute-start.8) | collective-permute-done | bytes 131104 | tf_op jit(solution)/shard_map/ppermute | solution.py:56
  90.6 0.8 copy.190
  (117 shorter events, 3.0 us)
Async XLA Ops:
  0.0 12.1 %copy-start = (bf16[3,128,512]{2,1,0:T(8,128)(2,1)S(1)}, bf16[3,128,512]{2,1,0:T(8,128)(2,1)}, u32[]{:S(2)}) copy-start(bf16[3,128,512]{2,1,0:T(8,128)(2,1)} %param.20) | copy-start | bytes 1179652
  0.0 10.5 %copy-start.28 = (f32[512]{0:T(512)S(1)}, f32[512]{0:T(512)}, u32[]{:S(2)}) copy-start(f32[512]{0:T(512)} %param.19) | copy-start | bytes 6148
  13.7 8.6 %copy-start.8 = (bf16[128,512]{1,0:T(8,128)(2,1)S(1)}, bf16[128,512]{1,0:T(8,128)(2,1)}, u32[]{:S(2)}) copy-start(bf16[128,512]{1,0:T(8,128)(2,1)} %param.21) | copy-start | bytes 393220
  13.7 8.7 %copy-start.9 = (f32[2,9,128]{2,0,1:T(2,128)S(1)}, f32[2,9,128]{2,0,1:T(2,128)}, u32[]{:S(2)}) copy-start(f32[2,9,128]{2,0,1:T(2,128)} %param.22) | copy-start | bytes 27652
  13.8 9.3 %copy-start.1 = (bf16[2,512,512]{2,1,0:T(8,128)(2,1)S(1)}, bf16[2,512,512]{2,1,0:T(8,128)(2,1)}, u32[]{:S(2)}) copy-start(bf16[2,512,512]{2,1,0:T(8,128)(2,1)} %param.25) | copy-start | bytes 3145732
  16.9 11.4 %collective-permute-start = (bf16[264,4,128]{2,0,1:T(8,128)(2,1)}, bf16[264,4,128]{2,0,1:T(8,128)(2,1)}, u32[]{:S(2)}, u32[]{:S(2)}) collective-permute-start(bf16[264,4,128]{2,0,1:T(8,128)(2,1)} %pad_maximum_fusion.1), channel_id=1, source_target_pairs={{0,4},{4,8},{8,12},{12,0},{1,5},{5,9},{9,13},{13,1},{2,6},{6,10},{... | collective-permute-start | bytes 811016 | tf_op jit(solution)/shard_map/ppermute | solution.py:152
  18.5 14.6 %collective-permute-start.1 = (bf16[264,4,128]{2,0,1:T(8,128)(2,1)}, bf16[264,4,128]{2,0,1:T(8,128)(2,1)}, u32[]{:S(2)}, u32[]{:S(2)}) collective-permute-start(bf16[264,4,128]{2,0,1:T(8,128)(2,1)} %pad_maximum_fusion.1), channel_id=1, source_target_pairs={{0,12},{4,0},{8,4},{12,8},{1,13},{5,1},{9,5},{13,9},{2,14},{6,2},{... | collective-permute-start | bytes 811016 | tf_op jit(solution)/shard_map/ppermute | solution.py:152
  20.8 24.1 %collective-permute-start.2 = (bf16[256,4,128]{2,0,1:T(8,128)(2,1)}, bf16[256,4,128]{2,0,1:T(8,128)(2,1)}, u32[]{:S(2)}, u32[]{:S(2)}) collective-permute-start(bf16[256,4,128]{2,0,1:T(8,128)(2,1)} %bitcast.6), channel_id=1, source_target_pairs={{0,8},{4,12},{8,0},{12,4},{1,9},{5,13},{9,1},{13,5},{2,10},{6,14},... | collective-permute-start | bytes 786440 | tf_op jit(solution)/shard_map/ppermute | solution.py:152
  33.8 11.1 %copy-start.4 = (bf16[1,2,2,64,4,128]{5,3,0,4,2,1:T(8,128)(2,1)S(1)}, bf16[1,2,2,64,4,128]{5,3,0,4,2,1:T(8,128)(2,1)}, u32[]{:S(2)}) copy-start(bf16[1,2,2,64,4,128]{5,3,0,4,2,1:T(8,128)(2,1)} %get-tuple-element.86) | copy-start | bytes 786436
  36.4 9.5 %copy-start.5 = (bf16[2,64,4,128]{3,1,2,0:T(8,128)(2,1)S(1)}, bf16[2,64,4,128]{3,1,2,0:T(8,128)(2,1)}, u32[]{:S(2)}) copy-start(bf16[2,64,4,128]{3,1,2,0:T(8,128)(2,1)} %fusion.88) | copy-start | bytes 393220
  46.8 1.0 %copy-start.7 = (bf16[128,2,1,128]{0,3,2,1:T(8,128)(2,1)S(1)}, bf16[128,2,1,128]{0,3,2,1:T(8,128)(2,1)}, u32[]{:S(2)}) copy-start(bf16[128,2,1,128]{0,3,2,1:T(8,128)(2,1)} %get-tuple-element.88) | copy-start | bytes 196612
  47.4 0.8 copy-start.24
  47.4 1.4 %copy-start.6 = (bf16[128,2,1,128]{0,3,2,1:T(8,128)(2,1)S(1)}, bf16[128,2,1,128]{0,3,2,1:T(8,128)(2,1)}, u32[]{:S(2)}) copy-start(bf16[128,2,1,128]{0,3,2,1:T(8,128)(2,1)} %get-tuple-element.89) | copy-start | bytes 196612
  48.1 1.6 %collective-permute-start.3 = (bf16[2,128,528]{1,2,0:T(8,128)(2,1)S(1)}, bf16[2,128,528]{1,2,0:T(8,128)(2,1)S(1)}, u32[]{:S(2)}, u32[]{:S(2)}) collective-permute-start(bf16[2,128,528]{1,2,0:T(8,128)(2,1)S(1)} %bitcast.221), channel_id=1, source_target_pairs={{0,1},{1,0},{2,3},{3,2},{4,5},{5,4},{6,7},{7,6},{8,9},{9,8},{10,11... | collective-permute-start | bytes 811016 | tf_op jit(solution)/shard_map/ppermute | solution.py:51
  49.8 5.8 %collective-permute-start.4 = (bf16[128,528]{0,1:T(8,128)(2,1)S(1)}, bf16[128,528]{0,1:T(8,128)(2,1)}, u32[]{:S(2)}, u32[]{:S(2)}) collective-permute-start(bf16[128,528]{0,1:T(8,128)(2,1)S(1)} %bitcast_convert_fusion), channel_id=1, source_target_pairs={{0,2},{1,3},{2,0},{3,1},{4,6},{5,7},{6,4},{7,5},{8,10},{9,11},{10,... | collective-permute-start | bytes 405512 | tf_op jit(solution)/shard_map/ppermute | solution.py:56
  52.1 4.5 %copy-start.18 = (f32[128,4]{0,1:T(4,128)S(1)}, f32[128,4]{0,1:T(4,128)}, u32[]{:S(2)}) copy-start(f32[128,4]{0,1:T(4,128)} %get-tuple-element.115) | copy-start | bytes 6148
  52.1 4.6 %copy-start.19 = (f32[128,4]{0,1:T(4,128)S(1)}, f32[128,4]{0,1:T(4,128)}, u32[]{:S(2)}) copy-start(f32[128,4]{0,1:T(4,128)} %get-tuple-element.116) | copy-start | bytes 6148
  52.1 4.6 %copy-start.20 = (f32[128,4]{0,1:T(4,128)S(1)}, f32[128,4]{0,1:T(4,128)}, u32[]{:S(2)}) copy-start(f32[128,4]{0,1:T(4,128)} %get-tuple-element.117) | copy-start | bytes 6148
  52.1 4.5 %copy-start.21 = (f32[128,4]{0,1:T(4,128)S(1)}, f32[128,4]{0,1:T(4,128)}, u32[]{:S(2)}) copy-start(f32[128,4]{0,1:T(4,128)} %get-tuple-element.118) | copy-start | bytes 6148
  52.1 4.5 %copy-start.22 = (f32[128,4]{0,1:T(4,128)S(1)}, f32[128,4]{0,1:T(4,128)}, u32[]{:S(2)}) copy-start(f32[128,4]{0,1:T(4,128)} %get-tuple-element.119) | copy-start | bytes 6148
  52.1 4.5 %copy-start.23 = (f32[128,4]{0,1:T(4,128)S(1)}, f32[128,4]{0,1:T(4,128)}, u32[]{:S(2)}) copy-start(f32[128,4]{0,1:T(4,128)} %get-tuple-element.125) | copy-start | bytes 6148
  52.1 4.5 %copy-start.29 = (f32[128]{0:T(128)S(1)}, f32[128]{0:T(128)}, u32[]{:S(2)}) copy-start(f32[128]{0:T(128)} %get-tuple-element.102) | copy-start | bytes 1540
  52.1 4.5 %copy-start.30 = (f32[128]{0:T(128)S(1)}, f32[128]{0:T(128)}, u32[]{:S(2)}) copy-start(f32[128]{0:T(128)} %get-tuple-element.105) | copy-start | bytes 1540
  52.2 4.5 %copy-start.31 = (f32[128]{0:T(128)S(1)}, f32[128]{0:T(128)}, u32[]{:S(2)}) copy-start(f32[128]{0:T(128)} %get-tuple-element.108) | copy-start | bytes 1540
  56.7 7.5 %copy-start.11 = (f32[1,512]{1,0:T(1,128)S(1)}, f32[1,512]{1,0:T(1,128)}, u32[]{:S(2)}) copy-start(f32[1,512]{1,0:T(1,128)} %get-tuple-element.113) | copy-start | bytes 6148
  64.1 1.2 %copy-start.32 = (bf16[2,512,512]{2,1,0:T(8,128)(2,1)S(1)}, bf16[2,512,512]{2,1,0:T(8,128)(2,1)}, u32[]{:S(2)}) copy-start(bf16[2,512,512]{2,1,0:T(8,128)(2,1)} %param.24) | copy-start | bytes 3145732
  65.4 0.9 %copy-start.3 = (bf16[512,2,1,128]{0,3,2,1:T(8,128)(2,1)S(1)}, bf16[512,2,1,128]{0,3,2,1:T(8,128)(2,1)}, u32[]{:S(2)}) copy-start(bf16[512,2,1,128]{0,3,2,1:T(8,128)(2,1)} %get-tuple-element.129) | copy-start | bytes 786436
  66.0 1.1 %copy-start.2 = (bf16[512,2,1,128]{0,3,2,1:T(8,128)(2,1)S(1)}, bf16[512,2,1,128]{0,3,2,1:T(8,128)(2,1)}, u32[]{:S(2)}) copy-start(bf16[512,2,1,128]{0,3,2,1:T(8,128)(2,1)} %get-tuple-element.128) | copy-start | bytes 786436
  66.7 1.6 %collective-permute-start.5 = (bf16[2,128,520]{1,2,0:T(8,128)(2,1)S(1)}, bf16[2,128,520]{1,2,0:T(8,128)(2,1)S(1)}, u32[]{:S(2)}, u32[]{:S(2)}) collective-permute-start(bf16[2,128,520]{1,2,0:T(8,128)(2,1)S(1)} %bitcast.222), channel_id=1, source_target_pairs={{0,1},{1,0},{2,3},{3,2},{4,5},{5,4},{6,7},{7,6},{8,9},{9,8},{10,11... | collective-permute-start | bytes 798728 | tf_op jit(solution)/shard_map/ppermute | solution.py:51
  68.3 6.1 %copy-start.12 = (f32[128,4]{0,1:T(4,128)S(1)}, f32[128,4]{0,1:T(4,128)}, u32[]{:S(2)}) copy-start(f32[128,4]{0,1:T(4,128)} %get-tuple-element.114) | copy-start | bytes 6148
  68.4 6.1 %copy-start.13 = (f32[128,4]{0,1:T(4,128)S(1)}, f32[128,4]{0,1:T(4,128)}, u32[]{:S(2)}) copy-start(f32[128,4]{0,1:T(4,128)} %get-tuple-element.120) | copy-start | bytes 6148
  68.4 6.1 %copy-start.14 = (f32[128,4]{0,1:T(4,128)S(1)}, f32[128,4]{0,1:T(4,128)}, u32[]{:S(2)}) copy-start(f32[128,4]{0,1:T(4,128)} %get-tuple-element.121) | copy-start | bytes 6148
  68.4 6.1 %copy-start.15 = (f32[128,4]{0,1:T(4,128)S(1)}, f32[128,4]{0,1:T(4,128)}, u32[]{:S(2)}) copy-start(f32[128,4]{0,1:T(4,128)} %get-tuple-element.122) | copy-start | bytes 6148
  68.4 6.1 %copy-start.16 = (f32[128,4]{0,1:T(4,128)S(1)}, f32[128,4]{0,1:T(4,128)}, u32[]{:S(2)}) copy-start(f32[128,4]{0,1:T(4,128)} %get-tuple-element.123) | copy-start | bytes 6148
  68.4 6.1 %copy-start.17 = (f32[128,4]{0,1:T(4,128)S(1)}, f32[128,4]{0,1:T(4,128)}, u32[]{:S(2)}) copy-start(f32[128,4]{0,1:T(4,128)} %get-tuple-element.124) | copy-start | bytes 6148
  68.4 6.1 %copy-start.25 = (f32[128]{0:T(128)S(1)}, f32[128]{0:T(128)}, u32[]{:S(2)}) copy-start(f32[128]{0:T(128)} %get-tuple-element.97) | copy-start | bytes 1540
  68.4 6.1 %copy-start.26 = (f32[128]{0:T(128)S(1)}, f32[128]{0:T(128)}, u32[]{:S(2)}) copy-start(f32[128]{0:T(128)} %get-tuple-element.100) | copy-start | bytes 1540
  68.4 6.1 %copy-start.27 = (f32[128]{0:T(128)S(1)}, f32[128]{0:T(128)}, u32[]{:S(2)}) copy-start(f32[128]{0:T(128)} %get-tuple-element.111) | copy-start | bytes 1540
  68.5 5.9 %collective-permute-start.6 = (bf16[128,520]{0,1:T(8,128)(2,1)S(1)}, bf16[128,520]{0,1:T(8,128)(2,1)S(1)}, u32[]{:S(2)}, u32[]{:S(2)}) collective-permute-start(bf16[128,520]{0,1:T(8,128)(2,1)S(1)} %bitcast_convert_fusion.1), channel_id=1, source_target_pairs={{0,2},{1,3},{2,0},{3,1},{4,6},{5,7},{6,4},{7,5},{8,10},{9,11},{10,... | collective-permute-start | bytes 399368 | tf_op jit(solution)/shard_map/ppermute | solution.py:56
  74.6 7.0 %copy-start.10 = (f32[1,512]{1,0:T(1,128)S(1)}, f32[1,512]{1,0:T(1,128)}, u32[]{:S(2)}) copy-start(f32[1,512]{1,0:T(1,128)} %get-tuple-element.112) | copy-start | bytes 6148
  83.0 1.6 %collective-permute-start.7 = (bf16[2,128,512]{1,2,0:T(8,128)(2,1)S(1)}, bf16[2,128,512]{1,2,0:T(8,128)(2,1)S(1)}, u32[]{:S(2)}, u32[]{:S(2)}) collective-permute-start(bf16[2,128,512]{1,2,0:T(8,128)(2,1)S(1)} %copy.188), channel_id=1, source_target_pairs={{0,1},{1,0},{2,3},{3,2},{4,5},{5,4},{6,7},{7,6},{8,9},{9,8},{10,11... | collective-permute-start | bytes 786440 | tf_op jit(solution)/shard_map/ppermute | solution.py:51
  84.7 5.8 %collective-permute-start.8 = (bf16[128,512]{0,1:T(8,128)(2,1)S(1)}, bf16[128,512]{0,1:T(8,128)(2,1)S(1)}, u32[]{:S(2)}, u32[]{:S(2)}) collective-permute-start(bf16[128,512]{0,1:T(8,128)(2,1)S(1)} %bitcast_convert_fusion.2), channel_id=1, source_target_pairs={{0,2},{1,3},{2,0},{3,1},{4,6},{5,7},{6,4},{7,5},{8,10},{9,11},{10,... | collective-permute-start | bytes 393224 | tf_op jit(solution)/shard_map/ppermute | solution.py:56

commit v14 on v12

--- a/solution.py
+++ b/solution.py
@@ -76,11 +76,16 @@
 
 def gather_half(values):
     devices = lax.axis_size("lev")
-    core = lax.axis_index("lev") % 2
-    mine = values.reshape(devices // 2, -1, *values.shape[1:])
-    theirs = lax.ppermute(mine, "lev", [(i, i ^ 1) for i in range(devices)])
-    both = jnp.where(core == 0, jnp.stack([mine, theirs], axis=1), jnp.stack([theirs, mine], axis=1))
-    return both.reshape(-1, *values.shape[1:])
+    theirs = lax.ppermute(values, "lev", [(i, i ^ 1) for i in range(devices)])
+    return jnp.concatenate([values, theirs], axis=0)
+
+
+def mine_first(values, axis):
+    devices = lax.axis_size("lev")
+    grouped = values.reshape(*values.shape[:axis], devices // 2, 2, -1, *values.shape[axis + 1 :])
+    swapped = jnp.flip(grouped, axis=axis + 1)
+    chosen = jnp.where(lax.axis_index("lev") % 2 == 0, grouped, swapped)
+    return jnp.moveaxis(chosen, axis + 1, axis).reshape(values.shape)
 
 
 def half_weights(weights):
@@ -144,12 +149,11 @@
                 stencil_sum = stencil_sum + tap_row * shifted
     smoothed = stencil_sum.astype(jnp.bfloat16)
     full_channels = gather_half(smoothed)
-    block_normed = norm_channels(full_channels.astype(jnp.float32), block_gain[block_index]).astype(
-        jnp.bfloat16
-    )
+    gain = mine_first(block_gain[block_index], 0)
+    block_normed = norm_channels(full_channels.astype(jnp.float32), gain).astype(jnp.bfloat16)
     block_normed = block_normed.reshape(full_channels.shape[0], -1)
     hidden = jax.nn.gelu(
-        jnp.dot(up_weight[block_index], block_normed, preferred_element_type=jnp.float32)
+        jnp.dot(mine_first(up_weight[block_index], 1), block_normed, preferred_element_type=jnp.float32)
     ).astype(jnp.bfloat16)
     partial = group_partial(down_weight[block_index], hidden)
     center = state[:, :, 1:-1]

time: 95 us -> 88.7 us (0.934)
  other arithmetic: 12.4 us -> 7.48 us
  waiting for transfers between devices: 46 us -> 41.5 us
  local copies, waits for them, and re-layouts: 10.5 us -> 13.4 us
    reduce_sum x3, other arithmetic: 5.28 us -> 0.95 us  [norm_channels(): jnp.mean(values * values, axis=0, keepdims=True) + epsilon]
    ppermute x3, waiting for transfers between devices: 20.5 us -> 16.8 us  [per_device(): got = lax.ppermute(sent, 'lon', pairs)]
    ppermute x1, waiting for transfers between devices: 2.48 us -> 0.01 us  [half_weights(): stacked.append(lax.ppermute(weights, 'lev', pairs))]
    unnamed x14 -> x30, local copies, waits for them, and re-layouts: 0.36 us -> 2.62 us
    convert_element_type x2 -> x0, other arithmetic: 1.44 us -> none  [block_apply(): norm_channels(full_channels.astype(jnp.float32), block_gain[block_index])]
    ppermute x2, waiting for transfers between devices: 1.4 us -> 2.55 us  [reduce_half(): lax.ppermute(theirs, 'lev', [(i, i ^ 1) for i in range(devices)])]
    slice x2, local copies, waits for them, and re-layouts: 0.04 us -> 1.01 us  [per_device(): pieces.append(got[:key_value.shape[0]])]
  transfers between devices with their start and end apart: 12 -> 12, of which waited for: 11 -> 11; matrix products, arithmetic and copies ran while one was open for 3% -> 12% of each run, Pallas kernels for 0% -> 0%
where the time goes in v14:
time: 88.7 us; the launch traced here: 88.3 us
  waiting for transfers between devices  41.5 us (47%)
  local copies, waits for them, and re-layouts  13.4 us (15%)
  starting transfers between devices  9.89 us (11%)
  blocking collectives  8.95 us (10%)
  other arithmetic  7.48 us (8%)
  matrix products  6.28 us (7%)
    ppermute x3, waiting for transfers between devices, per_device(): got = lax.ppermute(sent, 'lon', pairs)  16.8 us
    ppermute x2, waiting for transfers between devices, reduce_half(): total = total + lax.ppermute(pair, 'lev', pairs).astype(jnp.float32)  14 us
    all_gather x1, blocking collectives, gather_channels(): return lax.all_gather(values, 'lev', axis=0, tiled=True)  8.95 us
    ppermute x3, starting transfers between devices, per_device(): got = lax.ppermute(sent, 'lon', pairs)  4.62 us
    dot_general x3, matrix products, group_partial(): lax.dot_general(weight, activation, (((0,), (0,)), ((), ())), preferred_e...  4.48 us
    ppermute x1, waiting for transfers between devices, scatter_sum(): total = total + lax.ppermute(sent, axis, pairs).astype(jnp.float32)  4.17 us
    ppermute x2, waiting for transfers between devices, gather_half(): theirs = lax.ppermute(values, 'lev', [(i, i ^ 1) for i in range(devices)])  2.64 us
    unnamed x30, local copies, waits for them, and re-layouts  2.62 us
  transfers between devices with their start and end apart: 12, of which 11 were waited for; matrix products, arithmetic and copies ran while one was open for 12% of the time, Pallas kernels for 0%

profile of v14, /device:TPU:0, one launch (start us, length us, event | category | flops | bytes accessed | tf_op | source)
XLA Modules:
  0.0 88.3 jit_solution(15704722649834708371)
XLA Ops:
  0.0 8.9 %all_gather.3 = bf16[512,4,128]{2,1,0:T(4,128)(2,1)S(1)} all-gather(bf16[128,4,128]{2,1,0:T(4,128)(2,1)} %param.16), channel_id=1, replica_groups=mesh['member'=2,'lon'=4,'lev'=4] {'lev'}, dimensions={0}, use_global_device_ids=true | all-gather | bytes 655360 | tf_op jit(solution)/shard_map/all_gather | solution.py:34
  9.0 0.5 fusion.14
  9.5 1.5 %fusion.67 = bf16[512,4,128,1]{2,1,0,3:T(4,128)(2,1)S(1)} fusion(bf16[512,4,128]{2,1,0:T(4,128)(2,1)S(1)} %all_gather.3, f32[512]{0:T(512)S(1)} %copy-done.12, f32[4,128]{1,0:T(4,128)S(1)} %add_rsqrt_fusion.1), kind=kLoop, calls=%fused_computation.93 | loop fusion | flops 1048576 | bytes 1052672 | tf_op jit(solution)/shard_map/convert_element_type | solution.py:184
  11.1 0.4 convolution_bitcast_fusion
  11.6 0.2 copy.184
  11.9 0.2 broadcast_select_fusion
  12.1 0.2 select_n.116
  12.8 0.3 copy.143
  13.1 0.5 reshape.630
  13.9 0.7 pad_maximum_fusion.1
  14.6 1.6 %collective-permute-start = (bf16[268,4,128]{2,0,1:T(8,128)(2,1)}, bf16[268,4,128]{2,0,1:T(8,128)(2,1)S(1)}, u32[]{:S(2)}, u32[]{:S(2)}) collective-permute-start(bf16[268,4,128]{2,0,1:T(8,128)(2,1)} %pad_maximum_fusion.1), channel_id=1, source_target_pairs={{0,4},{4,8},{8,12},{12,0},{1,5},{5,9},{9,13},{13,1},{2,6},{6,10},{... | collective-permute-start | bytes 823304 | tf_op jit(solution)/shard_map/ppermute | solution.py:201
  16.2 2.2 %collective-permute-start.1 = (bf16[268,4,128]{2,0,1:T(8,128)(2,1)}, bf16[268,4,128]{2,0,1:T(8,128)(2,1)}, u32[]{:S(2)}, u32[]{:S(2)}) collective-permute-start(bf16[268,4,128]{2,0,1:T(8,128)(2,1)} %pad_maximum_fusion.1), channel_id=1, source_target_pairs={{0,12},{4,0},{8,4},{12,8},{1,13},{5,1},{9,5},{13,9},{2,14},{6,2},{... | collective-permute-start | bytes 823304 | tf_op jit(solution)/shard_map/ppermute | solution.py:201
  18.4 0.8 collective-permute-start.2
  19.2 1.1 %collective-permute-start.5 = (f32[2,9,128]{2,0,1:T(2,128)S(1)}, f32[2,9,128]{2,0,1:T(2,128)S(1)}, u32[]{:S(2)}, u32[]{:S(2)}) collective-permute-start(f32[2,9,128]{2,0,1:T(2,128)S(1)} %copy-done.10), channel_id=1, source_target_pairs={{0,2},{1,3},{2,0},{3,1},{4,6},{5,7},{6,4},{7,5},{8,10},{9,11},{10,... | collective-permute-start | bytes 27656 | tf_op jit(solution)/shard_map/ppermute | solution.py:98
  20.4 0.2 copy.187
  20.6 1.0 %copy.190 = bf16[1,512,512]{1,2,0:T(8,128)(2,1)} copy(bf16[1,512,512]{2,1,0:T(8,128)(2,1)S(1)} %get-tuple-element.80) | data formatting | bytes 1048576
  21.7 4.4 %collective-permute-done = bf16[268,4,128]{2,0,1:T(8,128)(2,1)S(1)} collective-permute-done((bf16[268,4,128]{2,0,1:T(8,128)(2,1)}, bf16[268,4,128]{2,0,1:T(8,128)(2,1)S(1)}, u32[]{:S(2)}, u32[]{:S(2)}) %collective-permute-start) | collective-permute-done | bytes 274464 | tf_op jit(solution)/shard_map/ppermute | solution.py:201
  26.1 0.7 copy-done.7
  26.8 0.8 reshape.631
  27.7 0.1 slice.380
  27.9 3.2 %collective-permute-done.1 = bf16[268,4,128]{2,0,1:T(8,128)(2,1)} collective-permute-done((bf16[268,4,128]{2,0,1:T(8,128)(2,1)}, bf16[268,4,128]{2,0,1:T(8,128)(2,1)}, u32[]{:S(2)}, u32[]{:S(2)}) %collective-permute-start.1) | collective-permute-done | bytes 274464 | tf_op jit(solution)/shard_map/ppermute | solution.py:201
  31.1 0.7 slice.375
  31.8 0.8 reshape.632
  32.8 1.0 %slice.378 = bf16[256,4,128]{2,0,1:T(8,128)(2,1)S(1)} slice(bf16[268,4,128]{2,0,1:T(8,128)(2,1)} %collective-permute-done.1), slice={[0:256], [0:4], [0:128]} | slice | bytes 524288 | tf_op jit(solution)/shard_map/slice | solution.py:202
  33.8 9.1 %collective-permute-done.2 = bf16[256,4,128]{2,0,1:T(8,128)(2,1)} collective-permute-done((bf16[256,4,128]{2,0,1:T(8,128)(2,1)S(1)}, bf16[256,4,128]{2,0,1:T(8,128)(2,1)}, u32[]{:S(2)}, u32[]{:S(2)}) %collective-permute-start.2) | collective-permute-done | bytes 262176 | tf_op jit(solution)/shard_map/ppermute | solution.py:201
  42.9 1.0 %pad_maximum_fusion = bf16[4,2,2,64,4,128]{5,3,0,4,2,1:T(8,128)(2,1)S(1)} fusion(bf16[1,2,2,64,4,128]{5,3,0,4,2,1:T(8,128)(2,1)S(1)} %get-tuple-element.88, bf16[1,2,2,64,4,128]{5,3,2,1,4,0:T(8,128)(2,1)S(1)} %bitcast.169, bf16[1,2,2,64,4,128]{5,3,2,1,4,0:T(8,128)(2,1)} %bitcast.13, bf16[1,2,2,64,4,128]{5,3,2,1,4,0:T(8,128)(2,1)S(1)} %bitcast.170), kind=kLoop, calls=%fused_computation.48 | loop fusion | flops 4194304 | bytes 2097152 | tf_op jit(solution)/shard_map/stack | solution.py:207
  43.9 0.9 %fusion = (f32[2,4,132]{2,1,0:T(4,128)S(1)}, f32[2,4,132,4,128]{4,2,3,1,0:T(8,128)S(1)}) fusion(bf16[4,2,2,64,4,128]{5,3,0,4,2,1:T(8,128)(2,1)S(1)} %pad_maximum_fusion, bf16[2,64,4,2]{3,1,2,0:T(8,128)(2,1)S(1)} %copy.156, bf16[2,64,4,128]{3,1,2,0:T(8,128)(2,1)S(1)} %fusion.115, bf16[2,64,4,2]{3,1,2,0:T(8,128)(2,1)S(1)} %copy.155), kind=kOutput, calls=%fused_computation.1 | convolution fusion | flops 70691808 | bytes 3084416 | tf_op jit(solution)/shard_map/hdri,phdrj->hripj/dot_general | solution.py:121
  44.8 0.5 fusion.31
  45.4 0.3 copy.157
  45.6 0.1 reshape.633
  45.8 0.3 fusion.2
  46.2 1.1 %constant_dynamic-slice_fusion.3 = (bf16[2,1,128,528]{2,1,0,3:T(2,128)(2,1)S(1)}, bf16[2,1,128,528]{2,1,0,3:T(2,128)(2,1)S(1)}) fusion(bf16[2,2,128,528]{2,1,0,3:T(2,128)(2,1)S(1)} %reshape.634, s32[]{:T(128)S(6)} %select_n.114, s32[]{:T(128)S(6)} %select_n.154), kind=kLoop, calls=%fused_computation.179 | loop fusion | bytes 1081352 | tf_op jit(solution)/shard_map/jit(_take) | solution.py:66
  47.5 0.2 fusion.64
  47.9 1.1 %collective-permute-done.3 = bf16[2,128,528]{1,2,0:T(8,128)(2,1)S(1)} collective-permute-done((bf16[2,128,528]{1,2,0:T(8,128)(2,1)S(1)}, bf16[2,128,528]{1,2,0:T(8,128)(2,1)S(1)}, u32[]{:S(2)}, u32[]{:S(2)}) %collective-permute-start.3) | collective-permute-done | bytes 270368 | tf_op jit(solution)/shard_map/ppermute | solution.py:68
  49.1 1.2 %collective-permute-start.4 = (bf16[2,128,528]{1,2,0:T(8,128)(2,1)S(1)}, bf16[2,128,528]{1,2,0:T(8,128)(2,1)S(1)}, u32[]{:S(2)}, u32[]{:S(2)}) collective-permute-start(bf16[2,128,528]{1,2,0:T(8,128)(2,1)S(1)} %add_convert_fusion.2), channel_id=1, source_target_pairs={{0,2},{1,3},{2,0},{3,1},{4,6},{5,7},{6,4},{7,5},{8,10},{9,11},{10,... | collective-permute-start | bytes 811016 | tf_op jit(solution)/shard_map/ppermute | solution.py:73
  50.4 0.2 slice.374
  50.7 0.2 copy.147
  50.9 0.2 copy.148
  51.1 6.6 %collective-permute-done.4 = bf16[2,128,528]{1,2,0:T(8,128)(2,1)S(1)} collective-permute-done((bf16[2,128,528]{1,2,0:T(8,128)(2,1)S(1)}, bf16[2,128,528]{1,2,0:T(8,128)(2,1)S(1)}, u32[]{:S(2)}, u32[]{:S(2)}) %collective-permute-start.4) | collective-permute-done | bytes 270368 | tf_op jit(solution)/shard_map/ppermute | solution.py:73
  57.8 0.3 copy.160
  58.1 0.4 reshape_reshape.6
  58.5 0.2 copy-done.5
  58.8 0.4 fusion.43
  59.3 0.2 copy-done.11
  59.7 1.2 %collective-permute-done.6 = bf16[256,4,130]{0,2,1:T(8,128)(2,1)S(1)} collective-permute-done((bf16[256,4,130]{0,2,1:T(8,128)(2,1)S(1)}, bf16[256,4,130]{0,2,1:T(8,128)(2,1)S(1)}, u32[]{:S(2)}, u32[]{:S(2)}) %collective-permute-start.6) | collective-permute-done | bytes 266272 | tf_op jit(solution)/shard_map/ppermute | solution.py:79
  60.8 0.2 multiply_reduce_fusion
  61.3 2.0 %fusion.3 = bf16[512,520]{0,1:T(8,128)(2,1)S(1)} fusion(bf16[512,512]{0,1:T(8,128)(2,1)S(1)} %bitcast.174, bf16[256,520]{0,1:T(8,128)(2,1)S(1)} %concatenate.59, bf16[256,520]{0,1:T(8,128)(2,1)S(1)} %concatenate.58, f32[512]{0:T(512)S(1)} %bitcast.202, f32[520]{0:T(1024)S(1)} %rsqrt.50, bf16[2,512,512]{2,1,0:T(8,128)(2,1)} %param.23), kind=kOutput, calls=%fused_computation.24 | convolution fusion | flops 549785600 | bytes 2117664 | tf_op jit(solution)/shard_map/dot_general | solution.py:104
  63.4 1.1 %constant_dynamic-slice_fusion.1 = (bf16[2,1,128,520]{2,1,0,3:T(2,128)(2,1)S(1)}, bf16[2,1,128,520]{2,1,0,3:T(2,128)(2,1)S(1)}) fusion(bf16[2,2,128,520]{2,1,0,3:T(2,128)(2,1)S(1)} %reshape.636, s32[]{:T(128)S(6)} %select_n.114, s32[]{:T(128)S(6)} %select_n.154), kind=kLoop, calls=%fused_computation.177 | loop fusion | bytes 1064968 | tf_op jit(solution)/shard_map/jit(_take) | solution.py:66
  64.6 0.2 collective-permute-start.7
  64.8 1.4 %collective-permute-done.7 = bf16[2,128,520]{1,2,0:T(8,128)(2,1)S(1)} collective-permute-done((bf16[2,128,520]{1,2,0:T(8,128)(2,1)S(1)}, bf16[2,128,520]{1,2,0:T(8,128)(2,1)S(1)}, u32[]{:S(2)}, u32[]{:S(2)}) %collective-permute-start.7) | collective-permute-done | bytes 266272 | tf_op jit(solution)/shard_map/ppermute | solution.py:68
  66.3 1.2 %collective-permute-start.8 = (bf16[2,128,520]{1,2,0:T(8,128)(2,1)S(1)}, bf16[2,128,520]{1,2,0:T(8,128)(2,1)S(1)}, u32[]{:S(2)}, u32[]{:S(2)}) collective-permute-start(bf16[2,128,520]{1,2,0:T(8,128)(2,1)S(1)} %add_convert_fusion.3), channel_id=1, source_target_pairs={{0,2},{1,3},{2,0},{3,1},{4,6},{5,7},{6,4},{7,5},{8,10},{9,11},{10,... | collective-permute-start | bytes 798728 | tf_op jit(solution)/shard_map/ppermute | solution.py:73
  67.5 7.3 %collective-permute-done.8 = bf16[2,128,520]{1,2,0:T(8,128)(2,1)S(1)} collective-permute-done((bf16[2,128,520]{1,2,0:T(8,128)(2,1)S(1)}, bf16[2,128,520]{1,2,0:T(8,128)(2,1)S(1)}, u32[]{:S(2)}, u32[]{:S(2)}) %collective-permute-start.8) | collective-permute-done | bytes 266272 | tf_op jit(solution)/shard_map/ppermute | solution.py:73
  74.9 0.3 copy.167
  75.1 0.4 reshape_reshape.7
  75.7 0.4 fusion.77
  76.2 1.5 %collective-permute-done.9 = bf16[256,4,128]{0,2,1:T(8,128)(2,1)S(1)} collective-permute-done((bf16[256,4,128]{0,2,1:T(8,128)(2,1)S(1)}, bf16[256,4,128]{0,2,1:T(8,128)(2,1)S(1)}, u32[]{:S(2)}, u32[]{:S(2)}) %collective-permute-start.9) | collective-permute-done | bytes 262176 | tf_op jit(solution)/shard_map/ppermute | solution.py:79
  77.6 0.2 multiply_reduce_fusion.1
  77.8 2.2 %convolution_convert_fusion.2 = bf16[512,512]{0,1:T(8,128)(2,1)S(1)} fusion(bf16[512,512]{0,1:T(8,128)(2,1)S(1)} %bitcast.175, bf16[256,512]{0,1:T(8,128)(2,1)S(1)} %bitcast.179, bf16[256,512]{0,1:T(8,128)(2,1)S(1)} %bitcast.166, bf16[2,512,512]{2,1,0:T(8,128)(2,1)} %param.23, f32[512]{0:T(512)S(1)} %bitcast.203, f32[512]{0:T(512)S(1)} %rsqrt_bitcast_fusion), kind=kOutput, calls=%fused_computation.9 | convolution fusion | flops 541327360 | bytes 2101248 | tf_op jit(solution)/shard_map/dot_general | solution.py:104
  80.1 0.2 collective-permute-start.10
  80.3 1.4 %collective-permute-done.10 = bf16[2,128,512]{2,1,0:T(8,128)(2,1)S(1)} collective-permute-done((bf16[2,128,512]{2,1,0:T(8,128)(2,1)S(1)}, bf16[2,128,512]{2,1,0:T(8,128)(2,1)S(1)}, u32[]{:S(2)}, u32[]{:S(2)}) %collective-permute-start.10) | collective-permute-done | bytes 262176 | tf_op jit(solution)/shard_map/ppermute | solution.py:45
  81.8 1.2 %collective-permute-start.11 = (bf16[128,512]{1,0:T(8,128)(2,1)S(1)}, bf16[128,512]{1,0:T(8,128)(2,1)S(1)}, u32[]{:S(2)}, u32[]{:S(2)}) collective-permute-start(bf16[128,512]{1,0:T(8,128)(2,1)S(1)} %bitcast_convert_fusion), channel_id=1, source_target_pairs={{0,2},{1,3},{2,0},{3,1},{4,6},{5,7},{6,4},{7,5},{8,10},{9,11},{10,... | collective-permute-start | bytes 393224 | tf_op jit(solution)/shard_map/ppermute | solution.py:50
  83.0 0.2 copy.183
  83.2 4.2 %collective-permute-done.11 = bf16[128,512]{1,0:T(8,128)(2,1)S(1)} collective-permute-done((bf16[128,512]{1,0:T(8,128)(2,1)S(1)}, bf16[128,512]{1,0:T(8,128)(2,1)S(1)}, u32[]{:S(2)}, u32[]{:S(2)}) %collective-permute-start.11) | collective-permute-done | bytes 131104 | tf_op jit(solution)/shard_map/ppermute | solution.py:50
  87.5 0.7 fusion.113
  (88 shorter events, 3.2 us)
Async XLA Ops:
  0.0 11.0 %copy-start = (bf16[3,128,512]{2,1,0:T(8,128)(2,1)S(1)}, bf16[3,128,512]{2,1,0:T(8,128)(2,1)}, u32[]{:S(2)}) copy-start(bf16[3,128,512]{2,1,0:T(8,128)(2,1)} %param.18) | copy-start | bytes 1179652
  0.0 9.5 %copy-start.12 = (f32[512]{0:T(512)S(1)}, f32[512]{0:T(512)}, u32[]{:S(2)}) copy-start(f32[512]{0:T(512)} %param.17) | copy-start | bytes 6148
  12.3 1.3 %copy-start.4 = (bf16[256,4,128]{0,2,1:T(8,128)(2,1)}, bf16[256,4,128]{0,2,1:T(8,128)(2,1)S(1)}, u32[]{:S(2)}) copy-start(bf16[256,4,128]{0,2,1:T(8,128)(2,1)S(1)} %select_n.116) | copy-start | bytes 786436
  13.7 5.6 %copy-start.10 = (f32[2,9,128]{2,0,1:T(2,128)S(1)}, f32[2,9,128]{2,0,1:T(2,128)}, u32[]{:S(2)}) copy-start(f32[2,9,128]{2,0,1:T(2,128)} %param.20) | copy-start | bytes 27652
  13.7 6.6 %copy-start.6 = (bf16[2,512,512]{2,1,0:T(8,128)(2,1)S(1)}, bf16[2,512,512]{2,1,0:T(8,128)(2,1)}, u32[]{:S(2)}) copy-start(bf16[2,512,512]{2,1,0:T(8,128)(2,1)} %param.22) | copy-start | bytes 3145732
  14.6 11.5 %collective-permute-start = (bf16[268,4,128]{2,0,1:T(8,128)(2,1)}, bf16[268,4,128]{2,0,1:T(8,128)(2,1)S(1)}, u32[]{:S(2)}, u32[]{:S(2)}) collective-permute-start(bf16[268,4,128]{2,0,1:T(8,128)(2,1)} %pad_maximum_fusion.1), channel_id=1, source_target_pairs={{0,4},{4,8},{8,12},{12,0},{1,5},{5,9},{9,13},{13,1},{2,6},{6,10},{... | collective-permute-start | bytes 823304 | tf_op jit(solution)/shard_map/ppermute | solution.py:201
  16.2 14.9 %collective-permute-start.1 = (bf16[268,4,128]{2,0,1:T(8,128)(2,1)}, bf16[268,4,128]{2,0,1:T(8,128)(2,1)}, u32[]{:S(2)}, u32[]{:S(2)}) collective-permute-start(bf16[268,4,128]{2,0,1:T(8,128)(2,1)} %pad_maximum_fusion.1), channel_id=1, source_target_pairs={{0,12},{4,0},{8,4},{12,8},{1,13},{5,1},{9,5},{13,9},{2,14},{6,2},{... | collective-permute-start | bytes 823304 | tf_op jit(solution)/shard_map/ppermute | solution.py:201
  18.4 24.5 %collective-permute-start.2 = (bf16[256,4,128]{2,0,1:T(8,128)(2,1)S(1)}, bf16[256,4,128]{2,0,1:T(8,128)(2,1)}, u32[]{:S(2)}, u32[]{:S(2)}) collective-permute-start(bf16[256,4,128]{2,0,1:T(8,128)(2,1)S(1)} %bitcast.168), channel_id=1, source_target_pairs={{0,8},{4,12},{8,0},{12,4},{1,9},{5,13},{9,1},{13,5},{2,10},{6,14},... | collective-permute-start | bytes 786440 | tf_op jit(solution)/shard_map/ppermute | solution.py:201
  19.2 28.6 %collective-permute-start.5 = (f32[2,9,128]{2,0,1:T(2,128)S(1)}, f32[2,9,128]{2,0,1:T(2,128)S(1)}, u32[]{:S(2)}, u32[]{:S(2)}) collective-permute-start(f32[2,9,128]{2,0,1:T(2,128)S(1)} %copy-done.10), channel_id=1, source_target_pairs={{0,2},{1,3},{2,0},{3,1},{4,6},{5,7},{6,4},{7,5},{8,10},{9,11},{10,... | collective-permute-start | bytes 27656 | tf_op jit(solution)/shard_map/ppermute | solution.py:98
  26.1 0.7 copy-start.7
  26.8 5.9 %copy-start.8 = (bf16[268,4,128]{2,0,1:T(8,128)(2,1)S(1)}, bf16[268,4,128]{2,0,1:T(8,128)(2,1)}, u32[]{:S(2)}) copy-start(bf16[268,4,128]{2,0,1:T(8,128)(2,1)} %copy-done.7) | copy-start | bytes 823300
  32.7 11.2 %copy-start.2 = (bf16[384,4,4]{2,1,0:T(4,128)(2,1)}, bf16[384,4,4]{2,1,0:T(4,128)(2,1)S(1)}, u32[]{:S(2)}) copy-start(bf16[384,4,4]{2,1,0:T(4,128)(2,1)S(1)} %reshape.632) | copy-start | bytes 36868
  44.8 1.0 %copy-start.9 = (bf16[128,512]{1,0:T(8,128)(2,1)S(1)}, bf16[128,512]{1,0:T(8,128)(2,1)}, u32[]{:S(2)}) copy-start(bf16[128,512]{1,0:T(8,128)(2,1)} %param.19) | copy-start | bytes 393220
  46.2 1.3 %copy-start.1 = (bf16[1,512,512]{1,2,0:T(8,128)(2,1)S(1)}, bf16[1,512,512]{1,2,0:T(8,128)(2,1)}, u32[]{:S(2)}) copy-start(bf16[1,512,512]{1,2,0:T(8,128)(2,1)} %copy.190) | copy-start | bytes 1572868
  47.4 1.6 %collective-permute-start.3 = (bf16[2,128,528]{1,2,0:T(8,128)(2,1)S(1)}, bf16[2,128,528]{1,2,0:T(8,128)(2,1)S(1)}, u32[]{:S(2)}, u32[]{:S(2)}) collective-permute-start(bf16[2,128,528]{1,2,0:T(8,128)(2,1)S(1)} %fusion.104), channel_id=1, source_target_pairs={{0,1},{1,0},{2,3},{3,2},{4,5},{5,4},{6,7},{7,6},{8,9},{9,8},{10,11... | collective-permute-start | bytes 811016 | tf_op jit(solution)/shard_map/ppermute | solution.py:68
  47.7 2.9 %copy-start.3 = (bf16[384,4,4]{2,1,0:T(4,128)(2,1)S(1)}, bf16[384,4,4]{2,1,0:T(4,128)(2,1)}, u32[]{:S(2)}) copy-start(bf16[384,4,4]{2,1,0:T(4,128)(2,1)} %copy-done.2) | copy-start | bytes 36868
  49.1 8.6 %collective-permute-start.4 = (bf16[2,128,528]{1,2,0:T(8,128)(2,1)S(1)}, bf16[2,128,528]{1,2,0:T(8,128)(2,1)S(1)}, u32[]{:S(2)}, u32[]{:S(2)}) collective-permute-start(bf16[2,128,528]{1,2,0:T(8,128)(2,1)S(1)} %add_convert_fusion.2), channel_id=1, source_target_pairs={{0,2},{1,3},{2,0},{3,1},{4,6},{5,7},{6,4},{7,5},{8,10},{9,11},{10,... | collective-permute-start | bytes 811016 | tf_op jit(solution)/shard_map/ppermute | solution.py:73
  57.8 1.0 %copy-start.5 = (bf16[256,4,128]{0,2,1:T(8,128)(2,1)S(1)}, bf16[256,4,128]{0,2,1:T(8,128)(2,1)}, u32[]{:S(2)}) copy-start(bf16[256,4,128]{0,2,1:T(8,128)(2,1)} %copy-done.4) | copy-start | bytes 786436
  58.8 0.7 copy-start.11
  59.2 1.6 %collective-permute-start.6 = (bf16[256,4,130]{0,2,1:T(8,128)(2,1)S(1)}, bf16[256,4,130]{0,2,1:T(8,128)(2,1)S(1)}, u32[]{:S(2)}, u32[]{:S(2)}) collective-permute-start(bf16[256,4,130]{0,2,1:T(8,128)(2,1)S(1)} %fusion.43), channel_id=1, source_target_pairs={{0,1},{1,0},{2,3},{3,2},{4,5},{5,4},{6,7},{7,6},{8,9},{9,8},{10,11... | collective-permute-start | bytes 798728 | tf_op jit(solution)/shard_map/ppermute | solution.py:79
  64.6 1.6 %collective-permute-start.7 = (bf16[2,128,520]{1,2,0:T(8,128)(2,1)S(1)}, bf16[2,128,520]{1,2,0:T(8,128)(2,1)S(1)}, u32[]{:S(2)}, u32[]{:S(2)}) collective-permute-start(bf16[2,128,520]{1,2,0:T(8,128)(2,1)S(1)} %fusion.106), channel_id=1, source_target_pairs={{0,1},{1,0},{2,3},{3,2},{4,5},{5,4},{6,7},{7,6},{8,9},{9,8},{10,11... | collective-permute-start | bytes 798728 | tf_op jit(solution)/shard_map/ppermute | solution.py:68
  66.3 8.5 %collective-permute-start.8 = (bf16[2,128,520]{1,2,0:T(8,128)(2,1)S(1)}, bf16[2,128,520]{1,2,0:T(8,128)(2,1)S(1)}, u32[]{:S(2)}, u32[]{:S(2)}) collective-permute-start(bf16[2,128,520]{1,2,0:T(8,128)(2,1)S(1)} %add_convert_fusion.3), channel_id=1, source_target_pairs={{0,2},{1,3},{2,0},{3,1},{4,6},{5,7},{6,4},{7,5},{8,10},{9,11},{10,... | collective-permute-start | bytes 798728 | tf_op jit(solution)/shard_map/ppermute | solution.py:73
  76.0 1.6 %collective-permute-start.9 = (bf16[256,4,128]{0,2,1:T(8,128)(2,1)S(1)}, bf16[256,4,128]{0,2,1:T(8,128)(2,1)S(1)}, u32[]{:S(2)}, u32[]{:S(2)}) collective-permute-start(bf16[256,4,128]{0,2,1:T(8,128)(2,1)S(1)} %fusion.77), channel_id=1, source_target_pairs={{0,1},{1,0},{2,3},{3,2},{4,5},{5,4},{6,7},{7,6},{8,9},{9,8},{10,11... | collective-permute-start | bytes 786440 | tf_op jit(solution)/shard_map/ppermute | solution.py:79
  80.1 1.6 %collective-permute-start.10 = (bf16[2,128,512]{2,1,0:T(8,128)(2,1)S(1)}, bf16[2,128,512]{2,1,0:T(8,128)(2,1)S(1)}, u32[]{:S(2)}, u32[]{:S(2)}) collective-permute-start(bf16[2,128,512]{2,1,0:T(8,128)(2,1)S(1)} %select_bitcast_fusion), channel_id=1, source_target_pairs={{0,1},{1,0},{2,3},{3,2},{4,5},{5,4},{6,7},{7,6},{8,9},{9,8},{10,11... | collective-permute-start | bytes 786440 | tf_op jit(solution)/shard_map/ppermute | solution.py:45
  81.8 5.6 %collective-permute-start.11 = (bf16[128,512]{1,0:T(8,128)(2,1)S(1)}, bf16[128,512]{1,0:T(8,128)(2,1)S(1)}, u32[]{:S(2)}, u32[]{:S(2)}) collective-permute-start(bf16[128,512]{1,0:T(8,128)(2,1)S(1)} %bitcast_convert_fusion), channel_id=1, source_target_pairs={{0,2},{1,3},{2,0},{3,1},{4,6},{5,7},{6,4},{7,5},{8,10},{9,11},{10,... | collective-permute-start | bytes 393224 | tf_op jit(solution)/shard_map/ppermute | solution.py:50

commit v15 on v14

--- a/solution.py
+++ b/solution.py
@@ -179,7 +179,6 @@
     heads_local = qkv_weight.shape[1] // head_size
     reach = BLOCKS
     gathered = gather_channels(latent)
-    taps = half_weights(stencil_weight)
     own_latent = core_half(gathered)
     normed = norm_channels(gathered.astype(jnp.float32), att_gain).astype(jnp.bfloat16)
     projected = jnp.einsum("koc,crw->korw", qkv_weight, normed, preferred_element_type=jnp.float32)
@@ -204,6 +203,7 @@
             from_left = got[key_value.shape[0] :].reshape(rim.shape)[..., reach:]
         if shift == strips - 1:
             from_right = got[key_value.shape[0] :].reshape(rim.shape)[..., :reach]
+    taps = half_weights(lax.optimization_barrier((stencil_weight, pieces[-1]))[0])
     all_keys = jnp.stack(pieces).reshape(strips, 2, heads_local, head_size, lat_rows, columns)
     wide_queries = jnp.concatenate(
         [from_left[:ch_local], queries.reshape(ch_local, lat_rows, columns), from_right[:ch_local]], axis=-1

time: 88.7 us -> 90.7 us (1.023)
  waiting for transfers between devices: 41.5 us -> 44.3 us
  other arithmetic: 7.48 us -> 9.11 us
  local copies, waits for them, and re-layouts: 13.4 us -> 12.2 us
  matrix products: 6.28 us -> 5.34 us
    ppermute x3, waiting for transfers between devices: 16.8 us -> 19.4 us  [per_device(): got = lax.ppermute(sent, 'lon', pairs)]
    ppermute x1, waiting for transfers between devices: 0.01 us -> 1.81 us  [half_weights(): stacked.append(lax.ppermute(weights, 'lev', pairs))]
    ppermute x2, waiting for transfers between devices: 2.55 us -> 1.42 us  [reduce_half(): lax.ppermute(theirs, 'lev', [(i, i ^ 1) for i in range(devices)])]
    convert_element_type x2, other arithmetic: 0.19 us -> 1.17 us  [reduce_half(): pair = pair.astype(jnp.bfloat16)]
    slice x2, local copies, waits for them, and re-layouts: 1.01 us -> 0.04 us  [per_device(): pieces.append(got[:key_value.shape[0]])]
    dot_general x3, matrix products: 4.48 us -> 3.54 us  [group_partial(): lax.dot_general(weight, activation, (((0,), (0,)), ((), ())), preferred_e...]
    unnamed x30 -> x28, local copies, waits for them, and re-layouts: 2.62 us -> 2.39 us
  transfers between devices with their start and end apart: 12 -> 12, of which waited for: 11 -> 10; matrix products, arithmetic and copies ran while one was open for 12% -> 5% of each run, Pallas kernels for 0% -> 0%
where the time goes in v15:
time: 90.7 us; the launch traced here: 90.4 us
  waiting for transfers between devices  44.3 us (49%)
  local copies, waits for them, and re-layouts  12.2 us (13%)
  starting transfers between devices  9.71 us (11%)
  other arithmetic  9.11 us (10%)
  blocking collectives  8.95 us (10%)
  matrix products  5.34 us (6%)
    ppermute x3, waiting for transfers between devices, per_device(): got = lax.ppermute(sent, 'lon', pairs)  19.4 us
    ppermute x2, waiting for transfers between devices, reduce_half(): total = total + lax.ppermute(pair, 'lev', pairs).astype(jnp.float32)  13.5 us
    all_gather x1, blocking collectives, gather_channels(): return lax.all_gather(values, 'lev', axis=0, tiled=True)  8.95 us
    ppermute x3, starting transfers between devices, per_device(): got = lax.ppermute(sent, 'lon', pairs)  4.62 us
    ppermute x1, waiting for transfers between devices, scatter_sum(): total = total + lax.ppermute(sent, axis, pairs).astype(jnp.float32)  4.19 us
    dot_general x3, matrix products, group_partial(): lax.dot_general(weight, activation, (((0,), (0,)), ((), ())), preferred_e...  3.54 us
    ppermute x2, waiting for transfers between devices, gather_half(): theirs = lax.ppermute(values, 'lev', [(i, i ^ 1) for i in range(devices)])  2.64 us
    unnamed x28, local copies, waits for them, and re-layouts  2.39 us
  transfers between devices with their start and end apart: 12, of which 10 were waited for; matrix products, arithmetic and copies ran while one was open for 5% of the time, Pallas kernels for 0%

profile of v15, /device:TPU:0, one launch (start us, length us, event | category | flops | bytes accessed | tf_op | source)
XLA Modules:
  0.0 90.4 jit_solution(17652448332841866552)
XLA Ops:
  0.0 8.9 %all_gather.3 = bf16[512,4,128]{2,1,0:T(4,128)(2,1)S(1)} all-gather(bf16[128,4,128]{2,1,0:T(4,128)(2,1)} %param.16), channel_id=1, replica_groups=mesh['member'=2,'lon'=4,'lev'=4] {'lev'}, dimensions={0}, use_global_device_ids=true | all-gather | bytes 655360 | tf_op jit(solution)/shard_map/all_gather | solution.py:34
  9.0 0.5 fusion.14
  9.5 1.5 %fusion.67 = bf16[512,4,128,1]{2,1,0,3:T(4,128)(2,1)S(1)} fusion(bf16[512,4,128]{2,1,0:T(4,128)(2,1)S(1)} %all_gather.3, f32[512]{0:T(512)S(1)} %copy-done.10, f32[4,128]{1,0:T(4,128)S(1)} %add_rsqrt_fusion.1), kind=kLoop, calls=%fused_computation.93 | loop fusion | flops 1048576 | bytes 1052672 | tf_op jit(solution)/shard_map/convert_element_type | solution.py:183
  11.1 0.4 convolution_bitcast_fusion
  11.6 0.2 copy.184
  11.9 0.2 broadcast_select_fusion
  12.1 0.2 select_n.116
  12.8 0.3 copy.143
  13.1 0.5 reshape.630
  13.8 0.7 pad_maximum_fusion.1
  14.5 3.6 %collective-permute-start.1 = (bf16[268,4,128]{2,0,1:T(8,128)(2,1)}, bf16[268,4,128]{2,0,1:T(8,128)(2,1)S(1)}, u32[]{:S(2)}, u32[]{:S(2)}) collective-permute-start(bf16[268,4,128]{2,0,1:T(8,128)(2,1)} %pad_maximum_fusion.1), channel_id=1, source_target_pairs={{0,12},{4,0},{8,4},{12,8},{1,13},{5,1},{9,5},{13,9},{2,14},{6,2},{... | collective-permute-start | bytes 823304 | tf_op jit(solution)/shard_map/ppermute | solution.py:200
  18.1 1.0 %collective-permute-start.2 = (bf16[256,4,128]{2,0,1:T(8,128)(2,1)S(1)}, bf16[256,4,128]{2,0,1:T(8,128)(2,1)}, u32[]{:S(2)}, u32[]{:S(2)}) collective-permute-start(bf16[256,4,128]{2,0,1:T(8,128)(2,1)S(1)} %bitcast.168), channel_id=1, source_target_pairs={{0,8},{4,12},{8,0},{12,4},{1,9},{5,13},{9,1},{13,5},{2,10},{6,14},... | collective-permute-start | bytes 786440 | tf_op jit(solution)/shard_map/ppermute | solution.py:200
  19.2 0.2 copy.187
  19.5 1.0 %copy.190 = bf16[1,512,512]{1,2,0:T(8,128)(2,1)} copy(bf16[1,512,512]{2,1,0:T(8,128)(2,1)S(1)} %get-tuple-element.82) | data formatting | bytes 1048576
  20.5 11.8 %collective-permute-done = bf16[268,4,128]{2,0,1:T(8,128)(2,1)S(1)} collective-permute-done((bf16[268,4,128]{2,0,1:T(8,128)(2,1)}, bf16[268,4,128]{2,0,1:T(8,128)(2,1)S(1)}, u32[]{:S(2)}, u32[]{:S(2)}) %collective-permute-start) | collective-permute-done | bytes 274464 | tf_op jit(solution)/shard_map/ppermute | solution.py:200
  32.3 0.8 reshape.631
  33.2 0.1 slice.380
  33.4 0.8 reshape.632
  34.4 7.6 %collective-permute-done.2 = bf16[256,4,128]{2,0,1:T(8,128)(2,1)} collective-permute-done((bf16[256,4,128]{2,0,1:T(8,128)(2,1)S(1)}, bf16[256,4,128]{2,0,1:T(8,128)(2,1)}, u32[]{:S(2)}, u32[]{:S(2)}) %collective-permute-start.2) | collective-permute-done | bytes 262176 | tf_op jit(solution)/shard_map/ppermute | solution.py:200
  42.0 1.0 %pad_maximum_fusion = bf16[4,2,2,64,4,128]{5,3,0,4,2,1:T(8,128)(2,1)S(1)} fusion(bf16[1,2,2,64,4,128]{5,3,0,4,2,1:T(8,128)(2,1)S(1)} %get-tuple-element.90, bf16[1,2,2,64,4,128]{5,3,2,1,4,0:T(8,128)(2,1)S(1)} %bitcast.170, bf16[1,2,2,64,4,128]{5,3,2,1,4,0:T(8,128)(2,1)} %bitcast.13, bf16[1,2,2,64,4,128]{5,3,2,1,4,0:T(8,128)(2,1)S(1)} %bitcast.169), kind=kLoop, calls=%fused_computation.48 | loop fusion | flops 4194304 | bytes 2097152 | tf_op jit(solution)/shard_map/stack | solution.py:207
  43.0 0.9 fusion
  43.9 0.5 fusion.31
  44.5 0.3 copy.157
  44.7 0.2 reshape.633
  44.9 0.3 fusion.2
  45.2 0.1 reshape.634
  45.3 1.1 %constant_dynamic-slice_fusion.3 = (bf16[2,1,128,528]{2,1,0,3:T(2,128)(2,1)S(1)}, bf16[2,1,128,528]{2,1,0,3:T(2,128)(2,1)S(1)}) fusion(bf16[2,2,128,528]{2,1,0,3:T(2,128)(2,1)S(1)} %reshape.634, s32[]{:T(128)S(6)} %select_n.114, s32[]{:T(128)S(6)} %select_n.154), kind=kLoop, calls=%fused_computation.179 | loop fusion | bytes 1081352 | tf_op jit(solution)/shard_map/jit(_take) | solution.py:66
  46.5 0.8 fusion.104
  47.2 0.2 fusion.64
  47.4 0.5 copy-done.8
  47.9 1.1 %collective-permute-start.5 = (f32[2,9,128]{2,0,1:T(2,128)S(1)}, f32[2,9,128]{2,0,1:T(2,128)S(1)}, u32[]{:S(2)}, u32[]{:S(2)}) collective-permute-start(f32[2,9,128]{2,0,1:T(2,128)S(1)} %copy-done.8), channel_id=1, source_target_pairs={{0,2},{1,3},{2,0},{3,1},{4,6},{5,7},{6,4},{7,5},{8,10},{9,11},{10,... | collective-permute-start | bytes 27656 | tf_op jit(solution)/shard_map/ppermute | solution.py:98
  49.1 0.2 slice.374
  49.4 0.2 copy.147
  49.6 0.2 copy.148
  49.8 1.8 %collective-permute-done.5 = f32[2,9,128]{2,0,1:T(2,128)S(1)} collective-permute-done((f32[2,9,128]{2,0,1:T(2,128)S(1)}, f32[2,9,128]{2,0,1:T(2,128)S(1)}, u32[]{:S(2)}, u32[]{:S(2)}) %collective-permute-start.5) | collective-permute-done | bytes 9248 | tf_op jit(solution)/shard_map/ppermute | solution.py:98
  51.6 1.1 %add_convert_fusion.2 = bf16[2,128,528]{1,2,0:T(8,128)(2,1)S(1)} fusion(bf16[2,128,528]{1,2,0:T(8,128)(2,1)} %collective-permute-done.3, bf16[2,1,128,528]{2,1,0,3:T(2,128)(2,1)S(1)} %get-tuple-element.86, pred[]{:T(512)S(6)} %and.69), kind=kLoop, calls=%fused_computation.77 | loop fusion | flops 675840 | bytes 811009 | tf_op jit(solution)/shard_map/convert_element_type | solution.py:69
  52.7 1.2 %collective-permute-start.4 = (bf16[2,128,528]{1,2,0:T(8,128)(2,1)S(1)}, bf16[2,128,528]{1,2,0:T(8,128)(2,1)S(1)}, u32[]{:S(2)}, u32[]{:S(2)}) collective-permute-start(bf16[2,128,528]{1,2,0:T(8,128)(2,1)S(1)} %add_convert_fusion.2), channel_id=1, source_target_pairs={{0,2},{1,3},{2,0},{3,1},{4,6},{5,7},{6,4},{7,5},{8,10},{9,11},{10,... | collective-permute-start | bytes 811016 | tf_op jit(solution)/shard_map/ppermute | solution.py:73
  54.0 6.1 %collective-permute-done.4 = bf16[2,128,528]{1,2,0:T(8,128)(2,1)S(1)} collective-permute-done((bf16[2,128,528]{1,2,0:T(8,128)(2,1)S(1)}, bf16[2,128,528]{1,2,0:T(8,128)(2,1)S(1)}, u32[]{:S(2)}, u32[]{:S(2)}) %collective-permute-start.4) | collective-permute-done | bytes 270368 | tf_op jit(solution)/shard_map/ppermute | solution.py:73
  60.2 0.3 copy.160
  60.5 0.4 reshape_reshape.6
  60.9 0.2 copy-done.5
  61.2 0.4 fusion.43
  61.7 0.2 copy-done.9
  62.1 1.2 %collective-permute-done.6 = bf16[256,4,130]{0,2,1:T(8,128)(2,1)S(1)} collective-permute-done((bf16[256,4,130]{0,2,1:T(8,128)(2,1)S(1)}, bf16[256,4,130]{0,2,1:T(8,128)(2,1)S(1)}, u32[]{:S(2)}, u32[]{:S(2)}) %collective-permute-start.6) | collective-permute-done | bytes 266272 | tf_op jit(solution)/shard_map/ppermute | solution.py:79
  63.2 0.2 multiply_reduce_fusion
  63.6 0.8 concatenate.59
  64.3 2.1 %fusion.3 = bf16[512,520]{0,1:T(8,128)(2,1)S(1)} fusion(bf16[512,512]{0,1:T(8,128)(2,1)S(1)} %bitcast.174, bf16[256,520]{0,1:T(8,128)(2,1)} %concatenate.59, bf16[256,520]{0,1:T(8,128)(2,1)S(1)} %concatenate.58, f32[512]{0:T(512)S(1)} %bitcast.202, f32[520]{0:T(1024)S(1)} %rsqrt.50, bf16[2,512,512]{2,1,0:T(8,128)(2,1)} %param.23), kind=kOutput, calls=%fused_computation.24 | convolution fusion | flops 549785600 | bytes 2117664 | tf_op jit(solution)/shard_map/dot_general | solution.py:104
  66.6 1.1 %constant_dynamic-slice_fusion.1 = (bf16[2,1,128,520]{2,1,0,3:T(2,128)(2,1)S(1)}, bf16[2,1,128,520]{2,1,0,3:T(2,128)(2,1)S(1)}) fusion(bf16[2,2,128,520]{2,1,0,3:T(2,128)(2,1)S(1)} %reshape.636, s32[]{:T(128)S(6)} %select_n.114, s32[]{:T(128)S(6)} %select_n.154), kind=kLoop, calls=%fused_computation.177 | loop fusion | bytes 1064968 | tf_op jit(solution)/shard_map/jit(_take) | solution.py:66
  67.8 0.2 collective-permute-start.7
  68.0 1.4 %collective-permute-done.7 = bf16[2,128,520]{1,2,0:T(8,128)(2,1)S(1)} collective-permute-done((bf16[2,128,520]{1,2,0:T(8,128)(2,1)S(1)}, bf16[2,128,520]{1,2,0:T(8,128)(2,1)S(1)}, u32[]{:S(2)}, u32[]{:S(2)}) %collective-permute-start.7) | collective-permute-done | bytes 266272 | tf_op jit(solution)/shard_map/ppermute | solution.py:68
  69.5 1.2 %collective-permute-start.8 = (bf16[2,128,520]{1,2,0:T(8,128)(2,1)S(1)}, bf16[2,128,520]{1,2,0:T(8,128)(2,1)S(1)}, u32[]{:S(2)}, u32[]{:S(2)}) collective-permute-start(bf16[2,128,520]{1,2,0:T(8,128)(2,1)S(1)} %add_convert_fusion.3), channel_id=1, source_target_pairs={{0,2},{1,3},{2,0},{3,1},{4,6},{5,7},{6,4},{7,5},{8,10},{9,11},{10,... | collective-permute-start | bytes 798728 | tf_op jit(solution)/shard_map/ppermute | solution.py:73
  70.6 7.3 %collective-permute-done.8 = bf16[2,128,520]{1,2,0:T(8,128)(2,1)S(1)} collective-permute-done((bf16[2,128,520]{1,2,0:T(8,128)(2,1)S(1)}, bf16[2,128,520]{1,2,0:T(8,128)(2,1)S(1)}, u32[]{:S(2)}, u32[]{:S(2)}) %collective-permute-start.8) | collective-permute-done | bytes 266272 | tf_op jit(solution)/shard_map/ppermute | solution.py:73
  78.0 0.3 copy.167
  78.3 0.4 reshape_reshape.7
  78.9 0.4 fusion.77
  79.4 1.5 %collective-permute-done.9 = bf16[256,4,128]{0,2,1:T(8,128)(2,1)S(1)} collective-permute-done((bf16[256,4,128]{0,2,1:T(8,128)(2,1)S(1)}, bf16[256,4,128]{0,2,1:T(8,128)(2,1)S(1)}, u32[]{:S(2)}, u32[]{:S(2)}) %collective-permute-start.9) | collective-permute-done | bytes 262176 | tf_op jit(solution)/shard_map/ppermute | solution.py:79
  80.8 0.2 multiply_reduce_fusion.1
  81.0 1.1 %convolution_convert_fusion.2 = bf16[512,512]{0,1:T(8,128)(2,1)S(1)} fusion(bf16[512,512]{0,1:T(8,128)(2,1)S(1)} %bitcast.175, bf16[256,512]{0,1:T(8,128)(2,1)S(1)} %bitcast.179, bf16[256,512]{0,1:T(8,128)(2,1)S(1)} %bitcast.166, bf16[2,512,512]{2,1,0:T(8,128)(2,1)S(1)} %copy-done.11, f32[512]{0:T(512)S(1)} %bitcast.203, f32[512]{0:T(512)S(1)} %rsqrt_bitcast_fusion), kind=kOutput, calls=%fused_computation.9 | convolution fusion | flops 541327360 | bytes 2101248 | tf_op jit(solution)/shard_map/dot_general | solution.py:104
  82.2 0.2 collective-permute-start.10
  82.4 1.4 %collective-permute-done.10 = bf16[2,128,512]{2,1,0:T(8,128)(2,1)S(1)} collective-permute-done((bf16[2,128,512]{2,1,0:T(8,128)(2,1)S(1)}, bf16[2,128,512]{2,1,0:T(8,128)(2,1)S(1)}, u32[]{:S(2)}, u32[]{:S(2)}) %collective-permute-start.10) | collective-permute-done | bytes 262176 | tf_op jit(solution)/shard_map/ppermute | solution.py:45
  84.0 1.2 %collective-permute-start.11 = (bf16[128,512]{1,0:T(8,128)(2,1)S(1)}, bf16[128,512]{1,0:T(8,128)(2,1)S(1)}, u32[]{:S(2)}, u32[]{:S(2)}) collective-permute-start(bf16[128,512]{1,0:T(8,128)(2,1)S(1)} %bitcast_convert_fusion), channel_id=1, source_target_pairs={{0,2},{1,3},{2,0},{3,1},{4,6},{5,7},{6,4},{7,5},{8,10},{9,11},{10,... | collective-permute-start | bytes 393224 | tf_op jit(solution)/shard_map/ppermute | solution.py:50
  85.2 0.2 copy.183
  85.4 4.2 %collective-permute-done.11 = bf16[128,512]{1,0:T(8,128)(2,1)S(1)} collective-permute-done((bf16[128,512]{1,0:T(8,128)(2,1)S(1)}, bf16[128,512]{1,0:T(8,128)(2,1)S(1)}, u32[]{:S(2)}, u32[]{:S(2)}) %collective-permute-start.11) | collective-permute-done | bytes 131104 | tf_op jit(solution)/shard_map/ppermute | solution.py:50
  89.7 0.7 fusion.113
  (86 shorter events, 2.7 us)
Async XLA Ops:
  0.0 11.0 %copy-start = (bf16[3,128,512]{2,1,0:T(8,128)(2,1)S(1)}, bf16[3,128,512]{2,1,0:T(8,128)(2,1)}, u32[]{:S(2)}) copy-start(bf16[3,128,512]{2,1,0:T(8,128)(2,1)} %param.18) | copy-start | bytes 1179652
  0.0 9.5 %copy-start.10 = (f32[512]{0:T(512)S(1)}, f32[512]{0:T(512)}, u32[]{:S(2)}) copy-start(f32[512]{0:T(512)} %param.17) | copy-start | bytes 6148
  12.3 1.3 %copy-start.4 = (bf16[256,4,128]{0,2,1:T(8,128)(2,1)}, bf16[256,4,128]{0,2,1:T(8,128)(2,1)S(1)}, u32[]{:S(2)}) copy-start(bf16[256,4,128]{0,2,1:T(8,128)(2,1)S(1)} %select_n.116) | copy-start | bytes 786436
  13.7 5.5 %copy-start.6 = (bf16[2,512,512]{2,1,0:T(8,128)(2,1)S(1)}, bf16[2,512,512]{2,1,0:T(8,128)(2,1)}, u32[]{:S(2)}) copy-start(bf16[2,512,512]{2,1,0:T(8,128)(2,1)} %param.22) | copy-start | bytes 3145732
  14.5 18.8 %collective-permute-start.1 = (bf16[268,4,128]{2,0,1:T(8,128)(2,1)}, bf16[268,4,128]{2,0,1:T(8,128)(2,1)S(1)}, u32[]{:S(2)}, u32[]{:S(2)}) collective-permute-start(bf16[268,4,128]{2,0,1:T(8,128)(2,1)} %pad_maximum_fusion.1), channel_id=1, source_target_pairs={{0,12},{4,0},{8,4},{12,8},{1,13},{5,1},{9,5},{13,9},{2,14},{6,2},{... | collective-permute-start | bytes 823304 | tf_op jit(solution)/shard_map/ppermute | solution.py:200
  18.1 14.2 %collective-permute-start = (bf16[268,4,128]{2,0,1:T(8,128)(2,1)}, bf16[268,4,128]{2,0,1:T(8,128)(2,1)S(1)}, u32[]{:S(2)}, u32[]{:S(2)}) collective-permute-start(bf16[268,4,128]{2,0,1:T(8,128)(2,1)} %pad_maximum_fusion.1), channel_id=1, source_target_pairs={{0,4},{4,8},{8,12},{12,0},{1,5},{5,9},{9,13},{13,1},{2,6},{6,10},{... | collective-permute-start | bytes 823304 | tf_op jit(solution)/shard_map/ppermute | solution.py:200
  18.1 23.8 %collective-permute-start.2 = (bf16[256,4,128]{2,0,1:T(8,128)(2,1)S(1)}, bf16[256,4,128]{2,0,1:T(8,128)(2,1)}, u32[]{:S(2)}, u32[]{:S(2)}) collective-permute-start(bf16[256,4,128]{2,0,1:T(8,128)(2,1)S(1)} %bitcast.168), channel_id=1, source_target_pairs={{0,8},{4,12},{8,0},{12,4},{1,9},{5,13},{9,1},{13,5},{2,10},{6,14},... | collective-permute-start | bytes 786440 | tf_op jit(solution)/shard_map/ppermute | solution.py:200
  34.2 8.8 %copy-start.2 = (bf16[384,4,4]{2,1,0:T(4,128)(2,1)}, bf16[384,4,4]{2,1,0:T(4,128)(2,1)S(1)}, u32[]{:S(2)}) copy-start(bf16[384,4,4]{2,1,0:T(4,128)(2,1)S(1)} %reshape.632) | copy-start | bytes 36868
  43.9 1.0 %copy-start.7 = (bf16[128,512]{1,0:T(8,128)(2,1)S(1)}, bf16[128,512]{1,0:T(8,128)(2,1)}, u32[]{:S(2)}) copy-start(bf16[128,512]{1,0:T(8,128)(2,1)} %param.19) | copy-start | bytes 393220
  45.3 1.9 %copy-start.1 = (bf16[1,512,512]{1,2,0:T(8,128)(2,1)S(1)}, bf16[1,512,512]{1,2,0:T(8,128)(2,1)}, u32[]{:S(2)}) copy-start(bf16[1,512,512]{1,2,0:T(8,128)(2,1)} %copy.190) | copy-start | bytes 1572868
  47.2 0.7 copy-start.8
  47.2 4.4 %collective-permute-start.3 = (bf16[2,128,528]{1,2,0:T(8,128)(2,1)}, bf16[2,128,528]{1,2,0:T(8,128)(2,1)}, u32[]{:S(2)}, u32[]{:S(2)}) collective-permute-start(bf16[2,128,528]{1,2,0:T(8,128)(2,1)} %fusion.104), channel_id=1, source_target_pairs={{0,1},{1,0},{2,3},{3,2},{4,5},{5,4},{6,7},{7,6},{8,9},{9,8},{10,11... | collective-permute-start | bytes 811016 | tf_op jit(solution)/shard_map/ppermute | solution.py:68
  47.2 2.1 %copy-start.3 = (bf16[384,4,4]{2,1,0:T(4,128)(2,1)S(1)}, bf16[384,4,4]{2,1,0:T(4,128)(2,1)}, u32[]{:S(2)}) copy-start(bf16[384,4,4]{2,1,0:T(4,128)(2,1)} %copy-done.2) | copy-start | bytes 36868
  47.9 3.7 %collective-permute-start.5 = (f32[2,9,128]{2,0,1:T(2,128)S(1)}, f32[2,9,128]{2,0,1:T(2,128)S(1)}, u32[]{:S(2)}, u32[]{:S(2)}) collective-permute-start(f32[2,9,128]{2,0,1:T(2,128)S(1)} %copy-done.8), channel_id=1, source_target_pairs={{0,2},{1,3},{2,0},{3,1},{4,6},{5,7},{6,4},{7,5},{8,10},{9,11},{10,... | collective-permute-start | bytes 27656 | tf_op jit(solution)/shard_map/ppermute | solution.py:98
  52.7 7.4 %collective-permute-start.4 = (bf16[2,128,528]{1,2,0:T(8,128)(2,1)S(1)}, bf16[2,128,528]{1,2,0:T(8,128)(2,1)S(1)}, u32[]{:S(2)}, u32[]{:S(2)}) collective-permute-start(bf16[2,128,528]{1,2,0:T(8,128)(2,1)S(1)} %add_convert_fusion.2), channel_id=1, source_target_pairs={{0,2},{1,3},{2,0},{3,1},{4,6},{5,7},{6,4},{7,5},{8,10},{9,11},{10,... | collective-permute-start | bytes 811016 | tf_op jit(solution)/shard_map/ppermute | solution.py:73
  60.2 1.0 %copy-start.5 = (bf16[256,4,128]{0,2,1:T(8,128)(2,1)S(1)}, bf16[256,4,128]{0,2,1:T(8,128)(2,1)}, u32[]{:S(2)}) copy-start(bf16[256,4,128]{0,2,1:T(8,128)(2,1)} %copy-done.4) | copy-start | bytes 786436
  61.2 0.7 copy-start.9
  61.6 1.6 %collective-permute-start.6 = (bf16[256,4,130]{0,2,1:T(8,128)(2,1)S(1)}, bf16[256,4,130]{0,2,1:T(8,128)(2,1)S(1)}, u32[]{:S(2)}, u32[]{:S(2)}) collective-permute-start(bf16[256,4,130]{0,2,1:T(8,128)(2,1)S(1)} %fusion.43), channel_id=1, source_target_pairs={{0,1},{1,0},{2,3},{3,2},{4,5},{5,4},{6,7},{7,6},{8,9},{9,8},{10,11... | collective-permute-start | bytes 798728 | tf_op jit(solution)/shard_map/ppermute | solution.py:79
  67.8 1.6 %collective-permute-start.7 = (bf16[2,128,520]{1,2,0:T(8,128)(2,1)S(1)}, bf16[2,128,520]{1,2,0:T(8,128)(2,1)S(1)}, u32[]{:S(2)}, u32[]{:S(2)}) collective-permute-start(bf16[2,128,520]{1,2,0:T(8,128)(2,1)S(1)} %fusion.106), channel_id=1, source_target_pairs={{0,1},{1,0},{2,3},{3,2},{4,5},{5,4},{6,7},{7,6},{8,9},{9,8},{10,11... | collective-permute-start | bytes 798728 | tf_op jit(solution)/shard_map/ppermute | solution.py:68
  69.5 8.5 %collective-permute-start.8 = (bf16[2,128,520]{1,2,0:T(8,128)(2,1)S(1)}, bf16[2,128,520]{1,2,0:T(8,128)(2,1)S(1)}, u32[]{:S(2)}, u32[]{:S(2)}) collective-permute-start(bf16[2,128,520]{1,2,0:T(8,128)(2,1)S(1)} %add_convert_fusion.3), channel_id=1, source_target_pairs={{0,2},{1,3},{2,0},{3,1},{4,6},{5,7},{6,4},{7,5},{8,10},{9,11},{10,... | collective-permute-start | bytes 798728 | tf_op jit(solution)/shard_map/ppermute | solution.py:73
  79.2 1.8 %copy-start.11 = (bf16[2,512,512]{2,1,0:T(8,128)(2,1)S(1)}, bf16[2,512,512]{2,1,0:T(8,128)(2,1)}, u32[]{:S(2)}) copy-start(bf16[2,512,512]{2,1,0:T(8,128)(2,1)} %param.23) | copy-start | bytes 3145732
  79.2 1.6 %collective-permute-start.9 = (bf16[256,4,128]{0,2,1:T(8,128)(2,1)S(1)}, bf16[256,4,128]{0,2,1:T(8,128)(2,1)S(1)}, u32[]{:S(2)}, u32[]{:S(2)}) collective-permute-start(bf16[256,4,128]{0,2,1:T(8,128)(2,1)S(1)} %fusion.77), channel_id=1, source_target_pairs={{0,1},{1,0},{2,3},{3,2},{4,5},{5,4},{6,7},{7,6},{8,9},{9,8},{10,11... | collective-permute-start | bytes 786440 | tf_op jit(solution)/shard_map/ppermute | solution.py:79
  82.2 1.6 %collective-permute-start.10 = (bf16[2,128,512]{2,1,0:T(8,128)(2,1)S(1)}, bf16[2,128,512]{2,1,0:T(8,128)(2,1)S(1)}, u32[]{:S(2)}, u32[]{:S(2)}) collective-permute-start(bf16[2,128,512]{2,1,0:T(8,128)(2,1)S(1)} %select_bitcast_fusion), channel_id=1, source_target_pairs={{0,1},{1,0},{2,3},{3,2},{4,5},{5,4},{6,7},{7,6},{8,9},{9,8},{10,11... | collective-permute-start | bytes 786440 | tf_op jit(solution)/shard_map/ppermute | solution.py:45
  84.0 5.6 %collective-permute-start.11 = (bf16[128,512]{1,0:T(8,128)(2,1)S(1)}, bf16[128,512]{1,0:T(8,128)(2,1)S(1)}, u32[]{:S(2)}, u32[]{:S(2)}) collective-permute-start(bf16[128,512]{1,0:T(8,128)(2,1)S(1)} %bitcast_convert_fusion), channel_id=1, source_target_pairs={{0,2},{1,3},{2,0},{3,1},{4,6},{5,7},{6,4},{7,5},{8,10},{9,11},{10,... | collective-permute-start | bytes 393224 | tf_op jit(solution)/shard_map/ppermute | solution.py:50

commit v16 on v14

--- a/solution.py
+++ b/solution.py
@@ -58,20 +58,34 @@
     return taken.reshape(*values.shape[:axis], -1, *values.shape[axis + 1 :])
 
 
-def reduce_half(partial):
+def reduce_half(partial, extra=None):
     devices = lax.axis_size("lev")
     me = lax.axis_index("lev")
     chips, core = devices // 2, me % 2
+    chip = me // 2
     blocks = partial.reshape(chips, 2, -1, *partial.shape[1:])
     mine = jnp.take(blocks, core, axis=1).astype(jnp.float32)
     theirs = jnp.take(blocks, 1 - core, axis=1)
     pair = mine + lax.ppermute(theirs, "lev", [(i, i ^ 1) for i in range(devices)]).astype(jnp.float32)
-    pair = pair.astype(jnp.bfloat16)
+    pair = pair.astype(jnp.bfloat16).reshape(-1, *partial.shape[1:])
     total = pair.astype(jnp.float32)
+    rows = pair.shape[0]
+    sent = pair
+    if extra is not None:
+        width = partial.shape[1]
+        flat = extra.reshape(-1)
+        spare = (-flat.shape[0]) % width
+        sent = jnp.concatenate([pair, jnp.pad(flat, (0, spare)).reshape(-1, width)], axis=0)
+    extras = [extra]
     for shift in range(1, chips):
-        pairs = [(i, ((i // 2 + shift) % chips) * 2 + i % 2) for i in range(devices)]
-        total = total + lax.ppermute(pair, "lev", pairs).astype(jnp.float32)
-    return total.reshape(-1, *partial.shape[1:])
+        pairs = [(i, ((i // 2 - shift) % chips) * 2 + i % 2) for i in range(devices)]
+        got = lax.ppermute(sent, "lev", pairs)
+        total = total + got[:rows].astype(jnp.float32)
+        if extra is not None:
+            extras.append(got[rows:].reshape(-1)[: extra.size].reshape(extra.shape))
+    if extra is None:
+        return total
+    return total, jnp.roll(jnp.stack(extras), chip, axis=0)
 
 
 def gather_half(values):
@@ -189,7 +203,7 @@
     value_rows = projected[2].astype(jnp.bfloat16)
 
     key_value = jnp.stack([key_rows, value_rows]).reshape(-1, lat_rows, columns)
-    rim = jnp.concatenate([edges(queries.reshape(ch_local, lat_rows, columns), reach), edges(own_latent, reach)])
+    rim = jnp.concatenate([edges(queries.reshape(ch_local, lat_rows, columns), reach), edges(latent, reach)])
     rim_rows = rim.size // (lat_rows * columns)
     payload = jnp.concatenate([key_value, rim.reshape(rim_rows, lat_rows, columns)], axis=0)
     strips = lax.axis_size("lon")
@@ -208,11 +222,13 @@
     wide_queries = jnp.concatenate(
         [from_left[:ch_local], queries.reshape(ch_local, lat_rows, columns), from_right[:ch_local]], axis=-1
     ).reshape(heads_local, head_size, lat_rows, -1)
-    wide_latent = jnp.concatenate([from_left[ch_local:], own_latent, from_right[ch_local:]], axis=-1)
 
     numerator, denominator = make_fold(wide_queries, (all_keys[:, 0], all_keys[:, 1]))
     attended = (numerator / denominator[:, None]).astype(jnp.bfloat16)
-    update = reduce_half(group_partial(out_weight, attended.reshape(ch_local, -1)))
+    halo = jnp.stack([from_left[ch_local:], from_right[ch_local:]])
+    update, halos = reduce_half(group_partial(out_weight, attended.reshape(ch_local, -1)), halo)
+    halos = jnp.moveaxis(halos, 0, 1).reshape(2, -1, lat_rows, reach)
+    wide_latent = jnp.concatenate([halos[0], own_latent, halos[1]], axis=-1)
     current = (wide_latent.astype(jnp.float32) + update.reshape(wide_latent.shape)).astype(
         jnp.bfloat16
     )

time: 88.7 us -> 97.2 us (1.096)
  other arithmetic: 7.48 us -> 13 us
  local copies, waits for them, and re-layouts: 13.4 us -> 17.7 us
  waiting for transfers between devices: 41.5 us -> 40.3 us
    ppermute x3, waiting for transfers between devices: 16.8 us -> 14 us  [per_device(): got = lax.ppermute(sent, 'lon', pairs)]
    ppermute x2, waiting for transfers between devices: 14 us -> 16.7 us  [reduce_half(): got = lax.ppermute(sent, 'lev', pairs)]
    ppermute x2, waiting for transfers between devices: 2.55 us -> 1.4 us  [reduce_half(): lax.ppermute(theirs, 'lev', [(i, i ^ 1) for i in range(devices)])]
    another operation x0 -> x1, other arithmetic: none -> 1.15 us  [reduce_half(): return (total, jnp.roll(jnp.stack(extras), chip, axis=0))]
    slice x4, local copies, waits for them, and re-layouts: 0.35 us -> 1.45 us  [edges(): return jnp.concatenate([values[..., :width], values[..., -width:]], axis=-1)]
    unnamed x30 -> x28, local copies, waits for them, and re-layouts: 2.62 us -> 3.14 us
  transfers between devices with their start and end apart: 12 -> 12, of which waited for: 11 -> 10; matrix products, arithmetic and copies ran while one was open for 12% -> 18% of each run, Pallas kernels for 0% -> 0%
where the time goes in v16:
time: 97.2 us; the launch traced here: 96.6 us
  waiting for transfers between devices  40.3 us (41%)
  local copies, waits for them, and re-layouts  17.7 us (18%)
  other arithmetic  13 us (13%)
  starting transfers between devices  9.78 us (10%)
  blocking collectives  8.95 us (9%)
  matrix products  6.27 us (6%)
    ppermute x2, waiting for transfers between devices, reduce_half(): got = lax.ppermute(sent, 'lev', pairs)  16.7 us
    ppermute x3, waiting for transfers between devices, per_device(): got = lax.ppermute(sent, 'lon', pairs)  14 us
    all_gather x1, blocking collectives, gather_channels(): return lax.all_gather(values, 'lev', axis=0, tiled=True)  8.95 us
    ppermute x3, starting transfers between devices, per_device(): got = lax.ppermute(sent, 'lon', pairs)  4.61 us
    dot_general x3, matrix products, group_partial(): lax.dot_general(weight, activation, (((0,), (0,)), ((), ())), preferred_e...  4.48 us
    ppermute x1, waiting for transfers between devices, scatter_sum(): total = total + lax.ppermute(sent, axis, pairs).astype(jnp.float32)  4.17 us
    unnamed x28, local copies, waits for them, and re-layouts  3.14 us
    ppermute x2, waiting for transfers between devices, gather_half(): theirs = lax.ppermute(values, 'lev', [(i, i ^ 1) for i in range(devices)])  2.62 us
  transfers between devices with their start and end apart: 12, of which 10 were waited for; matrix products, arithmetic and copies ran while one was open for 18% of the time, Pallas kernels for 0%

profile of v16, /device:TPU:0, one launch (start us, length us, event | category | flops | bytes accessed | tf_op | source)
XLA Modules:
  0.0 96.6 jit_solution(15076707754704138566)
XLA Ops:
  0.0 8.9 %all_gather.3 = bf16[512,4,128]{2,1,0:T(4,128)(2,1)S(1)} all-gather(bf16[128,4,128]{2,1,0:T(4,128)(2,1)} %param.16), channel_id=1, replica_groups=mesh['member'=2,'lon'=4,'lev'=4] {'lev'}, dimensions={0}, use_global_device_ids=true | all-gather | bytes 655360 | tf_op jit(solution)/shard_map/all_gather | solution.py:34
  9.0 1.1 %fusion.151 = (bf16[128,4,2]{2,1,0:T(4,128)(2,1)S(1)}, bf16[128,4,2]{2,1,0:T(4,128)(2,1)S(1)}) fusion(bf16[128,4,128]{2,1,0:T(4,128)(2,1)} %param.16), kind=kLoop, calls=%fused_computation.235 | loop fusion | bytes 8192 | tf_op jit(solution)/shard_map/slice | solution.py:185
  10.1 0.5 fusion.14
  10.6 1.5 %fusion.67 = bf16[512,4,128,1]{2,1,0,3:T(4,128)(2,1)S(1)} fusion(bf16[512,4,128]{2,1,0:T(4,128)(2,1)S(1)} %all_gather.3, f32[512]{0:T(512)S(1)} %copy-done.10, f32[4,128]{1,0:T(4,128)S(1)} %add_rsqrt_fusion.1), kind=kLoop, calls=%fused_computation.93 | loop fusion | flops 1048576 | bytes 1052672 | tf_op jit(solution)/shard_map/convert_element_type | solution.py:198
  12.2 0.4 convolution_bitcast_fusion
  13.4 0.2 copy.207
  13.6 0.3 reshape.655
  14.0 0.8 fusion.143
  14.8 0.7 copy.200
  15.5 1.7 %pad_maximum_fusion.2 = bf16[264,4,128]{2,0,1:T(8,128)(2,1)} fusion(bf16[8,4,128]{2,0,1:T(8,128)(2,1)S(1)} %copy.208, bf16[256,4,128]{2,0,1:T(8,128)(2,1)} %bitcast.6), kind=kLoop, calls=%fused_computation.135 | loop fusion | flops 540672 | bytes 540672 | tf_op jit(solution)/shard_map/concatenate | solution.py:208
  17.2 1.6 %collective-permute-start = (bf16[264,4,128]{2,0,1:T(8,128)(2,1)}, bf16[264,4,128]{2,0,1:T(8,128)(2,1)}, u32[]{:S(2)}, u32[]{:S(2)}) collective-permute-start(bf16[264,4,128]{2,0,1:T(8,128)(2,1)} %pad_maximum_fusion.2), channel_id=1, source_target_pairs={{0,4},{4,8},{8,12},{12,0},{1,5},{5,9},{9,13},{13,1},{2,6},{6,10},{... | collective-permute-start | bytes 811016 | tf_op jit(solution)/shard_map/ppermute | solution.py:215
  18.8 2.3 %collective-permute-start.1 = (bf16[264,4,128]{2,0,1:T(8,128)(2,1)}, bf16[264,4,128]{2,0,1:T(8,128)(2,1)}, u32[]{:S(2)}, u32[]{:S(2)}) collective-permute-start(bf16[264,4,128]{2,0,1:T(8,128)(2,1)} %pad_maximum_fusion.2), channel_id=1, source_target_pairs={{0,12},{4,0},{8,4},{12,8},{1,13},{5,1},{9,5},{13,9},{2,14},{6,2},{... | collective-permute-start | bytes 811016 | tf_op jit(solution)/shard_map/ppermute | solution.py:215
  21.0 0.8 collective-permute-start.2
  21.8 1.1 %collective-permute-start.5 = (f32[2,9,128]{2,0,1:T(2,128)S(1)}, f32[2,9,128]{2,0,1:T(2,128)S(1)}, u32[]{:S(2)}, u32[]{:S(2)}) collective-permute-start(f32[2,9,128]{2,0,1:T(2,128)S(1)} %copy-done.5), channel_id=1, source_target_pairs={{0,2},{1,3},{2,0},{3,1},{4,6},{5,7},{6,4},{7,5},{8,10},{9,11},{10,... | collective-permute-start | bytes 27656 | tf_op jit(solution)/shard_map/ppermute | solution.py:112
  23.0 0.9 copy.259
  24.0 0.2 copy.260
  24.2 0.2 copy.263
  24.7 0.7 copy-done.1
  25.4 0.2 broadcast_select_fusion
  25.7 3.0 %collective-permute-done = bf16[264,4,128]{2,0,1:T(8,128)(2,1)} collective-permute-done((bf16[264,4,128]{2,0,1:T(8,128)(2,1)}, bf16[264,4,128]{2,0,1:T(8,128)(2,1)}, u32[]{:S(2)}, u32[]{:S(2)}) %collective-permute-start) | collective-permute-done | bytes 270368 | tf_op jit(solution)/shard_map/ppermute | solution.py:215
  28.7 0.7 slice.393
  29.4 0.6 reshape.656
  29.9 3.4 %collective-permute-done.1 = bf16[264,4,128]{2,0,1:T(8,128)(2,1)} collective-permute-done((bf16[264,4,128]{2,0,1:T(8,128)(2,1)}, bf16[264,4,128]{2,0,1:T(8,128)(2,1)}, u32[]{:S(2)}, u32[]{:S(2)}) %collective-permute-start.1) | collective-permute-done | bytes 270368 | tf_op jit(solution)/shard_map/ppermute | solution.py:215
  33.3 0.7 slice.395
  34.1 0.6 reshape.657
  34.7 0.9 fusion.148
  35.6 1.0 %slice.397 = bf16[256,4,128]{2,0,1:T(8,128)(2,1)S(1)} slice(bf16[264,4,128]{2,0,1:T(8,128)(2,1)} %collective-permute-done), slice={[0:256], [0:4], [0:128]} | slice | bytes 524288 | tf_op jit(solution)/shard_map/slice | solution.py:216
  36.6 1.0 %slice.398 = bf16[256,4,128]{2,0,1:T(8,128)(2,1)S(1)} slice(bf16[264,4,128]{2,0,1:T(8,128)(2,1)} %collective-permute-done.1), slice={[0:256], [0:4], [0:128]} | slice | bytes 524288 | tf_op jit(solution)/shard_map/slice | solution.py:216
  37.6 7.6 %collective-permute-done.2 = bf16[256,4,128]{2,0,1:T(8,128)(2,1)} collective-permute-done((bf16[256,4,128]{2,0,1:T(8,128)(2,1)}, bf16[256,4,128]{2,0,1:T(8,128)(2,1)}, u32[]{:S(2)}, u32[]{:S(2)}) %collective-permute-start.2) | collective-permute-done | bytes 262176 | tf_op jit(solution)/shard_map/ppermute | solution.py:215
  45.1 1.0 %pad_maximum_fusion = bf16[4,2,2,64,4,128]{5,3,0,4,2,1:T(8,128)(2,1)S(1)} fusion(bf16[1,2,2,64,4,128]{5,3,0,4,2,1:T(8,128)(2,1)S(1)} %copy-done.3, bf16[1,2,2,64,4,128]{5,3,2,1,4,0:T(8,128)(2,1)S(1)} %bitcast.199, bf16[1,2,2,64,4,128]{5,3,2,1,4,0:T(8,128)(2,1)} %bitcast.15, bf16[1,2,2,64,4,128]{5,3,2,1,4,0:T(8,128)(2,1)S(1)} %bitcast.200), kind=kLoop, calls=%fused_computation.48 | loop fusion | flops 4194304 | bytes 2097152 | tf_op jit(solution)/shard_map/stack | solution.py:221
  46.2 0.9 fusion
  47.1 0.5 fusion.31
  47.6 0.3 copy.219
  48.1 0.3 fusion.2
  48.5 1.1 %constant_dynamic-slice_fusion.3 = (bf16[2,1,128,528]{2,1,0,3:T(2,128)(2,1)S(1)}, bf16[2,1,128,528]{2,1,0,3:T(2,128)(2,1)S(1)}) fusion(bf16[2,2,128,528]{2,1,0,3:T(2,128)(2,1)S(1)} %reshape.659, s32[]{:T(128)S(6)} %select_n.159, s32[]{:T(128)S(6)} %select_n.161), kind=kLoop, calls=%fused_computation.190 | loop fusion | bytes 1081352 | tf_op jit(solution)/shard_map/jit(_take) | solution.py:67
  49.6 0.8 fusion.105
  50.4 0.6 cosine_divide_fusion
  51.2 1.1 %fusion.144 = (bf16[1,2,128,4,2]{4,3,2,1,0:T(4,128)(2,1)S(1)}, bf16[2,128,4,2]{3,2,1,0:T(4,128)(2,1)S(1)}) fusion(bf16[1,128,4,2]{3,2,1,0:T(4,128)(2,1)} %get-tuple-element.136, bf16[1,128,4,2]{3,2,1,0:T(4,128)(2,1)S(1)} %get-tuple-element.91), kind=kLoop, calls=%fused_computation.228 | loop fusion | flops 2048 | bytes 12288 | tf_op jit(solution)/shard_map/stack | solution.py:88
  52.4 0.3 reshape.661
  53.1 0.8 pad_maximum_fusion.1
  53.9 1.1 %collective-permute-start.4 = (bf16[260,528]{0,1:T(8,128)(2,1)}, bf16[260,528]{0,1:T(8,128)(2,1)S(1)}, u32[]{:S(2)}, u32[]{:S(2)}) collective-permute-start(bf16[260,528]{0,1:T(8,128)(2,1)} %pad_maximum_fusion.1), channel_id=1, source_target_pairs={{0,2},{1,3},{2,0},{3,1},{4,6},{5,7},{6,4},{7,5},{8,10},{9,11},{10,... | collective-permute-start | bytes 823688 | tf_op jit(solution)/shard_map/ppermute | solution.py:82
  55.0 0.6 fusion.152
  55.6 0.7 broadcast_multiply_fusion.5
  56.4 9.4 %collective-permute-done.4 = bf16[260,528]{0,1:T(8,128)(2,1)S(1)} collective-permute-done((bf16[260,528]{0,1:T(8,128)(2,1)}, bf16[260,528]{0,1:T(8,128)(2,1)S(1)}, u32[]{:S(2)}, u32[]{:S(2)}) %collective-permute-start.4) | collective-permute-done | bytes 274592 | tf_op jit(solution)/shard_map/ppermute | solution.py:82
  66.1 0.5 stack_reshape.4
  67.2 0.5 copy-done.6
  67.8 0.4 fusion.43
  68.2 0.2 copy-done.9
  68.6 1.2 %collective-permute-done.6 = bf16[256,4,130]{0,2,1:T(8,128)(2,1)S(1)} collective-permute-done((bf16[256,4,130]{0,2,1:T(8,128)(2,1)S(1)}, bf16[256,4,130]{0,2,1:T(8,128)(2,1)S(1)}, u32[]{:S(2)}, u32[]{:S(2)}) %collective-permute-start.6) | collective-permute-done | bytes 266272 | tf_op jit(solution)/shard_map/ppermute | solution.py:93
  69.8 0.2 multiply_reduce_fusion
  70.2 2.0 %fusion.3 = bf16[512,520]{0,1:T(8,128)(2,1)S(1)} fusion(bf16[512,512]{0,1:T(8,128)(2,1)S(1)} %bitcast.204, bf16[256,520]{0,1:T(8,128)(2,1)S(1)} %concatenate.69, bf16[256,520]{0,1:T(8,128)(2,1)S(1)} %concatenate.68, f32[512]{0:T(512)S(1)} %bitcast.232, f32[520]{0:T(1024)S(1)} %rsqrt.50, bf16[2,512,512]{2,1,0:T(8,128)(2,1)} %param.23), kind=kOutput, calls=%fused_computation.24 | convolution fusion | flops 549785600 | bytes 2117664 | tf_op jit(solution)/shard_map/dot_general | solution.py:118
  72.4 1.1 %constant_dynamic-slice_fusion.1 = (bf16[2,1,128,520]{2,1,0,3:T(2,128)(2,1)S(1)}, bf16[2,1,128,520]{2,1,0,3:T(2,128)(2,1)S(1)}) fusion(bf16[2,2,128,520]{2,1,0,3:T(2,128)(2,1)S(1)} %reshape.667, s32[]{:T(128)S(6)} %select_n.159, s32[]{:T(128)S(6)} %select_n.161), kind=kLoop, calls=%fused_computation.188 | loop fusion | bytes 1064968 | tf_op jit(solution)/shard_map/jit(_take) | solution.py:67
  73.5 0.2 collective-permute-start.7
  73.7 1.4 %collective-permute-done.7 = bf16[2,128,520]{1,2,0:T(8,128)(2,1)S(1)} collective-permute-done((bf16[2,128,520]{1,2,0:T(8,128)(2,1)S(1)}, bf16[2,128,520]{1,2,0:T(8,128)(2,1)S(1)}, u32[]{:S(2)}, u32[]{:S(2)}) %collective-permute-start.7) | collective-permute-done | bytes 266272 | tf_op jit(solution)/shard_map/ppermute | solution.py:69
  75.2 1.2 %collective-permute-start.8 = (bf16[256,520]{0,1:T(8,128)(2,1)S(1)}, bf16[256,520]{0,1:T(8,128)(2,1)S(1)}, u32[]{:S(2)}, u32[]{:S(2)}) collective-permute-start(bf16[256,520]{0,1:T(8,128)(2,1)S(1)} %copy_bitcast_fusion.1), channel_id=1, source_target_pairs={{0,2},{1,3},{2,0},{3,1},{4,6},{5,7},{6,4},{7,5},{8,10},{9,11},{10,... | collective-permute-start | bytes 798728 | tf_op jit(solution)/shard_map/ppermute | solution.py:82
  76.4 7.3 %collective-permute-done.8 = bf16[256,520]{0,1:T(8,128)(2,1)S(1)} collective-permute-done((bf16[256,520]{0,1:T(8,128)(2,1)S(1)}, bf16[256,520]{0,1:T(8,128)(2,1)S(1)}, u32[]{:S(2)}, u32[]{:S(2)}) %collective-permute-start.8) | collective-permute-done | bytes 266272 | tf_op jit(solution)/shard_map/ppermute | solution.py:82
  84.0 0.4 fusion.77
  84.5 1.5 %collective-permute-done.9 = bf16[256,4,128]{0,2,1:T(8,128)(2,1)S(1)} collective-permute-done((bf16[256,4,128]{0,2,1:T(8,128)(2,1)S(1)}, bf16[256,4,128]{0,2,1:T(8,128)(2,1)S(1)}, u32[]{:S(2)}, u32[]{:S(2)}) %collective-permute-start.9) | collective-permute-done | bytes 262176 | tf_op jit(solution)/shard_map/ppermute | solution.py:93
  86.2 2.2 %convolution_convert_fusion.2 = bf16[512,512]{0,1:T(8,128)(2,1)S(1)} fusion(bf16[512,512]{0,1:T(8,128)(2,1)S(1)} %bitcast.205, bf16[256,512]{0,1:T(8,128)(2,1)S(1)} %bitcast.209, bf16[256,512]{0,1:T(8,128)(2,1)S(1)} %bitcast.198, bf16[2,512,512]{2,1,0:T(8,128)(2,1)} %param.23, f32[512]{0:T(512)S(1)} %bitcast.233, f32[512]{0:T(512)S(1)} %rsqrt_bitcast_fusion), kind=kOutput, calls=%fused_computation.9 | convolution fusion | flops 541327360 | bytes 2101248 | tf_op jit(solution)/shard_map/dot_general | solution.py:118
  88.4 0.2 collective-permute-start.10
  88.6 1.4 %collective-permute-done.10 = bf16[2,128,512]{2,1,0:T(8,128)(2,1)S(1)} collective-permute-done((bf16[2,128,512]{2,1,0:T(8,128)(2,1)S(1)}, bf16[2,128,512]{2,1,0:T(8,128)(2,1)S(1)}, u32[]{:S(2)}, u32[]{:S(2)}) %collective-permute-start.10) | collective-permute-done | bytes 262176 | tf_op jit(solution)/shard_map/ppermute | solution.py:45
  90.1 1.2 %collective-permute-start.11 = (bf16[128,512]{1,0:T(8,128)(2,1)S(1)}, bf16[128,512]{1,0:T(8,128)(2,1)S(1)}, u32[]{:S(2)}, u32[]{:S(2)}) collective-permute-start(bf16[128,512]{1,0:T(8,128)(2,1)S(1)} %bitcast_convert_fusion), channel_id=1, source_target_pairs={{0,2},{1,3},{2,0},{3,1},{4,6},{5,7},{6,4},{7,5},{8,10},{9,11},{10,... | collective-permute-start | bytes 393224 | tf_op jit(solution)/shard_map/ppermute | solution.py:50
  91.6 4.2 %collective-permute-done.11 = bf16[128,512]{1,0:T(8,128)(2,1)S(1)} collective-permute-done((bf16[128,512]{1,0:T(8,128)(2,1)S(1)}, bf16[128,512]{1,0:T(8,128)(2,1)S(1)}, u32[]{:S(2)}, u32[]{:S(2)}) %collective-permute-start.11) | collective-permute-done | bytes 131104 | tf_op jit(solution)/shard_map/ppermute | solution.py:50
  95.9 0.7 fusion.115
  (98 shorter events, 4.8 us)
Async XLA Ops:
  0.0 12.2 %copy-start = (bf16[3,128,512]{2,1,0:T(8,128)(2,1)S(1)}, bf16[3,128,512]{2,1,0:T(8,128)(2,1)}, u32[]{:S(2)}) copy-start(bf16[3,128,512]{2,1,0:T(8,128)(2,1)} %param.18) | copy-start | bytes 1179652
  0.0 10.6 %copy-start.10 = (f32[512]{0:T(512)S(1)}, f32[512]{0:T(512)}, u32[]{:S(2)}) copy-start(f32[512]{0:T(512)} %param.17) | copy-start | bytes 6148
  14.0 7.8 %copy-start.5 = (f32[2,9,128]{2,0,1:T(2,128)S(1)}, f32[2,9,128]{2,0,1:T(2,128)}, u32[]{:S(2)}) copy-start(f32[2,9,128]{2,0,1:T(2,128)} %param.20) | copy-start | bytes 27652
  14.8 9.1 %copy-start.2 = (bf16[2,512,512]{2,1,0:T(8,128)(2,1)S(1)}, bf16[2,512,512]{2,1,0:T(8,128)(2,1)}, u32[]{:S(2)}) copy-start(bf16[2,512,512]{2,1,0:T(8,128)(2,1)} %param.22) | copy-start | bytes 3145732
  17.2 11.4 %collective-permute-start = (bf16[264,4,128]{2,0,1:T(8,128)(2,1)}, bf16[264,4,128]{2,0,1:T(8,128)(2,1)}, u32[]{:S(2)}, u32[]{:S(2)}) collective-permute-start(bf16[264,4,128]{2,0,1:T(8,128)(2,1)} %pad_maximum_fusion.2), channel_id=1, source_target_pairs={{0,4},{4,8},{8,12},{12,0},{1,5},{5,9},{9,13},{13,1},{2,6},{6,10},{... | collective-permute-start | bytes 811016 | tf_op jit(solution)/shard_map/ppermute | solution.py:215
  18.8 14.6 %collective-permute-start.1 = (bf16[264,4,128]{2,0,1:T(8,128)(2,1)}, bf16[264,4,128]{2,0,1:T(8,128)(2,1)}, u32[]{:S(2)}, u32[]{:S(2)}) collective-permute-start(bf16[264,4,128]{2,0,1:T(8,128)(2,1)} %pad_maximum_fusion.2), channel_id=1, source_target_pairs={{0,12},{4,0},{8,4},{12,8},{1,13},{5,1},{9,5},{13,9},{2,14},{6,2},{... | collective-permute-start | bytes 811016 | tf_op jit(solution)/shard_map/ppermute | solution.py:215
  21.0 24.1 %collective-permute-start.2 = (bf16[256,4,128]{2,0,1:T(8,128)(2,1)}, bf16[256,4,128]{2,0,1:T(8,128)(2,1)}, u32[]{:S(2)}, u32[]{:S(2)}) collective-permute-start(bf16[256,4,128]{2,0,1:T(8,128)(2,1)} %bitcast.6), channel_id=1, source_target_pairs={{0,8},{4,12},{8,0},{12,4},{1,9},{5,13},{9,1},{13,5},{2,10},{6,14},... | collective-permute-start | bytes 786440 | tf_op jit(solution)/shard_map/ppermute | solution.py:215
  21.8 29.3 %collective-permute-start.5 = (f32[2,9,128]{2,0,1:T(2,128)S(1)}, f32[2,9,128]{2,0,1:T(2,128)S(1)}, u32[]{:S(2)}, u32[]{:S(2)}) collective-permute-start(f32[2,9,128]{2,0,1:T(2,128)S(1)} %copy-done.5), channel_id=1, source_target_pairs={{0,2},{1,3},{2,0},{3,1},{4,6},{5,7},{6,4},{7,5},{8,10},{9,11},{10,... | collective-permute-start | bytes 27656 | tf_op jit(solution)/shard_map/ppermute | solution.py:112
  24.4 1.0 copy-start.1
  34.6 10.5 %copy-start.3 = (bf16[1,2,2,64,4,128]{5,3,0,4,2,1:T(8,128)(2,1)S(1)}, bf16[1,2,2,64,4,128]{5,3,0,4,2,1:T(8,128)(2,1)}, u32[]{:S(2)}) copy-start(bf16[1,2,2,64,4,128]{5,3,0,4,2,1:T(8,128)(2,1)} %get-tuple-element.94) | copy-start | bytes 786436
  47.1 1.0 copy-start.4
  50.4 2.6 %collective-permute-start.3 = (bf16[2,128,528]{1,2,0:T(8,128)(2,1)}, bf16[2,128,528]{1,2,0:T(8,128)(2,1)S(1)}, u32[]{:S(2)}, u32[]{:S(2)}) collective-permute-start(bf16[2,128,528]{1,2,0:T(8,128)(2,1)} %fusion.105), channel_id=1, source_target_pairs={{0,1},{1,0},{2,3},{3,2},{4,5},{5,4},{6,7},{7,6},{8,9},{9,8},{10,11... | collective-permute-start | bytes 811016 | tf_op jit(solution)/shard_map/ppermute | solution.py:69
  53.9 12.0 %collective-permute-start.4 = (bf16[260,528]{0,1:T(8,128)(2,1)}, bf16[260,528]{0,1:T(8,128)(2,1)S(1)}, u32[]{:S(2)}, u32[]{:S(2)}) collective-permute-start(bf16[260,528]{0,1:T(8,128)(2,1)} %pad_maximum_fusion.1), channel_id=1, source_target_pairs={{0,2},{1,3},{2,0},{3,1},{4,6},{5,7},{6,4},{7,5},{8,10},{9,11},{10,... | collective-permute-start | bytes 823688 | tf_op jit(solution)/shard_map/ppermute | solution.py:82
  67.1 0.7 copy-start.6
  67.1 0.7 copy-start.7
  67.1 0.7 copy-start.8
  67.8 0.7 copy-start.9
  68.2 1.6 %collective-permute-start.6 = (bf16[256,4,130]{0,2,1:T(8,128)(2,1)S(1)}, bf16[256,4,130]{0,2,1:T(8,128)(2,1)S(1)}, u32[]{:S(2)}, u32[]{:S(2)}) collective-permute-start(bf16[256,4,130]{0,2,1:T(8,128)(2,1)S(1)} %fusion.43), channel_id=1, source_target_pairs={{0,1},{1,0},{2,3},{3,2},{4,5},{5,4},{6,7},{7,6},{8,9},{9,8},{10,11... | collective-permute-start | bytes 798728 | tf_op jit(solution)/shard_map/ppermute | solution.py:93
  73.5 1.6 %collective-permute-start.7 = (bf16[2,128,520]{1,2,0:T(8,128)(2,1)S(1)}, bf16[2,128,520]{1,2,0:T(8,128)(2,1)S(1)}, u32[]{:S(2)}, u32[]{:S(2)}) collective-permute-start(bf16[2,128,520]{1,2,0:T(8,128)(2,1)S(1)} %fusion.108), channel_id=1, source_target_pairs={{0,1},{1,0},{2,3},{3,2},{4,5},{5,4},{6,7},{7,6},{8,9},{9,8},{10,11... | collective-permute-start | bytes 798728 | tf_op jit(solution)/shard_map/ppermute | solution.py:69
  75.2 8.5 %collective-permute-start.8 = (bf16[256,520]{0,1:T(8,128)(2,1)S(1)}, bf16[256,520]{0,1:T(8,128)(2,1)S(1)}, u32[]{:S(2)}, u32[]{:S(2)}) collective-permute-start(bf16[256,520]{0,1:T(8,128)(2,1)S(1)} %copy_bitcast_fusion.1), channel_id=1, source_target_pairs={{0,2},{1,3},{2,0},{3,1},{4,6},{5,7},{6,4},{7,5},{8,10},{9,11},{10,... | collective-permute-start | bytes 798728 | tf_op jit(solution)/shard_map/ppermute | solution.py:82
  84.4 1.6 %collective-permute-start.9 = (bf16[256,4,128]{0,2,1:T(8,128)(2,1)S(1)}, bf16[256,4,128]{0,2,1:T(8,128)(2,1)S(1)}, u32[]{:S(2)}, u32[]{:S(2)}) collective-permute-start(bf16[256,4,128]{0,2,1:T(8,128)(2,1)S(1)} %fusion.77), channel_id=1, source_target_pairs={{0,1},{1,0},{2,3},{3,2},{4,5},{5,4},{6,7},{7,6},{8,9},{9,8},{10,11... | collective-permute-start | bytes 786440 | tf_op jit(solution)/shard_map/ppermute | solution.py:93
  88.4 1.6 %collective-permute-start.10 = (bf16[2,128,512]{2,1,0:T(8,128)(2,1)S(1)}, bf16[2,128,512]{2,1,0:T(8,128)(2,1)S(1)}, u32[]{:S(2)}, u32[]{:S(2)}) collective-permute-start(bf16[2,128,512]{2,1,0:T(8,128)(2,1)S(1)} %select_bitcast_fusion), channel_id=1, source_target_pairs={{0,1},{1,0},{2,3},{3,2},{4,5},{5,4},{6,7},{7,6},{8,9},{9,8},{10,11... | collective-permute-start | bytes 786440 | tf_op jit(solution)/shard_map/ppermute | solution.py:45
  90.1 5.6 %collective-permute-start.11 = (bf16[128,512]{1,0:T(8,128)(2,1)S(1)}, bf16[128,512]{1,0:T(8,128)(2,1)S(1)}, u32[]{:S(2)}, u32[]{:S(2)}) collective-permute-start(bf16[128,512]{1,0:T(8,128)(2,1)S(1)} %bitcast_convert_fusion), channel_id=1, source_target_pairs={{0,2},{1,3},{2,0},{3,1},{4,6},{5,7},{6,4},{7,5},{8,10},{9,11},{10,... | collective-permute-start | bytes 393224 | tf_op jit(solution)/shard_map/ppermute | solution.py:50

commit v17 on v10

--- a/solution.py
+++ b/solution.py
@@ -125,6 +125,7 @@
     head_size = C // H
     heads_local = qkv_weight.shape[1] // head_size
     reach = BLOCKS
+    latent_rim, latent = lax.optimization_barrier((edges(latent, reach), latent))
     gathered = gather_channels(latent)
     normed = norm_channels(gathered.astype(jnp.float32), att_gain).astype(jnp.bfloat16)
     projected = jnp.einsum("koc,crw->korw", qkv_weight, normed, preferred_element_type=jnp.float32)
@@ -134,7 +135,7 @@
     value_rows = projected[2].astype(jnp.bfloat16)
 
     key_value = jnp.stack([key_rows, value_rows]).reshape(-1, lat_rows, columns)
-    rim = jnp.stack([edges(queries.reshape(ch_local, lat_rows, columns), reach), edges(latent, reach)])
+    rim = jnp.stack([edges(queries.reshape(ch_local, lat_rows, columns), reach), latent_rim])
     rim_rows = rim.size // (lat_rows * columns)
     payload = jnp.concatenate([key_value, rim.reshape(rim_rows, lat_rows, columns)], axis=0)
     strips = lax.axis_size("lon")

time: 86.7 us -> 88.5 us (1.021)
  the two profiles are of different devices: /device:TPU:16 before, /device:TPU:20 now
where the time goes in v17:
time: 88.5 us; the launch traced here: 88.3 us
  waiting for transfers between devices  39 us (44%)
  blocking collectives  21.2 us (24%)
  local copies, waits for them, and re-layouts  9.17 us (10%)
  starting transfers between devices  7.41 us (8%)
  matrix products  6.21 us (7%)
  other arithmetic  4.55 us (5%)
    ppermute x3, waiting for transfers between devices, per_device(): got = lax.ppermute(sent, 'lon', pairs)  21.7 us
    all_gather x3, blocking collectives, gather_channels(): return lax.all_gather(values, 'lev', axis=0, tiled=True)  21.2 us
    ppermute x3, waiting for transfers between devices, scatter_sum(): total = total + lax.ppermute(sent, axis, pairs).astype(jnp.float32)  13.8 us
    dot_general x3, matrix products, spread_sum(): lax.dot_general(weight, activation, (((0,), (0,)), ((), ())), preferred_e...  4.41 us
    ppermute x3, waiting for transfers between devices, scatter_sum(): lax.ppermute(theirs, axis, [(i, i ^ 1) for i in range(devices)])  3.52 us
    ppermute x3, starting transfers between devices, scatter_sum(): total = total + lax.ppermute(sent, axis, pairs).astype(jnp.float32)  3.32 us
    ppermute x3, starting transfers between devices, per_device(): got = lax.ppermute(sent, 'lon', pairs)  3.15 us
    another operation x2, local copies, waits for them, and re-layouts, scatter_sum(): mine = jnp.take(blocks, core, axis=1).astype(jnp.float32)  2.23 us
  transfers between devices with their start and end apart: 9, of which 8 were waited for; matrix products, arithmetic and copies ran while one was open for 4% of the time, Pallas kernels for 0%

profile of v17, /device:TPU:20, one launch (start us, length us, event | category | flops | bytes accessed | tf_op | source)
XLA Modules:
  0.0 88.3 jit_solution(1956554527699727907)
XLA Ops:
  0.0 1.2 %fusion.122 = (bf16[128,4,2]{2,1,0:T(4,128)(2,1)S(1)}, bf16[128,4,2]{2,1,0:T(4,128)(2,1)S(1)}) fusion(bf16[128,4,128]{2,1,0:T(4,128)(2,1)} %param.20), kind=kLoop, calls=%fused_computation.220 | loop fusion | bytes 8192 | tf_op jit(solution)/shard_map/slice | solution.py:118
  1.2 0.1 copy.130
  1.3 0.1 copy.131
  1.4 7.4 %all_gather.9 = bf16[512,4,128]{2,1,0:T(4,128)(2,1)S(1)} all-gather(bf16[128,4,128]{2,1,0:T(4,128)(2,1)} %param.20), channel_id=1, replica_groups=mesh['member'=2,'lon'=4,'lev'=4] {'lev'}, dimensions={0}, use_global_device_ids=true | all-gather | bytes 655360 | tf_op jit(solution)/shard_map/all_gather | solution.py:34
  8.8 0.5 fusion.17
  9.4 1.5 %fusion.44 = bf16[512,4,128,1]{2,1,0,3:T(4,128)(2,1)S(1)} fusion(bf16[512,4,128]{2,1,0:T(4,128)(2,1)S(1)} %all_gather.9, f32[512]{0:T(512)S(1)} %copy-done.5, f32[4,128]{1,0:T(4,128)S(1)} %add_rsqrt_fusion.2), kind=kLoop, calls=%fused_computation.68 | loop fusion | flops 1048576 | bytes 1052672 | tf_op jit(solution)/shard_map/convert_element_type | solution.py:130
  10.9 0.4 convolution_bitcast_fusion.2
  11.5 0.1 fusion.118
  11.6 0.4 collective-permute-start.2
  12.1 0.1 fusion.121
  12.2 0.1 copy.96
  12.3 0.1 copy.97
  12.5 0.2 copy.98
  12.7 0.3 reshape.599
  13.1 2.7 %collective-permute-start.1 = (bf16[264,4,128]{2,0,1:T(8,128)(2,1)S(1)}, bf16[264,4,128]{2,0,1:T(8,128)(2,1)S(1)}, u32[]{:S(2)}, u32[]{:S(2)}) collective-permute-start(bf16[264,4,128]{2,0,1:T(8,128)(2,1)S(1)} %pad_maximum_fusion.1), channel_id=1, source_target_pairs={{0,12},{4,0},{8,4},{12,8},{1,13},{5,1},{9,5},{13,9},{2,14},{6,2},{... | collective-permute-start | bytes 811016 | tf_op jit(solution)/shard_map/ppermute | solution.py:147
  15.9 19.4 %collective-permute-done.1 = bf16[264,4,128]{2,0,1:T(8,128)(2,1)S(1)} collective-permute-done((bf16[264,4,128]{2,0,1:T(8,128)(2,1)S(1)}, bf16[264,4,128]{2,0,1:T(8,128)(2,1)S(1)}, u32[]{:S(2)}, u32[]{:S(2)}) %collective-permute-start.1) | collective-permute-done | bytes 270368 | tf_op jit(solution)/shard_map/ppermute | solution.py:147
  35.3 0.6 reshape.601
  35.9 0.1 slice_bitcast_fusion.4
  36.0 2.3 %collective-permute-done = bf16[264,4,128]{2,0,1:T(8,128)(2,1)S(1)} collective-permute-done((bf16[264,4,128]{2,0,1:T(8,128)(2,1)S(1)}, bf16[264,4,128]{2,0,1:T(8,128)(2,1)S(1)}, u32[]{:S(2)}, u32[]{:S(2)}) %collective-permute-start) | collective-permute-done | bytes 270368 | tf_op jit(solution)/shard_map/ppermute | solution.py:147
  38.4 0.6 reshape.600
  39.0 0.2 slice_bitcast_fusion.5
  39.3 0.1 pad_maximum_fusion
  39.3 0.9 %fusion = (f32[2,4,132]{2,1,0:T(4,128)S(1)}, f32[2,4,132,4,128]{4,2,3,1,0:T(8,128)S(1)}) fusion(bf16[4,2,2,64,4,128]{5,3,0,4,2,1:T(8,128)(2,1)S(1)} %pad_maximum_fusion, bf16[2,64,4,2]{3,1,2,0:T(8,128)(2,1)S(1)} %copy.112, bf16[2,64,4,128]{3,1,2,0:T(8,128)(2,1)S(1)} %fusion.104, bf16[2,64,4,2]{3,1,2,0:T(8,128)(2,1)S(1)} %copy.111), kind=kOutput, calls=%fused_computation.1 | convolution fusion | flops 70691808 | bytes 3084416 | tf_op jit(solution)/shard_map/hdri,phdrj->hripj/dot_general | solution.py:73
  40.3 0.5 fusion.37
  40.8 0.3 copy.113
  41.1 0.2 reshape.602
  41.2 0.3 fusion.2
  41.5 0.1 reshape.603
  41.7 1.1 %constant_dynamic-slice_fusion.3 = (bf16[2,1,128,528]{2,1,0,3:T(2,128)(2,1)S(1)}, bf16[2,1,128,528]{2,1,0,3:T(2,128)(2,1)S(1)}) fusion(bf16[2,2,128,528]{2,1,0,3:T(2,128)(2,1)S(1)} %reshape.603, s32[]{:T(128)S(6)} %select_n.94, s32[]{:T(128)S(6)} %select_n.96), kind=kLoop, calls=%fused_computation.171 | loop fusion | bytes 1081352 | tf_op jit(solution)/shard_map/jit(_take) | solution.py:43
  42.9 0.1 collective-permute-start.3
  43.1 0.1 copy.103
  43.2 0.1 broadcast_multiply_fusion.5
  43.3 1.1 %collective-permute-done.3 = bf16[2,128,528]{1,2,0:T(8,128)(2,1)S(1)} collective-permute-done((bf16[2,128,528]{1,2,0:T(8,128)(2,1)S(1)}, bf16[2,128,528]{1,2,0:T(8,128)(2,1)S(1)}, u32[]{:S(2)}, u32[]{:S(2)}) %collective-permute-start.3) | collective-permute-done | bytes 270368 | tf_op jit(solution)/shard_map/ppermute | solution.py:45
  44.5 0.1 convert_add_fusion
  44.6 1.2 %collective-permute-start.4 = (bf16[128,528]{0,1:T(8,128)(2,1)S(1)}, bf16[128,528]{0,1:T(8,128)(2,1)S(1)}, u32[]{:S(2)}, u32[]{:S(2)}) collective-permute-start(bf16[128,528]{0,1:T(8,128)(2,1)S(1)} %bitcast_convert_fusion), channel_id=1, source_target_pairs={{0,2},{1,3},{2,0},{3,1},{4,6},{5,7},{6,4},{7,5},{8,10},{9,11},{10,... | collective-permute-start | bytes 405512 | tf_op jit(solution)/shard_map/ppermute | solution.py:50
  45.8 0.1 copy.104
  45.9 0.1 copy.102
  46.0 4.3 %collective-permute-done.4 = bf16[128,528]{0,1:T(8,128)(2,1)S(1)} collective-permute-done((bf16[128,528]{0,1:T(8,128)(2,1)S(1)}, bf16[128,528]{0,1:T(8,128)(2,1)S(1)}, u32[]{:S(2)}, u32[]{:S(2)}) %collective-permute-start.4) | collective-permute-done | bytes 135200 | tf_op jit(solution)/shard_map/ppermute | solution.py:50
  50.4 0.2 fusion.73
  50.6 7.2 %all_gather.10 = bf16[512,4,130]{0,2,1:T(8,128)(2,1)S(1)} all-gather(bf16[128,4,130]{0,2,1:T(8,128)(2,1)S(1)} %fusion.73), channel_id=1, replica_groups=mesh['member'=2,'lon'=4,'lev'=4] {'lev'}, dimensions={0}, use_global_device_ids=true | all-gather | bytes 665600 | tf_op jit(solution)/shard_map/all_gather | solution.py:34
  57.8 0.2 fusion.4
  58.1 0.2 fusion.6
  58.3 0.1 reshape.605
  58.4 0.8 copy-done.6
  59.3 2.0 %fusion.3 = bf16[512,520]{0,1:T(8,128)(2,1)S(1)} fusion(bf16[512,520]{0,1:T(8,128)(2,1)S(1)} %reshape.605, bf16[2,512,512]{2,1,0:T(8,128)(2,1)S(1)} %copy-done.6, bf16[2,512,512]{2,1,0:T(8,128)(2,1)} %param.26), kind=kOutput, calls=%fused_computation.18 | convolution fusion | flops 547921920 | bytes 2113536 | tf_op jit(solution)/shard_map/dot_general | solution.py:55
  61.3 0.1 reshape.606
  61.4 1.1 %constant_dynamic-slice_fusion.1 = (bf16[2,1,128,520]{2,1,0,3:T(2,128)(2,1)S(1)}, bf16[2,1,128,520]{2,1,0,3:T(2,128)(2,1)S(1)}) fusion(bf16[2,2,128,520]{2,1,0,3:T(2,128)(2,1)S(1)} %reshape.606, s32[]{:T(128)S(6)} %select_n.94, s32[]{:T(128)S(6)} %select_n.96), kind=kLoop, calls=%fused_computation.169 | loop fusion | bytes 1064968 | tf_op jit(solution)/shard_map/jit(_take) | solution.py:43
  62.6 0.4 collective-permute-start.5
  63.0 1.2 %collective-permute-done.5 = bf16[2,128,520]{1,2,0:T(8,128)(2,1)S(1)} collective-permute-done((bf16[2,128,520]{1,2,0:T(8,128)(2,1)S(1)}, bf16[2,128,520]{1,2,0:T(8,128)(2,1)S(1)}, u32[]{:S(2)}, u32[]{:S(2)}) %collective-permute-start.5) | collective-permute-done | bytes 266272 | tf_op jit(solution)/shard_map/ppermute | solution.py:45
  64.2 0.1 convert_add_fusion.1
  64.3 1.0 %collective-permute-start.6 = (bf16[128,520]{0,1:T(8,128)(2,1)S(1)}, bf16[128,520]{0,1:T(8,128)(2,1)S(1)}, u32[]{:S(2)}, u32[]{:S(2)}) collective-permute-start(bf16[128,520]{0,1:T(8,128)(2,1)S(1)} %bitcast_convert_fusion.1), channel_id=1, source_target_pairs={{0,2},{1,3},{2,0},{3,1},{4,6},{5,7},{6,4},{7,5},{8,10},{9,11},{10,... | collective-permute-start | bytes 399368 | tf_op jit(solution)/shard_map/ppermute | solution.py:50
  65.3 4.9 %collective-permute-done.6 = bf16[128,520]{0,1:T(8,128)(2,1)S(1)} collective-permute-done((bf16[128,520]{0,1:T(8,128)(2,1)S(1)}, bf16[128,520]{0,1:T(8,128)(2,1)S(1)}, u32[]{:S(2)}, u32[]{:S(2)}) %collective-permute-start.6) | collective-permute-done | bytes 133152 | tf_op jit(solution)/shard_map/ppermute | solution.py:50
  70.3 0.2 fusion.92
  70.5 6.7 %all_gather.11 = bf16[512,4,128]{0,2,1:T(8,128)(2,1)S(1)} all-gather(bf16[128,4,128]{0,2,1:T(8,128)(2,1)S(1)} %fusion.92), channel_id=1, replica_groups=mesh['member'=2,'lon'=4,'lev'=4] {'lev'}, dimensions={0}, use_global_device_ids=true | all-gather | bytes 655360 | tf_op jit(solution)/shard_map/all_gather | solution.py:34
  77.1 0.2 fusion.20
  77.3 0.2 fusion.22
  77.5 2.1 %convolution_convert_fusion.2 = bf16[512,512]{0,1:T(8,128)(2,1)S(1)} fusion(bf16[512,512]{0,1:T(8,128)(2,1)S(1)} %bitcast.198, bf16[2,512,512]{2,1,0:T(8,128)(2,1)S(1)} %copy-done.6, bf16[2,512,512]{2,1,0:T(8,128)(2,1)} %param.26), kind=kOutput, calls=%fused_computation.15 | convolution fusion | flops 539492352 | bytes 2097152 | tf_op jit(solution)/shard_map/dot_general | solution.py:55
  79.7 0.4 collective-permute-start.7
  80.1 1.2 %collective-permute-done.7 = bf16[2,128,512]{2,1,0:T(8,128)(2,1)S(1)} collective-permute-done((bf16[2,128,512]{2,1,0:T(8,128)(2,1)S(1)}, bf16[2,128,512]{2,1,0:T(8,128)(2,1)S(1)}, u32[]{:S(2)}, u32[]{:S(2)}) %collective-permute-start.7) | collective-permute-done | bytes 262176 | tf_op jit(solution)/shard_map/ppermute | solution.py:45
  81.3 0.1 convert_add_fusion.2
  81.4 1.2 %collective-permute-start.8 = (bf16[128,512]{1,0:T(8,128)(2,1)S(1)}, bf16[128,512]{1,0:T(8,128)(2,1)S(1)}, u32[]{:S(2)}, u32[]{:S(2)}) collective-permute-start(bf16[128,512]{1,0:T(8,128)(2,1)S(1)} %bitcast_convert_fusion.2), channel_id=1, source_target_pairs={{0,2},{1,3},{2,0},{3,1},{4,6},{5,7},{6,4},{7,5},{8,10},{9,11},{10,... | collective-permute-start | bytes 393224 | tf_op jit(solution)/shard_map/ppermute | solution.py:50
  82.6 4.7 %collective-permute-done.8 = bf16[128,512]{1,0:T(8,128)(2,1)S(1)} collective-permute-done((bf16[128,512]{1,0:T(8,128)(2,1)S(1)}, bf16[128,512]{1,0:T(8,128)(2,1)S(1)}, u32[]{:S(2)}, u32[]{:S(2)}) %collective-permute-start.8) | collective-permute-done | bytes 131104 | tf_op jit(solution)/shard_map/ppermute | solution.py:50
  87.3 0.1 copy.119
  87.5 0.8 copy.120
  (59 shorter events, 1.1 us)
Async XLA Ops:
  0.0 10.9 %copy-start = (bf16[3,128,512]{2,1,0:T(8,128)(2,1)S(1)}, bf16[3,128,512]{2,1,0:T(8,128)(2,1)}, u32[]{:S(2)}) copy-start(bf16[3,128,512]{2,1,0:T(8,128)(2,1)} %param.22) | copy-start | bytes 1179652
  0.0 9.4 %copy-start.5 = (f32[512]{0:T(512)S(1)}, f32[512]{0:T(512)}, u32[]{:S(2)}) copy-start(f32[512]{0:T(512)} %param.21) | copy-start | bytes 6148
  11.6 27.7 %collective-permute-start.2 = (bf16[256,4,128]{2,0,1:T(8,128)(2,1)S(1)}, bf16[256,4,128]{2,0,1:T(8,128)(2,1)S(1)}, u32[]{:S(2)}, u32[]{:S(2)}) collective-permute-start(bf16[256,4,128]{2,0,1:T(8,128)(2,1)S(1)} %bitcast.191), channel_id=1, source_target_pairs={{0,8},{4,12},{8,0},{12,4},{1,9},{5,13},{9,1},{13,5},{2,10},{6,14},... | collective-permute-start | bytes 786440 | tf_op jit(solution)/shard_map/ppermute | solution.py:147
  12.1 3.8 %copy-start.3 = (f32[2,9,128]{2,0,1:T(2,128)S(1)}, f32[2,9,128]{2,0,1:T(2,128)}, u32[]{:S(2)}) copy-start(f32[2,9,128]{2,0,1:T(2,128)} %param.24) | copy-start | bytes 27652
  13.1 22.2 %collective-permute-start.1 = (bf16[264,4,128]{2,0,1:T(8,128)(2,1)S(1)}, bf16[264,4,128]{2,0,1:T(8,128)(2,1)S(1)}, u32[]{:S(2)}, u32[]{:S(2)}) collective-permute-start(bf16[264,4,128]{2,0,1:T(8,128)(2,1)S(1)} %pad_maximum_fusion.1), channel_id=1, source_target_pairs={{0,12},{4,0},{8,4},{12,8},{1,13},{5,1},{9,5},{13,9},{2,14},{6,2},{... | collective-permute-start | bytes 811016 | tf_op jit(solution)/shard_map/ppermute | solution.py:147
  15.8 22.5 %collective-permute-start = (bf16[264,4,128]{2,0,1:T(8,128)(2,1)S(1)}, bf16[264,4,128]{2,0,1:T(8,128)(2,1)S(1)}, u32[]{:S(2)}, u32[]{:S(2)}) collective-permute-start(bf16[264,4,128]{2,0,1:T(8,128)(2,1)S(1)} %pad_maximum_fusion.1), channel_id=1, source_target_pairs={{0,4},{4,8},{8,12},{12,0},{1,5},{5,9},{9,13},{13,1},{2,6},{6,10},{... | collective-permute-start | bytes 811016 | tf_op jit(solution)/shard_map/ppermute | solution.py:147
  40.2 1.0 %copy-start.2 = (bf16[128,512]{1,0:T(8,128)(2,1)S(1)}, bf16[128,512]{1,0:T(8,128)(2,1)}, u32[]{:S(2)}) copy-start(bf16[128,512]{1,0:T(8,128)(2,1)} %param.23) | copy-start | bytes 393220
  41.6 1.4 %copy-start.1 = (bf16[128,4,128]{2,1,0:T(4,128)(2,1)S(1)}, bf16[128,4,128]{2,1,0:T(4,128)(2,1)}, u32[]{:S(2)}) copy-start(bf16[128,4,128]{2,1,0:T(4,128)(2,1)} %param.20) | copy-start | bytes 393220
  42.8 2.9 %copy-start.4 = (f32[2,512]{1,0:T(2,128)S(1)}, f32[2,512]{1,0:T(2,128)}, u32[]{:S(2)}) copy-start(f32[2,512]{1,0:T(2,128)} %param.25) | copy-start | bytes 12292
  42.9 1.6 %collective-permute-start.3 = (bf16[2,128,528]{1,2,0:T(8,128)(2,1)S(1)}, bf16[2,128,528]{1,2,0:T(8,128)(2,1)S(1)}, u32[]{:S(2)}, u32[]{:S(2)}) collective-permute-start(bf16[2,128,528]{1,2,0:T(8,128)(2,1)S(1)} %fusion.79), channel_id=1, source_target_pairs={{0,1},{1,0},{2,3},{3,2},{4,5},{5,4},{6,7},{7,6},{8,9},{9,8},{10,11... | collective-permute-start | bytes 811016 | tf_op jit(solution)/shard_map/ppermute | solution.py:45
  44.6 5.7 %collective-permute-start.4 = (bf16[128,528]{0,1:T(8,128)(2,1)S(1)}, bf16[128,528]{0,1:T(8,128)(2,1)S(1)}, u32[]{:S(2)}, u32[]{:S(2)}) collective-permute-start(bf16[128,528]{0,1:T(8,128)(2,1)S(1)} %bitcast_convert_fusion), channel_id=1, source_target_pairs={{0,2},{1,3},{2,0},{3,1},{4,6},{5,7},{6,4},{7,5},{8,10},{9,11},{10,... | collective-permute-start | bytes 405512 | tf_op jit(solution)/shard_map/ppermute | solution.py:50
  58.0 1.2 %copy-start.6 = (bf16[2,512,512]{2,1,0:T(8,128)(2,1)S(1)}, bf16[2,512,512]{2,1,0:T(8,128)(2,1)}, u32[]{:S(2)}) copy-start(bf16[2,512,512]{2,1,0:T(8,128)(2,1)} %param.27) | copy-start | bytes 3145732
  62.6 1.6 %collective-permute-start.5 = (bf16[2,128,520]{1,2,0:T(8,128)(2,1)S(1)}, bf16[2,128,520]{1,2,0:T(8,128)(2,1)S(1)}, u32[]{:S(2)}, u32[]{:S(2)}) collective-permute-start(bf16[2,128,520]{1,2,0:T(8,128)(2,1)S(1)} %fusion.81), channel_id=1, source_target_pairs={{0,1},{1,0},{2,3},{3,2},{4,5},{5,4},{6,7},{7,6},{8,9},{9,8},{10,11... | collective-permute-start | bytes 798728 | tf_op jit(solution)/shard_map/ppermute | solution.py:45
  64.3 5.9 %collective-permute-start.6 = (bf16[128,520]{0,1:T(8,128)(2,1)S(1)}, bf16[128,520]{0,1:T(8,128)(2,1)S(1)}, u32[]{:S(2)}, u32[]{:S(2)}) collective-permute-start(bf16[128,520]{0,1:T(8,128)(2,1)S(1)} %bitcast_convert_fusion.1), channel_id=1, source_target_pairs={{0,2},{1,3},{2,0},{3,1},{4,6},{5,7},{6,4},{7,5},{8,10},{9,11},{10,... | collective-permute-start | bytes 399368 | tf_op jit(solution)/shard_map/ppermute | solution.py:50
  79.7 1.6 %collective-permute-start.7 = (bf16[2,128,512]{2,1,0:T(8,128)(2,1)S(1)}, bf16[2,128,512]{2,1,0:T(8,128)(2,1)S(1)}, u32[]{:S(2)}, u32[]{:S(2)}) collective-permute-start(bf16[2,128,512]{2,1,0:T(8,128)(2,1)S(1)} %select_bitcast_fusion), channel_id=1, source_target_pairs={{0,1},{1,0},{2,3},{3,2},{4,5},{5,4},{6,7},{7,6},{8,9},{9,8},{10,11... | collective-permute-start | bytes 786440 | tf_op jit(solution)/shard_map/ppermute | solution.py:45
  81.4 5.8 %collective-permute-start.8 = (bf16[128,512]{1,0:T(8,128)(2,1)S(1)}, bf16[128,512]{1,0:T(8,128)(2,1)S(1)}, u32[]{:S(2)}, u32[]{:S(2)}) collective-permute-start(bf16[128,512]{1,0:T(8,128)(2,1)S(1)} %bitcast_convert_fusion.2), channel_id=1, source_target_pairs={{0,2},{1,3},{2,0},{3,1},{4,6},{5,7},{6,4},{7,5},{8,10},{9,11},{10,... | collective-permute-start | bytes 393224 | tf_op jit(solution)/shard_map/ppermute | solution.py:50

commit v18 on v16

--- a/solution.py
+++ b/solution.py
@@ -49,13 +49,6 @@
         sent = jnp.take(pair, (chip + shift) % chips, axis=0).astype(jnp.bfloat16)
         total = total + lax.ppermute(sent, axis, pairs).astype(jnp.float32)
     return total
-
-
-def core_half(values, axis=0):
-    devices = lax.axis_size("lev")
-    grouped = values.reshape(*values.shape[:axis], devices // 2, 2, -1, *values.shape[axis + 1 :])
-    taken = jnp.take(grouped, lax.axis_index("lev") % 2, axis=axis + 1)
-    return taken.reshape(*values.shape[:axis], -1, *values.shape[axis + 1 :])
 
 
 def reduce_half(partial, extra=None):
@@ -102,22 +95,11 @@
     return jnp.moveaxis(chosen, axis + 1, axis).reshape(values.shape)
 
 
-def half_weights(weights):
-    devices = lax.axis_size("lev")
-    chips = devices // 2
-    chip = lax.axis_index("lev") // 2
-    stacked = [weights]
-    for shift in range(1, chips):
-        pairs = [(i, ((i // 2 - shift) % chips) * 2 + i % 2) for i in range(devices)]
-        stacked.append(lax.ppermute(weights, "lev", pairs))
-    ordered = jnp.roll(jnp.stack(stacked), chip, axis=0)
-    return jnp.moveaxis(ordered, 0, -2).reshape(*weights.shape[:-1], -1)
-
-
-def group_partial(weight, activation):
-    return lax.dot_general(
+def spread_sum(weight, activation):
+    partial = lax.dot_general(
         weight, activation, (((0,), (0,)), ((), ())), preferred_element_type=jnp.float32
     ).astype(jnp.bfloat16)
+    return scatter_sum(partial, "lev")
 
 
 def gather_strips(values, axis):
@@ -145,7 +127,7 @@
     return (numerator, jnp.sum(weights, axis=(3, 4)))
 
 
-def block_apply(state, block_index, tap_weights, block_gain, up_weight, down_weight, last):
+def smooth(state, tap_weights):
     lat_rows = state.shape[1]
     out_cols = state.shape[2] - 2
     secants = secant_rows(lat_rows)[None, :, None]
@@ -161,23 +143,43 @@
                 stencil_sum = stencil_sum + tap_row * secants * shifted
             else:
                 stencil_sum = stencil_sum + tap_row * shifted
-    smoothed = stencil_sum.astype(jnp.bfloat16)
-    full_channels = gather_half(smoothed)
-    gain = mine_first(block_gain[block_index], 0)
+    return stencil_sum.astype(jnp.bfloat16)
+
+
+def mlp_partial(full_channels, gain, up, down):
     block_normed = norm_channels(full_channels.astype(jnp.float32), gain).astype(jnp.bfloat16)
     block_normed = block_normed.reshape(full_channels.shape[0], -1)
-    hidden = jax.nn.gelu(
-        jnp.dot(mine_first(up_weight[block_index], 1), block_normed, preferred_element_type=jnp.float32)
+    hidden = jax.nn.gelu(jnp.dot(up, block_normed, preferred_element_type=jnp.float32)).astype(
+        jnp.bfloat16
+    )
+    return lax.dot_general(
+        down, hidden, (((0,), (0,)), ((), ())), preferred_element_type=jnp.float32
     ).astype(jnp.bfloat16)
-    partial = group_partial(down_weight[block_index], hidden)
+
+
+def run_blocks(state, stencil_weight, block_gain, up_weight, down_weight):
+    devices = lax.axis_size("lev")
+    chips, chip = devices // 2, lax.axis_index("lev") // 2
+    full = gather_channels(smooth(state, stencil_weight[0]))
+    partial = mlp_partial(full, block_gain[0], up_weight[0], down_weight[0])
     center = state[:, :, 1:-1]
-    if last:
-        chips = lax.axis_size("lev") // 2
-        chip = lax.axis_index("lev") // 2
-        center = jnp.take(center.reshape(chips, -1, *center.shape[1:]), chip, axis=0)
-        update = scatter_sum(partial, "lev")
-    else:
-        update = reduce_half(partial)
+    taps = stencil_weight[1]
+    high = taps.astype(jnp.bfloat16)
+    middle = (taps - high.astype(jnp.float32)).astype(jnp.bfloat16)
+    low = (taps - high.astype(jnp.float32) - middle.astype(jnp.float32)).astype(jnp.bfloat16)
+    extra = jnp.concatenate([center.reshape(-1), high.reshape(-1), middle.reshape(-1), low.reshape(-1)])
+    update, extras = reduce_half(partial, extra)
+    size = center.size
+    centers = extras[:, :size].reshape(chips * center.shape[0], *center.shape[1:])
+    pieces = extras[:, size:].astype(jnp.float32).reshape(chips, 3, *taps.shape)
+    half_taps = jnp.moveaxis(pieces[:, 0] + pieces[:, 1] + pieces[:, 2], 0, -2).reshape(taps.shape[0], -1)
+    state = (centers.astype(jnp.float32) + update.reshape(centers.shape)).astype(jnp.bfloat16)
+    full = gather_half(smooth(state, half_taps))
+    partial = mlp_partial(
+        full, mine_first(block_gain[1], 0), mine_first(up_weight[1], 1), down_weight[1]
+    )
+    center = jnp.take(state[:, :, 1:-1].reshape(chips, -1, *state.shape[1:2], state.shape[2] - 2), chip, axis=0)
+    update = scatter_sum(partial, "lev")
     return (center.astype(jnp.float32) + update.reshape(center.shape)).astype(jnp.bfloat16)
 
 
@@ -193,8 +195,6 @@
     heads_local = qkv_weight.shape[1] // head_size
     reach = BLOCKS
     gathered = gather_channels(latent)
-    taps = half_weights(stencil_weight)
-    own_latent = core_half(gathered)
     normed = norm_channels(gathered.astype(jnp.float32), att_gain).astype(jnp.bfloat16)
     projected = jnp.einsum("koc,crw->korw", qkv_weight, normed, preferred_element_type=jnp.float32)
     projected = projected.reshape(3, heads_local, head_size, lat_rows, columns)
@@ -203,7 +203,7 @@
     value_rows = projected[2].astype(jnp.bfloat16)
 
     key_value = jnp.stack([key_rows, value_rows]).reshape(-1, lat_rows, columns)
-    rim = jnp.concatenate([edges(queries.reshape(ch_local, lat_rows, columns), reach), edges(latent, reach)])
+    rim = jnp.stack([edges(queries.reshape(ch_local, lat_rows, columns), reach), edges(latent, reach)])
     rim_rows = rim.size // (lat_rows * columns)
     payload = jnp.concatenate([key_value, rim.reshape(rim_rows, lat_rows, columns)], axis=0)
     strips = lax.axis_size("lon")
@@ -220,23 +220,17 @@
             from_right = got[key_value.shape[0] :].reshape(rim.shape)[..., :reach]
     all_keys = jnp.stack(pieces).reshape(strips, 2, heads_local, head_size, lat_rows, columns)
     wide_queries = jnp.concatenate(
-        [from_left[:ch_local], queries.reshape(ch_local, lat_rows, columns), from_right[:ch_local]], axis=-1
+        [from_left[0], queries.reshape(ch_local, lat_rows, columns), from_right[0]], axis=-1
     ).reshape(heads_local, head_size, lat_rows, -1)
+    wide_latent = jnp.concatenate([from_left[1], latent, from_right[1]], axis=-1)
 
     numerator, denominator = make_fold(wide_queries, (all_keys[:, 0], all_keys[:, 1]))
     attended = (numerator / denominator[:, None]).astype(jnp.bfloat16)
-    halo = jnp.stack([from_left[ch_local:], from_right[ch_local:]])
-    update, halos = reduce_half(group_partial(out_weight, attended.reshape(ch_local, -1)), halo)
-    halos = jnp.moveaxis(halos, 0, 1).reshape(2, -1, lat_rows, reach)
-    wide_latent = jnp.concatenate([halos[0], own_latent, halos[1]], axis=-1)
+    update = spread_sum(out_weight, attended.reshape(ch_local, -1))
     current = (wide_latent.astype(jnp.float32) + update.reshape(wide_latent.shape)).astype(
         jnp.bfloat16
     )
-    for block_index in range(BLOCKS):
-        current = block_apply(
-            current, block_index, taps[block_index], block_gain, up_weight, down_weight,
-            block_index == BLOCKS - 1,
-        )
+    current = run_blocks(current, stencil_weight, block_gain, up_weight, down_weight)
     return current
 
 

time: 97.2 us -> 110 us (1.13)
  blocking collectives: 8.95 us -> 16.1 us
  waiting for transfers between devices: 40.3 us -> 45.4 us
  starting transfers between devices: 9.78 us -> 8.55 us
    ppermute x3, waiting for transfers between devices: 14 us -> 21.3 us  [per_device(): got = lax.ppermute(sent, 'lon', pairs)]
    all_gather x1 -> x2, blocking collectives: 8.95 us -> 16.1 us  [gather_channels(): return lax.all_gather(values, 'lev', axis=0, tiled=True)]
    convert_element_type x5 -> x8, other arithmetic: 1.68 us -> 6.64 us  [the longest x2 5.09 us: smooth(): return stencil_sum.astype(jnp.bfloat16)]
    ppermute x2 -> x1, waiting for transfers between devices: 16.7 us -> 11.9 us  [reduce_half(): got = lax.ppermute(sent, 'lev', pairs)]
    ppermute x1 -> x2, waiting for transfers between devices: 4.17 us -> 8.08 us  [scatter_sum(): total = total + lax.ppermute(sent, axis, pairs).astype(jnp.float32)]
    concatenate x1 -> x2, other arithmetic: 0.02 us -> 2.42 us  [the longest x1 2.4 us: reduce_half(): return (total, jnp.roll(jnp.stack(extras), chip, axis=0))]
    slice x2, local copies, waits for them, and re-layouts: 1.95 us -> 0.04 us  [per_device(): pieces.append(got[:key_value.shape[0]])]
    convert_element_type x0 -> x1, local copies, waits for them, and re-layouts: none -> 1.72 us  [run_blocks(): centers.astype(jnp.float32) + update.reshape(centers.shape)]
  transfers between devices with their start and end apart: 12 -> 10, of which waited for: 10 -> 10; matrix products, arithmetic and copies ran while one was open for 18% -> 5% of each run, Pallas kernels for 0% -> 0%
where the time goes in v18:
time: 110 us; the launch traced here: 109 us
  waiting for transfers between devices  45.4 us (41%)
  local copies, waits for them, and re-layouts  18.4 us (17%)
  blocking collectives  16.1 us (15%)
  other arithmetic  13.5 us (12%)
  starting transfers between devices  8.55 us (8%)
  matrix products  6.2 us (6%)
    ppermute x3, waiting for transfers between devices, per_device(): got = lax.ppermute(sent, 'lon', pairs)  21.3 us
    all_gather x2, blocking collectives, gather_channels(): return lax.all_gather(values, 'lev', axis=0, tiled=True)  16.1 us
    ppermute x1, waiting for transfers between devices, reduce_half(): got = lax.ppermute(sent, 'lev', pairs)  11.9 us
    ppermute x2, waiting for transfers between devices, scatter_sum(): total = total + lax.ppermute(sent, axis, pairs).astype(jnp.float32)  8.08 us
    convert_element_type x2, other arithmetic, smooth(): return stencil_sum.astype(jnp.bfloat16)  5.09 us
    ppermute x3, starting transfers between devices, per_device(): got = lax.ppermute(sent, 'lon', pairs)  4.67 us
    unnamed x49, local copies, waits for them, and re-layouts  4.2 us
    dot_general x2, matrix products, mlp_partial(): lax.dot_general(down, hidden, (((0,), (0,)), ((), ())), preferred_element...  4.13 us
  transfers between devices with their start and end apart: 10, of which 10 were waited for; matrix products, arithmetic and copies ran while one was open for 5% of the time, Pallas kernels for 0%

profile of v18, /device:TPU:0, one launch (start us, length us, event | category | flops | bytes accessed | tf_op | source)
XLA Modules:
  0.0 109.2 jit_solution(15750563057679275213)
XLA Ops:
  0.0 8.9 %all_gather.6 = bf16[512,4,128]{2,1,0:T(4,128)(2,1)S(1)} all-gather(bf16[128,4,128]{2,1,0:T(4,128)(2,1)} %param.18), channel_id=1, replica_groups=mesh['member'=2,'lon'=4,'lev'=4] {'lev'}, dimensions={0}, use_global_device_ids=true | all-gather | bytes 655360 | tf_op jit(solution)/shard_map/all_gather | solution.py:34
  9.0 1.0 copy.147
  10.0 0.5 fusion.17
  10.6 1.5 %fusion.43 = bf16[512,4,128,1]{2,1,0,3:T(4,128)(2,1)S(1)} fusion(bf16[512,4,128]{2,1,0:T(4,128)(2,1)S(1)} %all_gather.6, f32[512]{0:T(512)S(1)} %copy-done.18, f32[4,128]{1,0:T(4,128)S(1)} %add_rsqrt_fusion.1), kind=kLoop, calls=%fused_computation.74 | loop fusion | flops 1048576 | bytes 1052672 | tf_op jit(solution)/shard_map/convert_element_type | solution.py:198
  12.1 0.4 convolution_bitcast_fusion.1
  13.1 0.2 copy.149
  13.3 0.3 reshape.645
  13.9 1.6 %collective-permute-start = (bf16[264,4,128]{2,0,1:T(8,128)(2,1)S(1)}, bf16[264,4,128]{2,0,1:T(8,128)(2,1)S(1)}, u32[]{:S(2)}, u32[]{:S(2)}) collective-permute-start(bf16[264,4,128]{2,0,1:T(8,128)(2,1)S(1)} %pad_maximum_fusion.2), channel_id=1, source_target_pairs={{0,4},{4,8},{8,12},{12,0},{1,5},{5,9},{9,13},{13,1},{2,6},{6,10},{... | collective-permute-start | bytes 811016 | tf_op jit(solution)/shard_map/ppermute | solution.py:215
  15.5 2.2 %collective-permute-start.1 = (bf16[264,4,128]{2,0,1:T(8,128)(2,1)S(1)}, bf16[264,4,128]{2,0,1:T(8,128)(2,1)S(1)}, u32[]{:S(2)}, u32[]{:S(2)}) collective-permute-start(bf16[264,4,128]{2,0,1:T(8,128)(2,1)S(1)} %pad_maximum_fusion.2), channel_id=1, source_target_pairs={{0,12},{4,0},{8,4},{12,8},{1,13},{5,1},{9,5},{13,9},{2,14},{6,2},{... | collective-permute-start | bytes 811016 | tf_op jit(solution)/shard_map/ppermute | solution.py:215
  17.8 0.8 collective-permute-start.2
  18.7 6.4 %collective-permute-done = bf16[264,4,128]{2,0,1:T(8,128)(2,1)S(1)} collective-permute-done((bf16[264,4,128]{2,0,1:T(8,128)(2,1)S(1)}, bf16[264,4,128]{2,0,1:T(8,128)(2,1)S(1)}, u32[]{:S(2)}, u32[]{:S(2)}) %collective-permute-start) | collective-permute-done | bytes 270368 | tf_op jit(solution)/shard_map/ppermute | solution.py:215
  25.1 0.6 reshape.646
  25.6 0.2 slice_bitcast_fusion.5
  25.9 3.9 %collective-permute-done.1 = bf16[264,4,128]{2,0,1:T(8,128)(2,1)S(1)} collective-permute-done((bf16[264,4,128]{2,0,1:T(8,128)(2,1)S(1)}, bf16[264,4,128]{2,0,1:T(8,128)(2,1)S(1)}, u32[]{:S(2)}, u32[]{:S(2)}) %collective-permute-start.1) | collective-permute-done | bytes 270368 | tf_op jit(solution)/shard_map/ppermute | solution.py:215
  29.8 0.6 reshape.647
  30.5 11.0 %collective-permute-done.2 = bf16[256,4,128]{2,0,1:T(8,128)(2,1)S(1)} collective-permute-done((bf16[256,4,128]{2,0,1:T(8,128)(2,1)S(1)}, bf16[256,4,128]{2,0,1:T(8,128)(2,1)S(1)}, u32[]{:S(2)}, u32[]{:S(2)}) %collective-permute-start.2) | collective-permute-done | bytes 262176 | tf_op jit(solution)/shard_map/ppermute | solution.py:215
  41.6 0.9 fusion
  42.5 0.5 fusion.34
  43.1 0.3 copy.164
  43.3 0.1 reshape.648
  43.5 0.3 fusion.2
  43.9 1.1 %constant_dynamic-slice_fusion.3 = (bf16[2,1,128,528]{2,1,0,3:T(2,128)(2,1)S(1)}, bf16[2,1,128,528]{2,1,0,3:T(2,128)(2,1)S(1)}) fusion(bf16[2,2,128,528]{2,1,0,3:T(2,128)(2,1)S(1)} %reshape.649, s32[]{:T(128)S(6)} %select_n.132, s32[]{:T(128)S(6)} %select_n.134), kind=kLoop, calls=%fused_computation.202 | loop fusion | bytes 1081352 | tf_op jit(solution)/shard_map/jit(_take) | solution.py:43
  45.4 1.4 %collective-permute-done.3 = bf16[2,128,528]{1,2,0:T(8,128)(2,1)S(1)} collective-permute-done((bf16[2,128,528]{1,2,0:T(8,128)(2,1)S(1)}, bf16[2,128,528]{1,2,0:T(8,128)(2,1)S(1)}, u32[]{:S(2)}, u32[]{:S(2)}) %collective-permute-start.3) | collective-permute-done | bytes 270368 | tf_op jit(solution)/shard_map/ppermute | solution.py:45
  46.8 1.2 %collective-permute-start.4 = (bf16[128,528]{0,1:T(8,128)(2,1)S(1)}, bf16[128,528]{0,1:T(8,128)(2,1)S(1)}, u32[]{:S(2)}, u32[]{:S(2)}) collective-permute-start(bf16[128,528]{0,1:T(8,128)(2,1)S(1)} %bitcast_convert_fusion), channel_id=1, source_target_pairs={{0,2},{1,3},{2,0},{3,1},{4,6},{5,7},{6,4},{7,5},{8,10},{9,11},{10,... | collective-permute-start | bytes 405512 | tf_op jit(solution)/shard_map/ppermute | solution.py:50
  48.0 0.6 fusion.140
  48.9 3.7 %collective-permute-done.4 = bf16[128,528]{0,1:T(8,128)(2,1)S(1)} collective-permute-done((bf16[128,528]{0,1:T(8,128)(2,1)S(1)}, bf16[128,528]{0,1:T(8,128)(2,1)S(1)}, u32[]{:S(2)}, u32[]{:S(2)}) %collective-permute-start.4) | collective-permute-done | bytes 135200 | tf_op jit(solution)/shard_map/ppermute | solution.py:50
  52.7 0.2 fusion.96
  52.9 7.2 %all_gather.7 = bf16[512,4,130]{0,2,1:T(8,128)(2,1)S(1)} all-gather(bf16[128,4,130]{0,2,1:T(8,128)(2,1)S(1)} %fusion.96), channel_id=1, replica_groups=mesh['member'=2,'lon'=4,'lev'=4] {'lev'}, dimensions={0}, use_global_device_ids=true | all-gather | bytes 665600 | tf_op jit(solution)/shard_map/all_gather | solution.py:34
  60.1 0.2 fusion.4
  60.3 0.2 fusion.6
  60.7 0.8 copy-done.2
  61.5 2.0 %fusion.3 = bf16[512,520]{0,1:T(8,128)(2,1)S(1)} fusion(bf16[512,520]{0,1:T(8,128)(2,1)S(1)} %reshape.652, bf16[2,512,512]{2,1,0:T(8,128)(2,1)} %param.25, bf16[2,512,512]{2,1,0:T(8,128)(2,1)S(1)} %copy-done.2), kind=kOutput, calls=%fused_computation.21 | convolution fusion | flops 547921920 | bytes 2113536 | tf_op jit(solution)/shard_map/dot_general | solution.py:155
  63.7 1.1 %constant_dynamic-slice_fusion = (bf16[2,1,128,520]{2,1,0,3:T(2,128)(2,1)S(1)}, bf16[2,1,128,520]{2,1,0,3:T(2,128)(2,1)S(1)}) fusion(bf16[2,2,128,520]{2,1,0,3:T(2,128)(2,1)S(1)} %reshape.653, s32[]{:T(128)S(6)} %select_n.132, s32[]{:T(128)S(6)} %select_n.134), kind=kLoop, calls=%fused_computation.199 | loop fusion | bytes 1064968 | tf_op jit(solution)/shard_map/jit(_take) | solution.py:60
  64.8 0.4 collective-permute-start.5
  65.3 0.2 copy.167
  65.5 0.4 reshape.651
  65.9 0.3 reshape.655
  66.4 0.7 copy-done.3
  67.4 1.1 copy.173
  68.4 0.9 collective-permute-start.6
  69.3 1.0 copy.196
  70.5 11.9 %collective-permute-done.6 = bf16[391,520]{1,0:T(8,128)(2,1)} collective-permute-done((bf16[391,520]{1,0:T(8,128)(2,1)}, bf16[391,520]{1,0:T(8,128)(2,1)}, u32[]{:S(2)}, u32[]{:S(2)}) %collective-permute-start.6) | collective-permute-done | bytes 406672 | tf_op jit(solution)/shard_map/ppermute | solution.py:75
  82.4 0.9 slice.407
  83.4 0.3 reshape.656
  83.8 2.4 %fusion.86 = bf16[2,70016]{1,0:T(2,128)(2,1)S(1)} fusion(s32[]{:T(128)S(6)} %select_n.99, bf16[1,70016]{1,0:T(2,128)(2,1)S(1)} %stack.45, bf16[1,70016]{1,0:T(2,128)(2,1)S(1)} %stack.44), kind=kLoop, calls=%fused_computation.116 | loop fusion | flops 1120256 | bytes 560132 | tf_op jit(solution)/shard_map/jit(_roll_dynamic)/concatenate | solution.py:81
  86.2 0.2 slice_convert_fusion
  86.5 0.6 fusion.139
  87.1 1.0 slice.410
  88.1 0.2 copy.195
  88.5 0.4 copy.175
  88.9 1.7 %reshape.899 = f32[256,4,130]{2,1,0:T(4,128)S(1)} reshape(f32[2,66560]{1,0:T(2,128)S(1)} %slice_convert_fusion) | data formatting | bytes 1064960 | tf_op jit(solution)/shard_map/convert_element_type | solution.py:176
  90.7 0.4 fusion.135
  91.1 0.2 copy-done.8
  91.4 0.3 broadcast_multiply_fusion.5
  91.7 4.9 %fusion.82 = bf16[256,4,128]{2,1,0:T(4,128)(2,1)S(1)} fusion(f32[256,4,130]{2,1,0:T(4,128)S(1)} %get-tuple-element.76, f32[256,4]{1,0:T(8,128)S(1)} %get-tuple-element.124, f32[256]{0:T(256)S(1)} %bitcast.245, f32[256,4]{1,0:T(8,128)S(1)} %get-tuple-element.123, f32[256,4]{1,0:T(8,128)S(1)} %get-tuple-element.122, f32[256]{0:T(256)S(1)} %bitcast.246, ...), kind=kLoop, calls=%fused_computation.112 | loop fusion | flops 2359296 | bytes 3673088 | tf_op jit(solution)/shard_map/convert_element_type | solution.py:146
  96.9 1.3 %collective-permute-done.7 = bf16[256,4,128]{2,1,0:T(4,128)(2,1)S(1)} collective-permute-done((bf16[256,4,128]{2,1,0:T(4,128)(2,1)S(1)}, bf16[256,4,128]{2,1,0:T(4,128)(2,1)S(1)}, u32[]{:S(2)}, u32[]{:S(2)}) %collective-permute-start.7) | collective-permute-done | bytes 262176 | tf_op jit(solution)/shard_map/ppermute | solution.py:86
  98.2 0.5 multiply_reduce_fusion
  98.8 2.1 %convolution_convert_fusion.2 = bf16[512,512]{0,1:T(8,128)(2,1)S(1)} fusion(bf16[512,512]{0,1:T(8,128)(2,1)S(1)} %bitcast.229, bf16[256,512]{1,0:T(8,128)(2,1)S(1)} %bitcast.234, bf16[256,512]{1,0:T(8,128)(2,1)S(1)} %bitcast.233, bf16[2,512,512]{2,1,0:T(8,128)(2,1)} %param.25, f32[512]{0:T(512)S(1)} %bitcast.248, f32[512]{0:T(512)S(1)} %rsqrt_bitcast_fusion), kind=kOutput, calls=%fused_computation.18 | convolution fusion | flops 541327360 | bytes 2101248 | tf_op jit(solution)/shard_map/dot_general | solution.py:155
  101.0 0.2 collective-permute-start.8
  101.2 1.4 %collective-permute-done.8 = bf16[2,128,512]{2,1,0:T(8,128)(2,1)S(1)} collective-permute-done((bf16[2,128,512]{2,1,0:T(8,128)(2,1)S(1)}, bf16[2,128,512]{2,1,0:T(8,128)(2,1)S(1)}, u32[]{:S(2)}, u32[]{:S(2)}) %collective-permute-start.8) | collective-permute-done | bytes 262176 | tf_op jit(solution)/shard_map/ppermute | solution.py:45
  102.7 1.0 collective-permute-start.9
  103.7 0.2 slice.411
  103.9 4.4 %collective-permute-done.9 = bf16[128,512]{1,0:T(8,128)(2,1)S(1)} collective-permute-done((bf16[128,512]{1,0:T(8,128)(2,1)S(1)}, bf16[128,512]{1,0:T(8,128)(2,1)S(1)}, u32[]{:S(2)}, u32[]{:S(2)}) %collective-permute-start.9) | collective-permute-done | bytes 131104 | tf_op jit(solution)/shard_map/ppermute | solution.py:50
  108.4 0.7 fusion.112
  (119 shorter events, 3.9 us)
Async XLA Ops:
  0.0 12.1 %copy-start = (bf16[3,128,512]{2,1,0:T(8,128)(2,1)S(1)}, bf16[3,128,512]{2,1,0:T(8,128)(2,1)}, u32[]{:S(2)}) copy-start(bf16[3,128,512]{2,1,0:T(8,128)(2,1)} %param.20) | copy-start | bytes 1179652
  0.0 10.5 %copy-start.18 = (f32[512]{0:T(512)S(1)}, f32[512]{0:T(512)}, u32[]{:S(2)}) copy-start(f32[512]{0:T(512)} %param.19) | copy-start | bytes 6148
  13.7 4.8 %copy-start.6 = (f32[2,9,128]{2,0,1:T(2,128)S(1)}, f32[2,9,128]{2,0,1:T(2,128)}, u32[]{:S(2)}) copy-start(f32[2,9,128]{2,0,1:T(2,128)} %param.22) | copy-start | bytes 27652
  13.9 11.2 %collective-permute-start = (bf16[264,4,128]{2,0,1:T(8,128)(2,1)S(1)}, bf16[264,4,128]{2,0,1:T(8,128)(2,1)S(1)}, u32[]{:S(2)}, u32[]{:S(2)}) collective-permute-start(bf16[264,4,128]{2,0,1:T(8,128)(2,1)S(1)} %pad_maximum_fusion.2), channel_id=1, source_target_pairs={{0,4},{4,8},{8,12},{12,0},{1,5},{5,9},{9,13},{13,1},{2,6},{6,10},{... | collective-permute-start | bytes 811016 | tf_op jit(solution)/shard_map/ppermute | solution.py:215
  15.5 14.2 %collective-permute-start.1 = (bf16[264,4,128]{2,0,1:T(8,128)(2,1)S(1)}, bf16[264,4,128]{2,0,1:T(8,128)(2,1)S(1)}, u32[]{:S(2)}, u32[]{:S(2)}) collective-permute-start(bf16[264,4,128]{2,0,1:T(8,128)(2,1)S(1)} %pad_maximum_fusion.2), channel_id=1, source_target_pairs={{0,12},{4,0},{8,4},{12,8},{1,13},{5,1},{9,5},{13,9},{2,14},{6,2},{... | collective-permute-start | bytes 811016 | tf_op jit(solution)/shard_map/ppermute | solution.py:215
  17.8 23.8 %collective-permute-start.2 = (bf16[256,4,128]{2,0,1:T(8,128)(2,1)S(1)}, bf16[256,4,128]{2,0,1:T(8,128)(2,1)S(1)}, u32[]{:S(2)}, u32[]{:S(2)}) collective-permute-start(bf16[256,4,128]{2,0,1:T(8,128)(2,1)S(1)} %bitcast.221), channel_id=1, source_target_pairs={{0,8},{4,12},{8,0},{12,4},{1,9},{5,13},{9,1},{13,5},{2,10},{6,14},... | collective-permute-start | bytes 786440 | tf_op jit(solution)/shard_map/ppermute | solution.py:215
  18.6 26.6 %copy-start.19 = (f32[4]{0:T(128)}, f32[4]{0:T(128)S(1)}, u32[]{:S(2)}) copy-start(f32[4]{0:T(128)S(1)} %cosine_divide_fusion) | copy-start | bytes 52
  42.5 1.0 copy-start.5
  45.0 3.0 %copy-start.14 = (f32[2,512]{1,0:T(2,128)S(1)}, f32[2,512]{1,0:T(2,128)}, u32[]{:S(2)}) copy-start(f32[2,512]{1,0:T(2,128)} %param.23) | copy-start | bytes 12292
  45.1 1.6 %collective-permute-start.3 = (bf16[2,128,528]{1,2,0:T(8,128)(2,1)S(1)}, bf16[2,128,528]{1,2,0:T(8,128)(2,1)S(1)}, u32[]{:S(2)}, u32[]{:S(2)}) collective-permute-start(bf16[2,128,528]{1,2,0:T(8,128)(2,1)S(1)} %fusion.102), channel_id=1, source_target_pairs={{0,1},{1,0},{2,3},{3,2},{4,5},{5,4},{6,7},{7,6},{8,9},{9,8},{10,11... | collective-permute-start | bytes 811016 | tf_op jit(solution)/shard_map/ppermute | solution.py:45
  46.8 5.7 %collective-permute-start.4 = (bf16[128,528]{0,1:T(8,128)(2,1)S(1)}, bf16[128,528]{0,1:T(8,128)(2,1)S(1)}, u32[]{:S(2)}, u32[]{:S(2)}) collective-permute-start(bf16[128,528]{0,1:T(8,128)(2,1)S(1)} %bitcast_convert_fusion), channel_id=1, source_target_pairs={{0,2},{1,3},{2,0},{3,1},{4,6},{5,7},{6,4},{7,5},{8,10},{9,11},{10,... | collective-permute-start | bytes 405512 | tf_op jit(solution)/shard_map/ppermute | solution.py:50
  60.3 1.2 %copy-start.2 = (bf16[2,512,512]{2,1,0:T(8,128)(2,1)S(1)}, bf16[2,512,512]{2,1,0:T(8,128)(2,1)}, u32[]{:S(2)}) copy-start(bf16[2,512,512]{2,1,0:T(8,128)(2,1)} %param.24) | copy-start | bytes 3145732
  64.8 1.6 %collective-permute-start.5 = (bf16[2,128,520]{1,2,0:T(8,128)(2,1)S(1)}, bf16[2,128,520]{1,2,0:T(8,128)(2,1)S(1)}, u32[]{:S(2)}, u32[]{:S(2)}) collective-permute-start(bf16[2,128,520]{1,2,0:T(8,128)(2,1)S(1)} %fusion.105), channel_id=1, source_target_pairs={{0,1},{1,0},{2,3},{3,2},{4,5},{5,4},{6,7},{7,6},{8,9},{9,8},{10,11... | collective-permute-start | bytes 798728 | tf_op jit(solution)/shard_map/ppermute | solution.py:62
  66.4 0.7 copy-start.3
  67.3 2.0 %slice-start = ((bf16[2,512,512]{2,1,0:T(8,128)(2,1)}), bf16[1,512,512]{2,1,0:T(8,128)(2,1)S(1)}, s32[]{:S(2)}) async-start(bf16[2,512,512]{2,1,0:T(8,128)(2,1)} %param.24), calls=%async_computation | async-start | bytes 1048576 | tf_op jit(solution)/shard_map/slice | solution.py:179
  68.4 14.0 %collective-permute-start.6 = (bf16[391,520]{1,0:T(8,128)(2,1)}, bf16[391,520]{1,0:T(8,128)(2,1)}, u32[]{:S(2)}, u32[]{:S(2)}) collective-permute-start(bf16[391,520]{1,0:T(8,128)(2,1)} %copy.173), channel_id=1, source_target_pairs={{0,2},{1,3},{2,0},{3,1},{4,6},{5,7},{6,4},{7,5},{8,10},{9,11},{10,... | collective-permute-start | bytes 1219928 | tf_op jit(solution)/shard_map/ppermute | solution.py:75
  86.2 2.0 %copy-start.4 = (bf16[2,128,520]{1,2,0:T(8,128)(2,1)S(1)}, bf16[2,128,520]{1,2,0:T(8,128)(2,1)}, u32[]{:S(2)}) copy-start(bf16[2,128,520]{1,2,0:T(8,128)(2,1)} %copy-done.3) | copy-start | bytes 798724
  90.6 0.7 copy-start.8
  90.6 0.7 copy-start.9
  90.6 0.7 copy-start.10
  90.6 0.7 copy-start.11
  90.7 0.7 copy-start.12
  90.7 0.7 copy-start.13
  90.7 0.7 copy-start.20
  90.7 0.9 copy-start.15
  90.7 0.9 copy-start.16
  90.7 0.9 copy-start.17
  91.7 5.0 %copy-start.1 = (bf16[1,512,512]{1,2,0:T(8,128)(2,1)S(1)}, bf16[1,512,512]{1,2,0:T(8,128)(2,1)}, u32[]{:S(2)}) copy-start(bf16[1,512,512]{1,2,0:T(8,128)(2,1)} %copy.196) | copy-start | bytes 1572868
  91.7 5.1 %copy-start.7 = (f32[1,512]{1,0:T(1,128)S(1)}, f32[1,512]{1,0:T(1,128)}, u32[]{:S(2)}) copy-start(f32[1,512]{1,0:T(1,128)} %get-tuple-element.117) | copy-start | bytes 6148
  96.6 1.6 %collective-permute-start.7 = (bf16[256,4,128]{2,1,0:T(4,128)(2,1)S(1)}, bf16[256,4,128]{2,1,0:T(4,128)(2,1)S(1)}, u32[]{:S(2)}, u32[]{:S(2)}) collective-permute-start(bf16[256,4,128]{2,1,0:T(4,128)(2,1)S(1)} %fusion.82), channel_id=1, source_target_pairs={{0,1},{1,0},{2,3},{3,2},{4,5},{5,4},{6,7},{7,6},{8,9},{9,8},{10,11... | collective-permute-start | bytes 786440 | tf_op jit(solution)/shard_map/ppermute | solution.py:86
  101.0 1.6 %collective-permute-start.8 = (bf16[2,128,512]{2,1,0:T(8,128)(2,1)S(1)}, bf16[2,128,512]{2,1,0:T(8,128)(2,1)S(1)}, u32[]{:S(2)}, u32[]{:S(2)}) collective-permute-start(bf16[2,128,512]{2,1,0:T(8,128)(2,1)S(1)} %select_bitcast_fusion), channel_id=1, source_target_pairs={{0,1},{1,0},{2,3},{3,2},{4,5},{5,4},{6,7},{7,6},{8,9},{9,8},{10,11... | collective-permute-start | bytes 786440 | tf_op jit(solution)/shard_map/ppermute | solution.py:45
  102.7 5.6 %collective-permute-start.9 = (bf16[128,512]{1,0:T(8,128)(2,1)S(1)}, bf16[128,512]{1,0:T(8,128)(2,1)S(1)}, u32[]{:S(2)}, u32[]{:S(2)}) collective-permute-start(bf16[128,512]{1,0:T(8,128)(2,1)S(1)} %bitcast_convert_fusion.1), channel_id=1, source_target_pairs={{0,2},{1,3},{2,0},{3,1},{4,6},{5,7},{6,4},{7,5},{8,10},{9,11},{10,... | collective-permute-start | bytes 393224 | tf_op jit(solution)/shard_map/ppermute | solution.py:50

commit v19 on v10

--- a/solution.py
+++ b/solution.py
@@ -142,8 +142,7 @@
     from_left = from_right = None
     for shift in range(1, strips):
         pairs = [(i, (i + shift) % strips) for i in range(strips)]
-        sent = payload if shift in (1, strips - 1) else key_value
-        got = lax.ppermute(sent, "lon", pairs)
+        got = lax.ppermute(payload, "lon", pairs)
         pieces.append(got[: key_value.shape[0]])
         if shift == 1:
             from_left = got[key_value.shape[0] :].reshape(rim.shape)[..., reach:]

time: 86.7 us -> 89.1 us (1.028)
  waiting for transfers between devices: 39 us -> 40.7 us
    ppermute x3, waiting for transfers between devices: 21.5 us -> 23.2 us  [per_device(): got = lax.ppermute(payload, 'lon', pairs)]
  transfers between devices with their start and end apart: 9 -> 9, of which waited for: 8 -> 8; matrix products, arithmetic and copies ran while one was open for 4% -> 2% of each run, Pallas kernels for 0% -> 0%
where the time goes in v19:
time: 89.1 us; the launch traced here: 88.9 us
  waiting for transfers between devices  40.7 us (46%)
  blocking collectives  21.3 us (24%)
  local copies, waits for them, and re-layouts  7.89 us (9%)
  starting transfers between devices  7.36 us (8%)
  matrix products  6.38 us (7%)
  other arithmetic  4.54 us (5%)
    ppermute x3, waiting for transfers between devices, per_device(): got = lax.ppermute(payload, 'lon', pairs)  23.2 us
    all_gather x3, blocking collectives, gather_channels(): return lax.all_gather(values, 'lev', axis=0, tiled=True)  21.3 us
    ppermute x3, waiting for transfers between devices, scatter_sum(): total = total + lax.ppermute(sent, axis, pairs).astype(jnp.float32)  13.8 us
    dot_general x3, matrix products, spread_sum(): lax.dot_general(weight, activation, (((0,), (0,)), ((), ())), preferred_e...  4.58 us
    ppermute x3, waiting for transfers between devices, scatter_sum(): lax.ppermute(theirs, axis, [(i, i ^ 1) for i in range(devices)])  3.68 us
    ppermute x3, starting transfers between devices, scatter_sum(): total = total + lax.ppermute(sent, axis, pairs).astype(jnp.float32)  3.31 us
    ppermute x3, starting transfers between devices, per_device(): got = lax.ppermute(payload, 'lon', pairs)  3.11 us
    another operation x2, local copies, waits for them, and re-layouts, scatter_sum(): mine = jnp.take(blocks, core, axis=1).astype(jnp.float32)  2.23 us
  transfers between devices with their start and end apart: 9, of which 8 were waited for; matrix products, arithmetic and copies ran while one was open for 2% of the time, Pallas kernels for 0%

profile of v19, /device:TPU:16, one launch (start us, length us, event | category | flops | bytes accessed | tf_op | source)
XLA Modules:
  0.0 88.9 jit_solution(18324145986154233549)
XLA Ops:
  0.0 1.1 %copy.96 = bf16[128,4,128]{0,2,1:T(8,128)(2,1)S(1)} copy(bf16[128,4,128]{2,1,0:T(4,128)(2,1)} %param.20) | data formatting | bytes 262144 | tf_op args[0]
  1.1 7.4 %all_gather.9 = bf16[512,4,128]{2,1,0:T(4,128)(2,1)S(1)} all-gather(bf16[128,4,128]{2,1,0:T(4,128)(2,1)} %param.20), channel_id=1, replica_groups=mesh['member'=2,'lon'=4,'lev'=4] {'lev'}, dimensions={0}, use_global_device_ids=true | all-gather | bytes 655360 | tf_op jit(solution)/shard_map/all_gather | solution.py:34
  8.5 0.5 fusion.17
  9.1 1.5 %fusion.44 = bf16[512,4,128,1]{2,1,0,3:T(4,128)(2,1)S(1)} fusion(bf16[512,4,128]{2,1,0:T(4,128)(2,1)S(1)} %all_gather.9, f32[512]{0:T(512)S(1)} %copy-done.4, f32[4,128]{1,0:T(4,128)S(1)} %add_rsqrt_fusion.2), kind=kLoop, calls=%fused_computation.68 | loop fusion | flops 1048576 | bytes 1052672 | tf_op jit(solution)/shard_map/convert_element_type | solution.py:129
  10.6 0.4 convolution_bitcast_fusion.2
  11.0 0.1 slice_multiply_fusion.6
  11.2 0.1 fusion.121
  11.4 0.1 copy.94
  11.5 0.1 copy.95
  11.6 0.2 copy.98
  11.9 0.3 reshape.599
  12.3 0.1 fusion.118
  12.4 0.4 collective-permute-start.2
  12.8 2.7 %collective-permute-start.1 = (bf16[264,4,128]{2,0,1:T(8,128)(2,1)S(1)}, bf16[264,4,128]{2,0,1:T(8,128)(2,1)S(1)}, u32[]{:S(2)}, u32[]{:S(2)}) collective-permute-start(bf16[264,4,128]{2,0,1:T(8,128)(2,1)S(1)} %pad_maximum_fusion.1), channel_id=1, source_target_pairs={{0,12},{4,0},{8,4},{12,8},{1,13},{5,1},{9,5},{13,9},{2,14},{6,2},{... | collective-permute-start | bytes 811016 | tf_op jit(solution)/shard_map/ppermute | solution.py:145
  15.6 20.9 %collective-permute-done.1 = bf16[264,4,128]{2,0,1:T(8,128)(2,1)S(1)} collective-permute-done((bf16[264,4,128]{2,0,1:T(8,128)(2,1)S(1)}, bf16[264,4,128]{2,0,1:T(8,128)(2,1)S(1)}, u32[]{:S(2)}, u32[]{:S(2)}) %collective-permute-start.1) | collective-permute-done | bytes 270368 | tf_op jit(solution)/shard_map/ppermute | solution.py:145
  36.5 0.6 reshape.601
  37.1 0.1 slice_bitcast_fusion.4
  37.2 2.3 %collective-permute-done = bf16[264,4,128]{2,0,1:T(8,128)(2,1)S(1)} collective-permute-done((bf16[264,4,128]{2,0,1:T(8,128)(2,1)S(1)}, bf16[264,4,128]{2,0,1:T(8,128)(2,1)S(1)}, u32[]{:S(2)}, u32[]{:S(2)}) %collective-permute-start) | collective-permute-done | bytes 270368 | tf_op jit(solution)/shard_map/ppermute | solution.py:145
  39.5 0.6 reshape.600
  40.1 0.2 slice_bitcast_fusion.5
  40.4 0.1 pad_maximum_fusion
  40.5 0.9 %fusion = (f32[2,4,132]{2,1,0:T(4,128)S(1)}, f32[2,4,132,4,128]{4,2,3,1,0:T(8,128)S(1)}) fusion(bf16[4,2,2,64,4,128]{5,3,0,4,2,1:T(8,128)(2,1)S(1)} %pad_maximum_fusion, bf16[2,64,4,2]{3,1,2,0:T(8,128)(2,1)S(1)} %copy.112, bf16[2,64,4,128]{3,1,2,0:T(8,128)(2,1)S(1)} %fusion.104, bf16[2,64,4,2]{3,1,2,0:T(8,128)(2,1)S(1)} %copy.111), kind=kOutput, calls=%fused_computation.1 | convolution fusion | flops 70691808 | bytes 3084416 | tf_op jit(solution)/shard_map/hdri,phdrj->hripj/dot_general | solution.py:73
  41.4 0.5 fusion.37
  42.0 0.3 copy.113
  42.2 0.2 reshape.602
  42.4 0.3 fusion.2
  42.7 0.1 reshape.603
  42.8 1.1 %constant_dynamic-slice_fusion.3 = (bf16[2,1,128,528]{2,1,0,3:T(2,128)(2,1)S(1)}, bf16[2,1,128,528]{2,1,0,3:T(2,128)(2,1)S(1)}) fusion(bf16[2,2,128,528]{2,1,0,3:T(2,128)(2,1)S(1)} %reshape.603, s32[]{:T(128)S(6)} %select_n.94, s32[]{:T(128)S(6)} %select_n.96), kind=kLoop, calls=%fused_computation.171 | loop fusion | bytes 1081352 | tf_op jit(solution)/shard_map/jit(_take) | solution.py:43
  44.0 0.1 collective-permute-start.3
  44.3 0.1 broadcast_multiply_fusion.5
  44.3 1.3 %collective-permute-done.3 = bf16[2,128,528]{1,2,0:T(8,128)(2,1)S(1)} collective-permute-done((bf16[2,128,528]{1,2,0:T(8,128)(2,1)S(1)}, bf16[2,128,528]{1,2,0:T(8,128)(2,1)S(1)}, u32[]{:S(2)}, u32[]{:S(2)}) %collective-permute-start.3) | collective-permute-done | bytes 270368 | tf_op jit(solution)/shard_map/ppermute | solution.py:45
  45.6 0.1 convert_add_fusion
  45.8 1.1 %collective-permute-start.4 = (bf16[128,528]{0,1:T(8,128)(2,1)S(1)}, bf16[128,528]{0,1:T(8,128)(2,1)S(1)}, u32[]{:S(2)}, u32[]{:S(2)}) collective-permute-start(bf16[128,528]{0,1:T(8,128)(2,1)S(1)} %bitcast_convert_fusion), channel_id=1, source_target_pairs={{0,2},{1,3},{2,0},{3,1},{4,6},{5,7},{6,4},{7,5},{8,10},{9,11},{10,... | collective-permute-start | bytes 405512 | tf_op jit(solution)/shard_map/ppermute | solution.py:50
  46.9 0.1 copy.104
  47.0 0.1 copy.102
  47.2 4.3 %collective-permute-done.4 = bf16[128,528]{0,1:T(8,128)(2,1)S(1)} collective-permute-done((bf16[128,528]{0,1:T(8,128)(2,1)S(1)}, bf16[128,528]{0,1:T(8,128)(2,1)S(1)}, u32[]{:S(2)}, u32[]{:S(2)}) %collective-permute-start.4) | collective-permute-done | bytes 135200 | tf_op jit(solution)/shard_map/ppermute | solution.py:50
  51.5 0.1 fusion.120
  51.6 0.2 fusion.73
  51.8 7.2 %all_gather.10 = bf16[512,4,130]{0,2,1:T(8,128)(2,1)S(1)} all-gather(bf16[128,4,130]{0,2,1:T(8,128)(2,1)S(1)} %fusion.73), channel_id=1, replica_groups=mesh['member'=2,'lon'=4,'lev'=4] {'lev'}, dimensions={0}, use_global_device_ids=true | all-gather | bytes 665600 | tf_op jit(solution)/shard_map/all_gather | solution.py:34
  59.0 0.2 fusion.4
  59.2 0.2 fusion.6
  59.4 0.1 reshape.605
  59.5 2.2 %fusion.3 = bf16[512,520]{0,1:T(8,128)(2,1)S(1)} fusion(bf16[512,520]{0,1:T(8,128)(2,1)S(1)} %reshape.605, bf16[2,512,512]{2,1,0:T(8,128)(2,1)} %param.27, bf16[2,512,512]{2,1,0:T(8,128)(2,1)} %param.26), kind=kOutput, calls=%fused_computation.18 | convolution fusion | flops 547921920 | bytes 2113536 | tf_op jit(solution)/shard_map/dot_general | solution.py:55
  61.7 0.1 reshape.606
  61.9 1.1 %constant_dynamic-slice_fusion.1 = (bf16[2,1,128,520]{2,1,0,3:T(2,128)(2,1)S(1)}, bf16[2,1,128,520]{2,1,0,3:T(2,128)(2,1)S(1)}) fusion(bf16[2,2,128,520]{2,1,0,3:T(2,128)(2,1)S(1)} %reshape.606, s32[]{:T(128)S(6)} %select_n.94, s32[]{:T(128)S(6)} %select_n.96), kind=kLoop, calls=%fused_computation.169 | loop fusion | bytes 1064968 | tf_op jit(solution)/shard_map/jit(_take) | solution.py:43
  63.0 0.4 collective-permute-start.5
  63.4 1.2 %collective-permute-done.5 = bf16[2,128,520]{1,2,0:T(8,128)(2,1)S(1)} collective-permute-done((bf16[2,128,520]{1,2,0:T(8,128)(2,1)S(1)}, bf16[2,128,520]{1,2,0:T(8,128)(2,1)S(1)}, u32[]{:S(2)}, u32[]{:S(2)}) %collective-permute-start.5) | collective-permute-done | bytes 266272 | tf_op jit(solution)/shard_map/ppermute | solution.py:45
  64.6 0.1 convert_add_fusion.1
  64.8 1.0 %collective-permute-start.6 = (bf16[128,520]{0,1:T(8,128)(2,1)S(1)}, bf16[128,520]{0,1:T(8,128)(2,1)S(1)}, u32[]{:S(2)}, u32[]{:S(2)}) collective-permute-start(bf16[128,520]{0,1:T(8,128)(2,1)S(1)} %bitcast_convert_fusion.1), channel_id=1, source_target_pairs={{0,2},{1,3},{2,0},{3,1},{4,6},{5,7},{6,4},{7,5},{8,10},{9,11},{10,... | collective-permute-start | bytes 399368 | tf_op jit(solution)/shard_map/ppermute | solution.py:50
  65.8 4.9 %collective-permute-done.6 = bf16[128,520]{0,1:T(8,128)(2,1)S(1)} collective-permute-done((bf16[128,520]{0,1:T(8,128)(2,1)S(1)}, bf16[128,520]{0,1:T(8,128)(2,1)S(1)}, u32[]{:S(2)}, u32[]{:S(2)}) %collective-permute-start.6) | collective-permute-done | bytes 133152 | tf_op jit(solution)/shard_map/ppermute | solution.py:50
  70.7 0.1 fusion.119
  70.7 0.2 fusion.92
  70.9 6.8 %all_gather.11 = bf16[512,4,128]{0,2,1:T(8,128)(2,1)S(1)} all-gather(bf16[128,4,128]{0,2,1:T(8,128)(2,1)S(1)} %fusion.92), channel_id=1, replica_groups=mesh['member'=2,'lon'=4,'lev'=4] {'lev'}, dimensions={0}, use_global_device_ids=true | all-gather | bytes 655360 | tf_op jit(solution)/shard_map/all_gather | solution.py:34
  77.7 0.2 fusion.20
  77.9 0.2 fusion.22
  78.1 2.1 %convolution_convert_fusion.2 = bf16[512,512]{0,1:T(8,128)(2,1)S(1)} fusion(bf16[512,512]{0,1:T(8,128)(2,1)S(1)} %bitcast.199, bf16[2,512,512]{2,1,0:T(8,128)(2,1)S(1)} %copy-done.5, bf16[2,512,512]{2,1,0:T(8,128)(2,1)} %param.26), kind=kOutput, calls=%fused_computation.15 | convolution fusion | flops 539492352 | bytes 2097152 | tf_op jit(solution)/shard_map/dot_general | solution.py:55
  80.3 0.4 collective-permute-start.7
  80.7 1.2 %collective-permute-done.7 = bf16[2,128,512]{2,1,0:T(8,128)(2,1)S(1)} collective-permute-done((bf16[2,128,512]{2,1,0:T(8,128)(2,1)S(1)}, bf16[2,128,512]{2,1,0:T(8,128)(2,1)S(1)}, u32[]{:S(2)}, u32[]{:S(2)}) %collective-permute-start.7) | collective-permute-done | bytes 262176 | tf_op jit(solution)/shard_map/ppermute | solution.py:45
  81.9 0.1 convert_add_fusion.2
  82.0 1.1 %collective-permute-start.8 = (bf16[128,512]{1,0:T(8,128)(2,1)S(1)}, bf16[128,512]{1,0:T(8,128)(2,1)S(1)}, u32[]{:S(2)}, u32[]{:S(2)}) collective-permute-start(bf16[128,512]{1,0:T(8,128)(2,1)S(1)} %bitcast_convert_fusion.2), channel_id=1, source_target_pairs={{0,2},{1,3},{2,0},{3,1},{4,6},{5,7},{6,4},{7,5},{8,10},{9,11},{10,... | collective-permute-start | bytes 393224 | tf_op jit(solution)/shard_map/ppermute | solution.py:50
  83.2 4.7 %collective-permute-done.8 = bf16[128,512]{1,0:T(8,128)(2,1)S(1)} collective-permute-done((bf16[128,512]{1,0:T(8,128)(2,1)S(1)}, bf16[128,512]{1,0:T(8,128)(2,1)S(1)}, u32[]{:S(2)}, u32[]{:S(2)}) %collective-permute-start.8) | collective-permute-done | bytes 131104 | tf_op jit(solution)/shard_map/ppermute | solution.py:50
  87.9 0.1 copy.119
  88.0 0.1 add_convert_fusion.2
  88.1 0.8 copy.120
  (55 shorter events, 0.9 us)
Async XLA Ops:
  0.0 10.6 %copy-start = (bf16[3,128,512]{2,1,0:T(8,128)(2,1)S(1)}, bf16[3,128,512]{2,1,0:T(8,128)(2,1)}, u32[]{:S(2)}) copy-start(bf16[3,128,512]{2,1,0:T(8,128)(2,1)} %param.22) | copy-start | bytes 1179652
  0.0 9.0 %copy-start.4 = (f32[512]{0:T(512)S(1)}, f32[512]{0:T(512)}, u32[]{:S(2)}) copy-start(f32[512]{0:T(512)} %param.21) | copy-start | bytes 6148
  12.2 3.3 %copy-start.2 = (f32[2,9,128]{2,0,1:T(2,128)S(1)}, f32[2,9,128]{2,0,1:T(2,128)}, u32[]{:S(2)}) copy-start(f32[2,9,128]{2,0,1:T(2,128)} %param.24) | copy-start | bytes 27652
  12.4 28.0 %collective-permute-start.2 = (bf16[264,4,128]{2,0,1:T(8,128)(2,1)S(1)}, bf16[264,4,128]{2,0,1:T(8,128)(2,1)S(1)}, u32[]{:S(2)}, u32[]{:S(2)}) collective-permute-start(bf16[264,4,128]{2,0,1:T(8,128)(2,1)S(1)} %pad_maximum_fusion.1), channel_id=1, source_target_pairs={{0,8},{4,12},{8,0},{12,4},{1,9},{5,13},{9,1},{13,5},{2,10},{6,14},... | collective-permute-start | bytes 811016 | tf_op jit(solution)/shard_map/ppermute | solution.py:145
  12.8 23.7 %collective-permute-start.1 = (bf16[264,4,128]{2,0,1:T(8,128)(2,1)S(1)}, bf16[264,4,128]{2,0,1:T(8,128)(2,1)S(1)}, u32[]{:S(2)}, u32[]{:S(2)}) collective-permute-start(bf16[264,4,128]{2,0,1:T(8,128)(2,1)S(1)} %pad_maximum_fusion.1), channel_id=1, source_target_pairs={{0,12},{4,0},{8,4},{12,8},{1,13},{5,1},{9,5},{13,9},{2,14},{6,2},{... | collective-permute-start | bytes 811016 | tf_op jit(solution)/shard_map/ppermute | solution.py:145
  15.5 24.0 %collective-permute-start = (bf16[264,4,128]{2,0,1:T(8,128)(2,1)S(1)}, bf16[264,4,128]{2,0,1:T(8,128)(2,1)S(1)}, u32[]{:S(2)}, u32[]{:S(2)}) collective-permute-start(bf16[264,4,128]{2,0,1:T(8,128)(2,1)S(1)} %pad_maximum_fusion.1), channel_id=1, source_target_pairs={{0,4},{4,8},{8,12},{12,0},{1,5},{5,9},{9,13},{13,1},{2,6},{6,10},{... | collective-permute-start | bytes 811016 | tf_op jit(solution)/shard_map/ppermute | solution.py:145
  41.4 1.0 %copy-start.1 = (bf16[128,512]{1,0:T(8,128)(2,1)S(1)}, bf16[128,512]{1,0:T(8,128)(2,1)}, u32[]{:S(2)}) copy-start(bf16[128,512]{1,0:T(8,128)(2,1)} %param.23) | copy-start | bytes 393220
  44.0 3.0 %copy-start.3 = (f32[2,512]{1,0:T(2,128)S(1)}, f32[2,512]{1,0:T(2,128)}, u32[]{:S(2)}) copy-start(f32[2,512]{1,0:T(2,128)} %param.25) | copy-start | bytes 12292
  44.0 1.6 %collective-permute-start.3 = (bf16[2,128,528]{1,2,0:T(8,128)(2,1)S(1)}, bf16[2,128,528]{1,2,0:T(8,128)(2,1)S(1)}, u32[]{:S(2)}, u32[]{:S(2)}) collective-permute-start(bf16[2,128,528]{1,2,0:T(8,128)(2,1)S(1)} %fusion.79), channel_id=1, source_target_pairs={{0,1},{1,0},{2,3},{3,2},{4,5},{5,4},{6,7},{7,6},{8,9},{9,8},{10,11... | collective-permute-start | bytes 811016 | tf_op jit(solution)/shard_map/ppermute | solution.py:45
  45.8 5.7 %collective-permute-start.4 = (bf16[128,528]{0,1:T(8,128)(2,1)S(1)}, bf16[128,528]{0,1:T(8,128)(2,1)S(1)}, u32[]{:S(2)}, u32[]{:S(2)}) collective-permute-start(bf16[128,528]{0,1:T(8,128)(2,1)S(1)} %bitcast_convert_fusion), channel_id=1, source_target_pairs={{0,2},{1,3},{2,0},{3,1},{4,6},{5,7},{6,4},{7,5},{8,10},{9,11},{10,... | collective-permute-start | bytes 405512 | tf_op jit(solution)/shard_map/ppermute | solution.py:50
  63.0 1.6 %collective-permute-start.5 = (bf16[2,128,520]{1,2,0:T(8,128)(2,1)S(1)}, bf16[2,128,520]{1,2,0:T(8,128)(2,1)S(1)}, u32[]{:S(2)}, u32[]{:S(2)}) collective-permute-start(bf16[2,128,520]{1,2,0:T(8,128)(2,1)S(1)} %fusion.81), channel_id=1, source_target_pairs={{0,1},{1,0},{2,3},{3,2},{4,5},{5,4},{6,7},{7,6},{8,9},{9,8},{10,11... | collective-permute-start | bytes 798728 | tf_op jit(solution)/shard_map/ppermute | solution.py:45
  64.8 5.9 %collective-permute-start.6 = (bf16[128,520]{0,1:T(8,128)(2,1)S(1)}, bf16[128,520]{0,1:T(8,128)(2,1)S(1)}, u32[]{:S(2)}, u32[]{:S(2)}) collective-permute-start(bf16[128,520]{0,1:T(8,128)(2,1)S(1)} %bitcast_convert_fusion.1), channel_id=1, source_target_pairs={{0,2},{1,3},{2,0},{3,1},{4,6},{5,7},{6,4},{7,5},{8,10},{9,11},{10,... | collective-permute-start | bytes 399368 | tf_op jit(solution)/shard_map/ppermute | solution.py:50
  70.9 7.2 %copy-start.5 = (bf16[2,512,512]{2,1,0:T(8,128)(2,1)S(1)}, bf16[2,512,512]{2,1,0:T(8,128)(2,1)}, u32[]{:S(2)}) copy-start(bf16[2,512,512]{2,1,0:T(8,128)(2,1)} %param.27) | copy-start | bytes 3145732
  80.3 1.6 %collective-permute-start.7 = (bf16[2,128,512]{2,1,0:T(8,128)(2,1)S(1)}, bf16[2,128,512]{2,1,0:T(8,128)(2,1)S(1)}, u32[]{:S(2)}, u32[]{:S(2)}) collective-permute-start(bf16[2,128,512]{2,1,0:T(8,128)(2,1)S(1)} %select_bitcast_fusion), channel_id=1, source_target_pairs={{0,1},{1,0},{2,3},{3,2},{4,5},{5,4},{6,7},{7,6},{8,9},{9,8},{10,11... | collective-permute-start | bytes 786440 | tf_op jit(solution)/shard_map/ppermute | solution.py:45
  82.0 5.8 %collective-permute-start.8 = (bf16[128,512]{1,0:T(8,128)(2,1)S(1)}, bf16[128,512]{1,0:T(8,128)(2,1)S(1)}, u32[]{:S(2)}, u32[]{:S(2)}) collective-permute-start(bf16[128,512]{1,0:T(8,128)(2,1)S(1)} %bitcast_convert_fusion.2), channel_id=1, source_target_pairs={{0,2},{1,3},{2,0},{3,1},{4,6},{5,7},{6,4},{7,5},{8,10},{9,11},{10,... | collective-permute-start | bytes 393224 | tf_op jit(solution)/shard_map/ppermute | solution.py:50

commit v20 on v10

--- a/solution.py
+++ b/solution.py
@@ -157,7 +157,11 @@
 
     numerator, denominator = make_fold(wide_queries, (all_keys[:, 0], all_keys[:, 1]))
     attended = (numerator / denominator[:, None]).astype(jnp.bfloat16)
-    update = spread_sum(out_weight, attended.reshape(ch_local, -1))
+    partial = jnp.einsum(
+        "kc,krw->crw", out_weight, attended.reshape(ch_local, lat_rows, -1),
+        preferred_element_type=jnp.float32,
+    ).astype(jnp.bfloat16)
+    update = scatter_sum(partial, "lev")
     current = (wide_latent.astype(jnp.float32) + update.reshape(wide_latent.shape)).astype(
         jnp.bfloat16
     )

time: 86.7 us -> 87.6 us (1.010)
  other arithmetic: 4.59 us -> 5.9 us
    select_n x0 -> x1, other arithmetic: none -> 1.4 us  [scatter_sum(): mine = jnp.take(blocks, core, axis=1).astype(jnp.float32)]
    another operation x2 -> x1, local copies, waits for them, and re-layouts: 2.23 us -> 1.1 us  [scatter_sum(): mine = jnp.take(blocks, core, axis=1).astype(jnp.float32)]
    dot_general x3 -> x2, matrix products: 4.58 us -> 4.13 us  [spread_sum(): lax.dot_general(weight, activation, (((0,), (0,)), ((), ())), preferred_e...]
where the time goes in v20:
time: 87.6 us; the launch traced here: 87.4 us
  waiting for transfers between devices  39.1 us (45%)
  blocking collectives  21.3 us (24%)
  starting transfers between devices  7.18 us (8%)
  local copies, waits for them, and re-layouts  6.99 us (8%)
  matrix products  6.21 us (7%)
  other arithmetic  5.9 us (7%)
    ppermute x3, waiting for transfers between devices, per_device(): got = lax.ppermute(sent, 'lon', pairs)  21.5 us
    all_gather x3, blocking collectives, gather_channels(): return lax.all_gather(values, 'lev', axis=0, tiled=True)  21.3 us
    ppermute x3, waiting for transfers between devices, scatter_sum(): total = total + lax.ppermute(sent, axis, pairs).astype(jnp.float32)  13.9 us
    dot_general x2, matrix products, spread_sum(): lax.dot_general(weight, activation, (((0,), (0,)), ((), ())), preferred_e...  4.13 us
    ppermute x3, waiting for transfers between devices, scatter_sum(): lax.ppermute(theirs, axis, [(i, i ^ 1) for i in range(devices)])  3.7 us
    ppermute x3, starting transfers between devices, scatter_sum(): total = total + lax.ppermute(sent, axis, pairs).astype(jnp.float32)  3.32 us
    ppermute x3, starting transfers between devices, per_device(): got = lax.ppermute(sent, 'lon', pairs)  2.9 us
  transfers between devices with their start and end apart: 9, of which 8 were waited for; matrix products, arithmetic and copies ran while one was open for 4% of the time, Pallas kernels for 0%

profile of v20, /device:TPU:16, one launch (start us, length us, event | category | flops | bytes accessed | tf_op | source)
XLA Modules:
  0.0 87.4 jit_solution(14540315091284768735)
XLA Ops:
  0.0 7.5 %all_gather.9 = bf16[512,4,128]{2,1,0:T(4,128)(2,1)S(1)} all-gather(bf16[128,4,128]{2,1,0:T(4,128)(2,1)} %param.20), channel_id=1, replica_groups=mesh['member'=2,'lon'=4,'lev'=4] {'lev'}, dimensions={0}, use_global_device_ids=true | all-gather | bytes 655360 | tf_op jit(solution)/shard_map/all_gather | solution.py:34
  7.5 0.5 fusion.17
  8.1 1.5 %fusion.44 = bf16[512,4,128,1]{2,1,0,3:T(4,128)(2,1)S(1)} fusion(bf16[512,4,128]{2,1,0:T(4,128)(2,1)S(1)} %all_gather.9, f32[512]{0:T(512)S(1)} %copy-done.5, f32[4,128]{1,0:T(4,128)S(1)} %add_rsqrt_fusion.2), kind=kLoop, calls=%fused_computation.70 | loop fusion | flops 1048576 | bytes 1052672 | tf_op jit(solution)/shard_map/convert_element_type | solution.py:129
  9.6 0.4 convolution_bitcast_fusion.2
  10.0 0.1 slice_multiply_fusion.6
  10.2 0.1 fusion.119
  10.3 0.4 collective-permute-start.2
  10.7 0.3 copy-done.1
  11.0 0.1 copy.155
  11.3 0.1 fusion.123
  11.4 0.1 copy.153
  11.5 0.1 copy.154
  11.7 0.2 copy.157
  11.9 0.3 reshape.596
  12.3 2.5 %collective-permute-start.1 = (bf16[264,4,128]{2,0,1:T(8,128)(2,1)S(1)}, bf16[264,4,128]{2,0,1:T(8,128)(2,1)S(1)}, u32[]{:S(2)}, u32[]{:S(2)}) collective-permute-start(bf16[264,4,128]{2,0,1:T(8,128)(2,1)S(1)} %pad_maximum_fusion.1), channel_id=1, source_target_pairs={{0,12},{4,0},{8,4},{12,8},{1,13},{5,1},{9,5},{13,9},{2,14},{6,2},{... | collective-permute-start | bytes 811016 | tf_op jit(solution)/shard_map/ppermute | solution.py:146
  14.9 19.2 %collective-permute-done.1 = bf16[264,4,128]{2,0,1:T(8,128)(2,1)S(1)} collective-permute-done((bf16[264,4,128]{2,0,1:T(8,128)(2,1)S(1)}, bf16[264,4,128]{2,0,1:T(8,128)(2,1)S(1)}, u32[]{:S(2)}, u32[]{:S(2)}) %collective-permute-start.1) | collective-permute-done | bytes 270368 | tf_op jit(solution)/shard_map/ppermute | solution.py:146
  34.1 0.6 reshape.598
  34.6 0.1 slice_bitcast_fusion.4
  34.8 2.3 %collective-permute-done = bf16[264,4,128]{2,0,1:T(8,128)(2,1)S(1)} collective-permute-done((bf16[264,4,128]{2,0,1:T(8,128)(2,1)S(1)}, bf16[264,4,128]{2,0,1:T(8,128)(2,1)S(1)}, u32[]{:S(2)}, u32[]{:S(2)}) %collective-permute-start) | collective-permute-done | bytes 270368 | tf_op jit(solution)/shard_map/ppermute | solution.py:146
  37.1 0.6 reshape.597
  37.7 0.2 slice_bitcast_fusion.5
  38.0 0.1 pad_maximum_fusion
  38.1 0.9 %fusion = (f32[2,4,132]{2,1,0:T(4,128)S(1)}, f32[2,4,132,4,128]{4,2,3,1,0:T(8,128)S(1)}) fusion(bf16[4,2,2,64,4,128]{5,3,0,4,2,1:T(8,128)(2,1)S(1)} %pad_maximum_fusion, bf16[2,64,4,2]{3,1,2,0:T(8,128)(2,1)S(1)} %copy.171, bf16[2,64,4,128]{3,1,2,0:T(8,128)(2,1)S(1)} %fusion.104, bf16[2,64,4,2]{3,1,2,0:T(8,128)(2,1)S(1)} %copy.170), kind=kOutput, calls=%fused_computation.1 | convolution fusion | flops 70691808 | bytes 3084416 | tf_op jit(solution)/shard_map/hdri,phdrj->hripj/dot_general | solution.py:73
  39.0 0.5 fusion.37
  39.5 0.3 copy.172
  39.8 0.2 reshape.599
  40.0 0.3 fusion.2
  40.3 0.2 reshape.600
  40.5 1.4 %broadcast_select_fusion.1 = (bf16[2,1,128,4,132]{2,1,0,4,3:T(2,128)(2,1)S(1)}, bf16[2,1,128,4,132]{2,1,0,4,3:T(2,128)(2,1)S(1)}) fusion(pred[]{:T(512)S(6)} %and.60, bf16[2,2,128,4,132]{2,1,0,4,3:T(2,128)(2,1)S(1)} %reshape.600, s32[]{:T(128)S(6)} %select_n.94, s32[]{:T(128)S(6)} %select_n.96, pred[]{:T(512)S(6)} %and.61), kind=kLoop, calls=%fused_computation.25 | loop fusion | flops 270336 | bytes 1081354 | tf_op jit(solution)/shard_map/jit(_take)/select_n | solution.py:43
  41.9 0.1 collective-permute-start.3
  42.1 0.1 broadcast_multiply_fusion.5
  42.2 1.3 %collective-permute-done.3 = bf16[2,128,4,132]{1,3,2,0:T(8,128)(2,1)S(1)} collective-permute-done((bf16[2,128,4,132]{1,3,2,0:T(8,128)(2,1)S(1)}, bf16[2,128,4,132]{1,3,2,0:T(8,128)(2,1)S(1)}, u32[]{:S(2)}, u32[]{:S(2)}) %collective-permute-start.3) | collective-permute-done | bytes 270368 | tf_op jit(solution)/shard_map/ppermute | solution.py:45
  43.6 1.2 %collective-permute-start.4 = (bf16[128,4,132]{0,2,1:T(8,128)(2,1)S(1)}, bf16[128,4,132]{0,2,1:T(8,128)(2,1)S(1)}, u32[]{:S(2)}, u32[]{:S(2)}) collective-permute-start(bf16[128,4,132]{0,2,1:T(8,128)(2,1)S(1)} %bitcast_convert_fusion), channel_id=1, source_target_pairs={{0,2},{1,3},{2,0},{3,1},{4,6},{5,7},{6,4},{7,5},{8,10},{9,11},{10,... | collective-permute-start | bytes 405512 | tf_op jit(solution)/shard_map/ppermute | solution.py:50
  44.8 0.1 copy.163
  44.9 0.1 copy.161
  45.1 4.4 %collective-permute-done.4 = bf16[128,4,132]{0,2,1:T(8,128)(2,1)S(1)} collective-permute-done((bf16[128,4,132]{0,2,1:T(8,128)(2,1)S(1)}, bf16[128,4,132]{0,2,1:T(8,128)(2,1)S(1)}, u32[]{:S(2)}, u32[]{:S(2)}) %collective-permute-start.4) | collective-permute-done | bytes 135200 | tf_op jit(solution)/shard_map/ppermute | solution.py:50
  49.4 0.1 fusion.121
  49.5 0.2 fusion.73
  49.7 7.2 %all_gather.10 = bf16[512,4,130]{0,2,1:T(8,128)(2,1)S(1)} all-gather(bf16[128,4,130]{0,2,1:T(8,128)(2,1)S(1)} %fusion.73), channel_id=1, replica_groups=mesh['member'=2,'lon'=4,'lev'=4] {'lev'}, dimensions={0}, use_global_device_ids=true | all-gather | bytes 665600 | tf_op jit(solution)/shard_map/all_gather | solution.py:34
  56.9 0.2 fusion.4
  57.2 0.2 fusion.6
  57.4 0.1 reshape.601
  57.5 0.8 copy-done.6
  58.4 2.0 %fusion.3 = bf16[512,520]{0,1:T(8,128)(2,1)S(1)} fusion(bf16[512,520]{0,1:T(8,128)(2,1)S(1)} %reshape.601, bf16[2,512,512]{2,1,0:T(8,128)(2,1)S(1)} %copy-done.6, bf16[2,512,512]{2,1,0:T(8,128)(2,1)} %param.26), kind=kOutput, calls=%fused_computation.18 | convolution fusion | flops 547921920 | bytes 2113536 | tf_op jit(solution)/shard_map/dot_general | solution.py:55
  60.4 0.1 reshape.602
  60.5 1.1 %constant_dynamic-slice_fusion.1 = (bf16[2,1,128,520]{2,1,0,3:T(2,128)(2,1)S(1)}, bf16[2,1,128,520]{2,1,0,3:T(2,128)(2,1)S(1)}) fusion(bf16[2,2,128,520]{2,1,0,3:T(2,128)(2,1)S(1)} %reshape.602, s32[]{:T(128)S(6)} %select_n.94, s32[]{:T(128)S(6)} %select_n.96), kind=kLoop, calls=%fused_computation.170 | loop fusion | bytes 1064968 | tf_op jit(solution)/shard_map/jit(_take) | solution.py:43
  61.7 0.4 collective-permute-start.5
  62.1 1.2 %collective-permute-done.5 = bf16[2,128,520]{1,2,0:T(8,128)(2,1)S(1)} collective-permute-done((bf16[2,128,520]{1,2,0:T(8,128)(2,1)S(1)}, bf16[2,128,520]{1,2,0:T(8,128)(2,1)S(1)}, u32[]{:S(2)}, u32[]{:S(2)}) %collective-permute-start.5) | collective-permute-done | bytes 266272 | tf_op jit(solution)/shard_map/ppermute | solution.py:45
  63.3 0.1 convert_add_fusion.1
  63.4 1.0 %collective-permute-start.6 = (bf16[128,520]{0,1:T(8,128)(2,1)S(1)}, bf16[128,520]{0,1:T(8,128)(2,1)S(1)}, u32[]{:S(2)}, u32[]{:S(2)}) collective-permute-start(bf16[128,520]{0,1:T(8,128)(2,1)S(1)} %bitcast_convert_fusion.1), channel_id=1, source_target_pairs={{0,2},{1,3},{2,0},{3,1},{4,6},{5,7},{6,4},{7,5},{8,10},{9,11},{10,... | collective-permute-start | bytes 399368 | tf_op jit(solution)/shard_map/ppermute | solution.py:50
  64.4 4.9 %collective-permute-done.6 = bf16[128,520]{0,1:T(8,128)(2,1)S(1)} collective-permute-done((bf16[128,520]{0,1:T(8,128)(2,1)S(1)}, bf16[128,520]{0,1:T(8,128)(2,1)S(1)}, u32[]{:S(2)}, u32[]{:S(2)}) %collective-permute-start.6) | collective-permute-done | bytes 133152 | tf_op jit(solution)/shard_map/ppermute | solution.py:50
  69.3 0.1 fusion.120
  69.4 0.2 fusion.92
  69.6 6.7 %all_gather.11 = bf16[512,4,128]{0,2,1:T(8,128)(2,1)S(1)} all-gather(bf16[128,4,128]{0,2,1:T(8,128)(2,1)S(1)} %fusion.92), channel_id=1, replica_groups=mesh['member'=2,'lon'=4,'lev'=4] {'lev'}, dimensions={0}, use_global_device_ids=true | all-gather | bytes 655360 | tf_op jit(solution)/shard_map/all_gather | solution.py:34
  76.2 0.2 fusion.20
  76.4 0.2 fusion.22
  76.6 2.1 %convolution_convert_fusion.2 = bf16[512,512]{0,1:T(8,128)(2,1)S(1)} fusion(bf16[512,512]{0,1:T(8,128)(2,1)S(1)} %bitcast.203, bf16[2,512,512]{2,1,0:T(8,128)(2,1)S(1)} %copy-done.6, bf16[2,512,512]{2,1,0:T(8,128)(2,1)} %param.26), kind=kOutput, calls=%fused_computation.15 | convolution fusion | flops 539492352 | bytes 2097152 | tf_op jit(solution)/shard_map/dot_general | solution.py:55
  78.8 0.4 collective-permute-start.7
  79.2 1.2 %collective-permute-done.7 = bf16[2,128,512]{2,1,0:T(8,128)(2,1)S(1)} collective-permute-done((bf16[2,128,512]{2,1,0:T(8,128)(2,1)S(1)}, bf16[2,128,512]{2,1,0:T(8,128)(2,1)S(1)}, u32[]{:S(2)}, u32[]{:S(2)}) %collective-permute-start.7) | collective-permute-done | bytes 262176 | tf_op jit(solution)/shard_map/ppermute | solution.py:45
  80.4 0.1 convert_add_fusion.2
  80.5 1.2 %collective-permute-start.8 = (bf16[128,512]{1,0:T(8,128)(2,1)S(1)}, bf16[128,512]{1,0:T(8,128)(2,1)S(1)}, u32[]{:S(2)}, u32[]{:S(2)}) collective-permute-start(bf16[128,512]{1,0:T(8,128)(2,1)S(1)} %bitcast_convert_fusion.2), channel_id=1, source_target_pairs={{0,2},{1,3},{2,0},{3,1},{4,6},{5,7},{6,4},{7,5},{8,10},{9,11},{10,... | collective-permute-start | bytes 393224 | tf_op jit(solution)/shard_map/ppermute | solution.py:50
  81.7 4.7 %collective-permute-done.8 = bf16[128,512]{1,0:T(8,128)(2,1)S(1)} collective-permute-done((bf16[128,512]{1,0:T(8,128)(2,1)S(1)}, bf16[128,512]{1,0:T(8,128)(2,1)S(1)}, u32[]{:S(2)}, u32[]{:S(2)}) %collective-permute-start.8) | collective-permute-done | bytes 131104 | tf_op jit(solution)/shard_map/ppermute | solution.py:50
  86.4 0.1 copy.178
  86.6 0.8 copy.179
  (54 shorter events, 0.9 us)
Async XLA Ops:
  0.0 9.6 %copy-start = (bf16[3,128,512]{2,1,0:T(8,128)(2,1)S(1)}, bf16[3,128,512]{2,1,0:T(8,128)(2,1)}, u32[]{:S(2)}) copy-start(bf16[3,128,512]{2,1,0:T(8,128)(2,1)} %param.22) | copy-start | bytes 1179652
  0.0 8.1 %copy-start.5 = (f32[512]{0:T(512)S(1)}, f32[512]{0:T(512)}, u32[]{:S(2)}) copy-start(f32[512]{0:T(512)} %param.21) | copy-start | bytes 6148
  10.1 0.9 %copy-start.1 = (bf16[128,4,128]{2,1,0:T(4,128)(2,1)S(1)}, bf16[128,4,128]{2,1,0:T(4,128)(2,1)}, u32[]{:S(2)}) copy-start(bf16[128,4,128]{2,1,0:T(4,128)(2,1)} %param.20) | copy-start | bytes 393220
  10.3 27.7 %collective-permute-start.2 = (bf16[256,4,128]{2,0,1:T(8,128)(2,1)S(1)}, bf16[256,4,128]{2,0,1:T(8,128)(2,1)S(1)}, u32[]{:S(2)}, u32[]{:S(2)}) collective-permute-start(bf16[256,4,128]{2,0,1:T(8,128)(2,1)S(1)} %bitcast.196), channel_id=1, source_target_pairs={{0,8},{4,12},{8,0},{12,4},{1,9},{5,13},{9,1},{13,5},{2,10},{6,14},... | collective-permute-start | bytes 786440 | tf_op jit(solution)/shard_map/ppermute | solution.py:146
  11.2 3.5 %copy-start.3 = (f32[2,9,128]{2,0,1:T(2,128)S(1)}, f32[2,9,128]{2,0,1:T(2,128)}, u32[]{:S(2)}) copy-start(f32[2,9,128]{2,0,1:T(2,128)} %param.24) | copy-start | bytes 27652
  12.3 21.8 %collective-permute-start.1 = (bf16[264,4,128]{2,0,1:T(8,128)(2,1)S(1)}, bf16[264,4,128]{2,0,1:T(8,128)(2,1)S(1)}, u32[]{:S(2)}, u32[]{:S(2)}) collective-permute-start(bf16[264,4,128]{2,0,1:T(8,128)(2,1)S(1)} %pad_maximum_fusion.1), channel_id=1, source_target_pairs={{0,12},{4,0},{8,4},{12,8},{1,13},{5,1},{9,5},{13,9},{2,14},{6,2},{... | collective-permute-start | bytes 811016 | tf_op jit(solution)/shard_map/ppermute | solution.py:146
  14.8 22.3 %collective-permute-start = (bf16[264,4,128]{2,0,1:T(8,128)(2,1)S(1)}, bf16[264,4,128]{2,0,1:T(8,128)(2,1)S(1)}, u32[]{:S(2)}, u32[]{:S(2)}) collective-permute-start(bf16[264,4,128]{2,0,1:T(8,128)(2,1)S(1)} %pad_maximum_fusion.1), channel_id=1, source_target_pairs={{0,4},{4,8},{8,12},{12,0},{1,5},{5,9},{9,13},{13,1},{2,6},{6,10},{... | collective-permute-start | bytes 811016 | tf_op jit(solution)/shard_map/ppermute | solution.py:146
  39.0 1.0 %copy-start.2 = (bf16[128,512]{1,0:T(8,128)(2,1)S(1)}, bf16[128,512]{1,0:T(8,128)(2,1)}, u32[]{:S(2)}) copy-start(bf16[128,512]{1,0:T(8,128)(2,1)} %param.23) | copy-start | bytes 393220
  41.9 3.0 %copy-start.4 = (f32[2,512]{1,0:T(2,128)S(1)}, f32[2,512]{1,0:T(2,128)}, u32[]{:S(2)}) copy-start(f32[2,512]{1,0:T(2,128)} %param.25) | copy-start | bytes 12292
  41.9 1.6 %collective-permute-start.3 = (bf16[2,128,4,132]{1,3,2,0:T(8,128)(2,1)S(1)}, bf16[2,128,4,132]{1,3,2,0:T(8,128)(2,1)S(1)}, u32[]{:S(2)}, u32[]{:S(2)}) collective-permute-start(bf16[2,128,4,132]{1,3,2,0:T(8,128)(2,1)S(1)} %bitcast.207), channel_id=1, source_target_pairs={{0,1},{1,0},{2,3},{3,2},{4,5},{5,4},{6,7},{7,6},{8,9},{9,8},{10,11... | collective-permute-start | bytes 811016 | tf_op jit(solution)/shard_map/ppermute | solution.py:45
  43.6 5.8 %collective-permute-start.4 = (bf16[128,4,132]{0,2,1:T(8,128)(2,1)S(1)}, bf16[128,4,132]{0,2,1:T(8,128)(2,1)S(1)}, u32[]{:S(2)}, u32[]{:S(2)}) collective-permute-start(bf16[128,4,132]{0,2,1:T(8,128)(2,1)S(1)} %bitcast_convert_fusion), channel_id=1, source_target_pairs={{0,2},{1,3},{2,0},{3,1},{4,6},{5,7},{6,4},{7,5},{8,10},{9,11},{10,... | collective-permute-start | bytes 405512 | tf_op jit(solution)/shard_map/ppermute | solution.py:50
  57.1 1.2 %copy-start.6 = (bf16[2,512,512]{2,1,0:T(8,128)(2,1)S(1)}, bf16[2,512,512]{2,1,0:T(8,128)(2,1)}, u32[]{:S(2)}) copy-start(bf16[2,512,512]{2,1,0:T(8,128)(2,1)} %param.27) | copy-start | bytes 3145732
  61.7 1.6 %collective-permute-start.5 = (bf16[2,128,520]{1,2,0:T(8,128)(2,1)S(1)}, bf16[2,128,520]{1,2,0:T(8,128)(2,1)S(1)}, u32[]{:S(2)}, u32[]{:S(2)}) collective-permute-start(bf16[2,128,520]{1,2,0:T(8,128)(2,1)S(1)} %fusion.81), channel_id=1, source_target_pairs={{0,1},{1,0},{2,3},{3,2},{4,5},{5,4},{6,7},{7,6},{8,9},{9,8},{10,11... | collective-permute-start | bytes 798728 | tf_op jit(solution)/shard_map/ppermute | solution.py:45
  63.4 5.9 %collective-permute-start.6 = (bf16[128,520]{0,1:T(8,128)(2,1)S(1)}, bf16[128,520]{0,1:T(8,128)(2,1)S(1)}, u32[]{:S(2)}, u32[]{:S(2)}) collective-permute-start(bf16[128,520]{0,1:T(8,128)(2,1)S(1)} %bitcast_convert_fusion.1), channel_id=1, source_target_pairs={{0,2},{1,3},{2,0},{3,1},{4,6},{5,7},{6,4},{7,5},{8,10},{9,11},{10,... | collective-permute-start | bytes 399368 | tf_op jit(solution)/shard_map/ppermute | solution.py:50
  78.8 1.6 %collective-permute-start.7 = (bf16[2,128,512]{2,1,0:T(8,128)(2,1)S(1)}, bf16[2,128,512]{2,1,0:T(8,128)(2,1)S(1)}, u32[]{:S(2)}, u32[]{:S(2)}) collective-permute-start(bf16[2,128,512]{2,1,0:T(8,128)(2,1)S(1)} %select_bitcast_fusion), channel_id=1, source_target_pairs={{0,1},{1,0},{2,3},{3,2},{4,5},{5,4},{6,7},{7,6},{8,9},{9,8},{10,11... | collective-permute-start | bytes 786440 | tf_op jit(solution)/shard_map/ppermute | solution.py:45
  80.5 5.8 %collective-permute-start.8 = (bf16[128,512]{1,0:T(8,128)(2,1)S(1)}, bf16[128,512]{1,0:T(8,128)(2,1)S(1)}, u32[]{:S(2)}, u32[]{:S(2)}) collective-permute-start(bf16[128,512]{1,0:T(8,128)(2,1)S(1)} %bitcast_convert_fusion.2), channel_id=1, source_target_pairs={{0,2},{1,3},{2,0},{3,1},{4,6},{5,7},{6,4},{7,5},{8,10},{9,11},{10,... | collective-permute-start | bytes 393224 | tf_op jit(solution)/shard_map/ppermute | solution.py:50

commit v21 on v10

--- a/solution.py
+++ b/solution.py
@@ -109,7 +109,14 @@
     hidden = jax.nn.gelu(
         jnp.dot(up_weight[block_index], block_normed, preferred_element_type=jnp.float32)
     ).astype(jnp.bfloat16)
-    update = spread_sum(down_weight[block_index], hidden)
+    if block_index == BLOCKS - 1:
+        partial = jnp.einsum(
+            "hc,hrw->crw", down_weight[block_index], hidden.reshape(hidden.shape[0], lat_rows, out_cols),
+            preferred_element_type=jnp.float32,
+        ).astype(jnp.bfloat16)
+        update = scatter_sum(partial, "lev")
+    else:
+        update = spread_sum(down_weight[block_index], hidden)
     center = state[:, :, 1:-1]
     return (center.astype(jnp.float32) + update.reshape(center.shape)).astype(jnp.bfloat16)
 

time: 86.7 us -> 87.3 us (level)
  local copies, waits for them, and re-layouts: 7.18 us -> 8.82 us
  matrix products: 6.37 us -> 5.33 us
    dot_general x3 -> x2, matrix products: 4.58 us -> 2.45 us  [spread_sum(): lax.dot_general(weight, activation, (((0,), (0,)), ((), ())), preferred_e...]
    dot_general x0 -> x2, matrix products: none -> 1.09 us  [the longest x1 0.66 us: block_apply(): jnp.dot(up_weight[block_index], block_normed, preferred_element_type=jnp....]
    another operation x2 -> x3, local copies, waits for them, and re-layouts: 2.23 us -> 3.31 us  [scatter_sum(): mine = jnp.take(blocks, core, axis=1).astype(jnp.float32)]
where the time goes in v21:
time: 87.3 us; the launch traced here: 87.1 us
  waiting for transfers between devices  39 us (45%)
  blocking collectives  21.5 us (25%)
  local copies, waits for them, and re-layouts  8.82 us (10%)
  starting transfers between devices  7.18 us (8%)
  matrix products  5.33 us (6%)
  other arithmetic  4.6 us (5%)
    ppermute x3, waiting for transfers between devices, per_device(): got = lax.ppermute(sent, 'lon', pairs)  21.5 us
    all_gather x3, blocking collectives, gather_channels(): return lax.all_gather(values, 'lev', axis=0, tiled=True)  21.5 us
    ppermute x3, waiting for transfers between devices, scatter_sum(): total = total + lax.ppermute(sent, axis, pairs).astype(jnp.float32)  13.8 us
    ppermute x3, waiting for transfers between devices, scatter_sum(): lax.ppermute(theirs, axis, [(i, i ^ 1) for i in range(devices)])  3.68 us
    ppermute x3, starting transfers between devices, scatter_sum(): total = total + lax.ppermute(sent, axis, pairs).astype(jnp.float32)  3.33 us
    another operation x3, local copies, waits for them, and re-layouts, scatter_sum(): mine = jnp.take(blocks, core, axis=1).astype(jnp.float32)  3.31 us
    ppermute x3, starting transfers between devices, per_device(): got = lax.ppermute(sent, 'lon', pairs)  2.9 us
    dot_general x2, matrix products, spread_sum(): lax.dot_general(weight, activation, (((0,), (0,)), ((), ())), preferred_e...  2.45 us
  transfers between devices with their start and end apart: 9, of which 8 were waited for; matrix products, arithmetic and copies ran while one was open for 4% of the time, Pallas kernels for 0%

profile of v21, /device:TPU:16, one launch (start us, length us, event | category | flops | bytes accessed | tf_op | source)
XLA Modules:
  0.0 87.1 jit_solution(13508226314745371336)
XLA Ops:
  0.0 7.5 %all_gather.9 = bf16[512,4,128]{2,1,0:T(4,128)(2,1)S(1)} all-gather(bf16[128,4,128]{2,1,0:T(4,128)(2,1)} %param.20), channel_id=1, replica_groups=mesh['member'=2,'lon'=4,'lev'=4] {'lev'}, dimensions={0}, use_global_device_ids=true | all-gather | bytes 655360 | tf_op jit(solution)/shard_map/all_gather | solution.py:34
  7.5 0.5 fusion.18
  8.1 1.5 %fusion.45 = bf16[512,4,128,1]{2,1,0,3:T(4,128)(2,1)S(1)} fusion(bf16[512,4,128]{2,1,0:T(4,128)(2,1)S(1)} %all_gather.9, f32[512]{0:T(512)S(1)} %copy-done.5, f32[4,128]{1,0:T(4,128)S(1)} %add_rsqrt_fusion.2), kind=kLoop, calls=%fused_computation.69 | loop fusion | flops 1048576 | bytes 1052672 | tf_op jit(solution)/shard_map/convert_element_type | solution.py:136
  9.6 0.4 convolution_bitcast_fusion.2
  10.2 0.1 fusion.112
  10.3 0.4 collective-permute-start.2
  10.7 0.3 copy-done.1
  11.0 0.1 copy.97
  11.3 0.1 fusion.115
  11.4 0.1 copy.95
  11.5 0.1 copy.96
  11.7 0.2 copy.99
  11.9 0.3 reshape.599
  12.3 2.5 %collective-permute-start.1 = (bf16[264,4,128]{2,0,1:T(8,128)(2,1)S(1)}, bf16[264,4,128]{2,0,1:T(8,128)(2,1)S(1)}, u32[]{:S(2)}, u32[]{:S(2)}) collective-permute-start(bf16[264,4,128]{2,0,1:T(8,128)(2,1)S(1)} %pad_maximum_fusion.1), channel_id=1, source_target_pairs={{0,12},{4,0},{8,4},{12,8},{1,13},{5,1},{9,5},{13,9},{2,14},{6,2},{... | collective-permute-start | bytes 811016 | tf_op jit(solution)/shard_map/ppermute | solution.py:153
  14.9 19.2 %collective-permute-done.1 = bf16[264,4,128]{2,0,1:T(8,128)(2,1)S(1)} collective-permute-done((bf16[264,4,128]{2,0,1:T(8,128)(2,1)S(1)}, bf16[264,4,128]{2,0,1:T(8,128)(2,1)S(1)}, u32[]{:S(2)}, u32[]{:S(2)}) %collective-permute-start.1) | collective-permute-done | bytes 270368 | tf_op jit(solution)/shard_map/ppermute | solution.py:153
  34.1 0.6 reshape.601
  34.7 0.1 slice_bitcast_fusion.4
  34.8 2.3 %collective-permute-done = bf16[264,4,128]{2,0,1:T(8,128)(2,1)S(1)} collective-permute-done((bf16[264,4,128]{2,0,1:T(8,128)(2,1)S(1)}, bf16[264,4,128]{2,0,1:T(8,128)(2,1)S(1)}, u32[]{:S(2)}, u32[]{:S(2)}) %collective-permute-start) | collective-permute-done | bytes 270368 | tf_op jit(solution)/shard_map/ppermute | solution.py:153
  37.1 0.6 reshape.600
  37.7 0.2 slice_bitcast_fusion.5
  38.0 0.1 pad_maximum_fusion
  38.1 0.9 %fusion = (f32[2,4,132]{2,1,0:T(4,128)S(1)}, f32[2,4,132,4,128]{4,2,3,1,0:T(8,128)S(1)}) fusion(bf16[4,2,2,64,4,128]{5,3,0,4,2,1:T(8,128)(2,1)S(1)} %pad_maximum_fusion, bf16[2,64,4,2]{3,1,2,0:T(8,128)(2,1)S(1)} %copy.113, bf16[2,64,4,128]{3,1,2,0:T(8,128)(2,1)S(1)} %fusion.102, bf16[2,64,4,2]{3,1,2,0:T(8,128)(2,1)S(1)} %copy.112), kind=kOutput, calls=%fused_computation.1 | convolution fusion | flops 70691808 | bytes 3084416 | tf_op jit(solution)/shard_map/hdri,phdrj->hripj/dot_general | solution.py:73
  39.0 0.5 fusion.38
  39.5 0.3 copy.114
  39.8 0.2 reshape.602
  40.0 0.3 fusion.2
  40.3 0.1 reshape.603
  40.4 1.1 %constant_dynamic-slice_fusion.5 = (bf16[2,1,128,528]{2,1,0,3:T(2,128)(2,1)S(1)}, bf16[2,1,128,528]{2,1,0,3:T(2,128)(2,1)S(1)}) fusion(bf16[2,2,128,528]{2,1,0,3:T(2,128)(2,1)S(1)} %reshape.603, s32[]{:T(128)S(6)} %select_n.94, s32[]{:T(128)S(6)} %select_n.96), kind=kLoop, calls=%fused_computation.172 | loop fusion | bytes 1081352 | tf_op jit(solution)/shard_map/jit(_take) | solution.py:43
  41.6 0.1 collective-permute-start.3
  41.8 0.1 broadcast_multiply_fusion.5
  41.9 1.3 %collective-permute-done.3 = bf16[2,128,528]{1,2,0:T(8,128)(2,1)S(1)} collective-permute-done((bf16[2,128,528]{1,2,0:T(8,128)(2,1)S(1)}, bf16[2,128,528]{1,2,0:T(8,128)(2,1)S(1)}, u32[]{:S(2)}, u32[]{:S(2)}) %collective-permute-start.3) | collective-permute-done | bytes 270368 | tf_op jit(solution)/shard_map/ppermute | solution.py:45
  43.2 0.1 convert_add_fusion
  43.3 1.2 %collective-permute-start.4 = (bf16[128,528]{0,1:T(8,128)(2,1)S(1)}, bf16[128,528]{0,1:T(8,128)(2,1)S(1)}, u32[]{:S(2)}, u32[]{:S(2)}) collective-permute-start(bf16[128,528]{0,1:T(8,128)(2,1)S(1)} %bitcast_convert_fusion), channel_id=1, source_target_pairs={{0,2},{1,3},{2,0},{3,1},{4,6},{5,7},{6,4},{7,5},{8,10},{9,11},{10,... | collective-permute-start | bytes 405512 | tf_op jit(solution)/shard_map/ppermute | solution.py:50
  44.5 0.1 copy.105
  44.6 0.1 copy.103
  44.8 4.3 %collective-permute-done.4 = bf16[128,528]{0,1:T(8,128)(2,1)S(1)} collective-permute-done((bf16[128,528]{0,1:T(8,128)(2,1)S(1)}, bf16[128,528]{0,1:T(8,128)(2,1)S(1)}, u32[]{:S(2)}, u32[]{:S(2)}) %collective-permute-start.4) | collective-permute-done | bytes 135200 | tf_op jit(solution)/shard_map/ppermute | solution.py:50
  49.1 0.2 fusion.68
  49.3 7.2 %all_gather.10 = bf16[512,4,130]{0,2,1:T(8,128)(2,1)S(1)} all-gather(bf16[128,4,130]{0,2,1:T(8,128)(2,1)S(1)} %fusion.68), channel_id=1, replica_groups=mesh['member'=2,'lon'=4,'lev'=4] {'lev'}, dimensions={0}, use_global_device_ids=true | all-gather | bytes 665600 | tf_op jit(solution)/shard_map/all_gather | solution.py:34
  56.5 0.2 fusion.5
  56.8 0.2 fusion.7
  57.0 0.1 reshape.605
  57.1 2.2 %fusion.3 = bf16[512,520]{0,1:T(8,128)(2,1)S(1)} fusion(bf16[512,520]{0,1:T(8,128)(2,1)S(1)} %reshape.605, bf16[2,512,512]{2,1,0:T(8,128)(2,1)} %param.27, bf16[2,512,512]{2,1,0:T(8,128)(2,1)} %param.26), kind=kOutput, calls=%fused_computation.18 | convolution fusion | flops 547921920 | bytes 2113536 | tf_op jit(solution)/shard_map/dot_general | solution.py:55
  59.3 0.1 reshape.606
  59.4 1.1 %constant_dynamic-slice_fusion.2 = (bf16[2,1,128,520]{2,1,0,3:T(2,128)(2,1)S(1)}, bf16[2,1,128,520]{2,1,0,3:T(2,128)(2,1)S(1)}) fusion(bf16[2,2,128,520]{2,1,0,3:T(2,128)(2,1)S(1)} %reshape.606, s32[]{:T(128)S(6)} %select_n.94, s32[]{:T(128)S(6)} %select_n.96), kind=kLoop, calls=%fused_computation.169 | loop fusion | bytes 1064968 | tf_op jit(solution)/shard_map/jit(_take) | solution.py:43
  60.6 0.4 collective-permute-start.5
  61.0 1.2 %collective-permute-done.5 = bf16[2,128,520]{1,2,0:T(8,128)(2,1)S(1)} collective-permute-done((bf16[2,128,520]{1,2,0:T(8,128)(2,1)S(1)}, bf16[2,128,520]{1,2,0:T(8,128)(2,1)S(1)}, u32[]{:S(2)}, u32[]{:S(2)}) %collective-permute-start.5) | collective-permute-done | bytes 266272 | tf_op jit(solution)/shard_map/ppermute | solution.py:45
  62.3 1.0 %collective-permute-start.6 = (bf16[128,520]{0,1:T(8,128)(2,1)S(1)}, bf16[128,520]{0,1:T(8,128)(2,1)S(1)}, u32[]{:S(2)}, u32[]{:S(2)}) collective-permute-start(bf16[128,520]{0,1:T(8,128)(2,1)S(1)} %bitcast_convert_fusion.1), channel_id=1, source_target_pairs={{0,2},{1,3},{2,0},{3,1},{4,6},{5,7},{6,4},{7,5},{8,10},{9,11},{10,... | collective-permute-start | bytes 399368 | tf_op jit(solution)/shard_map/ppermute | solution.py:50
  63.3 4.9 %collective-permute-done.6 = bf16[128,520]{0,1:T(8,128)(2,1)S(1)} collective-permute-done((bf16[128,520]{0,1:T(8,128)(2,1)S(1)}, bf16[128,520]{0,1:T(8,128)(2,1)S(1)}, u32[]{:S(2)}, u32[]{:S(2)}) %collective-permute-start.6) | collective-permute-done | bytes 133152 | tf_op jit(solution)/shard_map/ppermute | solution.py:50
  68.3 0.2 fusion.87
  68.5 6.8 %all_gather.11 = bf16[512,4,128]{0,2,1:T(8,128)(2,1)S(1)} all-gather(bf16[128,4,128]{0,2,1:T(8,128)(2,1)S(1)} %fusion.87), channel_id=1, replica_groups=mesh['member'=2,'lon'=4,'lev'=4] {'lev'}, dimensions={0}, use_global_device_ids=true | all-gather | bytes 655360 | tf_op jit(solution)/shard_map/all_gather | solution.py:34
  75.3 0.2 fusion.21
  75.5 0.2 fusion.23
  75.7 0.7 fusion.31
  76.4 0.5 copy-done.7
  76.9 0.4 fusion.4
  77.4 0.1 reshape.610
  77.5 1.1 %constant_dynamic-slice_fusion.1 = (bf16[2,1,128,4,128]{2,1,0,4,3:T(2,128)(2,1)S(1)}, bf16[2,1,128,4,128]{2,1,0,4,3:T(2,128)(2,1)S(1)}) fusion(bf16[2,2,128,4,128]{2,1,0,4,3:T(2,128)(2,1)S(1)} %reshape.610, s32[]{:T(128)S(6)} %select_n.94, s32[]{:T(128)S(6)} %select_n.96), kind=kLoop, calls=%fused_computation.168 | loop fusion | bytes 1048584 | tf_op jit(solution)/shard_map/jit(_take) | solution.py:43
  78.7 0.4 collective-permute-start.7
  79.1 1.2 %collective-permute-done.7 = bf16[2,128,4,128]{1,3,2,0:T(8,128)(2,1)S(1)} collective-permute-done((bf16[2,128,4,128]{1,3,2,0:T(8,128)(2,1)S(1)}, bf16[2,128,4,128]{1,3,2,0:T(8,128)(2,1)S(1)}, u32[]{:S(2)}, u32[]{:S(2)}) %collective-permute-start.7) | collective-permute-done | bytes 262176 | tf_op jit(solution)/shard_map/ppermute | solution.py:45
  80.3 0.1 convert_add_fusion.2
  80.4 1.2 %collective-permute-start.8 = (bf16[128,4,128]{0,2,1:T(8,128)(2,1)S(1)}, bf16[128,4,128]{0,2,1:T(8,128)(2,1)S(1)}, u32[]{:S(2)}, u32[]{:S(2)}) collective-permute-start(bf16[128,4,128]{0,2,1:T(8,128)(2,1)S(1)} %bitcast_convert_fusion.2), channel_id=1, source_target_pairs={{0,2},{1,3},{2,0},{3,1},{4,6},{5,7},{6,4},{7,5},{8,10},{9,11},{10,... | collective-permute-start | bytes 393224 | tf_op jit(solution)/shard_map/ppermute | solution.py:50
  81.5 4.7 %collective-permute-done.8 = bf16[128,4,128]{0,2,1:T(8,128)(2,1)S(1)} collective-permute-done((bf16[128,4,128]{0,2,1:T(8,128)(2,1)S(1)}, bf16[128,4,128]{0,2,1:T(8,128)(2,1)S(1)}, u32[]{:S(2)}, u32[]{:S(2)}) %collective-permute-start.8) | collective-permute-done | bytes 131104 | tf_op jit(solution)/shard_map/ppermute | solution.py:50
  86.2 0.1 fusion.100
  86.3 0.8 copy.121
  (59 shorter events, 1.1 us)
Async XLA Ops:
  0.0 9.6 %copy-start = (bf16[3,128,512]{2,1,0:T(8,128)(2,1)S(1)}, bf16[3,128,512]{2,1,0:T(8,128)(2,1)}, u32[]{:S(2)}) copy-start(bf16[3,128,512]{2,1,0:T(8,128)(2,1)} %param.22) | copy-start | bytes 1179652
  0.0 8.1 %copy-start.5 = (f32[512]{0:T(512)S(1)}, f32[512]{0:T(512)}, u32[]{:S(2)}) copy-start(f32[512]{0:T(512)} %param.21) | copy-start | bytes 6148
  10.1 0.9 %copy-start.1 = (bf16[128,4,128]{2,1,0:T(4,128)(2,1)S(1)}, bf16[128,4,128]{2,1,0:T(4,128)(2,1)}, u32[]{:S(2)}) copy-start(bf16[128,4,128]{2,1,0:T(4,128)(2,1)} %param.20) | copy-start | bytes 393220
  10.3 27.7 %collective-permute-start.2 = (bf16[256,4,128]{2,0,1:T(8,128)(2,1)S(1)}, bf16[256,4,128]{2,0,1:T(8,128)(2,1)S(1)}, u32[]{:S(2)}, u32[]{:S(2)}) collective-permute-start(bf16[256,4,128]{2,0,1:T(8,128)(2,1)S(1)} %bitcast.190), channel_id=1, source_target_pairs={{0,8},{4,12},{8,0},{12,4},{1,9},{5,13},{9,1},{13,5},{2,10},{6,14},... | collective-permute-start | bytes 786440 | tf_op jit(solution)/shard_map/ppermute | solution.py:153
  11.3 3.5 %copy-start.3 = (f32[2,9,128]{2,0,1:T(2,128)S(1)}, f32[2,9,128]{2,0,1:T(2,128)}, u32[]{:S(2)}) copy-start(f32[2,9,128]{2,0,1:T(2,128)} %param.24) | copy-start | bytes 27652
  12.3 21.8 %collective-permute-start.1 = (bf16[264,4,128]{2,0,1:T(8,128)(2,1)S(1)}, bf16[264,4,128]{2,0,1:T(8,128)(2,1)S(1)}, u32[]{:S(2)}, u32[]{:S(2)}) collective-permute-start(bf16[264,4,128]{2,0,1:T(8,128)(2,1)S(1)} %pad_maximum_fusion.1), channel_id=1, source_target_pairs={{0,12},{4,0},{8,4},{12,8},{1,13},{5,1},{9,5},{13,9},{2,14},{6,2},{... | collective-permute-start | bytes 811016 | tf_op jit(solution)/shard_map/ppermute | solution.py:153
  14.8 22.3 %collective-permute-start = (bf16[264,4,128]{2,0,1:T(8,128)(2,1)S(1)}, bf16[264,4,128]{2,0,1:T(8,128)(2,1)S(1)}, u32[]{:S(2)}, u32[]{:S(2)}) collective-permute-start(bf16[264,4,128]{2,0,1:T(8,128)(2,1)S(1)} %pad_maximum_fusion.1), channel_id=1, source_target_pairs={{0,4},{4,8},{8,12},{12,0},{1,5},{5,9},{9,13},{13,1},{2,6},{6,10},{... | collective-permute-start | bytes 811016 | tf_op jit(solution)/shard_map/ppermute | solution.py:153
  39.0 1.0 %copy-start.2 = (bf16[128,512]{1,0:T(8,128)(2,1)S(1)}, bf16[128,512]{1,0:T(8,128)(2,1)}, u32[]{:S(2)}) copy-start(bf16[128,512]{1,0:T(8,128)(2,1)} %param.23) | copy-start | bytes 393220
  41.5 3.0 %copy-start.4 = (f32[2,512]{1,0:T(2,128)S(1)}, f32[2,512]{1,0:T(2,128)}, u32[]{:S(2)}) copy-start(f32[2,512]{1,0:T(2,128)} %param.25) | copy-start | bytes 12292
  41.6 1.6 %collective-permute-start.3 = (bf16[2,128,528]{1,2,0:T(8,128)(2,1)S(1)}, bf16[2,128,528]{1,2,0:T(8,128)(2,1)S(1)}, u32[]{:S(2)}, u32[]{:S(2)}) collective-permute-start(bf16[2,128,528]{1,2,0:T(8,128)(2,1)S(1)} %fusion.74), channel_id=1, source_target_pairs={{0,1},{1,0},{2,3},{3,2},{4,5},{5,4},{6,7},{7,6},{8,9},{9,8},{10,11... | collective-permute-start | bytes 811016 | tf_op jit(solution)/shard_map/ppermute | solution.py:45
  43.3 5.7 %collective-permute-start.4 = (bf16[128,528]{0,1:T(8,128)(2,1)S(1)}, bf16[128,528]{0,1:T(8,128)(2,1)S(1)}, u32[]{:S(2)}, u32[]{:S(2)}) collective-permute-start(bf16[128,528]{0,1:T(8,128)(2,1)S(1)} %bitcast_convert_fusion), channel_id=1, source_target_pairs={{0,2},{1,3},{2,0},{3,1},{4,6},{5,7},{6,4},{7,5},{8,10},{9,11},{10,... | collective-permute-start | bytes 405512 | tf_op jit(solution)/shard_map/ppermute | solution.py:50
  60.6 1.6 %collective-permute-start.5 = (bf16[2,128,520]{1,2,0:T(8,128)(2,1)S(1)}, bf16[2,128,520]{1,2,0:T(8,128)(2,1)S(1)}, u32[]{:S(2)}, u32[]{:S(2)}) collective-permute-start(bf16[2,128,520]{1,2,0:T(8,128)(2,1)S(1)} %fusion.76), channel_id=1, source_target_pairs={{0,1},{1,0},{2,3},{3,2},{4,5},{5,4},{6,7},{7,6},{8,9},{9,8},{10,11... | collective-permute-start | bytes 798728 | tf_op jit(solution)/shard_map/ppermute | solution.py:45
  62.3 5.9 %collective-permute-start.6 = (bf16[128,520]{0,1:T(8,128)(2,1)S(1)}, bf16[128,520]{0,1:T(8,128)(2,1)S(1)}, u32[]{:S(2)}, u32[]{:S(2)}) collective-permute-start(bf16[128,520]{0,1:T(8,128)(2,1)S(1)} %bitcast_convert_fusion.1), channel_id=1, source_target_pairs={{0,2},{1,3},{2,0},{3,1},{4,6},{5,7},{6,4},{7,5},{8,10},{9,11},{10,... | collective-permute-start | bytes 399368 | tf_op jit(solution)/shard_map/ppermute | solution.py:50
  68.5 7.2 %copy-start.6 = (bf16[2,512,512]{2,1,0:T(8,128)(2,1)S(1)}, bf16[2,512,512]{2,1,0:T(8,128)(2,1)}, u32[]{:S(2)}) copy-start(bf16[2,512,512]{2,1,0:T(8,128)(2,1)} %param.26) | copy-start | bytes 3145732
  75.7 1.2 %copy-start.7 = (bf16[2,512,512]{2,1,0:T(8,128)(2,1)S(1)}, bf16[2,512,512]{2,1,0:T(8,128)(2,1)}, u32[]{:S(2)}) copy-start(bf16[2,512,512]{2,1,0:T(8,128)(2,1)} %param.27) | copy-start | bytes 3145732
  78.7 1.6 %collective-permute-start.7 = (bf16[2,128,4,128]{1,3,2,0:T(8,128)(2,1)S(1)}, bf16[2,128,4,128]{1,3,2,0:T(8,128)(2,1)S(1)}, u32[]{:S(2)}, u32[]{:S(2)}) collective-permute-start(bf16[2,128,4,128]{1,3,2,0:T(8,128)(2,1)S(1)} %fusion.97), channel_id=1, source_target_pairs={{0,1},{1,0},{2,3},{3,2},{4,5},{5,4},{6,7},{7,6},{8,9},{9,8},{10,11... | collective-permute-start | bytes 786440 | tf_op jit(solution)/shard_map/ppermute | solution.py:45
  80.4 5.8 %collective-permute-start.8 = (bf16[128,4,128]{0,2,1:T(8,128)(2,1)S(1)}, bf16[128,4,128]{0,2,1:T(8,128)(2,1)S(1)}, u32[]{:S(2)}, u32[]{:S(2)}) collective-permute-start(bf16[128,4,128]{0,2,1:T(8,128)(2,1)S(1)} %bitcast_convert_fusion.2), channel_id=1, source_target_pairs={{0,2},{1,3},{2,0},{3,1},{4,6},{5,7},{6,4},{7,5},{8,10},{9,11},{10,... | collective-permute-start | bytes 393224 | tf_op jit(solution)/shard_map/ppermute | solution.py:50

commit v22 on v21

--- a/solution.py
+++ b/solution.py
@@ -164,7 +164,11 @@
 
     numerator, denominator = make_fold(wide_queries, (all_keys[:, 0], all_keys[:, 1]))
     attended = (numerator / denominator[:, None]).astype(jnp.bfloat16)
-    update = spread_sum(out_weight, attended.reshape(ch_local, -1))
+    partial = jnp.einsum(
+        "kc,krw->crw", out_weight, attended.reshape(ch_local, lat_rows, -1),
+        preferred_element_type=jnp.float32,
+    ).astype(jnp.bfloat16)
+    update = scatter_sum(partial, "lev")
     current = (wide_latent.astype(jnp.float32) + update.reshape(wide_latent.shape)).astype(
         jnp.bfloat16
     )

time: 87.3 us -> 88.3 us (1.011)
  other arithmetic: 4.6 us -> 5.91 us
    select_n x0 -> x1, other arithmetic: none -> 1.4 us  [scatter_sum(): mine = jnp.take(blocks, core, axis=1).astype(jnp.float32)]
    another operation x3 -> x2, local copies, waits for them, and re-layouts: 3.31 us -> 2.19 us  [scatter_sum(): mine = jnp.take(blocks, core, axis=1).astype(jnp.float32)]
    dot_general x2 -> x1, matrix products: 2.45 us -> 2.01 us  [spread_sum(): lax.dot_general(weight, activation, (((0,), (0,)), ((), ())), preferred_e...]
where the time goes in v22:
time: 88.3 us; the launch traced here: 88 us
  waiting for transfers between devices  39.1 us (44%)
  blocking collectives  21.3 us (24%)
  local copies, waits for them, and re-layouts  8.63 us (10%)
  starting transfers between devices  7.19 us (8%)
  other arithmetic  5.91 us (7%)
  matrix products  5.18 us (6%)
    ppermute x3, waiting for transfers between devices, per_device(): got = lax.ppermute(sent, 'lon', pairs)  21.5 us
    all_gather x3, blocking collectives, gather_channels(): return lax.all_gather(values, 'lev', axis=0, tiled=True)  21.3 us
    ppermute x3, waiting for transfers between devices, scatter_sum(): total = total + lax.ppermute(sent, axis, pairs).astype(jnp.float32)  13.9 us
    ppermute x3, waiting for transfers between devices, scatter_sum(): lax.ppermute(theirs, axis, [(i, i ^ 1) for i in range(devices)])  3.69 us
    ppermute x3, starting transfers between devices, scatter_sum(): total = total + lax.ppermute(sent, axis, pairs).astype(jnp.float32)  3.33 us
    ppermute x3, starting transfers between devices, per_device(): got = lax.ppermute(sent, 'lon', pairs)  2.9 us
    another operation x2, local copies, waits for them, and re-layouts, scatter_sum(): mine = jnp.take(blocks, core, axis=1).astype(jnp.float32)  2.19 us
    dot_general x1, matrix products, spread_sum(): lax.dot_general(weight, activation, (((0,), (0,)), ((), ())), preferred_e...  2.01 us
  transfers between devices with their start and end apart: 9, of which 8 were waited for; matrix products, arithmetic and copies ran while one was open for 4% of the time, Pallas kernels for 0%

profile of v22, /device:TPU:16, one launch (start us, length us, event | category | flops | bytes accessed | tf_op | source)
XLA Modules:
  0.0 88.0 jit_solution(15267247422510283184)
XLA Ops:
  0.0 7.5 %all_gather.9 = bf16[512,4,128]{2,1,0:T(4,128)(2,1)S(1)} all-gather(bf16[128,4,128]{2,1,0:T(4,128)(2,1)} %param.20), channel_id=1, replica_groups=mesh['member'=2,'lon'=4,'lev'=4] {'lev'}, dimensions={0}, use_global_device_ids=true | all-gather | bytes 655360 | tf_op jit(solution)/shard_map/all_gather | solution.py:34
  7.5 0.5 fusion.18
  8.1 1.5 %fusion.45 = bf16[512,4,128,1]{2,1,0,3:T(4,128)(2,1)S(1)} fusion(bf16[512,4,128]{2,1,0:T(4,128)(2,1)S(1)} %all_gather.9, f32[512]{0:T(512)S(1)} %copy-done.5, f32[4,128]{1,0:T(4,128)S(1)} %add_rsqrt_fusion.2), kind=kLoop, calls=%fused_computation.71 | loop fusion | flops 1048576 | bytes 1052672 | tf_op jit(solution)/shard_map/convert_element_type | solution.py:136
  9.6 0.4 convolution_bitcast_fusion.2
  10.2 0.1 fusion.113
  10.3 0.4 collective-permute-start.2
  10.7 0.3 copy-done.1
  11.0 0.1 copy.156
  11.3 0.1 fusion.117
  11.4 0.1 copy.154
  11.5 0.1 copy.155
  11.7 0.2 copy.158
  11.9 0.3 reshape.596
  12.3 2.5 %collective-permute-start.1 = (bf16[264,4,128]{2,0,1:T(8,128)(2,1)S(1)}, bf16[264,4,128]{2,0,1:T(8,128)(2,1)S(1)}, u32[]{:S(2)}, u32[]{:S(2)}) collective-permute-start(bf16[264,4,128]{2,0,1:T(8,128)(2,1)S(1)} %pad_maximum_fusion.1), channel_id=1, source_target_pairs={{0,12},{4,0},{8,4},{12,8},{1,13},{5,1},{9,5},{13,9},{2,14},{6,2},{... | collective-permute-start | bytes 811016 | tf_op jit(solution)/shard_map/ppermute | solution.py:153
  14.9 19.2 %collective-permute-done.1 = bf16[264,4,128]{2,0,1:T(8,128)(2,1)S(1)} collective-permute-done((bf16[264,4,128]{2,0,1:T(8,128)(2,1)S(1)}, bf16[264,4,128]{2,0,1:T(8,128)(2,1)S(1)}, u32[]{:S(2)}, u32[]{:S(2)}) %collective-permute-start.1) | collective-permute-done | bytes 270368 | tf_op jit(solution)/shard_map/ppermute | solution.py:153
  34.1 0.6 reshape.598
  34.6 0.1 slice_bitcast_fusion.4
  34.8 2.3 %collective-permute-done = bf16[264,4,128]{2,0,1:T(8,128)(2,1)S(1)} collective-permute-done((bf16[264,4,128]{2,0,1:T(8,128)(2,1)S(1)}, bf16[264,4,128]{2,0,1:T(8,128)(2,1)S(1)}, u32[]{:S(2)}, u32[]{:S(2)}) %collective-permute-start) | collective-permute-done | bytes 270368 | tf_op jit(solution)/shard_map/ppermute | solution.py:153
  37.1 0.6 reshape.597
  37.7 0.2 slice_bitcast_fusion.5
  38.0 0.1 pad_maximum_fusion
  38.1 0.9 %fusion = (f32[2,4,132]{2,1,0:T(4,128)S(1)}, f32[2,4,132,4,128]{4,2,3,1,0:T(8,128)S(1)}) fusion(bf16[4,2,2,64,4,128]{5,3,0,4,2,1:T(8,128)(2,1)S(1)} %pad_maximum_fusion, bf16[2,64,4,2]{3,1,2,0:T(8,128)(2,1)S(1)} %copy.172, bf16[2,64,4,128]{3,1,2,0:T(8,128)(2,1)S(1)} %fusion.102, bf16[2,64,4,2]{3,1,2,0:T(8,128)(2,1)S(1)} %copy.171), kind=kOutput, calls=%fused_computation.1 | convolution fusion | flops 70691808 | bytes 3084416 | tf_op jit(solution)/shard_map/hdri,phdrj->hripj/dot_general | solution.py:73
  39.0 0.5 fusion.38
  39.5 0.3 copy.173
  39.8 0.2 reshape.599
  40.0 0.3 fusion.2
  40.3 0.2 reshape.600
  40.5 1.4 %broadcast_select_fusion.1 = (bf16[2,1,128,4,132]{2,1,0,4,3:T(2,128)(2,1)S(1)}, bf16[2,1,128,4,132]{2,1,0,4,3:T(2,128)(2,1)S(1)}) fusion(pred[]{:T(512)S(6)} %and.60, bf16[2,2,128,4,132]{2,1,0,4,3:T(2,128)(2,1)S(1)} %reshape.600, s32[]{:T(128)S(6)} %select_n.94, s32[]{:T(128)S(6)} %select_n.96, pred[]{:T(512)S(6)} %and.61), kind=kLoop, calls=%fused_computation.26 | loop fusion | flops 270336 | bytes 1081354 | tf_op jit(solution)/shard_map/jit(_take)/select_n | solution.py:43
  41.9 0.1 collective-permute-start.3
  42.1 0.1 broadcast_multiply_fusion.5
  42.2 1.3 %collective-permute-done.3 = bf16[2,128,4,132]{1,3,2,0:T(8,128)(2,1)S(1)} collective-permute-done((bf16[2,128,4,132]{1,3,2,0:T(8,128)(2,1)S(1)}, bf16[2,128,4,132]{1,3,2,0:T(8,128)(2,1)S(1)}, u32[]{:S(2)}, u32[]{:S(2)}) %collective-permute-start.3) | collective-permute-done | bytes 270368 | tf_op jit(solution)/shard_map/ppermute | solution.py:45
  43.6 1.2 %collective-permute-start.4 = (bf16[128,4,132]{0,2,1:T(8,128)(2,1)S(1)}, bf16[128,4,132]{0,2,1:T(8,128)(2,1)S(1)}, u32[]{:S(2)}, u32[]{:S(2)}) collective-permute-start(bf16[128,4,132]{0,2,1:T(8,128)(2,1)S(1)} %bitcast_convert_fusion), channel_id=1, source_target_pairs={{0,2},{1,3},{2,0},{3,1},{4,6},{5,7},{6,4},{7,5},{8,10},{9,11},{10,... | collective-permute-start | bytes 405512 | tf_op jit(solution)/shard_map/ppermute | solution.py:50
  44.8 0.1 copy.164
  44.9 0.1 copy.162
  45.1 4.4 %collective-permute-done.4 = bf16[128,4,132]{0,2,1:T(8,128)(2,1)S(1)} collective-permute-done((bf16[128,4,132]{0,2,1:T(8,128)(2,1)S(1)}, bf16[128,4,132]{0,2,1:T(8,128)(2,1)S(1)}, u32[]{:S(2)}, u32[]{:S(2)}) %collective-permute-start.4) | collective-permute-done | bytes 135200 | tf_op jit(solution)/shard_map/ppermute | solution.py:50
  49.4 0.1 fusion.115
  49.5 0.2 fusion.68
  49.7 7.2 %all_gather.10 = bf16[512,4,130]{0,2,1:T(8,128)(2,1)S(1)} all-gather(bf16[128,4,130]{0,2,1:T(8,128)(2,1)S(1)} %fusion.68), channel_id=1, replica_groups=mesh['member'=2,'lon'=4,'lev'=4] {'lev'}, dimensions={0}, use_global_device_ids=true | all-gather | bytes 665600 | tf_op jit(solution)/shard_map/all_gather | solution.py:34
  56.9 0.2 fusion.5
  57.2 0.2 fusion.7
  57.4 0.1 reshape.601
  57.5 0.8 copy-done.6
  58.4 2.0 %fusion.3 = bf16[512,520]{0,1:T(8,128)(2,1)S(1)} fusion(bf16[512,520]{0,1:T(8,128)(2,1)S(1)} %reshape.601, bf16[2,512,512]{2,1,0:T(8,128)(2,1)} %param.27, bf16[2,512,512]{2,1,0:T(8,128)(2,1)S(1)} %copy-done.6), kind=kOutput, calls=%fused_computation.18 | convolution fusion | flops 547921920 | bytes 2113536 | tf_op jit(solution)/shard_map/dot_general | solution.py:55
  60.4 0.1 reshape.602
  60.5 1.1 %constant_dynamic-slice_fusion.2 = (bf16[2,1,128,520]{2,1,0,3:T(2,128)(2,1)S(1)}, bf16[2,1,128,520]{2,1,0,3:T(2,128)(2,1)S(1)}) fusion(bf16[2,2,128,520]{2,1,0,3:T(2,128)(2,1)S(1)} %reshape.602, s32[]{:T(128)S(6)} %select_n.94, s32[]{:T(128)S(6)} %select_n.96), kind=kLoop, calls=%fused_computation.170 | loop fusion | bytes 1064968 | tf_op jit(solution)/shard_map/jit(_take) | solution.py:43
  61.7 0.4 collective-permute-start.5
  62.1 1.2 %collective-permute-done.5 = bf16[2,128,520]{1,2,0:T(8,128)(2,1)S(1)} collective-permute-done((bf16[2,128,520]{1,2,0:T(8,128)(2,1)S(1)}, bf16[2,128,520]{1,2,0:T(8,128)(2,1)S(1)}, u32[]{:S(2)}, u32[]{:S(2)}) %collective-permute-start.5) | collective-permute-done | bytes 266272 | tf_op jit(solution)/shard_map/ppermute | solution.py:45
  63.4 1.0 %collective-permute-start.6 = (bf16[128,520]{0,1:T(8,128)(2,1)S(1)}, bf16[128,520]{0,1:T(8,128)(2,1)S(1)}, u32[]{:S(2)}, u32[]{:S(2)}) collective-permute-start(bf16[128,520]{0,1:T(8,128)(2,1)S(1)} %bitcast_convert_fusion.1), channel_id=1, source_target_pairs={{0,2},{1,3},{2,0},{3,1},{4,6},{5,7},{6,4},{7,5},{8,10},{9,11},{10,... | collective-permute-start | bytes 399368 | tf_op jit(solution)/shard_map/ppermute | solution.py:50
  64.4 4.9 %collective-permute-done.6 = bf16[128,520]{0,1:T(8,128)(2,1)S(1)} collective-permute-done((bf16[128,520]{0,1:T(8,128)(2,1)S(1)}, bf16[128,520]{0,1:T(8,128)(2,1)S(1)}, u32[]{:S(2)}, u32[]{:S(2)}) %collective-permute-start.6) | collective-permute-done | bytes 133152 | tf_op jit(solution)/shard_map/ppermute | solution.py:50
  69.4 0.2 fusion.87
  69.6 6.6 %all_gather.11 = bf16[512,4,128]{0,2,1:T(8,128)(2,1)S(1)} all-gather(bf16[128,4,128]{0,2,1:T(8,128)(2,1)S(1)} %fusion.87), channel_id=1, replica_groups=mesh['member'=2,'lon'=4,'lev'=4] {'lev'}, dimensions={0}, use_global_device_ids=true | all-gather | bytes 655360 | tf_op jit(solution)/shard_map/all_gather | solution.py:34
  76.2 0.2 fusion.21
  76.4 0.2 fusion.23
  76.6 0.7 fusion.31
  77.3 0.5 copy-done.7
  77.9 0.4 fusion.4
  78.3 0.1 reshape.606
  78.4 1.1 %constant_dynamic-slice_fusion.1 = (bf16[2,1,128,4,128]{2,1,0,4,3:T(2,128)(2,1)S(1)}, bf16[2,1,128,4,128]{2,1,0,4,3:T(2,128)(2,1)S(1)}) fusion(bf16[2,2,128,4,128]{2,1,0,4,3:T(2,128)(2,1)S(1)} %reshape.606, s32[]{:T(128)S(6)} %select_n.94, s32[]{:T(128)S(6)} %select_n.96), kind=kLoop, calls=%fused_computation.169 | loop fusion | bytes 1048584 | tf_op jit(solution)/shard_map/jit(_take) | solution.py:43
  79.6 0.4 collective-permute-start.7
  80.0 1.2 %collective-permute-done.7 = bf16[2,128,4,128]{1,3,2,0:T(8,128)(2,1)S(1)} collective-permute-done((bf16[2,128,4,128]{1,3,2,0:T(8,128)(2,1)S(1)}, bf16[2,128,4,128]{1,3,2,0:T(8,128)(2,1)S(1)}, u32[]{:S(2)}, u32[]{:S(2)}) %collective-permute-start.7) | collective-permute-done | bytes 262176 | tf_op jit(solution)/shard_map/ppermute | solution.py:45
  81.2 0.1 convert_add_fusion.2
  81.3 1.2 %collective-permute-start.8 = (bf16[128,4,128]{0,2,1:T(8,128)(2,1)S(1)}, bf16[128,4,128]{0,2,1:T(8,128)(2,1)S(1)}, u32[]{:S(2)}, u32[]{:S(2)}) collective-permute-start(bf16[128,4,128]{0,2,1:T(8,128)(2,1)S(1)} %bitcast_convert_fusion.2), channel_id=1, source_target_pairs={{0,2},{1,3},{2,0},{3,1},{4,6},{5,7},{6,4},{7,5},{8,10},{9,11},{10,... | collective-permute-start | bytes 393224 | tf_op jit(solution)/shard_map/ppermute | solution.py:50
  82.5 4.7 %collective-permute-done.8 = bf16[128,4,128]{0,2,1:T(8,128)(2,1)S(1)} collective-permute-done((bf16[128,4,128]{0,2,1:T(8,128)(2,1)S(1)}, bf16[128,4,128]{0,2,1:T(8,128)(2,1)S(1)}, u32[]{:S(2)}, u32[]{:S(2)}) %collective-permute-start.8) | collective-permute-done | bytes 131104 | tf_op jit(solution)/shard_map/ppermute | solution.py:50
  87.2 0.8 copy.180
  (57 shorter events, 1.1 us)
Async XLA Ops:
  0.0 9.6 %copy-start = (bf16[3,128,512]{2,1,0:T(8,128)(2,1)S(1)}, bf16[3,128,512]{2,1,0:T(8,128)(2,1)}, u32[]{:S(2)}) copy-start(bf16[3,128,512]{2,1,0:T(8,128)(2,1)} %param.22) | copy-start | bytes 1179652
  0.0 8.1 %copy-start.5 = (f32[512]{0:T(512)S(1)}, f32[512]{0:T(512)}, u32[]{:S(2)}) copy-start(f32[512]{0:T(512)} %param.21) | copy-start | bytes 6148
  10.1 0.9 %copy-start.1 = (bf16[128,4,128]{2,1,0:T(4,128)(2,1)S(1)}, bf16[128,4,128]{2,1,0:T(4,128)(2,1)}, u32[]{:S(2)}) copy-start(bf16[128,4,128]{2,1,0:T(4,128)(2,1)} %param.20) | copy-start | bytes 393220
  10.3 27.7 %collective-permute-start.2 = (bf16[256,4,128]{2,0,1:T(8,128)(2,1)S(1)}, bf16[256,4,128]{2,0,1:T(8,128)(2,1)S(1)}, u32[]{:S(2)}, u32[]{:S(2)}) collective-permute-start(bf16[256,4,128]{2,0,1:T(8,128)(2,1)S(1)} %bitcast.194), channel_id=1, source_target_pairs={{0,8},{4,12},{8,0},{12,4},{1,9},{5,13},{9,1},{13,5},{2,10},{6,14},... | collective-permute-start | bytes 786440 | tf_op jit(solution)/shard_map/ppermute | solution.py:153
  11.2 3.5 %copy-start.3 = (f32[2,9,128]{2,0,1:T(2,128)S(1)}, f32[2,9,128]{2,0,1:T(2,128)}, u32[]{:S(2)}) copy-start(f32[2,9,128]{2,0,1:T(2,128)} %param.24) | copy-start | bytes 27652
  12.3 21.8 %collective-permute-start.1 = (bf16[264,4,128]{2,0,1:T(8,128)(2,1)S(1)}, bf16[264,4,128]{2,0,1:T(8,128)(2,1)S(1)}, u32[]{:S(2)}, u32[]{:S(2)}) collective-permute-start(bf16[264,4,128]{2,0,1:T(8,128)(2,1)S(1)} %pad_maximum_fusion.1), channel_id=1, source_target_pairs={{0,12},{4,0},{8,4},{12,8},{1,13},{5,1},{9,5},{13,9},{2,14},{6,2},{... | collective-permute-start | bytes 811016 | tf_op jit(solution)/shard_map/ppermute | solution.py:153
  14.8 22.3 %collective-permute-start = (bf16[264,4,128]{2,0,1:T(8,128)(2,1)S(1)}, bf16[264,4,128]{2,0,1:T(8,128)(2,1)S(1)}, u32[]{:S(2)}, u32[]{:S(2)}) collective-permute-start(bf16[264,4,128]{2,0,1:T(8,128)(2,1)S(1)} %pad_maximum_fusion.1), channel_id=1, source_target_pairs={{0,4},{4,8},{8,12},{12,0},{1,5},{5,9},{9,13},{13,1},{2,6},{6,10},{... | collective-permute-start | bytes 811016 | tf_op jit(solution)/shard_map/ppermute | solution.py:153
  39.0 1.0 %copy-start.2 = (bf16[128,512]{1,0:T(8,128)(2,1)S(1)}, bf16[128,512]{1,0:T(8,128)(2,1)}, u32[]{:S(2)}) copy-start(bf16[128,512]{1,0:T(8,128)(2,1)} %param.23) | copy-start | bytes 393220
  41.9 3.0 %copy-start.4 = (f32[2,512]{1,0:T(2,128)S(1)}, f32[2,512]{1,0:T(2,128)}, u32[]{:S(2)}) copy-start(f32[2,512]{1,0:T(2,128)} %param.25) | copy-start | bytes 12292
  41.9 1.6 %collective-permute-start.3 = (bf16[2,128,4,132]{1,3,2,0:T(8,128)(2,1)S(1)}, bf16[2,128,4,132]{1,3,2,0:T(8,128)(2,1)S(1)}, u32[]{:S(2)}, u32[]{:S(2)}) collective-permute-start(bf16[2,128,4,132]{1,3,2,0:T(8,128)(2,1)S(1)} %bitcast.202), channel_id=1, source_target_pairs={{0,1},{1,0},{2,3},{3,2},{4,5},{5,4},{6,7},{7,6},{8,9},{9,8},{10,11... | collective-permute-start | bytes 811016 | tf_op jit(solution)/shard_map/ppermute | solution.py:45
  43.6 5.8 %collective-permute-start.4 = (bf16[128,4,132]{0,2,1:T(8,128)(2,1)S(1)}, bf16[128,4,132]{0,2,1:T(8,128)(2,1)S(1)}, u32[]{:S(2)}, u32[]{:S(2)}) collective-permute-start(bf16[128,4,132]{0,2,1:T(8,128)(2,1)S(1)} %bitcast_convert_fusion), channel_id=1, source_target_pairs={{0,2},{1,3},{2,0},{3,1},{4,6},{5,7},{6,4},{7,5},{8,10},{9,11},{10,... | collective-permute-start | bytes 405512 | tf_op jit(solution)/shard_map/ppermute | solution.py:50
  57.1 1.2 %copy-start.6 = (bf16[2,512,512]{2,1,0:T(8,128)(2,1)S(1)}, bf16[2,512,512]{2,1,0:T(8,128)(2,1)}, u32[]{:S(2)}) copy-start(bf16[2,512,512]{2,1,0:T(8,128)(2,1)} %param.26) | copy-start | bytes 3145732
  61.7 1.6 %collective-permute-start.5 = (bf16[2,128,520]{1,2,0:T(8,128)(2,1)S(1)}, bf16[2,128,520]{1,2,0:T(8,128)(2,1)S(1)}, u32[]{:S(2)}, u32[]{:S(2)}) collective-permute-start(bf16[2,128,520]{1,2,0:T(8,128)(2,1)S(1)} %fusion.76), channel_id=1, source_target_pairs={{0,1},{1,0},{2,3},{3,2},{4,5},{5,4},{6,7},{7,6},{8,9},{9,8},{10,11... | collective-permute-start | bytes 798728 | tf_op jit(solution)/shard_map/ppermute | solution.py:45
  63.4 5.9 %collective-permute-start.6 = (bf16[128,520]{0,1:T(8,128)(2,1)S(1)}, bf16[128,520]{0,1:T(8,128)(2,1)S(1)}, u32[]{:S(2)}, u32[]{:S(2)}) collective-permute-start(bf16[128,520]{0,1:T(8,128)(2,1)S(1)} %bitcast_convert_fusion.1), channel_id=1, source_target_pairs={{0,2},{1,3},{2,0},{3,1},{4,6},{5,7},{6,4},{7,5},{8,10},{9,11},{10,... | collective-permute-start | bytes 399368 | tf_op jit(solution)/shard_map/ppermute | solution.py:50
  76.6 1.2 %copy-start.7 = (bf16[2,512,512]{2,1,0:T(8,128)(2,1)S(1)}, bf16[2,512,512]{2,1,0:T(8,128)(2,1)}, u32[]{:S(2)}) copy-start(bf16[2,512,512]{2,1,0:T(8,128)(2,1)} %param.27) | copy-start | bytes 3145732
  79.6 1.6 %collective-permute-start.7 = (bf16[2,128,4,128]{1,3,2,0:T(8,128)(2,1)S(1)}, bf16[2,128,4,128]{1,3,2,0:T(8,128)(2,1)S(1)}, u32[]{:S(2)}, u32[]{:S(2)}) collective-permute-start(bf16[2,128,4,128]{1,3,2,0:T(8,128)(2,1)S(1)} %fusion.97), channel_id=1, source_target_pairs={{0,1},{1,0},{2,3},{3,2},{4,5},{5,4},{6,7},{7,6},{8,9},{9,8},{10,11... | collective-permute-start | bytes 786440 | tf_op jit(solution)/shard_map/ppermute | solution.py:45
  81.3 5.8 %collective-permute-start.8 = (bf16[128,4,128]{0,2,1:T(8,128)(2,1)S(1)}, bf16[128,4,128]{0,2,1:T(8,128)(2,1)S(1)}, u32[]{:S(2)}, u32[]{:S(2)}) collective-permute-start(bf16[128,4,128]{0,2,1:T(8,128)(2,1)S(1)} %bitcast_convert_fusion.2), channel_id=1, source_target_pairs={{0,2},{1,3},{2,0},{3,1},{4,6},{5,7},{6,4},{7,5},{8,10},{9,11},{10,... | collective-permute-start | bytes 393224 | tf_op jit(solution)/shard_map/ppermute | solution.py:50

commit v23 on v10

--- a/solution.py
+++ b/solution.py
@@ -125,7 +125,7 @@
     head_size = C // H
     heads_local = qkv_weight.shape[1] // head_size
     reach = BLOCKS
-    gathered = gather_channels(latent)
+    gathered = gather_channels(latent.reshape(ch_local, -1)).reshape(-1, lat_rows, columns)
     normed = norm_channels(gathered.astype(jnp.float32), att_gain).astype(jnp.bfloat16)
     projected = jnp.einsum("koc,crw->korw", qkv_weight, normed, preferred_element_type=jnp.float32)
     projected = projected.reshape(3, heads_local, head_size, lat_rows, columns)

time: 86.7 us -> 85.5 us (0.986)
  other arithmetic: 4.59 us -> 2.65 us
    convert_element_type x1 -> x0, other arithmetic: 1.52 us -> none  [per_device(): norm_channels(gathered.astype(jnp.float32), att_gain).astype(jnp.bfloat16)]
where the time goes in v23:
time: 85.5 us; the launch traced here: 85.2 us
  waiting for transfers between devices  39.1 us (46%)
  blocking collectives  21 us (25%)
  local copies, waits for them, and re-layouts  7.86 us (9%)
  starting transfers between devices  7.46 us (9%)
  matrix products  6.5 us (8%)
  other arithmetic  2.65 us (3%)
    ppermute x3, waiting for transfers between devices, per_device(): got = lax.ppermute(sent, 'lon', pairs)  21.7 us
    all_gather x3, blocking collectives, gather_channels(): return lax.all_gather(values, 'lev', axis=0, tiled=True)  21 us
    ppermute x3, waiting for transfers between devices, scatter_sum(): total = total + lax.ppermute(sent, axis, pairs).astype(jnp.float32)  13.8 us
    dot_general x3, matrix products, spread_sum(): lax.dot_general(weight, activation, (((0,), (0,)), ((), ())), preferred_e...  4.58 us
    ppermute x3, waiting for transfers between devices, scatter_sum(): lax.ppermute(theirs, axis, [(i, i ^ 1) for i in range(devices)])  3.68 us
    ppermute x3, starting transfers between devices, scatter_sum(): total = total + lax.ppermute(sent, axis, pairs).astype(jnp.float32)  3.35 us
    ppermute x3, starting transfers between devices, per_device(): got = lax.ppermute(sent, 'lon', pairs)  3.16 us
    another operation x2, local copies, waits for them, and re-layouts, scatter_sum(): mine = jnp.take(blocks, core, axis=1).astype(jnp.float32)  2.23 us
  transfers between devices with their start and end apart: 9, of which 8 were waited for; matrix products, arithmetic and copies ran while one was open for 4% of the time, Pallas kernels for 0%

profile of v23, /device:TPU:16, one launch (start us, length us, event | category | flops | bytes accessed | tf_op | source)
XLA Modules:
  0.0 85.2 jit_solution(5576280268845814695)
XLA Ops:
  0.0 1.1 %copy.88 = bf16[128,4,128]{0,2,1:T(8,128)(2,1)S(1)} copy(bf16[128,4,128]{2,1,0:T(4,128)(2,1)} %param.20) | data formatting | bytes 262144 | tf_op args[0]
  1.1 7.2 %all_gather.9 = bf16[512,512]{0,1:T(8,128)(2,1)S(1)} all-gather(bf16[128,512]{0,1:T(8,128)(2,1)S(1)} %bitcast.199), channel_id=1, replica_groups=mesh['member'=2,'lon'=4,'lev'=4] {'lev'}, dimensions={0}, use_global_device_ids=true | all-gather | bytes 655360 | tf_op jit(solution)/shard_map/all_gather | solution.py:34
  8.3 0.2 multiply_reduce_fusion
  8.5 0.5 convolution_bitcast_fusion.2
  9.0 0.1 slice_multiply_fusion.6
  9.2 0.1 fusion.117
  9.3 0.4 collective-permute-start.2
  9.8 0.1 fusion.120
  9.9 0.1 copy.96
  10.0 0.1 copy.97
  10.2 0.2 copy.100
  10.4 0.3 reshape.615
  10.8 2.8 %collective-permute-start.1 = (bf16[264,4,128]{2,0,1:T(8,128)(2,1)S(1)}, bf16[264,4,128]{2,0,1:T(8,128)(2,1)S(1)}, u32[]{:S(2)}, u32[]{:S(2)}) collective-permute-start(bf16[264,4,128]{2,0,1:T(8,128)(2,1)S(1)} %pad_maximum_fusion.1), channel_id=1, source_target_pairs={{0,12},{4,0},{8,4},{12,8},{1,13},{5,1},{9,5},{13,9},{2,14},{6,2},{... | collective-permute-start | bytes 811016 | tf_op jit(solution)/shard_map/ppermute | solution.py:146
  13.7 19.3 %collective-permute-done.1 = bf16[264,4,128]{2,0,1:T(8,128)(2,1)S(1)} collective-permute-done((bf16[264,4,128]{2,0,1:T(8,128)(2,1)S(1)}, bf16[264,4,128]{2,0,1:T(8,128)(2,1)S(1)}, u32[]{:S(2)}, u32[]{:S(2)}) %collective-permute-start.1) | collective-permute-done | bytes 270368 | tf_op jit(solution)/shard_map/ppermute | solution.py:146
  33.0 0.6 reshape.617
  33.6 0.1 slice_bitcast_fusion.4
  33.7 2.4 %collective-permute-done = bf16[264,4,128]{2,0,1:T(8,128)(2,1)S(1)} collective-permute-done((bf16[264,4,128]{2,0,1:T(8,128)(2,1)S(1)}, bf16[264,4,128]{2,0,1:T(8,128)(2,1)S(1)}, u32[]{:S(2)}, u32[]{:S(2)}) %collective-permute-start) | collective-permute-done | bytes 270368 | tf_op jit(solution)/shard_map/ppermute | solution.py:146
  36.1 0.6 reshape.616
  36.7 0.2 slice_bitcast_fusion.5
  37.0 0.1 pad_maximum_fusion
  37.1 0.9 %fusion = (f32[2,4,132]{2,1,0:T(4,128)S(1)}, f32[2,4,132,4,128]{4,2,3,1,0:T(8,128)S(1)}) fusion(bf16[4,2,2,64,4,128]{5,3,0,4,2,1:T(8,128)(2,1)S(1)} %pad_maximum_fusion, bf16[2,64,4,2]{3,1,2,0:T(8,128)(2,1)S(1)} %copy.114, bf16[2,64,4,128]{3,1,2,0:T(8,128)(2,1)S(1)} %fusion.103, bf16[2,64,4,2]{3,1,2,0:T(8,128)(2,1)S(1)} %copy.113), kind=kOutput, calls=%fused_computation.1 | convolution fusion | flops 70691808 | bytes 3084416 | tf_op jit(solution)/shard_map/hdri,phdrj->hripj/dot_general | solution.py:73
  38.0 0.5 fusion.34
  38.5 0.3 copy.115
  38.8 0.2 reshape.618
  38.9 0.3 fusion.2
  39.2 0.1 reshape.619
  39.4 1.1 %constant_dynamic-slice_fusion.3 = (bf16[2,1,128,528]{2,1,0,3:T(2,128)(2,1)S(1)}, bf16[2,1,128,528]{2,1,0,3:T(2,128)(2,1)S(1)}) fusion(bf16[2,2,128,528]{2,1,0,3:T(2,128)(2,1)S(1)} %reshape.619, s32[]{:T(128)S(6)} %select_n.94, s32[]{:T(128)S(6)} %select_n.96), kind=kLoop, calls=%fused_computation.169 | loop fusion | bytes 1081352 | tf_op jit(solution)/shard_map/jit(_take) | solution.py:43
  40.5 0.1 fusion.78
  40.6 0.1 collective-permute-start.3
  40.8 0.1 broadcast_multiply_fusion.5
  40.9 1.3 %collective-permute-done.3 = bf16[2,128,528]{1,2,0:T(8,128)(2,1)S(1)} collective-permute-done((bf16[2,128,528]{1,2,0:T(8,128)(2,1)S(1)}, bf16[2,128,528]{1,2,0:T(8,128)(2,1)S(1)}, u32[]{:S(2)}, u32[]{:S(2)}) %collective-permute-start.3) | collective-permute-done | bytes 270368 | tf_op jit(solution)/shard_map/ppermute | solution.py:45
  42.2 0.1 convert_add_fusion
  42.3 1.2 %collective-permute-start.4 = (bf16[128,528]{0,1:T(8,128)(2,1)S(1)}, bf16[128,528]{0,1:T(8,128)(2,1)S(1)}, u32[]{:S(2)}, u32[]{:S(2)}) collective-permute-start(bf16[128,528]{0,1:T(8,128)(2,1)S(1)} %bitcast_convert_fusion), channel_id=1, source_target_pairs={{0,2},{1,3},{2,0},{3,1},{4,6},{5,7},{6,4},{7,5},{8,10},{9,11},{10,... | collective-permute-start | bytes 405512 | tf_op jit(solution)/shard_map/ppermute | solution.py:50
  43.5 0.1 copy.106
  43.6 0.1 copy.104
  43.7 4.3 %collective-permute-done.4 = bf16[128,528]{0,1:T(8,128)(2,1)S(1)} collective-permute-done((bf16[128,528]{0,1:T(8,128)(2,1)S(1)}, bf16[128,528]{0,1:T(8,128)(2,1)S(1)}, u32[]{:S(2)}, u32[]{:S(2)}) %collective-permute-start.4) | collective-permute-done | bytes 135200 | tf_op jit(solution)/shard_map/ppermute | solution.py:50
  48.0 0.1 fusion.119
  48.1 0.2 fusion.72
  48.3 7.0 %all_gather.10 = bf16[512,4,130]{0,2,1:T(8,128)(2,1)S(1)} all-gather(bf16[128,4,130]{0,2,1:T(8,128)(2,1)S(1)} %fusion.72), channel_id=1, replica_groups=mesh['member'=2,'lon'=4,'lev'=4] {'lev'}, dimensions={0}, use_global_device_ids=true | all-gather | bytes 665600 | tf_op jit(solution)/shard_map/all_gather | solution.py:34
  55.3 0.2 fusion.4
  55.6 0.2 fusion.6
  55.8 0.1 reshape.621
  55.9 2.2 %fusion.3 = bf16[512,520]{0,1:T(8,128)(2,1)S(1)} fusion(bf16[512,520]{0,1:T(8,128)(2,1)S(1)} %reshape.621, bf16[2,512,512]{2,1,0:T(8,128)(2,1)} %param.27, bf16[2,512,512]{2,1,0:T(8,128)(2,1)} %param.26), kind=kOutput, calls=%fused_computation.16 | convolution fusion | flops 547921920 | bytes 2113536 | tf_op jit(solution)/shard_map/dot_general | solution.py:55
  58.1 0.1 reshape.622
  58.2 1.1 %constant_dynamic-slice_fusion.1 = (bf16[2,1,128,520]{2,1,0,3:T(2,128)(2,1)S(1)}, bf16[2,1,128,520]{2,1,0,3:T(2,128)(2,1)S(1)}) fusion(bf16[2,2,128,520]{2,1,0,3:T(2,128)(2,1)S(1)} %reshape.622, s32[]{:T(128)S(6)} %select_n.94, s32[]{:T(128)S(6)} %select_n.96), kind=kLoop, calls=%fused_computation.167 | loop fusion | bytes 1064968 | tf_op jit(solution)/shard_map/jit(_take) | solution.py:43
  59.4 0.4 collective-permute-start.5
  59.8 1.2 %collective-permute-done.5 = bf16[2,128,520]{1,2,0:T(8,128)(2,1)S(1)} collective-permute-done((bf16[2,128,520]{1,2,0:T(8,128)(2,1)S(1)}, bf16[2,128,520]{1,2,0:T(8,128)(2,1)S(1)}, u32[]{:S(2)}, u32[]{:S(2)}) %collective-permute-start.5) | collective-permute-done | bytes 266272 | tf_op jit(solution)/shard_map/ppermute | solution.py:45
  61.0 0.1 convert_add_fusion.1
  61.1 1.0 %collective-permute-start.6 = (bf16[128,520]{0,1:T(8,128)(2,1)S(1)}, bf16[128,520]{0,1:T(8,128)(2,1)S(1)}, u32[]{:S(2)}, u32[]{:S(2)}) collective-permute-start(bf16[128,520]{0,1:T(8,128)(2,1)S(1)} %bitcast_convert_fusion.1), channel_id=1, source_target_pairs={{0,2},{1,3},{2,0},{3,1},{4,6},{5,7},{6,4},{7,5},{8,10},{9,11},{10,... | collective-permute-start | bytes 399368 | tf_op jit(solution)/shard_map/ppermute | solution.py:50
  62.1 4.9 %collective-permute-done.6 = bf16[128,520]{0,1:T(8,128)(2,1)S(1)} collective-permute-done((bf16[128,520]{0,1:T(8,128)(2,1)S(1)}, bf16[128,520]{0,1:T(8,128)(2,1)S(1)}, u32[]{:S(2)}, u32[]{:S(2)}) %collective-permute-start.6) | collective-permute-done | bytes 133152 | tf_op jit(solution)/shard_map/ppermute | solution.py:50
  67.1 0.1 fusion.118
  67.1 0.2 fusion.91
  67.3 6.8 %all_gather.11 = bf16[512,4,128]{0,2,1:T(8,128)(2,1)S(1)} all-gather(bf16[128,4,128]{0,2,1:T(8,128)(2,1)S(1)} %fusion.91), channel_id=1, replica_groups=mesh['member'=2,'lon'=4,'lev'=4] {'lev'}, dimensions={0}, use_global_device_ids=true | all-gather | bytes 655360 | tf_op jit(solution)/shard_map/all_gather | solution.py:34
  74.1 0.2 fusion.17
  74.3 0.2 fusion.19
  74.5 2.1 %convolution_convert_fusion.2 = bf16[512,512]{0,1:T(8,128)(2,1)S(1)} fusion(bf16[512,512]{0,1:T(8,128)(2,1)S(1)} %bitcast.209, bf16[2,512,512]{2,1,0:T(8,128)(2,1)S(1)} %copy-done.5, bf16[2,512,512]{2,1,0:T(8,128)(2,1)} %param.26), kind=kOutput, calls=%fused_computation.13 | convolution fusion | flops 539492352 | bytes 2097152 | tf_op jit(solution)/shard_map/dot_general | solution.py:55
  76.7 0.4 collective-permute-start.7
  77.1 1.2 %collective-permute-done.7 = bf16[2,128,512]{2,1,0:T(8,128)(2,1)S(1)} collective-permute-done((bf16[2,128,512]{2,1,0:T(8,128)(2,1)S(1)}, bf16[2,128,512]{2,1,0:T(8,128)(2,1)S(1)}, u32[]{:S(2)}, u32[]{:S(2)}) %collective-permute-start.7) | collective-permute-done | bytes 262176 | tf_op jit(solution)/shard_map/ppermute | solution.py:45
  78.3 0.1 convert_add_fusion.2
  78.4 1.2 %collective-permute-start.8 = (bf16[128,512]{1,0:T(8,128)(2,1)S(1)}, bf16[128,512]{1,0:T(8,128)(2,1)S(1)}, u32[]{:S(2)}, u32[]{:S(2)}) collective-permute-start(bf16[128,512]{1,0:T(8,128)(2,1)S(1)} %bitcast_convert_fusion.2), channel_id=1, source_target_pairs={{0,2},{1,3},{2,0},{3,1},{4,6},{5,7},{6,4},{7,5},{8,10},{9,11},{10,... | collective-permute-start | bytes 393224 | tf_op jit(solution)/shard_map/ppermute | solution.py:50
  79.6 4.6 %collective-permute-done.8 = bf16[128,512]{1,0:T(8,128)(2,1)S(1)} collective-permute-done((bf16[128,512]{1,0:T(8,128)(2,1)S(1)}, bf16[128,512]{1,0:T(8,128)(2,1)S(1)}, u32[]{:S(2)}, u32[]{:S(2)}) %collective-permute-start.8) | collective-permute-done | bytes 131104 | tf_op jit(solution)/shard_map/ppermute | solution.py:50
  84.2 0.1 copy.121
  84.4 0.1 add_convert_fusion.2
  84.4 0.8 copy.122
  (53 shorter events, 0.8 us)
Async XLA Ops:
  0.0 8.5 %copy-start = (bf16[3,128,512]{2,1,0:T(8,128)(2,1)S(1)}, bf16[3,128,512]{2,1,0:T(8,128)(2,1)}, u32[]{:S(2)}) copy-start(bf16[3,128,512]{2,1,0:T(8,128)(2,1)} %param.22) | copy-start | bytes 1179652
  0.0 8.5 %copy-start.4 = (f32[512]{0:T(512)S(1)}, f32[512]{0:T(512)}, u32[]{:S(2)}) copy-start(f32[512]{0:T(512)} %param.21) | copy-start | bytes 6148
  9.3 27.7 %collective-permute-start.2 = (bf16[256,4,128]{2,0,1:T(8,128)(2,1)S(1)}, bf16[256,4,128]{2,0,1:T(8,128)(2,1)S(1)}, u32[]{:S(2)}, u32[]{:S(2)}) collective-permute-start(bf16[256,4,128]{2,0,1:T(8,128)(2,1)S(1)} %bitcast.202), channel_id=1, source_target_pairs={{0,8},{4,12},{8,0},{12,4},{1,9},{5,13},{9,1},{13,5},{2,10},{6,14},... | collective-permute-start | bytes 786440 | tf_op jit(solution)/shard_map/ppermute | solution.py:146
  9.8 3.8 %copy-start.2 = (f32[2,9,128]{2,0,1:T(2,128)S(1)}, f32[2,9,128]{2,0,1:T(2,128)}, u32[]{:S(2)}) copy-start(f32[2,9,128]{2,0,1:T(2,128)} %param.24) | copy-start | bytes 27652
  10.8 22.2 %collective-permute-start.1 = (bf16[264,4,128]{2,0,1:T(8,128)(2,1)S(1)}, bf16[264,4,128]{2,0,1:T(8,128)(2,1)S(1)}, u32[]{:S(2)}, u32[]{:S(2)}) collective-permute-start(bf16[264,4,128]{2,0,1:T(8,128)(2,1)S(1)} %pad_maximum_fusion.1), channel_id=1, source_target_pairs={{0,12},{4,0},{8,4},{12,8},{1,13},{5,1},{9,5},{13,9},{2,14},{6,2},{... | collective-permute-start | bytes 811016 | tf_op jit(solution)/shard_map/ppermute | solution.py:146
  13.6 22.5 %collective-permute-start = (bf16[264,4,128]{2,0,1:T(8,128)(2,1)S(1)}, bf16[264,4,128]{2,0,1:T(8,128)(2,1)S(1)}, u32[]{:S(2)}, u32[]{:S(2)}) collective-permute-start(bf16[264,4,128]{2,0,1:T(8,128)(2,1)S(1)} %pad_maximum_fusion.1), channel_id=1, source_target_pairs={{0,4},{4,8},{8,12},{12,0},{1,5},{5,9},{9,13},{13,1},{2,6},{6,10},{... | collective-permute-start | bytes 811016 | tf_op jit(solution)/shard_map/ppermute | solution.py:146
  38.0 1.0 %copy-start.1 = (bf16[128,512]{1,0:T(8,128)(2,1)S(1)}, bf16[128,512]{1,0:T(8,128)(2,1)}, u32[]{:S(2)}) copy-start(bf16[128,512]{1,0:T(8,128)(2,1)} %param.23) | copy-start | bytes 393220
  40.5 3.0 %copy-start.3 = (f32[2,512]{1,0:T(2,128)S(1)}, f32[2,512]{1,0:T(2,128)}, u32[]{:S(2)}) copy-start(f32[2,512]{1,0:T(2,128)} %param.25) | copy-start | bytes 12292
  40.6 1.6 %collective-permute-start.3 = (bf16[2,128,528]{1,2,0:T(8,128)(2,1)S(1)}, bf16[2,128,528]{1,2,0:T(8,128)(2,1)S(1)}, u32[]{:S(2)}, u32[]{:S(2)}) collective-permute-start(bf16[2,128,528]{1,2,0:T(8,128)(2,1)S(1)} %fusion.78), channel_id=1, source_target_pairs={{0,1},{1,0},{2,3},{3,2},{4,5},{5,4},{6,7},{7,6},{8,9},{9,8},{10,11... | collective-permute-start | bytes 811016 | tf_op jit(solution)/shard_map/ppermute | solution.py:45
  42.3 5.7 %collective-permute-start.4 = (bf16[128,528]{0,1:T(8,128)(2,1)S(1)}, bf16[128,528]{0,1:T(8,128)(2,1)S(1)}, u32[]{:S(2)}, u32[]{:S(2)}) collective-permute-start(bf16[128,528]{0,1:T(8,128)(2,1)S(1)} %bitcast_convert_fusion), channel_id=1, source_target_pairs={{0,2},{1,3},{2,0},{3,1},{4,6},{5,7},{6,4},{7,5},{8,10},{9,11},{10,... | collective-permute-start | bytes 405512 | tf_op jit(solution)/shard_map/ppermute | solution.py:50
  59.4 1.6 %collective-permute-start.5 = (bf16[2,128,520]{1,2,0:T(8,128)(2,1)S(1)}, bf16[2,128,520]{1,2,0:T(8,128)(2,1)S(1)}, u32[]{:S(2)}, u32[]{:S(2)}) collective-permute-start(bf16[2,128,520]{1,2,0:T(8,128)(2,1)S(1)} %fusion.80), channel_id=1, source_target_pairs={{0,1},{1,0},{2,3},{3,2},{4,5},{5,4},{6,7},{7,6},{8,9},{9,8},{10,11... | collective-permute-start | bytes 798728 | tf_op jit(solution)/shard_map/ppermute | solution.py:45
  61.1 5.9 %collective-permute-start.6 = (bf16[128,520]{0,1:T(8,128)(2,1)S(1)}, bf16[128,520]{0,1:T(8,128)(2,1)S(1)}, u32[]{:S(2)}, u32[]{:S(2)}) collective-permute-start(bf16[128,520]{0,1:T(8,128)(2,1)S(1)} %bitcast_convert_fusion.1), channel_id=1, source_target_pairs={{0,2},{1,3},{2,0},{3,1},{4,6},{5,7},{6,4},{7,5},{8,10},{9,11},{10,... | collective-permute-start | bytes 399368 | tf_op jit(solution)/shard_map/ppermute | solution.py:50
  67.3 7.2 %copy-start.5 = (bf16[2,512,512]{2,1,0:T(8,128)(2,1)S(1)}, bf16[2,512,512]{2,1,0:T(8,128)(2,1)}, u32[]{:S(2)}) copy-start(bf16[2,512,512]{2,1,0:T(8,128)(2,1)} %param.27) | copy-start | bytes 3145732
  76.7 1.6 %collective-permute-start.7 = (bf16[2,128,512]{2,1,0:T(8,128)(2,1)S(1)}, bf16[2,128,512]{2,1,0:T(8,128)(2,1)S(1)}, u32[]{:S(2)}, u32[]{:S(2)}) collective-permute-start(bf16[2,128,512]{2,1,0:T(8,128)(2,1)S(1)} %select_bitcast_fusion), channel_id=1, source_target_pairs={{0,1},{1,0},{2,3},{3,2},{4,5},{5,4},{6,7},{7,6},{8,9},{9,8},{10,11... | collective-permute-start | bytes 786440 | tf_op jit(solution)/shard_map/ppermute | solution.py:45
  78.4 5.8 %collective-permute-start.8 = (bf16[128,512]{1,0:T(8,128)(2,1)S(1)}, bf16[128,512]{1,0:T(8,128)(2,1)S(1)}, u32[]{:S(2)}, u32[]{:S(2)}) collective-permute-start(bf16[128,512]{1,0:T(8,128)(2,1)S(1)} %bitcast_convert_fusion.2), channel_id=1, source_target_pairs={{0,2},{1,3},{2,0},{3,1},{4,6},{5,7},{6,4},{7,5},{8,10},{9,11},{10,... | collective-permute-start | bytes 393224 | tf_op jit(solution)/shard_map/ppermute | solution.py:50

commit v24 on v23

--- a/solution.py
+++ b/solution.py
@@ -101,7 +101,7 @@
             else:
                 stencil_sum = stencil_sum + tap_row * shifted
     smoothed = stencil_sum.astype(jnp.bfloat16)
-    full_channels = gather_channels(smoothed)
+    full_channels = gather_channels(smoothed.reshape(smoothed.shape[0], -1)).reshape(-1, *smoothed.shape[1:])
     block_normed = norm_channels(full_channels.astype(jnp.float32), block_gain[block_index]).astype(
         jnp.bfloat16
     )

time: 85.5 us -> 84.7 us (level)
  no operation moved by 1% of the time
where the time goes in v24:
time: 84.7 us; the launch traced here: 84.5 us
  waiting for transfers between devices  39.2 us (46%)
  blocking collectives  20.9 us (25%)
  local copies, waits for them, and re-layouts  7.75 us (9%)
  starting transfers between devices  7.44 us (9%)
  matrix products  6.41 us (8%)
  other arithmetic  2.24 us (3%)
    ppermute x3, waiting for transfers between devices, per_device(): got = lax.ppermute(sent, 'lon', pairs)  21.7 us
    all_gather x3, blocking collectives, gather_channels(): return lax.all_gather(values, 'lev', axis=0, tiled=True)  20.9 us
    ppermute x3, waiting for transfers between devices, scatter_sum(): total = total + lax.ppermute(sent, axis, pairs).astype(jnp.float32)  13.8 us
    dot_general x3, matrix products, spread_sum(): lax.dot_general(weight, activation, (((0,), (0,)), ((), ())), preferred_e...  4.49 us
    ppermute x3, waiting for transfers between devices, scatter_sum(): lax.ppermute(theirs, axis, [(i, i ^ 1) for i in range(devices)])  3.69 us
    ppermute x3, starting transfers between devices, scatter_sum(): total = total + lax.ppermute(sent, axis, pairs).astype(jnp.float32)  3.34 us
    ppermute x3, starting transfers between devices, per_device(): got = lax.ppermute(sent, 'lon', pairs)  3.16 us
    another operation x2, local copies, waits for them, and re-layouts, scatter_sum(): mine = jnp.take(blocks, core, axis=1).astype(jnp.float32)  2.23 us
  transfers between devices with their start and end apart: 9, of which 8 were waited for; matrix products, arithmetic and copies ran while one was open for 4% of the time, Pallas kernels for 0%

profile of v24, /device:TPU:16, one launch (start us, length us, event | category | flops | bytes accessed | tf_op | source)
XLA Modules:
  0.0 84.5 jit_solution(3306220149589290437)
XLA Ops:
  0.0 1.1 %copy.88 = bf16[128,4,128]{0,2,1:T(8,128)(2,1)S(1)} copy(bf16[128,4,128]{2,1,0:T(4,128)(2,1)} %param.20) | data formatting | bytes 262144 | tf_op args[0]
  1.1 7.2 %all_gather.9 = bf16[512,512]{0,1:T(8,128)(2,1)S(1)} all-gather(bf16[128,512]{0,1:T(8,128)(2,1)S(1)} %bitcast.197), channel_id=1, replica_groups=mesh['member'=2,'lon'=4,'lev'=4] {'lev'}, dimensions={0}, use_global_device_ids=true | all-gather | bytes 655360 | tf_op jit(solution)/shard_map/all_gather | solution.py:34
  8.3 0.2 multiply_reduce_fusion
  8.5 0.5 convolution_bitcast_fusion.2
  9.0 0.1 slice_multiply_fusion.6
  9.2 0.1 fusion.129
  9.3 0.4 collective-permute-start.2
  9.8 0.0 copy-start.2
  9.8 0.1 fusion.132
  9.9 0.1 copy.96
  10.0 0.1 copy.97
  10.2 0.2 copy.100
  10.4 0.3 reshape.629
  10.8 2.8 %collective-permute-start.1 = (bf16[264,4,128]{2,0,1:T(8,128)(2,1)S(1)}, bf16[264,4,128]{2,0,1:T(8,128)(2,1)S(1)}, u32[]{:S(2)}, u32[]{:S(2)}) collective-permute-start(bf16[264,4,128]{2,0,1:T(8,128)(2,1)S(1)} %pad_maximum_fusion.1), channel_id=1, source_target_pairs={{0,12},{4,0},{8,4},{12,8},{1,13},{5,1},{9,5},{13,9},{2,14},{6,2},{... | collective-permute-start | bytes 811016 | tf_op jit(solution)/shard_map/ppermute | solution.py:146
  13.7 19.3 %collective-permute-done.1 = bf16[264,4,128]{2,0,1:T(8,128)(2,1)S(1)} collective-permute-done((bf16[264,4,128]{2,0,1:T(8,128)(2,1)S(1)}, bf16[264,4,128]{2,0,1:T(8,128)(2,1)S(1)}, u32[]{:S(2)}, u32[]{:S(2)}) %collective-permute-start.1) | collective-permute-done | bytes 270368 | tf_op jit(solution)/shard_map/ppermute | solution.py:146
  33.0 0.6 reshape.631
  33.6 0.1 slice_bitcast_fusion.4
  33.7 2.4 %collective-permute-done = bf16[264,4,128]{2,0,1:T(8,128)(2,1)S(1)} collective-permute-done((bf16[264,4,128]{2,0,1:T(8,128)(2,1)S(1)}, bf16[264,4,128]{2,0,1:T(8,128)(2,1)S(1)}, u32[]{:S(2)}, u32[]{:S(2)}) %collective-permute-start) | collective-permute-done | bytes 270368 | tf_op jit(solution)/shard_map/ppermute | solution.py:146
  36.1 0.6 reshape.630
  36.7 0.2 slice_bitcast_fusion.5
  37.0 0.1 pad_maximum_fusion
  37.1 0.9 %fusion = (f32[2,4,132]{2,1,0:T(4,128)S(1)}, f32[2,4,132,4,128]{4,2,3,1,0:T(8,128)S(1)}) fusion(bf16[4,2,2,64,4,128]{5,3,0,4,2,1:T(8,128)(2,1)S(1)} %pad_maximum_fusion, bf16[2,64,4,2]{3,1,2,0:T(8,128)(2,1)S(1)} %copy.114, bf16[2,64,4,128]{3,1,2,0:T(8,128)(2,1)S(1)} %fusion.115, bf16[2,64,4,2]{3,1,2,0:T(8,128)(2,1)S(1)} %copy.113), kind=kOutput, calls=%fused_computation.1 | convolution fusion | flops 70691808 | bytes 3084416 | tf_op jit(solution)/shard_map/hdri,phdrj->hripj/dot_general | solution.py:73
  38.0 0.0 copy-start.1
  38.0 0.5 fusion.34
  38.5 0.3 copy.115
  38.8 0.2 reshape.632
  38.9 0.3 fusion.2
  39.2 0.1 reshape.633
  39.4 1.1 %constant_dynamic-slice_fusion.3 = (bf16[2,1,128,528]{2,1,0,3:T(2,128)(2,1)S(1)}, bf16[2,1,128,528]{2,1,0,3:T(2,128)(2,1)S(1)}) fusion(bf16[2,2,128,528]{2,1,0,3:T(2,128)(2,1)S(1)} %reshape.633, s32[]{:T(128)S(6)} %select_n.94, s32[]{:T(128)S(6)} %select_n.96), kind=kLoop, calls=%fused_computation.173 | loop fusion | bytes 1081352 | tf_op jit(solution)/shard_map/jit(_take) | solution.py:43
  40.5 0.1 fusion.90
  40.5 0.0 copy-start.3
  40.6 0.1 collective-permute-start.3
  40.8 0.1 broadcast_multiply_fusion.5
  40.9 1.3 %collective-permute-done.3 = bf16[2,128,528]{1,2,0:T(8,128)(2,1)S(1)} collective-permute-done((bf16[2,128,528]{1,2,0:T(8,128)(2,1)S(1)}, bf16[2,128,528]{1,2,0:T(8,128)(2,1)S(1)}, u32[]{:S(2)}, u32[]{:S(2)}) %collective-permute-start.3) | collective-permute-done | bytes 270368 | tf_op jit(solution)/shard_map/ppermute | solution.py:45
  42.2 0.1 convert_add_fusion
  42.3 1.2 %collective-permute-start.4 = (bf16[128,528]{0,1:T(8,128)(2,1)S(1)}, bf16[128,528]{0,1:T(8,128)(2,1)S(1)}, u32[]{:S(2)}, u32[]{:S(2)}) collective-permute-start(bf16[128,528]{0,1:T(8,128)(2,1)S(1)} %bitcast_convert_fusion), channel_id=1, source_target_pairs={{0,2},{1,3},{2,0},{3,1},{4,6},{5,7},{6,4},{7,5},{8,10},{9,11},{10,... | collective-permute-start | bytes 405512 | tf_op jit(solution)/shard_map/ppermute | solution.py:50
  43.5 0.1 copy.106
  43.6 0.1 copy.104
  43.7 4.3 %collective-permute-done.4 = bf16[128,528]{0,1:T(8,128)(2,1)S(1)} collective-permute-done((bf16[128,528]{0,1:T(8,128)(2,1)S(1)}, bf16[128,528]{0,1:T(8,128)(2,1)S(1)}, u32[]{:S(2)}, u32[]{:S(2)}) %collective-permute-start.4) | collective-permute-done | bytes 135200 | tf_op jit(solution)/shard_map/ppermute | solution.py:50
  48.1 0.1 fusion.131
  48.1 0.2 fusion.84
  48.4 7.0 %all_gather.10 = bf16[512,520]{0,1:T(8,128)(2,1)S(1)} all-gather(bf16[128,520]{0,1:T(8,128)(2,1)S(1)} %reshape.635), channel_id=1, replica_groups=mesh['member'=2,'lon'=4,'lev'=4] {'lev'}, dimensions={0}, use_global_device_ids=true | all-gather | bytes 665600 | tf_op jit(solution)/shard_map/all_gather | solution.py:34
  55.4 0.2 fusion.6
  55.6 2.1 %fusion.3 = bf16[512,520]{0,1:T(8,128)(2,1)S(1)} fusion(bf16[512,520]{0,1:T(8,128)(2,1)S(1)} %all_gather.10, f32[512]{0:T(512)S(1)} %bitcast.213, f32[520]{0:T(1024)S(1)} %add_rsqrt_fusion, bf16[2,512,512]{2,1,0:T(8,128)(2,1)S(1)} %copy-done.5, bf16[2,512,512]{2,1,0:T(8,128)(2,1)} %param.26), kind=kOutput, calls=%fused_computation.16 | convolution fusion | flops 548986880 | bytes 2119680 | tf_op jit(solution)/shard_map/dot_general | solution.py:55
  57.7 0.1 reshape.636
  57.8 1.1 %constant_dynamic-slice_fusion.1 = (bf16[2,1,128,520]{2,1,0,3:T(2,128)(2,1)S(1)}, bf16[2,1,128,520]{2,1,0,3:T(2,128)(2,1)S(1)}) fusion(bf16[2,2,128,520]{2,1,0,3:T(2,128)(2,1)S(1)} %reshape.636, s32[]{:T(128)S(6)} %select_n.94, s32[]{:T(128)S(6)} %select_n.96), kind=kLoop, calls=%fused_computation.171 | loop fusion | bytes 1064968 | tf_op jit(solution)/shard_map/jit(_take) | solution.py:43
  59.0 0.4 collective-permute-start.5
  59.4 1.2 %collective-permute-done.5 = bf16[2,128,520]{1,2,0:T(8,128)(2,1)S(1)} collective-permute-done((bf16[2,128,520]{1,2,0:T(8,128)(2,1)S(1)}, bf16[2,128,520]{1,2,0:T(8,128)(2,1)S(1)}, u32[]{:S(2)}, u32[]{:S(2)}) %collective-permute-start.5) | collective-permute-done | bytes 266272 | tf_op jit(solution)/shard_map/ppermute | solution.py:45
  60.6 0.1 convert_add_fusion.1
  60.7 1.0 %collective-permute-start.6 = (bf16[128,520]{0,1:T(8,128)(2,1)S(1)}, bf16[128,520]{0,1:T(8,128)(2,1)S(1)}, u32[]{:S(2)}, u32[]{:S(2)}) collective-permute-start(bf16[128,520]{0,1:T(8,128)(2,1)S(1)} %bitcast_convert_fusion.1), channel_id=1, source_target_pairs={{0,2},{1,3},{2,0},{3,1},{4,6},{5,7},{6,4},{7,5},{8,10},{9,11},{10,... | collective-permute-start | bytes 399368 | tf_op jit(solution)/shard_map/ppermute | solution.py:50
  61.7 4.9 %collective-permute-done.6 = bf16[128,520]{0,1:T(8,128)(2,1)S(1)} collective-permute-done((bf16[128,520]{0,1:T(8,128)(2,1)S(1)}, bf16[128,520]{0,1:T(8,128)(2,1)S(1)}, u32[]{:S(2)}, u32[]{:S(2)}) %collective-permute-start.6) | collective-permute-done | bytes 133152 | tf_op jit(solution)/shard_map/ppermute | solution.py:50
  66.6 0.1 fusion.130
  66.7 0.2 fusion.103
  66.9 6.6 %all_gather.11 = bf16[512,512]{0,1:T(8,128)(2,1)S(1)} all-gather(bf16[128,512]{0,1:T(8,128)(2,1)S(1)} %bitcast.205), channel_id=1, replica_groups=mesh['member'=2,'lon'=4,'lev'=4] {'lev'}, dimensions={0}, use_global_device_ids=true | all-gather | bytes 655360 | tf_op jit(solution)/shard_map/all_gather | solution.py:34
  73.5 0.2 fusion.17
  73.7 2.1 %convolution_convert_fusion.2 = bf16[512,512]{0,1:T(8,128)(2,1)S(1)} fusion(bf16[512,512]{0,1:T(8,128)(2,1)S(1)} %all_gather.11, bf16[2,512,512]{2,1,0:T(8,128)(2,1)S(1)} %copy-done.5, bf16[2,512,512]{2,1,0:T(8,128)(2,1)} %param.26, f32[512]{0:T(512)S(1)} %bitcast.212, f32[512]{0:T(512)S(1)} %add_rsqrt_fusion.1), kind=kOutput, calls=%fused_computation.13 | convolution fusion | flops 540540928 | bytes 2101248 | tf_op jit(solution)/shard_map/dot_general | solution.py:55
  75.9 0.4 collective-permute-start.7
  76.3 1.2 %collective-permute-done.7 = bf16[2,128,512]{2,1,0:T(8,128)(2,1)S(1)} collective-permute-done((bf16[2,128,512]{2,1,0:T(8,128)(2,1)S(1)}, bf16[2,128,512]{2,1,0:T(8,128)(2,1)S(1)}, u32[]{:S(2)}, u32[]{:S(2)}) %collective-permute-start.7) | collective-permute-done | bytes 262176 | tf_op jit(solution)/shard_map/ppermute | solution.py:45
  77.5 0.1 convert_add_fusion.2
  77.6 1.2 %collective-permute-start.8 = (bf16[128,512]{1,0:T(8,128)(2,1)S(1)}, bf16[128,512]{1,0:T(8,128)(2,1)S(1)}, u32[]{:S(2)}, u32[]{:S(2)}) collective-permute-start(bf16[128,512]{1,0:T(8,128)(2,1)S(1)} %bitcast_convert_fusion.2), channel_id=1, source_target_pairs={{0,2},{1,3},{2,0},{3,1},{4,6},{5,7},{6,4},{7,5},{8,10},{9,11},{10,... | collective-permute-start | bytes 393224 | tf_op jit(solution)/shard_map/ppermute | solution.py:50
  78.8 4.6 %collective-permute-done.8 = bf16[128,512]{1,0:T(8,128)(2,1)S(1)} collective-permute-done((bf16[128,512]{1,0:T(8,128)(2,1)S(1)}, bf16[128,512]{1,0:T(8,128)(2,1)S(1)}, u32[]{:S(2)}, u32[]{:S(2)}) %collective-permute-start.8) | collective-permute-done | bytes 131104 | tf_op jit(solution)/shard_map/ppermute | solution.py:50
  83.5 0.1 copy.121
  83.6 0.1 add_convert_fusion.2
  83.7 0.8 copy.122
  (51 shorter events, 0.8 us)
Async XLA Ops:
  0.0 8.5 %copy-start = (bf16[3,128,512]{2,1,0:T(8,128)(2,1)S(1)}, bf16[3,128,512]{2,1,0:T(8,128)(2,1)}, u32[]{:S(2)}) copy-start(bf16[3,128,512]{2,1,0:T(8,128)(2,1)} %param.22) | copy-start | bytes 1179652
  0.0 8.5 %copy-start.4 = (f32[512]{0:T(512)S(1)}, f32[512]{0:T(512)}, u32[]{:S(2)}) copy-start(f32[512]{0:T(512)} %param.21) | copy-start | bytes 6148
  9.3 27.7 %collective-permute-start.2 = (bf16[256,4,128]{2,0,1:T(8,128)(2,1)S(1)}, bf16[256,4,128]{2,0,1:T(8,128)(2,1)S(1)}, u32[]{:S(2)}, u32[]{:S(2)}) collective-permute-start(bf16[256,4,128]{2,0,1:T(8,128)(2,1)S(1)} %bitcast.200), channel_id=1, source_target_pairs={{0,8},{4,12},{8,0},{12,4},{1,9},{5,13},{9,1},{13,5},{2,10},{6,14},... | collective-permute-start | bytes 786440 | tf_op jit(solution)/shard_map/ppermute | solution.py:146
  9.8 3.8 %copy-start.2 = (f32[2,9,128]{2,0,1:T(2,128)S(1)}, f32[2,9,128]{2,0,1:T(2,128)}, u32[]{:S(2)}) copy-start(f32[2,9,128]{2,0,1:T(2,128)} %param.24) | copy-start | bytes 27652
  10.8 22.2 %collective-permute-start.1 = (bf16[264,4,128]{2,0,1:T(8,128)(2,1)S(1)}, bf16[264,4,128]{2,0,1:T(8,128)(2,1)S(1)}, u32[]{:S(2)}, u32[]{:S(2)}) collective-permute-start(bf16[264,4,128]{2,0,1:T(8,128)(2,1)S(1)} %pad_maximum_fusion.1), channel_id=1, source_target_pairs={{0,12},{4,0},{8,4},{12,8},{1,13},{5,1},{9,5},{13,9},{2,14},{6,2},{... | collective-permute-start | bytes 811016 | tf_op jit(solution)/shard_map/ppermute | solution.py:146
  13.6 22.5 %collective-permute-start = (bf16[264,4,128]{2,0,1:T(8,128)(2,1)S(1)}, bf16[264,4,128]{2,0,1:T(8,128)(2,1)S(1)}, u32[]{:S(2)}, u32[]{:S(2)}) collective-permute-start(bf16[264,4,128]{2,0,1:T(8,128)(2,1)S(1)} %pad_maximum_fusion.1), channel_id=1, source_target_pairs={{0,4},{4,8},{8,12},{12,0},{1,5},{5,9},{9,13},{13,1},{2,6},{6,10},{... | collective-permute-start | bytes 811016 | tf_op jit(solution)/shard_map/ppermute | solution.py:146
  38.0 1.0 %copy-start.1 = (bf16[128,512]{1,0:T(8,128)(2,1)S(1)}, bf16[128,512]{1,0:T(8,128)(2,1)}, u32[]{:S(2)}) copy-start(bf16[128,512]{1,0:T(8,128)(2,1)} %param.23) | copy-start | bytes 393220
  40.5 2.9 %copy-start.3 = (f32[2,512]{1,0:T(2,128)S(1)}, f32[2,512]{1,0:T(2,128)}, u32[]{:S(2)}) copy-start(f32[2,512]{1,0:T(2,128)} %param.25) | copy-start | bytes 12292
  40.6 1.6 %collective-permute-start.3 = (bf16[2,128,528]{1,2,0:T(8,128)(2,1)S(1)}, bf16[2,128,528]{1,2,0:T(8,128)(2,1)S(1)}, u32[]{:S(2)}, u32[]{:S(2)}) collective-permute-start(bf16[2,128,528]{1,2,0:T(8,128)(2,1)S(1)} %fusion.90), channel_id=1, source_target_pairs={{0,1},{1,0},{2,3},{3,2},{4,5},{5,4},{6,7},{7,6},{8,9},{9,8},{10,11... | collective-permute-start | bytes 811016 | tf_op jit(solution)/shard_map/ppermute | solution.py:45
  42.3 5.7 %collective-permute-start.4 = (bf16[128,528]{0,1:T(8,128)(2,1)S(1)}, bf16[128,528]{0,1:T(8,128)(2,1)S(1)}, u32[]{:S(2)}, u32[]{:S(2)}) collective-permute-start(bf16[128,528]{0,1:T(8,128)(2,1)S(1)} %bitcast_convert_fusion), channel_id=1, source_target_pairs={{0,2},{1,3},{2,0},{3,1},{4,6},{5,7},{6,4},{7,5},{8,10},{9,11},{10,... | collective-permute-start | bytes 405512 | tf_op jit(solution)/shard_map/ppermute | solution.py:50
  48.1 7.5 %copy-start.5 = (bf16[2,512,512]{2,1,0:T(8,128)(2,1)S(1)}, bf16[2,512,512]{2,1,0:T(8,128)(2,1)}, u32[]{:S(2)}) copy-start(bf16[2,512,512]{2,1,0:T(8,128)(2,1)} %param.27) | copy-start | bytes 3145732
  59.0 1.6 %collective-permute-start.5 = (bf16[2,128,520]{1,2,0:T(8,128)(2,1)S(1)}, bf16[2,128,520]{1,2,0:T(8,128)(2,1)S(1)}, u32[]{:S(2)}, u32[]{:S(2)}) collective-permute-start(bf16[2,128,520]{1,2,0:T(8,128)(2,1)S(1)} %fusion.92), channel_id=1, source_target_pairs={{0,1},{1,0},{2,3},{3,2},{4,5},{5,4},{6,7},{7,6},{8,9},{9,8},{10,11... | collective-permute-start | bytes 798728 | tf_op jit(solution)/shard_map/ppermute | solution.py:45
  60.7 5.9 %collective-permute-start.6 = (bf16[128,520]{0,1:T(8,128)(2,1)S(1)}, bf16[128,520]{0,1:T(8,128)(2,1)S(1)}, u32[]{:S(2)}, u32[]{:S(2)}) collective-permute-start(bf16[128,520]{0,1:T(8,128)(2,1)S(1)} %bitcast_convert_fusion.1), channel_id=1, source_target_pairs={{0,2},{1,3},{2,0},{3,1},{4,6},{5,7},{6,4},{7,5},{8,10},{9,11},{10,... | collective-permute-start | bytes 399368 | tf_op jit(solution)/shard_map/ppermute | solution.py:50
  75.9 1.6 %collective-permute-start.7 = (bf16[2,128,512]{2,1,0:T(8,128)(2,1)S(1)}, bf16[2,128,512]{2,1,0:T(8,128)(2,1)S(1)}, u32[]{:S(2)}, u32[]{:S(2)}) collective-permute-start(bf16[2,128,512]{2,1,0:T(8,128)(2,1)S(1)} %select_bitcast_fusion), channel_id=1, source_target_pairs={{0,1},{1,0},{2,3},{3,2},{4,5},{5,4},{6,7},{7,6},{8,9},{9,8},{10,11... | collective-permute-start | bytes 786440 | tf_op jit(solution)/shard_map/ppermute | solution.py:45
  77.6 5.8 %collective-permute-start.8 = (bf16[128,512]{1,0:T(8,128)(2,1)S(1)}, bf16[128,512]{1,0:T(8,128)(2,1)S(1)}, u32[]{:S(2)}, u32[]{:S(2)}) collective-permute-start(bf16[128,512]{1,0:T(8,128)(2,1)S(1)} %bitcast_convert_fusion.2), channel_id=1, source_target_pairs={{0,2},{1,3},{2,0},{3,1},{4,6},{5,7},{6,4},{7,5},{8,10},{9,11},{10,... | collective-permute-start | bytes 393224 | tf_op jit(solution)/shard_map/ppermute | solution.py:50
